TPU v7x, 32 devices: a whole 2x2x4 slice. The times are simulated.
32 devices in a mesh: dp: 16 (over z, x, core), head: 2 (over y).
Axes of the slice: x: 2, y: 2, z: 4, core: 2. Of those that a mesh axis runs over, the one named last changes fastest.
Arguments:
- inputs: float32 [512, 96, 512], P('dp', None, 'head'), may hold values from -6 to 6
- out_grad: float32 [512, 96, 512], P('dp', None, 'head'), may hold values from -6 to 6
- modes: int32 [8, 48], P('head'), may hold values from 0 to 48
- gates: int32 [2, 512, 96], P(None, 'dp'), may hold values from 0 to 4
- query_weight: float32 [512, 512], P(None, 'head'), may hold values from -0.25 to 0.25
- mixer_weight: float32 [8, 3072, 128], P('head'), may hold values from -0.42 to 0.42
- output_weight: float32 [512, 512], P('head'), may hold values from -0.25 to 0.25
- inner_weight: float32 [512, 2048], P(None, 'head'), may hold values from -0.25 to 0.25
- outer_weight: float32 [2048, 512], P('head'), may hold values from -0.125 to 0.125
- query_momentum: float32 [512, 512], P('dp', 'head'), may hold values from -80 to 80
- query_average: float32 [512, 512], P('dp', 'head'), may hold values from -0.25 to 0.25
- mixer_momentum: float32 [8, 3072, 128], P('head', 'dp'), may hold values from -32 to 32
- mixer_average: float32 [8, 3072, 128], P('head', 'dp'), may hold values from -0.42 to 0.42
- output_momentum: float32 [512, 512], P('head', 'dp'), may hold values from -128 to 128
- output_average: float32 [512, 512], P('head', 'dp'), may hold values from -0.25 to 0.25
- inner_momentum: float32 [512, 2048], P('dp', 'head'), may hold values from -40 to 40
- inner_average: float32 [512, 2048], P('dp', 'head'), may hold values from -0.25 to 0.25
- outer_momentum: float32 [2048, 512], P('head', 'dp'), may hold values from -80 to 80
- outer_average: float32 [2048, 512], P('head', 'dp'), may hold values from -0.125 to 0.125
Outputs:
- output: float32 [512, 96, 512], P('dp', None, 'head')
- input_grad: float32 [512, 96, 512], P('dp', None, 'head')
- query_momentum_new: float32 [512, 512], P('dp', 'head')
- query_weight_new: float32 [512, 512], P('dp', 'head')
- query_average_new: float32 [512, 512], P('dp', 'head')
- mixer_momentum_new: float32 [8, 3072, 128], P('head', 'dp')
- mixer_weight_new: float32 [8, 3072, 128], P('head', 'dp')
- mixer_average_new: float32 [8, 3072, 128], P('head', 'dp')
- output_momentum_new: float32 [512, 512], P('head', 'dp')
- output_weight_new: float32 [512, 512], P('head', 'dp')
- output_average_new: float32 [512, 512], P('head', 'dp')
- inner_momentum_new: float32 [512, 2048], P('dp', 'head')
- inner_weight_new: float32 [512, 2048], P('dp', 'head')
- inner_average_new: float32 [512, 2048], P('dp', 'head')
- outer_momentum_new: float32 [2048, 512], P('head', 'dp')
- outer_weight_new: float32 [2048, 512], P('head', 'dp')
- outer_average_new: float32 [2048, 512], P('head', 'dp')
Inputs may be any that keep to these rules, and one draw needn't show every extreme that they name: `modes`: bins of the real transform of a 96-step window; a head may name a bin more than once. `gates`: number of the pool (sizes 7, 12, 14, 24, 48 in this order).
All inputs are finite; a program needn't handle non-finite values.
Results may differ from a plain program's by a relative error of at most 0.018.
Values may be sent and summed in bfloat16 or wider, within the bound.
No kernel may reach another device: no remote copies, remote signals or barrier semaphores. Data moves between devices by JAX's collectives and lax.ppermute only.
A program may use at most 192 MiB of HBM per device.

v0:
```python
import math

import jax
import jax.numpy as jnp
import numpy as np
from jax import lax
from jax.sharding import PartitionSpec as P

D = 512
FF = 2048


highest = lax.Precision.HIGHEST
pool_sizes = (7, 12, 14, 24, 48)
mixer_spread = 0.07
momentum_decay = 0.9
average_decay = 0.9


def pool_tables(length):
    tables = np.zeros((len(pool_sizes), length, length), np.float32)
    rows_all = np.arange(length)
    for pool_index, pool_width in enumerate(pool_sizes):
        lead_pad = (pool_width - 1) // 2
        for offset in range(pool_width):
            source = np.clip(rows_all - lead_pad + offset, 0, length - 1)
            tables[pool_index][rows_all, source] += np.float32(1.0 / pool_width)
    return jnp.asarray(tables)


def spectral_tables(modes, length):
    positions = jnp.arange(length, dtype=jnp.int32)
    phase = modes[:, :, None] * positions[None, None, :] % length
    angle = phase.astype(jnp.float32) * (2.0 * math.pi / length)
    cosine = jnp.cos(angle)
    sine = jnp.sin(angle)
    doubled = jnp.where((modes == 0) | (2 * modes == length), 1.0, 2.0).astype(jnp.float32) / length
    inv_cos = jnp.transpose(doubled[:, :, None] * cosine, (0, 2, 1))
    inv_sin = jnp.transpose(-doubled[:, :, None] * sine, (0, 2, 1))
    return (cosine, -sine, inv_cos, inv_sin)


def product(form, left, right):
    return jnp.einsum(form, left, right, preferred_element_type=jnp.float32)


def pool_rows(picks, pools):
    rows = jnp.zeros(picks.shape + (pools.shape[-1],), jnp.float32)
    for pool_index in range(len(pool_sizes)):
        rows = jnp.where((picks == pool_index)[..., None], pools[pool_index][None], rows)
    return rows


def trend_local(values, rows):
    return jnp.einsum("wts,wsd->wtd", rows, values, precision=highest)


def trend_back(grads, rows):
    return jnp.einsum("wts,wtd->wsd", rows, grads, precision=highest)


def mixer_block(mixer_low, head_size):
    head_count = mixer_low.shape[0]
    shaped = mixer_low.reshape(head_count, -1, head_size, 2 * head_size)
    real_part = shaped[..., :head_size]
    imag_part = shaped[..., head_size:]
    upper = jnp.concatenate([real_part, imag_part], axis=-1)
    lower = jnp.concatenate([-imag_part, real_part], axis=-1)
    return jnp.concatenate([upper, lower], axis=2)


def exact_gelu(values):
    return jax.nn.gelu(values, approximate=False)


def on_device(
    inputs,
    out_grad,
    modes,
    gates,
    query_weight,
    mixer_weight,
    output_weight,
    inner_weight,
    outer_weight,
    query_momentum,
    query_average,
    mixer_momentum,
    mixer_average,
    output_momentum,
    output_average,
    inner_momentum,
    inner_average,
    outer_momentum,
    outer_average,
):
    windows, length, local_width = inputs.shape
    head_count, mode_count = modes.shape
    head_size = local_width // head_count
    hidden_width = inner_weight.shape[1]
    head_parts = lax.axis_size("head")
    me = lax.axis_index("head")
    shifts = list(range(1, head_parts))

    def peer(shift):
        return (me + shift) % head_parts

    def swap(values, shift):
        pairs = [(j, (j + shift) % head_parts) for j in range(head_parts)]
        return lax.ppermute(values, "head", pairs)

    def rows_of(weight, block, size):
        return lax.dynamic_slice_in_dim(weight, block * size, size, 0)

    def cols_of(weight, block, size):
        return lax.dynamic_slice_in_dim(weight, block * size, size, 1)

    def gathered_product(mine, weight_low, size):
        received = {s: swap(mine, s) for s in shifts}
        total = product("wtd,de->wte", mine, rows_of(weight_low, me, size))
        for s in shifts:
            owner = (me - s) % head_parts
            total = total + product("wtd,de->wte", received[s], rows_of(weight_low, owner, size))
        return total, received

    def scattered_product(values, weight_low, size):
        sent = {
            s: swap(product("wte,ed->wtd", values, cols_of(weight_low, peer(s), size)).astype(jnp.bfloat16), s)
            for s in shifts
        }
        total = product("wte,ed->wtd", values, cols_of(weight_low, me, size))
        for s in shifts:
            total = total + sent[s].astype(jnp.float32)
        return total

    def placed_rows(parts, size, total_rows):
        out = jnp.zeros((total_rows,) + parts[0][1].shape[1:], jnp.float32)
        for block, part in parts:
            out = lax.dynamic_update_slice_in_dim(out, part, block * size, 0)
        return out

    def placed_cols(parts, size, total_cols):
        out = jnp.zeros(parts[0][1].shape[:1] + (total_cols,), jnp.float32)
        for block, part in parts:
            out = lax.dynamic_update_slice_in_dim(out, part, block * size, 1)
        return out

    model_width = local_width * head_parts
    pools = pool_tables(length)
    fwd_cos, fwd_sin, inv_cos, inv_sin = [
        one_table.astype(jnp.bfloat16) for one_table in spectral_tables(modes, length)
    ]
    query_low = query_weight.astype(jnp.bfloat16)
    output_low = output_weight.astype(jnp.bfloat16)
    inner_low = inner_weight.astype(jnp.bfloat16)
    outer_low = outer_weight.astype(jnp.bfloat16)
    inner_t = jnp.transpose(inner_low)
    query_t = jnp.transpose(query_low)
    block = mixer_block(mixer_weight.astype(jnp.bfloat16), head_size)

    def chunk_pass(inputs, out_grad, first_rows, second_rows):
        windows = inputs.shape[0]
        grad_comb = out_grad - trend_back(out_grad, second_rows)
        grad_feed_mine = grad_comb.astype(jnp.bfloat16)
        grad_feed_recv = {s: swap(grad_feed_mine, s) for s in shifts}

        inputs_mine = inputs.astype(jnp.bfloat16)
        query, inputs_recv = gathered_product(inputs_mine, query_low, local_width)
        query = query.astype(jnp.bfloat16)
        query_heads = query.reshape(windows, length, head_count, head_size)
        spectrum = jnp.concatenate(
            [
                product("hmt,wthe->whme", fwd_cos, query_heads),
                product("hmt,wthe->whme", fwd_sin, query_heads),
            ],
            axis=-1,
        ).astype(jnp.bfloat16)
        mixed = product("whmi,hmio->whmo", spectrum, block).astype(jnp.bfloat16)
        field = product("htm,whme->wthe", inv_cos, mixed[..., :head_size]) + product(
            "htm,whme->wthe", inv_sin, mixed[..., head_size:]
        )
        field = field.reshape(windows, length, local_width).astype(jnp.bfloat16)
        attended = scattered_product(field, output_low, local_width)
        resid_one = inputs + attended
        seasonal = resid_one - trend_local(resid_one, first_rows)
        seasonal_mine = seasonal.astype(jnp.bfloat16)
        pre, seasonal_recv = gathered_product(seasonal_mine, inner_low, local_width)
        activated, gelu_pull = jax.vjp(exact_gelu, pre)
        hidden = activated.astype(jnp.bfloat16)
        feed = scattered_product(hidden, outer_low, local_width)
        combined = seasonal + feed
        output = combined - trend_local(combined, second_rows)

        outer_grad_t = placed_rows(
            [(me, product("wtd,wtf->df", grad_feed_mine, hidden))]
            + [((me - s) % head_parts, product("wtd,wtf->df", grad_feed_recv[s], hidden)) for s in shifts],
            local_width,
            model_width,
        )
        grad_hidden = product("wtd,fd->wtf", grad_feed_mine, cols_of(outer_low, me, local_width))
        for s in shifts:
            grad_hidden = grad_hidden + product(
                "wtd,fd->wtf", grad_feed_recv[s], cols_of(outer_low, (me - s) % head_parts, local_width)
            )
        grad_pre = gelu_pull(grad_hidden)[0].astype(jnp.bfloat16)
        inner_grad = placed_rows(
            [(me, product("wtd,wtf->df", seasonal_mine, grad_pre))]
            + [((me - s) % head_parts, product("wtd,wtf->df", seasonal_recv[s], grad_pre)) for s in shifts],
            local_width,
            model_width,
        )
        grad_season = grad_comb + scattered_product(grad_pre, inner_t, local_width)
        grad_resid = grad_season - trend_back(grad_season, first_rows)
        grad_attend_mine = grad_resid.astype(jnp.bfloat16)
        grad_attend_recv = {s: swap(grad_attend_mine, s) for s in shifts}
        output_grad_t = placed_rows(
            [(me, product("wtd,wte->de", grad_attend_mine, field))]
            + [((me - s) % head_parts, product("wtd,wte->de", grad_attend_recv[s], field)) for s in shifts],
            local_width,
            model_width,
        )
        grad_field = product("wtd,ed->wte", grad_attend_mine, cols_of(output_low, me, local_width))
        for s in shifts:
            grad_field = grad_field + product(
                "wtd,ed->wte", grad_attend_recv[s], cols_of(output_low, (me - s) % head_parts, local_width)
            )
        grad_field = grad_field.astype(jnp.bfloat16)
        grad_field = grad_field.reshape(windows, length, head_count, head_size)
        grad_mixed = jnp.concatenate(
            [
                product("htm,wthe->whme", inv_cos, grad_field),
                product("htm,wthe->whme", inv_sin, grad_field),
            ],
            axis=-1,
        ).astype(jnp.bfloat16)
        grad_spectrum = product("whmo,hmio->whmi", grad_mixed, block).astype(jnp.bfloat16)
        grad_query = product("hmt,whme->wthe", fwd_cos, grad_spectrum[..., :head_size]) + product(
            "hmt,whme->wthe", fwd_sin, grad_spectrum[..., head_size:]
        )
        grad_query = grad_query.reshape(windows, length, local_width).astype(jnp.bfloat16)
        query_grad = placed_rows(
            [(me, product("wtd,wte->de", inputs_mine, grad_query))]
            + [((me - s) % head_parts, product("wtd,wte->de", inputs_recv[s], grad_query)) for s in shifts],
            local_width,
            model_width,
        )
        input_grad = grad_resid + scattered_product(grad_query, query_t, local_width)
        spectrum_parts = spectrum.reshape(windows, head_count, mode_count, 2, head_size)
        grad_real = grad_mixed[..., :head_size]
        grad_imag = grad_mixed[..., head_size:]
        paired = jnp.stack(
            [grad_mixed, jnp.concatenate([grad_imag, -grad_real], axis=-1)], axis=3
        )
        mixer_full = product("whmci,whmco->hmio", spectrum_parts, paired).reshape(
            head_count, mode_count * head_size, 2 * head_size
        )
        return output, input_grad, (query_grad, mixer_full, output_grad_t, inner_grad, outer_grad_t)

    chunks = 1
    span = windows // chunks
    first_all = pool_rows(gates[0], pools)
    second_all = pool_rows(gates[1], pools)
    results = [
        chunk_pass(
            inputs[c * span : (c + 1) * span],
            out_grad[c * span : (c + 1) * span],
            first_all[c * span : (c + 1) * span],
            second_all[c * span : (c + 1) * span],
        )
        for c in range(chunks)
    ]
    output = jnp.concatenate([r[0] for r in results], axis=0)
    input_grad = jnp.concatenate([r[1] for r in results], axis=0)
    query_grad, mixer_full, output_grad_t, inner_grad, outer_grad_t = [
        sum(r[2][i] for r in results[1:]) + results[0][2][i] if chunks > 1 else results[0][2][i]
        for i in range(5)
    ]

    dp_count = lax.axis_size("dp")
    dp_rank = lax.axis_index("dp")

    lanes = 128

    def lead(grad, axis_number):
        shape = grad.shape
        split = shape[:axis_number] + (dp_count, shape[axis_number] // dp_count) + shape[axis_number + 1 :]
        owned_shape = shape[:axis_number] + (shape[axis_number] // dp_count,) + shape[axis_number + 1 :]
        return jnp.moveaxis(grad.reshape(split), axis_number, 0).reshape(dp_count, -1, lanes), owned_shape

    def reduced_over_dp(grads_axes):
        laid = [lead(grad, axis_number) for grad, axis_number in grads_axes]
        joined = jnp.concatenate([flat for flat, _ in laid], axis=1)
        reduced = lax.psum_scatter(
            joined.reshape(-1, lanes), "dp", scatter_dimension=0, tiled=True
        )
        parts = []
        offset = 0
        for flat, owned_shape in laid:
            rows = flat.shape[1]
            parts.append(reduced[offset : offset + rows].reshape(owned_shape))
            offset += rows
        return parts

    inner_part, outer_part_t = reduced_over_dp([(inner_grad, 0), (outer_grad_t, 0)])
    mixer_part, output_part_t, query_part = reduced_over_dp(
        [(mixer_full, 1), (output_grad_t, 0), (query_grad, 0)]
    )
    output_part = jnp.transpose(output_part_t)
    outer_part = jnp.transpose(outer_part_t)
    token_total = windows * length * dp_count

    def owned(weight, share, axis_number):
        return lax.dynamic_slice_in_dim(weight, dp_rank * share, share, axis_number)

    def stepped(grad, momentum, average, old_weight, spread):
        rate = 0.5 * spread / math.sqrt(token_total)
        new_momentum = momentum_decay * momentum + grad
        new_weight = old_weight - rate * (grad + momentum_decay * new_momentum)
        new_average = average_decay * average + (1 - average_decay) * new_weight
        return (new_momentum, new_weight, new_average)

    query_new = stepped(
        query_part,
        query_momentum,
        query_average,
        owned(query_weight, query_momentum.shape[0], 0),
        D ** (-0.5),
    )
    mixer_new = stepped(
        mixer_part,
        mixer_momentum,
        mixer_average,
        owned(mixer_weight, mixer_momentum.shape[1], 1),
        mixer_spread,
    )
    output_new = stepped(
        output_part,
        output_momentum,
        output_average,
        owned(output_weight, output_momentum.shape[1], 1),
        D ** (-0.5),
    )
    inner_new = stepped(
        inner_part,
        inner_momentum,
        inner_average,
        owned(inner_weight, inner_momentum.shape[0], 0),
        D ** (-0.5),
    )
    outer_new = stepped(
        outer_part,
        outer_momentum,
        outer_average,
        owned(outer_weight, outer_momentum.shape[1], 1),
        FF ** (-0.5),
    )
    return (
        output,
        input_grad,
        query_new[0],
        query_new[1],
        query_new[2],
        mixer_new[0],
        mixer_new[1],
        mixer_new[2],
        output_new[0],
        output_new[1],
        output_new[2],
        inner_new[0],
        inner_new[1],
        inner_new[2],
        outer_new[0],
        outer_new[1],
        outer_new[2],
    )


def solution(mesh):
    return jax.shard_map(
        on_device,
        mesh=mesh,
        in_specs=(
            P("dp", None, "head"),
            P("dp", None, "head"),
            P("head", None),
            P(None, "dp", None),
            P(None, "head"),
            P("head", None, None),
            P("head", None),
            P(None, "head"),
            P("head", None),
            P("dp", "head"),
            P("dp", "head"),
            P("head", "dp", None),
            P("head", "dp", None),
            P("head", "dp"),
            P("head", "dp"),
            P("dp", "head"),
            P("dp", "head"),
            P("head", "dp"),
            P("head", "dp"),
        ),
        out_specs=(
            P("dp", None, "head"),
            P("dp", None, "head"),
            P("dp", "head"),
            P("dp", "head"),
            P("dp", "head"),
            P("head", "dp", None),
            P("head", "dp", None),
            P("head", "dp", None),
            P("head", "dp"),
            P("head", "dp"),
            P("head", "dp"),
            P("dp", "head"),
            P("dp", "head"),
            P("dp", "head"),
            P("head", "dp"),
            P("head", "dp"),
            P("head", "dp"),
        ),
        check_vma=False,
    )
```

profile of v0, /device:TPU:0, one launch (start us, length us, event | category | flops | bytes accessed | tf_op | source)
XLA Modules:
  0.0 446.0 jit_solution(10576309844355246182)
XLA Ops:
  7.2 3.3 convert_element_type.127
  10.5 3.0 collective-permute-start
  13.6 3.3 convert_element_type.125
  17.7 2.0 fusion.128
  19.7 4.0 slice_negate_fusion
  23.6 24.6 %collective-permute-done = bf16[32,96,256]{2,1,0:T(8,128)(2,1)} collective-permute-done((bf16[32,96,256]{2,1,0:T(8,128)(2,1)}, bf16[32,96,256]{2,1,0:T(8,128)(2,1)}, u32[]{:S(2)}, u32[]{:S(2)}) %collective-permute-start) | collective-permute-done | bytes 1572896 | tf_op jit(solution)/shard_map/ppermute | solution.py:110
  48.2 3.1 fusion.39
  51.4 3.8 copy.55
  55.2 3.9 fusion.20
  59.2 2.2 fusion.17
  63.9 3.2 fusion.43
  72.7 1.8 collective-permute-start.1
  75.4 32.8 %collective-permute-done.1 = bf16[32,96,256]{2,1,0:T(8,128)(2,1)S(1)} collective-permute-done((bf16[32,96,256]{2,1,0:T(8,128)(2,1)S(1)}, bf16[32,96,256]{2,1,0:T(8,128)(2,1)S(1)}, u32[]{:S(2)}, u32[]{:S(2)}) %collective-permute-start.1) | collective-permute-done | bytes 1572896 | tf_op jit(solution)/shard_map/ppermute | solution.py:110
  108.3 5.3 %fusion.221 = (bf16[32,96,256]{2,1,0:T(8,128)(2,1)S(1)}, f32[32,96,256]{2,1,0:T(8,128)}) fusion(f32[96,96]{0,1:T(8,128)S(1)} %copy-done.37, f32[96,96]{0,1:T(8,128)S(1)} %copy-done.38, f32[96,96]{0,1:T(8,128)S(1)} %copy-done.39, f32[96,96]{0,1:T(8,128)S(1)} %copy-done.40, f32[96,96]{0,1:T(8,128)S(1)} %copy-done.43, ...), kind=kOutput, calls=%fused_computation.289 | convolution fusion | flops 911376384 | bytes 12782592 | tf_op jit(solution)/shard_map/wts,wsd->wtd/dot_general | solution.py:55
  115.2 5.1 %fusion.222 = (bf16[32,96,256]{2,1,0:T(8,128)(2,1)S(1)}, f32[32,96,256]{2,1,0:T(8,128)}) fusion(f32[32,96,256]{2,1,0:T(8,128)S(1)} %copy-done.24, f32[96,96]{0,1:T(8,128)S(1)} %copy-done.37, f32[96,96]{0,1:T(8,128)S(1)} %copy-done.38, f32[96,96]{0,1:T(8,128)S(1)} %copy-done.39, f32[96,96]{0,1:T(8,128)S(1)} %copy-done.40, f32[96,96]{0,1:T(8,128)S(1)} %copy-done.43, ...), kind=kOutput, calls=%fused_computation.290 | convolution fusion | flops 909017088 | bytes 8064000 | tf_op jit(solution)/shard_map/wts,wtd->wsd/dot_general | solution.py:59
  122.6 6.4 %fusion.99 = f32[32,96,1024]{2,1,0:T(8,128)} fusion(bf16[32,96,256]{2,1,0:T(8,128)(2,1)S(1)} %get-tuple-element.63, bf16[1024,512]{1,0:T(8,128)(2,1)S(1)} %convert_element_type.147, s32[]{:T(128)S(6)} %select_n.115), kind=kOutput, calls=%fused_computation.140 | convolution fusion | flops 1610612736 | bytes 14680068 | tf_op jit(solution)/shard_map/wtd,fd->wtf/dot_general | solution.py:44
  129.1 1.8 fusion.106
  130.9 20.1 %collective-permute-done.2 = bf16[32,96,256]{2,1,0:T(8,128)(2,1)S(1)} collective-permute-done((bf16[32,96,256]{2,1,0:T(8,128)(2,1)S(1)}, bf16[32,96,256]{2,1,0:T(8,128)(2,1)S(1)}, u32[]{:S(2)}, u32[]{:S(2)}) %collective-permute-start.2) | collective-permute-done | bytes 1572896 | tf_op jit(solution)/shard_map/ppermute | solution.py:110
  151.0 8.0 %convert_reduce_fusion.1 = (u32[96,1024]{1,0:T(8,128)S(1)}, u32[96,1024]{1,0:T(8,128)S(1)}, f32[32,96,1024]{2,1,0:T(8,128)}) fusion(f32[32,96,1024]{2,1,0:T(8,128)S(1)} %fusion.106, bf16[32,96,256]{2,1,0:T(8,128)(2,1)S(1)} %collective-permute-done.2, bf16[512,1024]{1,0:T(8,128)(2,1)S(1)} %convert_element_type.145, s32[]{:T(128)S(6)} %select_n.117), kind=kOutput, calls=%fused_computation.6 | convolution fusion | flops 1648164864 | bytes 28049412 | tf_op jit(solution)/shard_map/wtd,de->wte/dot_general | solution.py:44
  159.0 30.3 %multiply_convert_fusion = (bf16[32,96,1024]{2,1,0:T(8,128)(2,1)}, f32[32,96,1024]{2,1,0:T(8,128)}) fusion(f32[32,96,1024]{2,1,0:T(8,128)} %get-tuple-element.62, u32[96,1024]{1,0:T(8,128)S(1)} %get-tuple-element.18, u32[96,1024]{1,0:T(8,128)S(1)} %get-tuple-element.17), kind=kLoop, calls=%fused_computation.8 | loop fusion | flops 213909504 | bytes 32243712 | tf_op jit(solution)/shard_map/convert_element_type | solution.py:189
  190.5 18.6 %add_convert_fusion = bf16[32,96,1024]{2,1,0:T(8,128)(2,1)} fusion(f32[32,96,1024]{2,1,0:T(8,128)} %get-tuple-element.35, f32[32,96,1024]{2,1,0:T(8,128)} %fusion.99, f32[32,96,1024]{2,1,0:T(8,128)} %get-tuple-element.62, bf16[32,96,256]{2,1,0:T(8,128)(2,1)} %copy-done.21, bf16[1024,512]{1,0:T(8,128)(2,1)} %copy-done.30, s32[]{:T(128)S(6)} %select_n.117), kind=kOutput, calls=%fused_computation.7 | convolution fusion | flops 1657798656 | bytes 46137348 | tf_op jit(solution)/shard_map/wtd,fd->wtf/dot_general | solution.py:44
  209.1 4.8 %convolution_convert_fusion.3 = bf16[32,96,256]{2,1,0:T(8,128)(2,1)S(1)} fusion(bf16[32,96,1024]{2,1,0:T(8,128)(2,1)} %add_convert_fusion, bf16[512,1024]{1,0:T(8,128)(2,1)} %copy-done.32, s32[]{:T(128)S(6)} %select_n.122), kind=kOutput, calls=%fused_computation.58 | convolution fusion | flops 1611399168 | bytes 8388612 | tf_op jit(solution)/shard_map/wte,ed->wtd/dot_general | solution.py:44
  215.5 1.6 broadcast.137.clone.1
  217.1 2.8 fusion.49
  219.9 1.8 fusion.104
  223.2 1.8 fusion.47
  225.1 1.8 fusion.46
  226.9 18.4 %collective-permute-done.5 = bf16[32,96,256]{2,1,0:T(8,128)(2,1)S(1)} collective-permute-done((bf16[32,96,256]{2,1,0:T(8,128)(2,1)S(1)}, bf16[32,96,256]{2,1,0:T(8,128)(2,1)S(1)}, u32[]{:S(2)}, u32[]{:S(2)}) %collective-permute-start.5) | collective-permute-done | bytes 1572896 | tf_op jit(solution)/shard_map/ppermute | solution.py:110
  245.4 5.4 %fusion.223 = (bf16[32,96,256]{2,1,0:T(8,128)(2,1)}, f32[32,96,256]{2,1,0:T(8,128)}) fusion(f32[96,96]{0,1:T(8,128)S(1)} %copy-done.37, f32[96,96]{0,1:T(8,128)S(1)} %copy-done.38, f32[96,96]{0,1:T(8,128)S(1)} %copy-done.39, f32[96,96]{0,1:T(8,128)S(1)} %copy-done.41, f32[96,96]{0,1:T(8,128)S(1)} %copy-done.44, pred[32,96]{1,0:T(8,128)(4,1)S(1)} %copy-done.74, ...), kind=kOutput, calls=%fused_computation.291 | convolution fusion | flops 911376384 | bytes 12782592 | tf_op jit(solution)/shard_map/wts,wtd->wsd/dot_general | solution.py:59
  251.6 2.8 fusion.48
  254.4 2.7 reshape_reshape.19
  257.1 2.8 reshape_reshape.18
  259.9 4.7 %pad_maximum_fusion.1 = f32[16,512,128]{2,1,0:T(8,128)} fusion(f32[16,256,128]{2,1,0:T(8,128)} %reshape_reshape.19, f32[16,256,128]{2,1,0:T(8,128)} %reshape_reshape.18), kind=kLoop, calls=%fused_computation.24 | loop fusion | flops 1048576 | bytes 8388608 | tf_op jit(solution)/shard_map/concatenate | solution.py:292
  264.6 4.4 pad_maximum_fusion.2
  269.0 2.2 fusion.51
  272.1 2.1 fusion.121
  274.2 7.3 %collective-permute-done.6 = bf16[32,96,256]{2,1,0:T(8,128)(2,1)} collective-permute-done((bf16[32,96,256]{2,1,0:T(8,128)(2,1)}, bf16[32,96,256]{2,1,0:T(8,128)(2,1)}, u32[]{:S(2)}, u32[]{:S(2)}) %collective-permute-start.6) | collective-permute-done | bytes 1572896 | tf_op jit(solution)/shard_map/ppermute | solution.py:110
  281.5 3.2 add_convert_fusion.3
  284.7 4.1 copy.66
  288.9 3.9 fusion.26
  292.8 2.2 bitcast_negate_fusion
  295.0 3.4 maximum_bitcast_fusion
  298.5 8.0 %fusion.40 = bf16[32,4,48,128]{3,0,2,1:T(8,128)(2,1)} fusion(bf16[32,4,48,128]{3,2,0,1:T(8,128)(2,1)} %get-tuple-element.39, bf16[4,48,64,64]{3,2,1,0:T(8,128)(2,1)} %get-tuple-element.37, bf16[4,48,64,64]{3,2,1,0:T(8,128)(2,1)} %get-tuple-element.36, bf16[4,48,64,128]{3,2,1,0:T(8,128)(2,1)S(1)} %bitcast.222), kind=kOutput, calls=%fused_computation.77 | convolution fusion | flops 220987392 | bytes 9437184 | tf_op jit(solution)/shard_map/whmo,hmio->whmi/dot_general | solution.py:44
  306.4 2.6 fusion.217
  312.2 2.0 convolution_bitcast_fusion.5
  314.3 2.3 convolution_bitcast_fusion.4
  317.0 3.6 fusion.50
  321.7 3.6 pad_maximum_fusion.3
  327.4 3.3 pad_maximum_fusion
  331.9 5.8 %convolution_convert_fusion.4 = bf16[32,96,256]{2,1,0:T(8,128)(2,1)} fusion(bf16[32,96,1024]{2,1,0:T(8,128)(2,1)} %get-tuple-element.34, bf16[1024,512]{1,0:T(8,128)(2,1)S(1)} %copy-done.31, s32[]{:T(128)S(6)} %select_n.122), kind=kOutput, calls=%fused_computation.59 | convolution fusion | flops 1611399168 | bytes 8388612 | tf_op jit(solution)/shard_map/wte,ed->wtd/dot_general | solution.py:44
  337.9 2.0 convolution_convert_fusion.1
  339.9 1.9 collective-permute-start.7
  341.8 1.7 constant_dynamic-slice_fusion.1
  343.5 1.6 copy.101
  345.1 2.0 constant_dynamic-slice_fusion
  347.1 1.9 copy.102
  349.1 5.3 %fusion.101 = f32[32,96,256]{2,1,0:T(8,128)S(1)} fusion(bf16[32,96,1024]{2,1,0:T(8,128)(2,1)} %get-tuple-element.34, bf16[1024,512]{1,0:T(8,128)(2,1)S(1)} %copy-done.31, s32[]{:T(128)S(6)} %select_n.115), kind=kOutput, calls=%fused_computation.142 | convolution fusion | flops 1610612736 | bytes 9961476 | tf_op jit(solution)/shard_map/wte,ed->wtd/dot_general | solution.py:44
  354.4 21.0 %collective-permute-done.3 = bf16[32,96,256]{2,1,0:T(8,128)(2,1)} collective-permute-done((bf16[32,96,256]{2,1,0:T(8,128)(2,1)}, bf16[32,96,256]{2,1,0:T(8,128)(2,1)}, u32[]{:S(2)}, u32[]{:S(2)}) %collective-permute-start.3) | collective-permute-done | bytes 1572896 | tf_op jit(solution)/shard_map/ppermute | solution.py:110
  375.4 6.7 %convolution_subtract_fusion.2 = f32[32,96,256]{2,1,0:T(8,128)} fusion(f32[32,96,256]{2,1,0:T(8,128)S(1)} %copy-done.17, f32[32,96,256]{2,1,0:T(8,128)S(1)} %fusion.101, bf16[32,96,256]{2,1,0:T(8,128)(2,1)} %collective-permute-done.3, f32[96,96]{0,1:T(8,128)S(1)} %copy-done.37, f32[96,96]{0,1:T(8,128)S(1)} %copy-done.38, f32[96,96]{0,1:T(8,128)S(1)} %copy-done.39, ...), kind=kOutput, calls=%fused_computation.41 | convolution fusion | flops 910589952 | bytes 11209728 | tf_op jit(solution)/shard_map/wts,wsd->wtd/dot_general | solution.py:55
  382.2 19.5 %collective-permute-done.7 = bf16[32,96,256]{2,1,0:T(8,128)(2,1)} collective-permute-done((bf16[32,96,256]{2,1,0:T(8,128)(2,1)}, bf16[32,96,256]{2,1,0:T(8,128)(2,1)}, u32[]{:S(2)}, u32[]{:S(2)}) %collective-permute-start.7) | collective-permute-done | bytes 1572896 | tf_op jit(solution)/shard_map/ppermute | solution.py:110
  401.7 4.0 add_add_fusion
  407.0 1.7 multiply_add_fusion.3
  409.5 23.1 %reduce-scatter.3.cloned.1.call-done = f32[896,128]{1,0:T(8,128)} async-done(((f32[14336,128]{1,0:T(8,128)}), f32[896,128]{1,0:T(8,128)}) %reduce-scatter.3.cloned.1.call-update) | async-done | bytes 458768 | tf_op jit(solution)/shard_map/reduce_scatter | solution.py:293
  435.9 2.1 multiply_add_fusion
  (225 shorter events, 33.3 us)
Async XLA Ops:
  7.2 398.6 %reduce-scatter.5.cloned.1.call-start = ((), (), s32[]{:S(2)}) async-start(), calls=%async_computation.3 | async-start | bytes 4456448 | tf_op jit(solution)/shard_map/reduce_scatter | solution.py:293
  10.5 37.7 %collective-permute-start = (bf16[32,96,256]{2,1,0:T(8,128)(2,1)}, bf16[32,96,256]{2,1,0:T(8,128)(2,1)}, u32[]{:S(2)}, u32[]{:S(2)}) collective-permute-start(bf16[32,96,256]{2,1,0:T(8,128)(2,1)} %convert_element_type.127), channel_id=1, source_target_pairs={{0,1},{1,0},{2,3},{3,2},{4,5},{5,4},{6,7},{7,6},{8,9},{9,8},{10,11... | collective-permute-start | bytes 4718600 | tf_op jit(solution)/shard_map/ppermute | solution.py:110
  13.5 34.7 %copy-start.28 = (bf16[512,256]{1,0:T(8,128)(2,1)}, bf16[512,256]{1,0:T(8,128)(2,1)S(1)}, u32[]{:S(2)}) copy-start(bf16[512,256]{1,0:T(8,128)(2,1)S(1)} %convert_element_type.126) | copy-start | bytes 786436
  17.6 50.2 %copy-start.82 = (f32[4,48]{1,0:T(4,128)}, f32[4,48]{1,0:T(4,128)S(1)}, u32[]{:S(2)}) copy-start(f32[4,48]{1,0:T(4,128)S(1)} %get-tuple-element.59) | copy-start | bytes 2308
  17.6 51.6 %copy-start.84 = (f32[4,48]{1,0:T(4,128)}, f32[4,48]{1,0:T(4,128)S(1)}, u32[]{:S(2)}) copy-start(f32[4,48]{1,0:T(4,128)S(1)} %get-tuple-element.58) | copy-start | bytes 2308
  72.6 35.7 %copy-start.15 = (f32[32,96,256]{2,1,0:T(8,128)S(1)}, f32[32,96,256]{2,1,0:T(8,128)}, u32[]{:S(2)}) copy-start(f32[32,96,256]{2,1,0:T(8,128)} %param.20) | copy-start | bytes 9437188
  72.6 35.7 %copy-start.37 = (f32[96,96]{0,1:T(8,128)S(1)}, f32[96,96]{0,1:T(8,128)}, u32[]{:S(2)}) copy-start(f32[96,96]{0,1:T(8,128)} %constant.184) | copy-start | bytes 110596
  72.6 35.7 %copy-start.38 = (f32[96,96]{0,1:T(8,128)S(1)}, f32[96,96]{0,1:T(8,128)}, u32[]{:S(2)}) copy-start(f32[96,96]{0,1:T(8,128)} %constant.182) | copy-start | bytes 110596
  72.6 35.7 %copy-start.39 = (f32[96,96]{0,1:T(8,128)S(1)}, f32[96,96]{0,1:T(8,128)}, u32[]{:S(2)}) copy-start(f32[96,96]{0,1:T(8,128)} %constant.180) | copy-start | bytes 110596
  72.6 35.7 %copy-start.40 = (f32[96,96]{0,1:T(8,128)S(1)}, f32[96,96]{0,1:T(8,128)}, u32[]{:S(2)}) copy-start(f32[96,96]{0,1:T(8,128)} %constant.178) | copy-start | bytes 110596
  72.6 35.7 %copy-start.43 = (f32[96,96]{0,1:T(8,128)S(1)}, f32[96,96]{0,1:T(8,128)}, u32[]{:S(2)}) copy-start(f32[96,96]{0,1:T(8,128)} %constant.176) | copy-start | bytes 110596
  72.7 35.6 %collective-permute-start.1 = (bf16[32,96,256]{2,1,0:T(8,128)(2,1)S(1)}, bf16[32,96,256]{2,1,0:T(8,128)(2,1)S(1)}, u32[]{:S(2)}, u32[]{:S(2)}) collective-permute-start(bf16[32,96,256]{2,1,0:T(8,128)(2,1)S(1)} %convolution_convert_fusion.5), channel_id=1, source_target_pairs={{0,1},{1,0},{2,3},{3,2},{4,5},{5,4},{6,7},{7,6},{8,9},{9,8},{10,11... | collective-permute-start | bytes 4718600 | tf_op jit(solution)/shard_map/ppermute | solution.py:110
  74.5 39.1 %copy-start.67 = (pred[32,96]{1,0:T(8,128)(4,1)}, pred[32,96]{1,0:T(8,128)(4,1)S(1)}, u32[]{:S(2)}) copy-start(pred[32,96]{1,0:T(8,128)(4,1)S(1)} %get-tuple-element.49) | copy-start | bytes 9220
  74.5 39.1 %copy-start.69 = (pred[32,96]{1,0:T(8,128)(4,1)}, pred[32,96]{1,0:T(8,128)(4,1)S(1)}, u32[]{:S(2)}) copy-start(pred[32,96]{1,0:T(8,128)(4,1)S(1)} %get-tuple-element.50) | copy-start | bytes 9220
  74.5 39.1 %copy-start.71 = (pred[32,96]{1,0:T(8,128)(4,1)}, pred[32,96]{1,0:T(8,128)(4,1)S(1)}, u32[]{:S(2)}) copy-start(pred[32,96]{1,0:T(8,128)(4,1)S(1)} %get-tuple-element.51) | copy-start | bytes 9220
  74.5 39.1 %copy-start.73 = (pred[32,96]{1,0:T(8,128)(4,1)}, pred[32,96]{1,0:T(8,128)(4,1)S(1)}, u32[]{:S(2)}) copy-start(pred[32,96]{1,0:T(8,128)(4,1)S(1)} %get-tuple-element.52) | copy-start | bytes 9220
  74.5 39.1 %copy-start.75 = (pred[32,96]{1,0:T(8,128)(4,1)}, pred[32,96]{1,0:T(8,128)(4,1)S(1)}, u32[]{:S(2)}) copy-start(pred[32,96]{1,0:T(8,128)(4,1)S(1)} %get-tuple-element.57) | copy-start | bytes 9220
  74.5 40.6 %copy-start.57 = (pred[32,96]{1,0:T(8,128)(4,1)}, pred[32,96]{1,0:T(8,128)(4,1)S(1)}, u32[]{:S(2)}) copy-start(pred[32,96]{1,0:T(8,128)(4,1)S(1)} %get-tuple-element.48) | copy-start | bytes 9220
  74.6 40.6 %copy-start.59 = (pred[32,96]{1,0:T(8,128)(4,1)}, pred[32,96]{1,0:T(8,128)(4,1)S(1)}, u32[]{:S(2)}) copy-start(pred[32,96]{1,0:T(8,128)(4,1)S(1)} %get-tuple-element.53) | copy-start | bytes 9220
  74.6 40.6 %copy-start.61 = (pred[32,96]{1,0:T(8,128)(4,1)}, pred[32,96]{1,0:T(8,128)(4,1)S(1)}, u32[]{:S(2)}) copy-start(pred[32,96]{1,0:T(8,128)(4,1)S(1)} %get-tuple-element.54) | copy-start | bytes 9220
  74.6 40.6 %copy-start.63 = (pred[32,96]{1,0:T(8,128)(4,1)}, pred[32,96]{1,0:T(8,128)(4,1)S(1)}, u32[]{:S(2)}) copy-start(pred[32,96]{1,0:T(8,128)(4,1)S(1)} %get-tuple-element.55) | copy-start | bytes 9220
  74.6 40.6 %copy-start.65 = (pred[32,96]{1,0:T(8,128)(4,1)}, pred[32,96]{1,0:T(8,128)(4,1)S(1)}, u32[]{:S(2)}) copy-start(pred[32,96]{1,0:T(8,128)(4,1)S(1)} %get-tuple-element.56) | copy-start | bytes 9220
  108.3 6.9 %copy-start.24 = (f32[32,96,256]{2,1,0:T(8,128)S(1)}, f32[32,96,256]{2,1,0:T(8,128)}, u32[]{:S(2)}) copy-start(f32[32,96,256]{2,1,0:T(8,128)} %param.21) | copy-start | bytes 9437188
  113.6 15.4 %copy-start.3 = (bf16[32,96,256]{2,1,0:T(8,128)(2,1)}, bf16[32,96,256]{2,1,0:T(8,128)(2,1)S(1)}, u32[]{:S(2)}) copy-start(bf16[32,96,256]{2,1,0:T(8,128)(2,1)S(1)} %get-tuple-element.60) | copy-start | bytes 4718596
  113.6 37.3 %collective-permute-start.2 = (bf16[32,96,256]{2,1,0:T(8,128)(2,1)S(1)}, bf16[32,96,256]{2,1,0:T(8,128)(2,1)S(1)}, u32[]{:S(2)}, u32[]{:S(2)}) collective-permute-start(bf16[32,96,256]{2,1,0:T(8,128)(2,1)S(1)} %get-tuple-element.60), channel_id=1, source_target_pairs={{0,1},{1,0},{2,3},{3,2},{4,5},{5,4},{6,7},{7,6},{8,9},{9,8},{10,11... | collective-permute-start | bytes 4718600 | tf_op jit(solution)/shard_map/ppermute | solution.py:110
  120.3 69.0 %collective-permute-start.4 = (bf16[32,96,256]{2,1,0:T(8,128)(2,1)S(1)}, bf16[32,96,256]{2,1,0:T(8,128)(2,1)S(1)}, u32[]{:S(2)}, u32[]{:S(2)}) collective-permute-start(bf16[32,96,256]{2,1,0:T(8,128)(2,1)S(1)} %get-tuple-element.63), channel_id=1, source_target_pairs={{0,1},{1,0},{2,3},{3,2},{4,5},{5,4},{6,7},{7,6},{8,9},{9,8},{10,11... | collective-permute-start | bytes 4718600 | tf_op jit(solution)/shard_map/ppermute | solution.py:110
  122.5 28.5 %copy-start.32 = (bf16[512,1024]{1,0:T(8,128)(2,1)}, bf16[512,1024]{1,0:T(8,128)(2,1)S(1)}, u32[]{:S(2)}) copy-start(bf16[512,1024]{1,0:T(8,128)(2,1)S(1)} %convert_element_type.145) | copy-start | bytes 3145732
  122.6 6.4 %copy-start.30 = (bf16[1024,512]{1,0:T(8,128)(2,1)}, bf16[1024,512]{1,0:T(8,128)(2,1)S(1)}, u32[]{:S(2)}) copy-start(bf16[1024,512]{1,0:T(8,128)(2,1)S(1)} %convert_element_type.147) | copy-start | bytes 3145732
  151.0 8.0 %copy-start.19 = (bf16[32,96,256]{2,1,0:T(8,128)(2,1)}, bf16[32,96,256]{2,1,0:T(8,128)(2,1)S(1)}, u32[]{:S(2)}) copy-start(bf16[32,96,256]{2,1,0:T(8,128)(2,1)S(1)} %collective-permute-done.2) | copy-start | bytes 4718596
  209.1 8.0 %copy-start = (bf16[32,96,1024]{2,1,0:T(8,128)(2,1)S(1)}, bf16[32,96,1024]{2,1,0:T(8,128)(2,1)}, u32[]{:S(2)}) copy-start(bf16[32,96,1024]{2,1,0:T(8,128)(2,1)} %add_convert_fusion) | copy-start | bytes 18874372
  213.9 31.3 %collective-permute-start.5 = (bf16[32,96,256]{2,1,0:T(8,128)(2,1)S(1)}, bf16[32,96,256]{2,1,0:T(8,128)(2,1)S(1)}, u32[]{:S(2)}, u32[]{:S(2)}) collective-permute-start(bf16[32,96,256]{2,1,0:T(8,128)(2,1)S(1)} %convolution_convert_fusion.3), channel_id=1, source_target_pairs={{0,1},{1,0},{2,3},{3,2},{4,5},{5,4},{6,7},{7,6},{8,9},{9,8},{10,11... | collective-permute-start | bytes 4718600 | tf_op jit(solution)/shard_map/ppermute | solution.py:110
  225.0 20.3 %copy-start.14 = (f32[32,96,256]{2,1,0:T(8,128)S(1)}, f32[32,96,256]{2,1,0:T(8,128)}, u32[]{:S(2)}) copy-start(f32[32,96,256]{2,1,0:T(8,128)} %get-tuple-element.64) | copy-start | bytes 9437188
  225.0 20.3 %copy-start.41 = (f32[96,96]{0,1:T(8,128)S(1)}, f32[96,96]{0,1:T(8,128)}, u32[]{:S(2)}) copy-start(f32[96,96]{0,1:T(8,128)} %constant.178) | copy-start | bytes 110596
  225.0 20.3 %copy-start.44 = (f32[96,96]{0,1:T(8,128)S(1)}, f32[96,96]{0,1:T(8,128)}, u32[]{:S(2)}) copy-start(f32[96,96]{0,1:T(8,128)} %constant.176) | copy-start | bytes 110596
  225.0 20.3 %copy-start.68 = (pred[32,96]{1,0:T(8,128)(4,1)S(1)}, pred[32,96]{1,0:T(8,128)(4,1)}, u32[]{:S(2)}) copy-start(pred[32,96]{1,0:T(8,128)(4,1)} %copy-done.67) | copy-start | bytes 9220
  225.0 20.3 %copy-start.70 = (pred[32,96]{1,0:T(8,128)(4,1)S(1)}, pred[32,96]{1,0:T(8,128)(4,1)}, u32[]{:S(2)}) copy-start(pred[32,96]{1,0:T(8,128)(4,1)} %copy-done.69) | copy-start | bytes 9220
  225.0 20.3 %copy-start.72 = (pred[32,96]{1,0:T(8,128)(4,1)S(1)}, pred[32,96]{1,0:T(8,128)(4,1)}, u32[]{:S(2)}) copy-start(pred[32,96]{1,0:T(8,128)(4,1)} %copy-done.71) | copy-start | bytes 9220
  225.0 20.3 %copy-start.74 = (pred[32,96]{1,0:T(8,128)(4,1)S(1)}, pred[32,96]{1,0:T(8,128)(4,1)}, u32[]{:S(2)}) copy-start(pred[32,96]{1,0:T(8,128)(4,1)} %copy-done.73) | copy-start | bytes 9220
  225.0 20.3 %copy-start.76 = (pred[32,96]{1,0:T(8,128)(4,1)S(1)}, pred[32,96]{1,0:T(8,128)(4,1)}, u32[]{:S(2)}) copy-start(pred[32,96]{1,0:T(8,128)(4,1)} %copy-done.75) | copy-start | bytes 9220
  226.9 23.8 %copy-start.18 = (f32[512,1024]{1,0:T(8,128)}, f32[512,1024]{1,0:T(8,128)S(1)}, u32[]{:S(2)}) copy-start(f32[512,1024]{1,0:T(8,128)S(1)} %fusion.46) | copy-start | bytes 6291460
  250.7 30.7 %collective-permute-start.6 = (bf16[32,96,256]{2,1,0:T(8,128)(2,1)}, bf16[32,96,256]{2,1,0:T(8,128)(2,1)}, u32[]{:S(2)}, u32[]{:S(2)}) collective-permute-start(bf16[32,96,256]{2,1,0:T(8,128)(2,1)} %get-tuple-element.65), channel_id=1, source_target_pairs={{0,1},{1,0},{2,3},{3,2},{4,5},{5,4},{6,7},{7,6},{8,9},{9,8},{10,11... | collective-permute-start | bytes 4718600 | tf_op jit(solution)/shard_map/ppermute | solution.py:110
  264.6 168.0 %reduce-scatter.3.cloned.1.call-start = ((), (), s32[]{:S(2)}) async-start(), calls=%async_computation.2 | async-start | bytes 7798784 | tf_op jit(solution)/shard_map/reduce_scatter | solution.py:293
  284.7 8.1 %copy-start.83 = (f32[4,48]{1,0:T(4,128)S(1)}, f32[4,48]{1,0:T(4,128)}, u32[]{:S(2)}) copy-start(f32[4,48]{1,0:T(4,128)} %copy-done.82) | copy-start | bytes 2308
  337.8 37.6 %collective-permute-start.3 = (bf16[32,96,256]{2,1,0:T(8,128)(2,1)}, bf16[32,96,256]{2,1,0:T(8,128)(2,1)}, u32[]{:S(2)}, u32[]{:S(2)}) collective-permute-start(bf16[32,96,256]{2,1,0:T(8,128)(2,1)} %convolution_convert_fusion.4), channel_id=1, source_target_pairs={{0,1},{1,0},{2,3},{3,2},{4,5},{5,4},{6,7},{7,6},{8,9},{9,8},{10,11... | collective-permute-start | bytes 4718600 | tf_op jit(solution)/shard_map/ppermute | solution.py:110
  339.9 61.8 %collective-permute-start.7 = (bf16[32,96,256]{2,1,0:T(8,128)(2,1)}, bf16[32,96,256]{2,1,0:T(8,128)(2,1)}, u32[]{:S(2)}, u32[]{:S(2)}) collective-permute-start(bf16[32,96,256]{2,1,0:T(8,128)(2,1)} %convolution_convert_fusion.1), channel_id=1, source_target_pairs={{0,1},{1,0},{2,3},{3,2},{4,5},{5,4},{6,7},{7,6},{8,9},{9,8},{10,11... | collective-permute-start | bytes 4718600 | tf_op jit(solution)/shard_map/ppermute | solution.py:110
  349.0 26.3 %copy-start.17 = (f32[32,96,256]{2,1,0:T(8,128)S(1)}, f32[32,96,256]{2,1,0:T(8,128)}, u32[]{:S(2)}) copy-start(f32[32,96,256]{2,1,0:T(8,128)} %get-tuple-element.61) | copy-start | bytes 9437188
  349.0 26.3 %copy-start.42 = (f32[96,96]{0,1:T(8,128)S(1)}, f32[96,96]{0,1:T(8,128)}, u32[]{:S(2)}) copy-start(f32[96,96]{0,1:T(8,128)} %constant.178) | copy-start | bytes 110596
  349.0 26.3 %copy-start.45 = (f32[96,96]{0,1:T(8,128)S(1)}, f32[96,96]{0,1:T(8,128)}, u32[]{:S(2)}) copy-start(f32[96,96]{0,1:T(8,128)} %constant.176) | copy-start | bytes 110596
  349.0 26.3 %copy-start.58 = (pred[32,96]{1,0:T(8,128)(4,1)S(1)}, pred[32,96]{1,0:T(8,128)(4,1)}, u32[]{:S(2)}) copy-start(pred[32,96]{1,0:T(8,128)(4,1)} %copy-done.57) | copy-start | bytes 9220
  349.0 26.3 %copy-start.60 = (pred[32,96]{1,0:T(8,128)(4,1)S(1)}, pred[32,96]{1,0:T(8,128)(4,1)}, u32[]{:S(2)}) copy-start(pred[32,96]{1,0:T(8,128)(4,1)} %copy-done.59) | copy-start | bytes 9220
  349.0 26.3 %copy-start.62 = (pred[32,96]{1,0:T(8,128)(4,1)S(1)}, pred[32,96]{1,0:T(8,128)(4,1)}, u32[]{:S(2)}) copy-start(pred[32,96]{1,0:T(8,128)(4,1)} %copy-done.61) | copy-start | bytes 9220
  349.1 26.3 %copy-start.64 = (pred[32,96]{1,0:T(8,128)(4,1)S(1)}, pred[32,96]{1,0:T(8,128)(4,1)}, u32[]{:S(2)}) copy-start(pred[32,96]{1,0:T(8,128)(4,1)} %copy-done.63) | copy-start | bytes 9220
  349.1 26.3 %copy-start.66 = (pred[32,96]{1,0:T(8,128)(4,1)S(1)}, pred[32,96]{1,0:T(8,128)(4,1)}, u32[]{:S(2)}) copy-start(pred[32,96]{1,0:T(8,128)(4,1)} %copy-done.65) | copy-start | bytes 9220
  375.4 26.3 %copy-start.13 = (f32[32,96,256]{2,1,0:T(8,128)S(1)}, f32[32,96,256]{2,1,0:T(8,128)}, u32[]{:S(2)}) copy-start(f32[32,96,256]{2,1,0:T(8,128)} %get-tuple-element.66) | copy-start | bytes 9437188
  401.7 7.0 %copy-start.47 = (f32[1024,32]{0,1:T(8,128)S(1)}, f32[1024,32]{0,1:T(8,128)}, u32[]{:S(2)}) copy-start(f32[1024,32]{0,1:T(8,128)} %copy.102) | copy-start | bytes 393220
  401.7 7.0 %copy-start.54 = (f32[1024,32]{0,1:T(8,128)S(1)}, f32[1024,32]{0,1:T(8,128)}, u32[]{:S(2)}) copy-start(f32[1024,32]{0,1:T(8,128)} %param.38) | copy-start | bytes 393220
  401.7 7.0 %copy-start.55 = (f32[1024,32]{0,1:T(8,128)S(1)}, f32[1024,32]{0,1:T(8,128)}, u32[]{:S(2)}) copy-start(f32[1024,32]{0,1:T(8,128)} %param.37) | copy-start | bytes 393220
  405.8 27.6 %copy-start.77 = (f32[32,256]{1,0:T(8,128)S(1)}, f32[32,256]{1,0:T(8,128)}, u32[]{:S(2)}) copy-start(f32[32,256]{1,0:T(8,128)} %param.30) | copy-start | bytes 98308
  405.8 27.7 %copy-start.78 = (f32[32,256]{1,0:T(8,128)S(1)}, f32[32,256]{1,0:T(8,128)}, u32[]{:S(2)}) copy-start(f32[32,256]{1,0:T(8,128)} %param.29) | copy-start | bytes 98308
  405.8 30.1 %copy-start.48 = (f32[4,192,128]{2,1,0:T(8,128)S(1)}, f32[4,192,128]{2,1,0:T(8,128)}, u32[]{:S(2)}) copy-start(f32[4,192,128]{2,1,0:T(8,128)} %param.32) | copy-start | bytes 1179652
  405.8 30.1 %copy-start.49 = (f32[4,192,128]{2,1,0:T(8,128)S(1)}, f32[4,192,128]{2,1,0:T(8,128)}, u32[]{:S(2)}) copy-start(f32[4,192,128]{2,1,0:T(8,128)} %param.31) | copy-start | bytes 1179652
  406.9 31.1 %copy-start.56 = (f32[256,32]{0,1:T(8,128)S(1)}, f32[256,32]{0,1:T(8,128)}, u32[]{:S(2)}) copy-start(f32[256,32]{0,1:T(8,128)} %copy.101) | copy-start | bytes 98308
  406.9 31.1 %copy-start.79 = (f32[256,32]{0,1:T(8,128)S(1)}, f32[256,32]{0,1:T(8,128)}, u32[]{:S(2)}) copy-start(f32[256,32]{0,1:T(8,128)} %param.34) | copy-start | bytes 98308
  406.9 31.1 %copy-start.80 = (f32[256,32]{0,1:T(8,128)S(1)}, f32[256,32]{0,1:T(8,128)}, u32[]{:S(2)}) copy-start(f32[256,32]{0,1:T(8,128)} %param.33) | copy-start | bytes 98308
  (34 other events, 118.8 us)
Sparse Core Ops, SparseCore 0:
  264.7 73.0 reduce-scatter.4
  341.8 90.7 reduce-scatter.2
where the time goes:
time: 453 us; the launch traced here: 446 us
  waiting for transfers between devices  167 us (37%)
  matrix products  143 us (32%)
  other arithmetic  68.9 us (15%)
  local copies, waits for them, and re-layouts  39.9 us (9%)
  between operations  15.7 us (3%)
  starting transfers between devices  11.4 us (3%)
    ppermute x8, waiting for transfers between devices, swap(): return lax.ppermute(values, 'head', pairs)  144 us
    dot_general x35, matrix products, product(): return jnp.einsum(form, left, right, preferred_element_type=jnp.float32)  121 us
    convert_element_type x1, other arithmetic, chunk_pass(): hidden = activated.astype(jnp.bfloat16)  30.3 us
    reduce_scatter x2, waiting for transfers between devices, reduced_over_dp(): lax.psum_scatter(joined.reshape(-1, lanes), 'dp', scatter_dimension=0, ti...  23.1 us
    dot_general x2, matrix products, trend_local(): return jnp.einsum('wts,wsd->wtd', rows, values, precision=highest)  12 us
    unnamed x178, local copies, waits for them, and re-layouts  12 us
    ppermute x8, starting transfers between devices, swap(): return lax.ppermute(values, 'head', pairs)  11.4 us
    dot_general x2, matrix products, trend_back(): return jnp.einsum('wts,wtd->wsd', rows, grads, precision=highest)  10.5 us
  transfers between devices with their start and end apart: 10, of which 8 were waited for; matrix products, arithmetic and copies ran while one was open for 40% of the time, Pallas kernels for 0%

commit v1 on v0

--- a/solution.py
+++ b/solution.py
@@ -44,19 +44,49 @@
     return jnp.einsum(form, left, right, preferred_element_type=jnp.float32)
 
 
-def pool_rows(picks, pools):
-    rows = jnp.zeros(picks.shape + (pools.shape[-1],), jnp.float32)
-    for pool_index in range(len(pool_sizes)):
-        rows = jnp.where((picks == pool_index)[..., None], pools[pool_index][None], rows)
-    return rows
+def pool_counts(length):
+    counts = np.zeros((len(pool_sizes), length, length), np.float32)
+    rows_all = np.arange(length)
+    for pool_index, pool_width in enumerate(pool_sizes):
+        lead_pad = (pool_width - 1) // 2
+        for offset in range(pool_width):
+            source = np.clip(rows_all - lead_pad + offset, 0, length - 1)
+            counts[pool_index][rows_all, source] += 1.0
+    return counts
+
+
+def pool_rows(picks, length):
+    counts = pool_counts(length)
+    rows = jnp.zeros(picks.shape + (length,), jnp.float32)
+    scale = jnp.zeros(picks.shape, jnp.float32)
+    for pool_index, pool_width in enumerate(pool_sizes):
+        chosen = picks == pool_index
+        rows = jnp.where(chosen[..., None], jnp.asarray(counts[pool_index])[None], rows)
+        scale = jnp.where(chosen, np.float32(1.0 / pool_width), scale)
+    return rows.astype(jnp.bfloat16), scale
+
+
+def split_three(values):
+    high = values.astype(jnp.bfloat16)
+    rest = values - high.astype(jnp.float32)
+    middle = rest.astype(jnp.bfloat16)
+    low = (rest - middle.astype(jnp.float32)).astype(jnp.bfloat16)
+    return high, middle, low
 
 
 def trend_local(values, rows):
-    return jnp.einsum("wts,wsd->wtd", rows, values, precision=highest)
+    counts, scale = rows
+    parts = jnp.concatenate(split_three(values), axis=1)
+    tiled = jnp.concatenate([counts] * 3, axis=2)
+    summed = jnp.einsum("wts,wsd->wtd", tiled, parts, preferred_element_type=jnp.float32)
+    return summed * scale[..., None]
 
 
 def trend_back(grads, rows):
-    return jnp.einsum("wts,wtd->wsd", rows, grads, precision=highest)
+    counts, scale = rows
+    parts = jnp.concatenate(split_three(grads * scale[..., None]), axis=1)
+    tiled = jnp.concatenate([counts] * 3, axis=1)
+    return jnp.einsum("wts,wtd->wsd", tiled, parts, preferred_element_type=jnp.float32)
 
 
 def mixer_block(mixer_low, head_size):
@@ -162,10 +192,11 @@
         windows = inputs.shape[0]
         grad_comb = out_grad - trend_back(out_grad, second_rows)
         grad_feed_mine = grad_comb.astype(jnp.bfloat16)
-        grad_feed_recv = {s: swap(grad_feed_mine, s) for s in shifts}
 
         inputs_mine = inputs.astype(jnp.bfloat16)
         query, inputs_recv = gathered_product(inputs_mine, query_low, local_width)
+        grad_feed_mine, _ = lax.optimization_barrier((grad_feed_mine, tuple(inputs_recv.values())))
+        grad_feed_recv = {s: swap(grad_feed_mine, s) for s in shifts}
         query = query.astype(jnp.bfloat16)
         query_heads = query.reshape(windows, length, head_count, head_size)
         spectrum = jnp.concatenate(
@@ -180,6 +211,7 @@
             "htm,whme->wthe", inv_sin, mixed[..., head_size:]
         )
         field = field.reshape(windows, length, local_width).astype(jnp.bfloat16)
+        field, _ = lax.optimization_barrier((field, tuple(grad_feed_recv.values())))
         attended = scattered_product(field, output_low, local_width)
         resid_one = inputs + attended
         seasonal = resid_one - trend_local(resid_one, first_rows)
@@ -258,14 +290,14 @@
 
     chunks = 1
     span = windows // chunks
-    first_all = pool_rows(gates[0], pools)
-    second_all = pool_rows(gates[1], pools)
+    first_all = pool_rows(gates[0], length)
+    second_all = pool_rows(gates[1], length)
     results = [
         chunk_pass(
             inputs[c * span : (c + 1) * span],
             out_grad[c * span : (c + 1) * span],
-            first_all[c * span : (c + 1) * span],
-            second_all[c * span : (c + 1) * span],
+            tuple(part[c * span : (c + 1) * span] for part in first_all),
+            tuple(part[c * span : (c + 1) * span] for part in second_all),
         )
         for c in range(chunks)
     ]

time: 453 us -> 476 us (1.051)
  waiting for transfers between devices: 167 us -> 194 us
  other arithmetic: 68.9 us -> 76 us
  matrix products: 143 us -> 136 us
  local copies, waits for them, and re-layouts: 39.9 us -> 33.7 us
    ppermute x8, waiting for transfers between devices: 144 us -> 173 us  [swap(): return lax.ppermute(values, 'head', pairs)]
    dot_general x4, matrix products: 22.5 us -> 14.2 us  [the longest x2 7.8 us: trend_back(): jnp.einsum('wts,wtd->wsd', tiled, parts, preferred_element_type=jnp.float32)]
    convert_element_type x0 -> x2, other arithmetic: none -> 6.19 us  [the longest x1 3.61 us: pool_rows(): return (rows.astype(jnp.bfloat16), scale)]
    unnamed x178 -> x148, local copies, waits for them, and re-layouts: 12 us -> 6.17 us
  transfers between devices with their start and end apart: 10 -> 10, of which waited for: 8 -> 9; matrix products, arithmetic and copies ran while one was open for 40% -> 31% of each run, Pallas kernels for 0% -> 0%
where the time goes in v1:
time: 476 us; the launch traced here: 467 us
  waiting for transfers between devices  194 us (41%)
  matrix products  136 us (29%)
  other arithmetic  76 us (16%)
  local copies, waits for them, and re-layouts  33.7 us (7%)
  between operations  15.3 us (3%)
  starting transfers between devices  11.4 us (2%)
    ppermute x8, waiting for transfers between devices, swap(): return lax.ppermute(values, 'head', pairs)  173 us
    dot_general x35, matrix products, product(): return jnp.einsum(form, left, right, preferred_element_type=jnp.float32)  122 us
    convert_element_type x1, other arithmetic, chunk_pass(): hidden = activated.astype(jnp.bfloat16)  30.3 us
    reduce_scatter x2, waiting for transfers between devices, reduced_over_dp(): lax.psum_scatter(joined.reshape(-1, lanes), 'dp', scatter_dimension=0, ti...  21.4 us
    ppermute x8, starting transfers between devices, swap(): return lax.ppermute(values, 'head', pairs)  11.3 us
  transfers between devices with their start and end apart: 10, of which 9 were waited for; matrix products, arithmetic and copies ran while one was open for 31% of the time, Pallas kernels for 0%

profile of v1, /device:TPU:0, one launch (start us, length us, event | category | flops | bytes accessed | tf_op | source)
XLA Modules:
  0.0 466.8 jit_solution(7788459377333348312)
XLA Ops:
  7.2 3.3 convert_element_type.193
  10.6 3.0 collective-permute-start
  13.7 3.3 convert_element_type.191
  19.1 3.6 fusion.153
  22.8 3.6 select_convert_fusion
  26.4 2.6 multiply_convert_fusion.2
  29.0 3.9 slice_negate_fusion
  33.0 3.9 fusion.248
  36.9 11.4 %collective-permute-done = bf16[32,96,256]{2,1,0:T(8,128)(2,1)} collective-permute-done((bf16[32,96,256]{2,1,0:T(8,128)(2,1)}, bf16[32,96,256]{2,1,0:T(8,128)(2,1)}, u32[]{:S(2)}, u32[]{:S(2)}) %collective-permute-start) | collective-permute-done | bytes 1572896 | tf_op jit(solution)/shard_map/ppermute | solution.py:140
  48.3 3.1 fusion.87
  51.4 3.8 copy.64
  55.3 3.9 fusion.68
  59.3 2.2 fusion.65
  61.5 1.8 collective-permute-start.1
  64.2 3.6 fusion.91
  71.6 25.5 %collective-permute-done.1 = bf16[32,96,256]{2,1,0:T(8,128)(2,1)S(1)} collective-permute-done((bf16[32,96,256]{2,1,0:T(8,128)(2,1)S(1)}, bf16[32,96,256]{2,1,0:T(8,128)(2,1)S(1)}, u32[]{:S(2)}, u32[]{:S(2)}) %collective-permute-start.1) | collective-permute-done | bytes 1572896 | tf_op jit(solution)/shard_map/ppermute | solution.py:140
  98.0 1.5 collective-permute-start.2
  99.5 33.2 %collective-permute-done.2 = bf16[32,96,256]{2,1,0:T(8,128)(2,1)S(1)} collective-permute-done((bf16[32,96,256]{2,1,0:T(8,128)(2,1)S(1)}, bf16[32,96,256]{2,1,0:T(8,128)(2,1)S(1)}, u32[]{:S(2)}, u32[]{:S(2)}) %collective-permute-start.2) | collective-permute-done | bytes 1572896 | tf_op jit(solution)/shard_map/ppermute | solution.py:140
  133.9 3.2 fusion.108
  139.4 6.4 %fusion.116 = f32[32,96,1024]{2,1,0:T(8,128)} fusion(bf16[32,96,256]{2,1,0:T(8,128)(2,1)S(1)} %collective-permute-done.1, bf16[1024,512]{1,0:T(8,128)(2,1)S(1)} %convert_element_type.226, s32[]{:T(128)S(6)} %select_n.188), kind=kOutput, calls=%fused_computation.153 | convolution fusion | flops 1610612736 | bytes 14680068 | tf_op jit(solution)/shard_map/wtd,fd->wtf/dot_general | solution.py:44
  145.8 1.8 fusion.127
  147.6 23.3 %collective-permute-done.3 = bf16[32,96,256]{2,1,0:T(8,128)(2,1)S(1)} collective-permute-done((bf16[32,96,256]{2,1,0:T(8,128)(2,1)S(1)}, bf16[32,96,256]{2,1,0:T(8,128)(2,1)S(1)}, u32[]{:S(2)}, u32[]{:S(2)}) %collective-permute-start.3) | collective-permute-done | bytes 1572896 | tf_op jit(solution)/shard_map/ppermute | solution.py:140
  170.9 8.4 %convert_reduce_fusion.1 = (u32[96,1024]{1,0:T(8,128)S(1)}, u32[96,1024]{1,0:T(8,128)S(1)}, f32[32,96,1024]{2,1,0:T(8,128)}) fusion(f32[32,96,1024]{2,1,0:T(8,128)S(1)} %fusion.127, bf16[32,96,256]{2,1,0:T(8,128)(2,1)S(1)} %collective-permute-done.3, bf16[512,1024]{1,0:T(8,128)(2,1)S(1)} %convert_element_type.224, s32[]{:T(128)S(6)} %select_n.188), kind=kOutput, calls=%fused_computation.6 | convolution fusion | flops 1648164864 | bytes 28049412 | tf_op jit(solution)/shard_map/wtd,de->wte/dot_general | solution.py:44
  179.3 30.3 %multiply_convert_fusion = (bf16[32,96,1024]{2,1,0:T(8,128)(2,1)}, f32[32,96,1024]{2,1,0:T(8,128)}) fusion(f32[32,96,1024]{2,1,0:T(8,128)} %get-tuple-element.91, u32[96,1024]{1,0:T(8,128)S(1)} %get-tuple-element.22, u32[96,1024]{1,0:T(8,128)S(1)} %get-tuple-element.21), kind=kLoop, calls=%fused_computation.8 | loop fusion | flops 213909504 | bytes 32243712 | tf_op jit(solution)/shard_map/convert_element_type | solution.py:221
  209.6 18.3 %add_convert_fusion = bf16[32,96,1024]{2,1,0:T(8,128)(2,1)} fusion(f32[32,96,1024]{2,1,0:T(8,128)} %get-tuple-element.39, f32[32,96,1024]{2,1,0:T(8,128)} %fusion.116, f32[32,96,1024]{2,1,0:T(8,128)} %get-tuple-element.91, bf16[32,96,256]{2,1,0:T(8,128)(2,1)} %get-tuple-element.19, bf16[1024,512]{1,0:T(8,128)(2,1)} %copy-done.23, s32[]{:T(128)S(6)} %select_n.186), kind=kOutput, calls=%fused_computation.7 | convolution fusion | flops 1657798656 | bytes 46137348 | tf_op jit(solution)/shard_map/wtd,fd->wtf/dot_general | solution.py:44
  228.0 4.8 %convolution_convert_fusion.3 = bf16[32,96,256]{2,1,0:T(8,128)(2,1)S(1)} fusion(bf16[32,96,1024]{2,1,0:T(8,128)(2,1)} %add_convert_fusion, bf16[512,1024]{1,0:T(8,128)(2,1)} %copy-done.25, s32[]{:T(128)S(6)} %select_n.203), kind=kOutput, calls=%fused_computation.114 | convolution fusion | flops 1611399168 | bytes 8388612 | tf_op jit(solution)/shard_map/wte,ed->wtd/dot_general | solution.py:44
  233.9 1.6 broadcast.229.clone.1
  235.4 2.8 fusion.97
  239.6 1.8 fusion.95
  241.5 1.8 fusion.94
  243.3 22.6 %collective-permute-done.5 = bf16[32,96,256]{2,1,0:T(8,128)(2,1)S(1)} collective-permute-done((bf16[32,96,256]{2,1,0:T(8,128)(2,1)S(1)}, bf16[32,96,256]{2,1,0:T(8,128)(2,1)S(1)}, u32[]{:S(2)}, u32[]{:S(2)}) %collective-permute-start.5) | collective-permute-done | bytes 1572896 | tf_op jit(solution)/shard_map/ppermute | solution.py:140
  265.9 2.4 multiply_convert_fusion.1
  268.3 3.9 fusion.249
  272.9 2.8 fusion.96
  275.7 2.7 reshape_reshape.19
  278.4 2.7 reshape_reshape.18
  281.2 4.6 pad_maximum_fusion.1
  285.9 4.4 pad_maximum_fusion.2
  290.3 2.2 fusion.110
  293.3 2.1 fusion.147
  295.4 9.3 %collective-permute-done.6 = bf16[32,96,256]{2,1,0:T(8,128)(2,1)} collective-permute-done((bf16[32,96,256]{2,1,0:T(8,128)(2,1)}, bf16[32,96,256]{2,1,0:T(8,128)(2,1)}, u32[]{:S(2)}, u32[]{:S(2)}) %collective-permute-start.6) | collective-permute-done | bytes 1572896 | tf_op jit(solution)/shard_map/ppermute | solution.py:140
  304.7 3.3 add_convert_fusion.3
  308.0 4.3 copy.75
  312.3 3.9 fusion.74
  316.2 2.2 bitcast_negate_fusion
  318.4 3.4 maximum_bitcast_fusion
  321.8 7.9 %fusion.88 = bf16[32,4,48,128]{3,0,2,1:T(8,128)(2,1)} fusion(bf16[32,4,48,128]{3,2,0,1:T(8,128)(2,1)} %get-tuple-element.67, bf16[4,48,64,64]{3,2,1,0:T(8,128)(2,1)} %get-tuple-element.65, bf16[4,48,64,64]{3,2,1,0:T(8,128)(2,1)} %get-tuple-element.64, bf16[4,48,64,128]{3,2,1,0:T(8,128)(2,1)S(1)} %bitcast.243), kind=kOutput, calls=%fused_computation.133 | convolution fusion | flops 220987392 | bytes 9437184 | tf_op jit(solution)/shard_map/whmo,hmio->whmi/dot_general | solution.py:44
  329.7 2.7 fusion.244
  335.6 2.1 convolution_bitcast_fusion.5
  337.8 2.2 convolution_bitcast_fusion.4
  340.3 3.6 fusion.109
  345.0 3.4 pad_maximum_fusion.3
  350.5 3.3 pad_maximum_fusion
  355.0 5.8 %convolution_convert_fusion.4 = bf16[32,96,256]{2,1,0:T(8,128)(2,1)} fusion(bf16[32,96,1024]{2,1,0:T(8,128)(2,1)} %get-tuple-element.38, bf16[1024,512]{1,0:T(8,128)(2,1)S(1)} %copy-done.24, s32[]{:T(128)S(6)} %select_n.203), kind=kOutput, calls=%fused_computation.115 | convolution fusion | flops 1611399168 | bytes 8388612 | tf_op jit(solution)/shard_map/wte,ed->wtd/dot_general | solution.py:44
  363.0 2.1 constant_dynamic-slice_fusion
  367.1 1.6 collective-permute-start.7
  368.7 29.7 %collective-permute-done.4 = bf16[32,96,256]{2,1,0:T(8,128)(2,1)} collective-permute-done((bf16[32,96,256]{2,1,0:T(8,128)(2,1)}, bf16[32,96,256]{2,1,0:T(8,128)(2,1)}, u32[]{:S(2)}, u32[]{:S(2)}) %collective-permute-start.4) | collective-permute-done | bytes 1572896 | tf_op jit(solution)/shard_map/ppermute | solution.py:140
  398.4 6.8 %fusion.242 = (bf16[32,96,256]{2,1,0:T(8,128)(2,1)S(1)}, bf16[32,96,256]{2,1,0:T(8,128)(2,1)S(1)}, bf16[32,96,256]{2,1,0:T(8,128)(2,1)S(1)}, f32[32,96,256]{2,1,0:T(8,128)S(1)}) fusion(bf16[32,96,256]{2,1,0:T(8,128)(2,1)} %collective-permute-done.4, bf16[32,96,1024]{2,1,0:T(8,128)(2,1)} %get-tuple-element.38, bf16[1024,512]{1,0:T(8,128)(2,1)S(1)} %copy-done.24, ...), kind=kOutput, calls=%fused_computation.302 | convolution fusion | flops 1620049920 | bytes 22560772 | tf_op jit(solution)/shard_map/wte,ed->wtd/dot_general | solution.py:44
  405.2 3.2 multiply_subtract_fusion
  408.4 17.6 %collective-permute-done.7 = bf16[32,96,256]{2,1,0:T(8,128)(2,1)S(1)} collective-permute-done((bf16[32,96,256]{2,1,0:T(8,128)(2,1)S(1)}, bf16[32,96,256]{2,1,0:T(8,128)(2,1)S(1)}, u32[]{:S(2)}, u32[]{:S(2)}) %collective-permute-start.7) | collective-permute-done | bytes 1572896 | tf_op jit(solution)/shard_map/ppermute | solution.py:140
  426.1 2.6 add_add_fusion
  429.9 1.7 multiply_add_fusion.3
  432.3 21.4 %reduce-scatter.3.cloned.1.call-done = f32[896,128]{1,0:T(8,128)} async-done(((f32[14336,128]{1,0:T(8,128)}), f32[896,128]{1,0:T(8,128)}) %reduce-scatter.3.cloned.1.call-update) | async-done | bytes 458768 | tf_op jit(solution)/shard_map/reduce_scatter | solution.py:325
  457.0 2.1 multiply_add_fusion
  (197 shorter events, 33.0 us)
Async XLA Ops:
  7.2 6.4 %copy-start.43 = (f32[512,256]{1,0:T(8,128)S(1)}, f32[512,256]{1,0:T(8,128)}, u32[]{:S(2)}) copy-start(f32[512,256]{1,0:T(8,128)} %param.33) | copy-start | bytes 1572868
  7.2 421.5 %reduce-scatter.5.cloned.1.call-start = ((), (), s32[]{:S(2)}) async-start(), calls=%async_computation.3 | async-start | bytes 4456448 | tf_op jit(solution)/shard_map/reduce_scatter | solution.py:325
  10.6 37.7 %collective-permute-start = (bf16[32,96,256]{2,1,0:T(8,128)(2,1)}, bf16[32,96,256]{2,1,0:T(8,128)(2,1)}, u32[]{:S(2)}, u32[]{:S(2)}) collective-permute-start(bf16[32,96,256]{2,1,0:T(8,128)(2,1)} %convert_element_type.193), channel_id=1, source_target_pairs={{0,1},{1,0},{2,3},{3,2},{4,5},{5,4},{6,7},{7,6},{8,9},{9,8},{10,11... | collective-permute-start | bytes 4718600 | tf_op jit(solution)/shard_map/ppermute | solution.py:140
  13.6 34.7 %copy-start.34 = (bf16[512,256]{1,0:T(8,128)(2,1)}, bf16[512,256]{1,0:T(8,128)(2,1)S(1)}, u32[]{:S(2)}) copy-start(bf16[512,256]{1,0:T(8,128)(2,1)S(1)} %convert_element_type.192) | copy-start | bytes 786436
  13.6 4.0 copy-start.58
  13.7 4.6 copy-start.38
  17.0 5.8 %copy-start.59 = (bf16[96,96]{0,1:T(8,128)(2,1)S(1)}, bf16[96,96]{0,1:T(8,128)(2,1)}, u32[]{:S(2)}) copy-start(bf16[96,96]{0,1:T(8,128)(2,1)} %constant.454) | copy-start | bytes 55300
  17.0 5.8 %copy-start.60 = (bf16[96,96]{0,1:T(8,128)(2,1)S(1)}, bf16[96,96]{0,1:T(8,128)(2,1)}, u32[]{:S(2)}) copy-start(bf16[96,96]{0,1:T(8,128)(2,1)} %constant.455) | copy-start | bytes 55300
  17.0 5.7 %copy-start.61 = (bf16[96,96]{0,1:T(8,128)(2,1)S(1)}, bf16[96,96]{0,1:T(8,128)(2,1)}, u32[]{:S(2)}) copy-start(bf16[96,96]{0,1:T(8,128)(2,1)} %constant.456) | copy-start | bytes 55300
  18.3 8.2 %copy-start.52 = (f32[32,96]{1,0:T(8,128)}, f32[32,96]{1,0:T(8,128)S(1)}, u32[]{:S(2)}) copy-start(f32[32,96]{1,0:T(8,128)S(1)} %get-tuple-element.78) | copy-start | bytes 36868
  18.3 4.5 copy-start.63
  18.3 4.5 copy-start.64
  18.3 4.5 copy-start.65
  18.3 4.5 copy-start.66
  18.3 4.5 copy-start.67
  18.3 4.5 copy-start.68
  18.3 4.5 copy-start.69
  18.3 4.5 copy-start.70
  26.4 6.6 %copy-start.39 = (bf16[32,96,96]{1,2,0:T(8,128)(2,1)}, bf16[32,96,96]{1,2,0:T(8,128)(2,1)S(1)}, u32[]{:S(2)}) copy-start(bf16[32,96,96]{1,2,0:T(8,128)(2,1)S(1)} %get-tuple-element.77) | copy-start | bytes 1769476
  29.0 4.0 copy-start.30
  33.0 15.3 %copy-start.9 = (f32[256,32,96]{0,2,1:T(8,128)S(1)}, f32[256,32,96]{0,2,1:T(8,128)}, u32[]{:S(2)}) copy-start(f32[256,32,96]{0,2,1:T(8,128)} %fusion.153) | copy-start | bytes 9437188
  55.3 6.2 %copy-start.19 = (bf16[32,96,256]{2,1,0:T(8,128)(2,1)S(1)}, bf16[32,96,256]{2,1,0:T(8,128)(2,1)}, u32[]{:S(2)}) copy-start(bf16[32,96,256]{2,1,0:T(8,128)(2,1)} %get-tuple-element.19) | copy-start | bytes 4718596
  59.2 4.9 %copy-start.5 = (bf16[4,32,64,48]{2,3,1,0:T(8,128)(2,1)}, bf16[4,32,64,48]{2,3,1,0:T(8,128)(2,1)S(1)}, u32[]{:S(2)}) copy-start(bf16[4,32,64,48]{2,3,1,0:T(8,128)(2,1)S(1)} %fusion.68) | copy-start | bytes 2359300
  59.2 4.9 %copy-start.32 = (bf16[4,48,64,64]{3,2,1,0:T(8,128)(2,1)S(1)}, bf16[4,48,64,64]{3,2,1,0:T(8,128)(2,1)}, u32[]{:S(2)}) copy-start(bf16[4,48,64,64]{3,2,1,0:T(8,128)(2,1)} %get-tuple-element.65) | copy-start | bytes 4718596
  61.5 35.6 %collective-permute-start.1 = (bf16[32,96,256]{2,1,0:T(8,128)(2,1)S(1)}, bf16[32,96,256]{2,1,0:T(8,128)(2,1)S(1)}, u32[]{:S(2)}, u32[]{:S(2)}) collective-permute-start(bf16[32,96,256]{2,1,0:T(8,128)(2,1)S(1)} %copy-done.19), channel_id=1, source_target_pairs={{0,1},{1,0},{2,3},{3,2},{4,5},{5,4},{6,7},{7,6},{8,9},{9,8},{10,11... | collective-permute-start | bytes 4718600 | tf_op jit(solution)/shard_map/ppermute | solution.py:140
  71.4 25.7 %copy-start.36 = (bf16[256,512]{1,0:T(8,128)(2,1)S(1)}, bf16[256,512]{1,0:T(8,128)(2,1)}, u32[]{:S(2)}) copy-start(bf16[256,512]{1,0:T(8,128)(2,1)} %convert_element_type.214) | copy-start | bytes 786436
  71.4 61.3 %copy-start.10 = (f32[32,96,256]{2,1,0:T(8,128)S(1)}, f32[32,96,256]{2,1,0:T(8,128)}, u32[]{:S(2)}) copy-start(f32[32,96,256]{2,1,0:T(8,128)} %param.29) | copy-start | bytes 9437188
  71.6 62.2 %copy-start.3 = (bf16[32,96,4,64]{1,3,2,0:T(8,128)(2,1)}, bf16[32,96,4,64]{1,3,2,0:T(8,128)(2,1)S(1)}, u32[]{:S(2)}) copy-start(bf16[32,96,4,64]{1,3,2,0:T(8,128)(2,1)S(1)} %copy.70) | copy-start | bytes 4718596
  97.1 42.3 %copy-start.14 = (bf16[32,96,256]{2,1,0:T(8,128)(2,1)}, bf16[32,96,256]{2,1,0:T(8,128)(2,1)S(1)}, u32[]{:S(2)}) copy-start(bf16[32,96,256]{2,1,0:T(8,128)(2,1)S(1)} %collective-permute-done.1) | copy-start | bytes 4718596
  97.9 35.9 %copy-start.41 = (bf16[32,96,96]{1,2,0:T(8,128)(2,1)S(1)}, bf16[32,96,96]{1,2,0:T(8,128)(2,1)}, u32[]{:S(2)}) copy-start(bf16[32,96,96]{1,2,0:T(8,128)(2,1)} %get-tuple-element.76) | copy-start | bytes 1769476
  98.0 34.8 %collective-permute-start.2 = (bf16[32,96,256]{2,1,0:T(8,128)(2,1)S(1)}, bf16[32,96,256]{2,1,0:T(8,128)(2,1)S(1)}, u32[]{:S(2)}, u32[]{:S(2)}) collective-permute-start(bf16[32,96,256]{2,1,0:T(8,128)(2,1)S(1)} %convolution_convert_fusion.5), channel_id=1, source_target_pairs={{0,1},{1,0},{2,3},{3,2},{4,5},{5,4},{6,7},{7,6},{8,9},{9,8},{10,11... | collective-permute-start | bytes 4718600 | tf_op jit(solution)/shard_map/ppermute | solution.py:140
  133.9 4.4 copy-start.33
  137.1 8.8 %copy-start.16 = (bf16[32,96,256]{2,1,0:T(8,128)(2,1)}, bf16[32,96,256]{2,1,0:T(8,128)(2,1)S(1)}, u32[]{:S(2)}) copy-start(bf16[32,96,256]{2,1,0:T(8,128)(2,1)S(1)} %get-tuple-element.89) | copy-start | bytes 4718596
  137.1 33.8 %collective-permute-start.3 = (bf16[32,96,256]{2,1,0:T(8,128)(2,1)S(1)}, bf16[32,96,256]{2,1,0:T(8,128)(2,1)S(1)}, u32[]{:S(2)}, u32[]{:S(2)}) collective-permute-start(bf16[32,96,256]{2,1,0:T(8,128)(2,1)S(1)} %get-tuple-element.89), channel_id=1, source_target_pairs={{0,1},{1,0},{2,3},{3,2},{4,5},{5,4},{6,7},{7,6},{8,9},{9,8},{10,11... | collective-permute-start | bytes 4718600 | tf_op jit(solution)/shard_map/ppermute | solution.py:140
  139.2 31.7 %copy-start.25 = (bf16[512,1024]{1,0:T(8,128)(2,1)}, bf16[512,1024]{1,0:T(8,128)(2,1)S(1)}, u32[]{:S(2)}) copy-start(bf16[512,1024]{1,0:T(8,128)(2,1)S(1)} %convert_element_type.224) | copy-start | bytes 3145732
  139.4 6.4 %copy-start.23 = (bf16[1024,512]{1,0:T(8,128)(2,1)}, bf16[1024,512]{1,0:T(8,128)(2,1)S(1)}, u32[]{:S(2)}) copy-start(bf16[1024,512]{1,0:T(8,128)(2,1)S(1)} %convert_element_type.226) | copy-start | bytes 3145732
  170.9 8.4 %copy-start.21 = (bf16[32,96,256]{2,1,0:T(8,128)(2,1)}, bf16[32,96,256]{2,1,0:T(8,128)(2,1)S(1)}, u32[]{:S(2)}) copy-start(bf16[32,96,256]{2,1,0:T(8,128)(2,1)S(1)} %collective-permute-done.3) | copy-start | bytes 4718596
  228.0 7.4 %copy-start = (bf16[32,96,1024]{2,1,0:T(8,128)(2,1)S(1)}, bf16[32,96,1024]{2,1,0:T(8,128)(2,1)}, u32[]{:S(2)}) copy-start(bf16[32,96,1024]{2,1,0:T(8,128)(2,1)} %add_convert_fusion) | copy-start | bytes 18874372
  232.9 33.1 %collective-permute-start.5 = (bf16[32,96,256]{2,1,0:T(8,128)(2,1)S(1)}, bf16[32,96,256]{2,1,0:T(8,128)(2,1)S(1)}, u32[]{:S(2)}, u32[]{:S(2)}) collective-permute-start(bf16[32,96,256]{2,1,0:T(8,128)(2,1)S(1)} %convolution_convert_fusion.3), channel_id=1, source_target_pairs={{0,1},{1,0},{2,3},{3,2},{4,5},{5,4},{6,7},{7,6},{8,9},{9,8},{10,11... | collective-permute-start | bytes 4718600 | tf_op jit(solution)/shard_map/ppermute | solution.py:140
  233.9 4.6 slice-start
  241.4 24.5 %copy-start.26 = (bf16[512,1024]{1,0:T(8,128)(2,1)S(1)}, bf16[512,1024]{1,0:T(8,128)(2,1)}, u32[]{:S(2)}) copy-start(bf16[512,1024]{1,0:T(8,128)(2,1)} %copy-done.25) | copy-start | bytes 3145732
  241.4 24.5 %copy-start.29 = (f32[32,96,256]{2,1,0:T(8,128)S(1)}, f32[32,96,256]{2,1,0:T(8,128)}, u32[]{:S(2)}) copy-start(f32[32,96,256]{2,1,0:T(8,128)} %get-tuple-element.87) | copy-start | bytes 9437188
  243.3 25.0 %copy-start.18 = (f32[512,1024]{1,0:T(8,128)}, f32[512,1024]{1,0:T(8,128)S(1)}, u32[]{:S(2)}) copy-start(f32[512,1024]{1,0:T(8,128)S(1)} %fusion.94) | copy-start | bytes 6291460
  268.3 4.6 copy-start.22
  272.2 32.5 %collective-permute-start.6 = (bf16[32,96,256]{2,1,0:T(8,128)(2,1)}, bf16[32,96,256]{2,1,0:T(8,128)(2,1)}, u32[]{:S(2)}, u32[]{:S(2)}) collective-permute-start(bf16[32,96,256]{2,1,0:T(8,128)(2,1)} %get-tuple-element.94), channel_id=1, source_target_pairs={{0,1},{1,0},{2,3},{3,2},{4,5},{5,4},{6,7},{7,6},{8,9},{9,8},{10,11... | collective-permute-start | bytes 4718600 | tf_op jit(solution)/shard_map/ppermute | solution.py:140
  285.8 167.9 %reduce-scatter.3.cloned.1.call-start = ((), (), s32[]{:S(2)}) async-start(), calls=%async_computation.2 | async-start | bytes 7798784 | tf_op jit(solution)/shard_map/reduce_scatter | solution.py:325
  285.9 4.4 copy-start.4
  316.2 5.6 %copy-start.7 = (bf16[4,32,64,48]{2,3,1,0:T(8,128)(2,1)}, bf16[4,32,64,48]{2,3,1,0:T(8,128)(2,1)S(1)}, u32[]{:S(2)}) copy-start(bf16[4,32,64,48]{2,3,1,0:T(8,128)(2,1)S(1)} %fusion.74) | copy-start | bytes 2359300
  355.0 11.2 %copy-start.35 = (bf16[512,256]{1,0:T(8,128)(2,1)S(1)}, bf16[512,256]{1,0:T(8,128)(2,1)}, u32[]{:S(2)}) copy-start(bf16[512,256]{1,0:T(8,128)(2,1)} %copy-done.34) | copy-start | bytes 786436
  360.8 37.6 %collective-permute-start.4 = (bf16[32,96,256]{2,1,0:T(8,128)(2,1)}, bf16[32,96,256]{2,1,0:T(8,128)(2,1)}, u32[]{:S(2)}, u32[]{:S(2)}) collective-permute-start(bf16[32,96,256]{2,1,0:T(8,128)(2,1)} %convolution_convert_fusion.4), channel_id=1, source_target_pairs={{0,1},{1,0},{2,3},{3,2},{4,5},{5,4},{6,7},{7,6},{8,9},{9,8},{10,11... | collective-permute-start | bytes 4718600 | tf_op jit(solution)/shard_map/ppermute | solution.py:140
  366.2 32.2 %copy-start.13 = (f32[32,96,256]{2,1,0:T(8,128)S(1)}, f32[32,96,256]{2,1,0:T(8,128)}, u32[]{:S(2)}) copy-start(f32[32,96,256]{2,1,0:T(8,128)} %copy-done.12) | copy-start | bytes 9437188
  367.1 59.0 %collective-permute-start.7 = (bf16[32,96,256]{2,1,0:T(8,128)(2,1)S(1)}, bf16[32,96,256]{2,1,0:T(8,128)(2,1)S(1)}, u32[]{:S(2)}, u32[]{:S(2)}) collective-permute-start(bf16[32,96,256]{2,1,0:T(8,128)(2,1)S(1)} %convolution_convert_fusion.1), channel_id=1, source_target_pairs={{0,1},{1,0},{2,3},{3,2},{4,5},{5,4},{6,7},{7,6},{8,9},{9,8},{10,11... | collective-permute-start | bytes 4718600 | tf_op jit(solution)/shard_map/ppermute | solution.py:140
  398.4 6.8 %copy-start.40 = (bf16[32,96,96]{1,2,0:T(8,128)(2,1)S(1)}, bf16[32,96,96]{1,2,0:T(8,128)(2,1)}, u32[]{:S(2)}) copy-start(bf16[32,96,96]{1,2,0:T(8,128)(2,1)} %copy-done.39) | copy-start | bytes 1769476
  398.4 6.8 %copy-start.53 = (f32[32,96]{1,0:T(8,128)S(1)}, f32[32,96]{1,0:T(8,128)}, u32[]{:S(2)}) copy-start(f32[32,96]{1,0:T(8,128)} %copy-done.52) | copy-start | bytes 36868
  405.2 20.8 %copy-start.28 = (f32[32,96,256]{2,1,0:T(8,128)S(1)}, f32[32,96,256]{2,1,0:T(8,128)}, u32[]{:S(2)}) copy-start(f32[32,96,256]{2,1,0:T(8,128)} %get-tuple-element.95) | copy-start | bytes 9437188
  426.0 5.5 %copy-start.49 = (f32[1024,32]{0,1:T(8,128)S(1)}, f32[1024,32]{0,1:T(8,128)}, u32[]{:S(2)}) copy-start(f32[1024,32]{0,1:T(8,128)} %param.47) | copy-start | bytes 393220
  426.0 5.5 %copy-start.50 = (f32[1024,32]{0,1:T(8,128)S(1)}, f32[1024,32]{0,1:T(8,128)}, u32[]{:S(2)}) copy-start(f32[1024,32]{0,1:T(8,128)} %param.46) | copy-start | bytes 393220
  428.6 25.9 %copy-start.54 = (f32[32,256]{1,0:T(8,128)S(1)}, f32[32,256]{1,0:T(8,128)}, u32[]{:S(2)}) copy-start(f32[32,256]{1,0:T(8,128)} %param.39) | copy-start | bytes 98308
  428.6 25.9 %copy-start.55 = (f32[32,256]{1,0:T(8,128)S(1)}, f32[32,256]{1,0:T(8,128)}, u32[]{:S(2)}) copy-start(f32[32,256]{1,0:T(8,128)} %param.38) | copy-start | bytes 98308
  428.6 28.4 %copy-start.44 = (f32[4,192,128]{2,1,0:T(8,128)S(1)}, f32[4,192,128]{2,1,0:T(8,128)}, u32[]{:S(2)}) copy-start(f32[4,192,128]{2,1,0:T(8,128)} %param.41) | copy-start | bytes 1179652
  428.6 28.4 %copy-start.45 = (f32[4,192,128]{2,1,0:T(8,128)S(1)}, f32[4,192,128]{2,1,0:T(8,128)}, u32[]{:S(2)}) copy-start(f32[4,192,128]{2,1,0:T(8,128)} %param.40) | copy-start | bytes 1179652
  429.7 29.4 %copy-start.51 = (f32[256,32]{0,1:T(8,128)S(1)}, f32[256,32]{0,1:T(8,128)}, u32[]{:S(2)}) copy-start(f32[256,32]{0,1:T(8,128)} %copy.110) | copy-start | bytes 98308
  429.8 29.4 %copy-start.56 = (f32[256,32]{0,1:T(8,128)S(1)}, f32[256,32]{0,1:T(8,128)}, u32[]{:S(2)}) copy-start(f32[256,32]{0,1:T(8,128)} %param.43) | copy-start | bytes 98308
  429.8 29.4 %copy-start.57 = (f32[256,32]{0,1:T(8,128)S(1)}, f32[256,32]{0,1:T(8,128)}, u32[]{:S(2)}) copy-start(f32[256,32]{0,1:T(8,128)} %param.42) | copy-start | bytes 98308
  (19 other events, 51.2 us)
Sparse Core Ops, SparseCore 0:
  285.9 73.0 reduce-scatter.4
  363.0 90.6 reduce-scatter.2

commit v2 on v1

--- a/solution.py
+++ b/solution.py
@@ -153,15 +153,18 @@
             total = total + product("wtd,de->wte", received[s], rows_of(weight_low, owner, size))
         return total, received
 
-    def scattered_product(values, weight_low, size):
-        sent = {
-            s: swap(product("wte,ed->wtd", values, cols_of(weight_low, peer(s), size)).astype(jnp.bfloat16), s)
+    def scattered_product(values, weight_low, size, after=()):
+        outgoing = {
+            s: product("wte,ed->wtd", values, cols_of(weight_low, peer(s), size)).astype(jnp.bfloat16)
             for s in shifts
         }
+        if after:
+            outgoing, _ = lax.optimization_barrier((outgoing, tuple(after)))
+        sent = {s: swap(outgoing[s], s) for s in shifts}
         total = product("wte,ed->wtd", values, cols_of(weight_low, me, size))
         for s in shifts:
             total = total + sent[s].astype(jnp.float32)
-        return total
+        return total, sent
 
     def placed_rows(parts, size, total_rows):
         out = jnp.zeros((total_rows,) + parts[0][1].shape[1:], jnp.float32)
@@ -195,7 +198,6 @@
 
         inputs_mine = inputs.astype(jnp.bfloat16)
         query, inputs_recv = gathered_product(inputs_mine, query_low, local_width)
-        grad_feed_mine, _ = lax.optimization_barrier((grad_feed_mine, tuple(inputs_recv.values())))
         grad_feed_recv = {s: swap(grad_feed_mine, s) for s in shifts}
         query = query.astype(jnp.bfloat16)
         query_heads = query.reshape(windows, length, head_count, head_size)
@@ -211,17 +213,13 @@
             "htm,whme->wthe", inv_sin, mixed[..., head_size:]
         )
         field = field.reshape(windows, length, local_width).astype(jnp.bfloat16)
-        field, _ = lax.optimization_barrier((field, tuple(grad_feed_recv.values())))
-        attended = scattered_product(field, output_low, local_width)
+        attended, _ = scattered_product(field, output_low, local_width)
         resid_one = inputs + attended
         seasonal = resid_one - trend_local(resid_one, first_rows)
         seasonal_mine = seasonal.astype(jnp.bfloat16)
         pre, seasonal_recv = gathered_product(seasonal_mine, inner_low, local_width)
         activated, gelu_pull = jax.vjp(exact_gelu, pre)
         hidden = activated.astype(jnp.bfloat16)
-        feed = scattered_product(hidden, outer_low, local_width)
-        combined = seasonal + feed
-        output = combined - trend_local(combined, second_rows)
 
         outer_grad_t = placed_rows(
             [(me, product("wtd,wtf->df", grad_feed_mine, hidden))]
@@ -241,10 +239,14 @@
             local_width,
             model_width,
         )
-        grad_season = grad_comb + scattered_product(grad_pre, inner_t, local_width)
+        grad_season_part, _ = scattered_product(grad_pre, inner_t, local_width)
+        grad_season = grad_comb + grad_season_part
         grad_resid = grad_season - trend_back(grad_season, first_rows)
         grad_attend_mine = grad_resid.astype(jnp.bfloat16)
         grad_attend_recv = {s: swap(grad_attend_mine, s) for s in shifts}
+        feed, feed_sent = scattered_product(hidden, outer_low, local_width, after=grad_attend_recv.values())
+        combined = seasonal + feed
+        output = combined - trend_local(combined, second_rows)
         output_grad_t = placed_rows(
             [(me, product("wtd,wte->de", grad_attend_mine, field))]
             + [((me - s) % head_parts, product("wtd,wte->de", grad_attend_recv[s], field)) for s in shifts],
@@ -276,7 +278,8 @@
             local_width,
             model_width,
         )
-        input_grad = grad_resid + scattered_product(grad_query, query_t, local_width)
+        input_part, _ = scattered_product(grad_query, query_t, local_width, after=feed_sent.values())
+        input_grad = grad_resid + input_part
         spectrum_parts = spectrum.reshape(windows, head_count, mode_count, 2, head_size)
         grad_real = grad_mixed[..., :head_size]
         grad_imag = grad_mixed[..., head_size:]

time: 476 us -> 455 us (0.956); the launches traced: 467 us -> 451 us
  waiting for transfers between devices: 194 us -> 160 us
  local copies, waits for them, and re-layouts: 33.7 us -> 46.5 us
    ppermute x8, waiting for transfers between devices: 173 us -> 139 us  [swap(): return lax.ppermute(values, 'head', pairs)]
    add x0 -> x1, other arithmetic: none -> 4.86 us  [chunk_pass(): input_grad = grad_resid + input_part]
    unnamed x148 -> x118, local copies, waits for them, and re-layouts: 6.17 us -> 9.92 us
  transfers between devices with their start and end apart: 10 -> 10, of which waited for: 9 -> 8; matrix products, arithmetic and copies ran while one was open for 31% -> 41% of each run, Pallas kernels for 0% -> 0%
where the time goes in v2:
time: 455 us; the launch traced here: 451 us
  waiting for transfers between devices  160 us (35%)
  matrix products  140 us (31%)
  other arithmetic  78.9 us (17%)
  local copies, waits for them, and re-layouts  46.5 us (10%)
  between operations  15.1 us (3%)
  starting transfers between devices  10 us (2%)
    ppermute x8, waiting for transfers between devices, swap(): return lax.ppermute(values, 'head', pairs)  139 us
    dot_general x35, matrix products, product(): return jnp.einsum(form, left, right, preferred_element_type=jnp.float32)  123 us
    convert_element_type x1, other arithmetic, chunk_pass(): hidden = activated.astype(jnp.bfloat16)  30.4 us
    reduce_scatter x2, waiting for transfers between devices, reduced_over_dp(): lax.psum_scatter(joined.reshape(-1, lanes), 'dp', scatter_dimension=0, ti...  21.1 us
    dot_general x2, matrix products, trend_back(): jnp.einsum('wts,wtd->wsd', tiled, parts, preferred_element_type=jnp.float32)  10 us
    ppermute x8, starting transfers between devices, swap(): return lax.ppermute(values, 'head', pairs)  9.95 us
    unnamed x118, local copies, waits for them, and re-layouts  9.92 us
    concatenate x2, other arithmetic, reduced_over_dp(): joined = jnp.concatenate([flat for flat, _ in laid], axis=1)  9.7 us
  transfers between devices with their start and end apart: 10, of which 8 were waited for; matrix products, arithmetic and copies ran while one was open for 41% of the time, Pallas kernels for 0%

profile of v2, /device:TPU:0, one launch (start us, length us, event | category | flops | bytes accessed | tf_op | source)
XLA Modules:
  0.0 450.8 jit_solution(7138036541679360779)
XLA Ops:
  7.2 3.3 convert_element_type.193
  10.6 3.0 collective-permute-start
  14.3 3.2 convert_element_type.191
  17.7 2.1 fusion.156
  19.8 4.0 slice_negate_fusion
  23.7 24.5 %collective-permute-done = bf16[32,96,256]{2,1,0:T(8,128)(2,1)} collective-permute-done((bf16[32,96,256]{2,1,0:T(8,128)(2,1)}, bf16[32,96,256]{2,1,0:T(8,128)(2,1)}, u32[]{:S(2)}, u32[]{:S(2)}) %collective-permute-start) | collective-permute-done | bytes 1572896 | tf_op jit(solution)/shard_map/ppermute | solution.py:140
  48.3 3.1 fusion.87
  51.4 4.0 copy.64
  55.4 3.9 fusion.68
  59.4 2.2 fusion.65
  64.2 3.1 fusion.91
  72.0 1.8 collective-permute-start.1
  73.9 4.6 %select_convert_fusion = (bf16[32,96,96]{2,1,0:T(8,128)(2,1)S(1)}, bf16[32,96,96]{2,1,0:T(8,128)(2,1)S(1)}) fusion(bf16[96,96]{1,0:T(8,128)(2,1)S(1)} %copy-done.49, bf16[96,96]{1,0:T(8,128)(2,1)S(1)} %copy-done.50, bf16[96,96]{1,0:T(8,128)(2,1)S(1)} %copy-done.51, bf16[96,96]{1,0:T(8,128)(2,1)S(1)} %copy-done.52, bf16[96,96]{1,0:T(8,128)(2,1)S(1)} %copy-done.53, ...), kind=kLoop, calls=%fused_computation.130 | loop fusion | flops 2949120 | bytes 1302528 | tf_op jit(solution)/shard_map/convert_element_type | solution.py:66
  79.3 28.4 %collective-permute-done.1 = bf16[32,96,256]{2,1,0:T(8,128)(2,1)S(1)} collective-permute-done((bf16[32,96,256]{2,1,0:T(8,128)(2,1)S(1)}, bf16[32,96,256]{2,1,0:T(8,128)(2,1)S(1)}, u32[]{:S(2)}, u32[]{:S(2)}) %collective-permute-start.1) | collective-permute-done | bytes 1572896 | tf_op jit(solution)/shard_map/ppermute | solution.py:140
  108.7 3.9 fusion.108
  114.1 2.9 fusion.249
  119.3 6.5 %fusion.118 = f32[32,96,1024]{2,1,0:T(8,128)} fusion(bf16[32,96,256]{2,1,0:T(8,128)(2,1)S(1)} %get-tuple-element.90, bf16[1024,512]{1,0:T(8,128)(2,1)S(1)} %convert_element_type.219, s32[]{:T(128)S(6)} %select_n.186), kind=kOutput, calls=%fused_computation.155 | convolution fusion | flops 1610612736 | bytes 14680068 | tf_op jit(solution)/shard_map/wtd,fd->wtf/dot_general | solution.py:44
  125.8 1.8 fusion.127
  127.6 22.3 %collective-permute-done.2 = bf16[32,96,256]{2,1,0:T(8,128)(2,1)S(1)} collective-permute-done((bf16[32,96,256]{2,1,0:T(8,128)(2,1)S(1)}, bf16[32,96,256]{2,1,0:T(8,128)(2,1)S(1)}, u32[]{:S(2)}, u32[]{:S(2)}) %collective-permute-start.2) | collective-permute-done | bytes 1572896 | tf_op jit(solution)/shard_map/ppermute | solution.py:140
  149.9 7.9 %convert_reduce_fusion.1 = (u32[96,1024]{1,0:T(8,128)S(1)}, u32[96,1024]{1,0:T(8,128)S(1)}, f32[32,96,1024]{2,1,0:T(8,128)}) fusion(f32[32,96,1024]{2,1,0:T(8,128)S(1)} %fusion.127, bf16[32,96,256]{2,1,0:T(8,128)(2,1)S(1)} %collective-permute-done.2, bf16[512,1024]{1,0:T(8,128)(2,1)S(1)} %convert_element_type.217, s32[]{:T(128)S(6)} %select_n.188), kind=kOutput, calls=%fused_computation.6 | convolution fusion | flops 1648164864 | bytes 28049412 | tf_op jit(solution)/shard_map/wtd,de->wte/dot_general | solution.py:44
  157.8 30.4 %multiply_convert_fusion = (bf16[32,96,1024]{2,1,0:T(8,128)(2,1)}, f32[32,96,1024]{2,1,0:T(8,128)}) fusion(f32[32,96,1024]{2,1,0:T(8,128)} %get-tuple-element.89, u32[96,1024]{1,0:T(8,128)S(1)} %get-tuple-element.22, u32[96,1024]{1,0:T(8,128)S(1)} %get-tuple-element.21), kind=kLoop, calls=%fused_computation.8 | loop fusion | flops 213909504 | bytes 32243712 | tf_op jit(solution)/shard_map/convert_element_type | solution.py:222
  189.4 18.7 %add_convert_fusion = bf16[32,96,1024]{2,1,0:T(8,128)(2,1)} fusion(f32[32,96,1024]{2,1,0:T(8,128)} %get-tuple-element.45, f32[32,96,1024]{2,1,0:T(8,128)} %fusion.118, f32[32,96,1024]{2,1,0:T(8,128)} %get-tuple-element.89, bf16[32,96,256]{2,1,0:T(8,128)(2,1)} %copy-done.18, bf16[1024,512]{1,0:T(8,128)(2,1)} %copy-done.22, s32[]{:T(128)S(6)} %select_n.188), kind=kOutput, calls=%fused_computation.7 | convolution fusion | flops 1657798656 | bytes 46137348 | tf_op jit(solution)/shard_map/wtd,fd->wtf/dot_general | solution.py:44
  208.0 4.8 %convolution_convert_fusion.3 = bf16[32,96,256]{2,1,0:T(8,128)(2,1)S(1)} fusion(bf16[32,96,1024]{2,1,0:T(8,128)(2,1)} %add_convert_fusion, bf16[512,1024]{1,0:T(8,128)(2,1)} %copy-done.24, s32[]{:T(128)S(6)} %select_n.193), kind=kOutput, calls=%fused_computation.114 | convolution fusion | flops 1611399168 | bytes 8388612 | tf_op jit(solution)/shard_map/wte,ed->wtd/dot_general | solution.py:44
  214.7 1.8 fusion.97
  218.5 2.8 fusion.95
  221.3 1.8 fusion.96
  223.1 21.1 %collective-permute-done.4 = bf16[32,96,256]{2,1,0:T(8,128)(2,1)S(1)} collective-permute-done((bf16[32,96,256]{2,1,0:T(8,128)(2,1)S(1)}, bf16[32,96,256]{2,1,0:T(8,128)(2,1)S(1)}, u32[]{:S(2)}, u32[]{:S(2)}) %collective-permute-start.4) | collective-permute-done | bytes 1572896 | tf_op jit(solution)/shard_map/ppermute | solution.py:140
  244.2 4.5 multiply_convert_fusion.1
  248.7 7.1 %fusion.250 = (bf16[32,96,256]{2,1,0:T(8,128)(2,1)}, f32[32,96,256]{2,1,0:T(8,128)}) fusion(f32[32,96,256]{2,1,0:T(8,128)} %get-tuple-element.92, bf16[32,96,256]{2,1,0:T(8,128)(2,1)} %get-tuple-element.53, bf16[32,96,256]{2,1,0:T(8,128)(2,1)} %get-tuple-element.54, bf16[32,96,256]{2,1,0:T(8,128)(2,1)S(1)} %get-tuple-element.52, ...), kind=kOutput, calls=%fused_computation.310 | convolution fusion | flops 474021888 | bytes 13172736 | tf_op jit(solution)/shard_map/wts,wtd->wsd/dot_general | solution.py:89
  256.8 2.8 fusion.94
  259.6 2.7 reshape_reshape.18
  262.3 2.7 reshape_reshape.19
  265.0 4.6 %pad_maximum_fusion.1 = f32[16,512,128]{2,1,0:T(8,128)} fusion(f32[16,256,128]{2,1,0:T(8,128)} %reshape_reshape.19, f32[16,256,128]{2,1,0:T(8,128)} %reshape_reshape.18), kind=kLoop, calls=%fused_computation.48 | loop fusion | flops 1048576 | bytes 8388608 | tf_op jit(solution)/shard_map/concatenate | solution.py:327
  269.7 4.4 pad_maximum_fusion.2
  274.9 2.9 fusion.110
  277.8 2.1 fusion.147
  279.9 6.7 %collective-permute-done.5 = bf16[32,96,256]{2,1,0:T(8,128)(2,1)} collective-permute-done((bf16[32,96,256]{2,1,0:T(8,128)(2,1)}, bf16[32,96,256]{2,1,0:T(8,128)(2,1)}, u32[]{:S(2)}, u32[]{:S(2)}) %collective-permute-start.5) | collective-permute-done | bytes 1572896 | tf_op jit(solution)/shard_map/ppermute | solution.py:140
  286.6 3.2 add_convert_fusion.3
  289.8 3.9 copy.75
  293.7 3.9 fusion.74
  297.7 2.2 bitcast_negate_fusion
  299.8 2.9 maximum_bitcast_fusion
  306.0 3.1 copy.86
  309.1 3.0 fusion.109
  312.1 1.9 reshape_reshape.16
  314.0 8.1 %fusion.88 = bf16[32,4,48,128]{3,0,2,1:T(8,128)(2,1)} fusion(bf16[32,4,48,128]{3,2,0,1:T(8,128)(2,1)} %get-tuple-element.67, bf16[4,48,64,64]{3,2,1,0:T(8,128)(2,1)} %get-tuple-element.65, bf16[4,48,64,64]{3,2,1,0:T(8,128)(2,1)} %get-tuple-element.64, bf16[4,48,64,128]{3,2,1,0:T(8,128)(2,1)S(1)} %bitcast.243), kind=kOutput, calls=%fused_computation.133 | convolution fusion | flops 220987392 | bytes 9437184 | tf_op jit(solution)/shard_map/whmo,hmio->whmi/dot_general | solution.py:44
  322.0 2.6 fusion.245
  328.0 2.1 convolution_bitcast_fusion.4
  330.2 2.1 convolution_bitcast_fusion.5
  335.8 5.1 %pad_maximum_fusion = f32[16,896,128]{2,1,0:T(8,128)} fusion(f32[16,64,128]{2,1,0:T(8,128)S(1)} %reshape_reshape.17, f32[16,64,128]{2,1,0:T(8,128)S(1)} %copy-done.35, f32[16,768,128]{2,1,0:T(8,128)} %bitcast.244), kind=kLoop, calls=%fused_computation.21 | loop fusion | flops 3670016 | bytes 14680064 | tf_op jit(solution)/shard_map/concatenate | solution.py:327
  342.2 5.8 %convolution_convert_fusion.4 = bf16[32,96,256]{2,1,0:T(8,128)(2,1)} fusion(bf16[32,96,1024]{2,1,0:T(8,128)(2,1)} %get-tuple-element.44, bf16[1024,512]{1,0:T(8,128)(2,1)S(1)} %copy-done.23, s32[]{:T(128)S(6)} %select_n.193), kind=kOutput, calls=%fused_computation.115 | convolution fusion | flops 1611399168 | bytes 8388612 | tf_op jit(solution)/shard_map/wte,ed->wtd/dot_general | solution.py:44
  348.4 2.0 constant_dynamic-slice_fusion
  351.7 1.7 constant_dynamic-slice_fusion.1
  355.0 2.0 convolution_convert_fusion.1
  357.0 2.5 fusion.154
  359.5 23.0 %collective-permute-done.6 = bf16[32,96,256]{2,1,0:T(8,128)(2,1)} collective-permute-done((bf16[32,96,256]{2,1,0:T(8,128)(2,1)}, bf16[32,96,256]{2,1,0:T(8,128)(2,1)}, u32[]{:S(2)}, u32[]{:S(2)}) %collective-permute-start.6) | collective-permute-done | bytes 1572896 | tf_op jit(solution)/shard_map/ppermute | solution.py:140
  382.8 5.9 %fusion.243 = (bf16[32,96,256]{2,1,0:T(8,128)(2,1)S(1)}, bf16[32,96,256]{2,1,0:T(8,128)(2,1)S(1)}, bf16[32,96,256]{2,1,0:T(8,128)(2,1)S(1)}, f32[32,96,256]{2,1,0:T(8,128)S(1)}) fusion(bf16[32,96,256]{2,1,0:T(8,128)(2,1)} %collective-permute-done.6, bf16[32,96,1024]{2,1,0:T(8,128)(2,1)} %get-tuple-element.44, bf16[1024,512]{1,0:T(8,128)(2,1)S(1)} %copy-done.23, ...), kind=kOutput, calls=%fused_computation.303 | convolution fusion | flops 1620049920 | bytes 22560772 | tf_op jit(solution)/shard_map/wte,ed->wtd/dot_general | solution.py:44
  388.7 3.4 multiply_subtract_fusion
  394.7 1.8 multiply_add_fusion.3
  396.5 1.7 multiply_add_fusion.2
  398.3 13.3 %collective-permute-done.7 = bf16[32,96,256]{2,1,0:T(8,128)(2,1)} collective-permute-done((bf16[32,96,256]{2,1,0:T(8,128)(2,1)}, bf16[32,96,256]{2,1,0:T(8,128)(2,1)}, u32[]{:S(2)}, u32[]{:S(2)}) %collective-permute-start.7) | collective-permute-done | bytes 1572896 | tf_op jit(solution)/shard_map/ppermute | solution.py:140
  411.6 4.9 %add_add_fusion = f32[32,96,256]{2,1,0:T(8,128)} fusion(f32[32,96,256]{2,1,0:T(8,128)} %get-tuple-element.94, f32[32,96,256]{2,1,0:T(8,128)S(1)} %copy-done.10, bf16[32,96,256]{2,1,0:T(8,128)(2,1)} %collective-permute-done.7), kind=kLoop, calls=%fused_computation.57 | loop fusion | flops 2359296 | bytes 11010048 | tf_op jit(solution)/shard_map/add | solution.py:282
  416.5 21.1 %reduce-scatter.3.cloned.1.call-done = f32[896,128]{1,0:T(8,128)} async-done(((f32[14336,128]{1,0:T(8,128)}), f32[896,128]{1,0:T(8,128)}) %reduce-scatter.3.cloned.1.call-update) | async-done | bytes 458768 | tf_op jit(solution)/shard_map/reduce_scatter | solution.py:328
  440.8 2.2 multiply_add_fusion
  (168 shorter events, 42.0 us)
Async XLA Ops:
  7.2 6.4 %copy-start.40 = (f32[512,256]{1,0:T(8,128)S(1)}, f32[512,256]{1,0:T(8,128)}, u32[]{:S(2)}) copy-start(f32[512,256]{1,0:T(8,128)} %param.33) | copy-start | bytes 1572868
  7.2 384.9 %reduce-scatter.5.cloned.1.call-start = ((), (), s32[]{:S(2)}) async-start(), calls=%async_computation.3 | async-start | bytes 4456448 | tf_op jit(solution)/shard_map/reduce_scatter | solution.py:328
  10.6 37.7 %collective-permute-start = (bf16[32,96,256]{2,1,0:T(8,128)(2,1)}, bf16[32,96,256]{2,1,0:T(8,128)(2,1)}, u32[]{:S(2)}, u32[]{:S(2)}) collective-permute-start(bf16[32,96,256]{2,1,0:T(8,128)(2,1)} %convert_element_type.193), channel_id=1, source_target_pairs={{0,1},{1,0},{2,3},{3,2},{4,5},{5,4},{6,7},{7,6},{8,9},{9,8},{10,11... | collective-permute-start | bytes 4718600 | tf_op jit(solution)/shard_map/ppermute | solution.py:140
  14.3 3.3 copy-start.36
  14.3 3.3 copy-start.42
  17.7 51.7 %copy-start.54 = (f32[4,48]{1,0:T(4,128)}, f32[4,48]{1,0:T(4,128)S(1)}, u32[]{:S(2)}) copy-start(f32[4,48]{1,0:T(4,128)S(1)} %get-tuple-element.84) | copy-start | bytes 2308
  19.7 28.6 %copy-start.33 = (bf16[512,256]{1,0:T(8,128)(2,1)S(1)}, bf16[512,256]{1,0:T(8,128)(2,1)}, u32[]{:S(2)}) copy-start(bf16[512,256]{1,0:T(8,128)(2,1)} %convert_element_type.192) | copy-start | bytes 786436
  55.4 4.0 copy-start.2
  59.4 3.1 copy-start.6
  59.4 3.4 copy-start.30
  61.6 2.5 copy-start.29
  70.8 3.0 copy-start.48
  70.9 3.0 copy-start.49
  70.9 3.0 copy-start.50
  70.9 3.0 copy-start.51
  70.9 3.0 copy-start.52
  70.9 3.0 copy-start.53
  71.1 36.5 %copy-start.3 = (bf16[32,96,4,64]{1,3,2,0:T(8,128)(2,1)}, bf16[32,96,4,64]{1,3,2,0:T(8,128)(2,1)S(1)}, u32[]{:S(2)}) copy-start(bf16[32,96,4,64]{1,3,2,0:T(8,128)(2,1)S(1)} %copy.70) | copy-start | bytes 4718596
  71.2 7.4 %copy-start.28 = (f32[32,96,256]{2,1,0:T(8,128)S(1)}, f32[32,96,256]{2,1,0:T(8,128)}, u32[]{:S(2)}) copy-start(f32[32,96,256]{2,1,0:T(8,128)} %param.30) | copy-start | bytes 9437188
  72.0 35.6 %collective-permute-start.1 = (bf16[32,96,256]{2,1,0:T(8,128)(2,1)S(1)}, bf16[32,96,256]{2,1,0:T(8,128)(2,1)S(1)}, u32[]{:S(2)}, u32[]{:S(2)}) collective-permute-start(bf16[32,96,256]{2,1,0:T(8,128)(2,1)S(1)} %convolution_convert_fusion.5), channel_id=1, source_target_pairs={{0,1},{1,0},{2,3},{3,2},{4,5},{5,4},{6,7},{7,6},{8,9},{9,8},{10,11... | collective-permute-start | bytes 4718600 | tf_op jit(solution)/shard_map/ppermute | solution.py:140
  73.8 5.4 %copy-start.44 = (f32[32,96]{1,0:T(8,128)}, f32[32,96]{1,0:T(8,128)S(1)}, u32[]{:S(2)}) copy-start(f32[32,96]{1,0:T(8,128)S(1)} %get-tuple-element.38) | copy-start | bytes 36868
  78.5 30.2 %copy-start.39 = (bf16[32,96,96]{2,1,0:T(8,128)(2,1)}, bf16[32,96,96]{2,1,0:T(8,128)(2,1)S(1)}, u32[]{:S(2)}) copy-start(bf16[32,96,96]{2,1,0:T(8,128)(2,1)S(1)} %get-tuple-element.77) | copy-start | bytes 1769476
  78.5 35.6 %copy-start.37 = (bf16[32,96,96]{2,1,0:T(8,128)(2,1)}, bf16[32,96,96]{2,1,0:T(8,128)(2,1)S(1)}, u32[]{:S(2)}) copy-start(bf16[32,96,96]{2,1,0:T(8,128)(2,1)S(1)} %get-tuple-element.76) | copy-start | bytes 1769476
  78.5 29.1 %copy-start.8 = (f32[32,96,256]{2,1,0:T(8,128)S(1)}, f32[32,96,256]{2,1,0:T(8,128)}, u32[]{:S(2)}) copy-start(f32[32,96,256]{2,1,0:T(8,128)} %param.29) | copy-start | bytes 9437188
  108.7 3.9 copy-start.11
  112.6 13.2 %copy-start.13 = (bf16[32,96,256]{2,1,0:T(8,128)(2,1)}, bf16[32,96,256]{2,1,0:T(8,128)(2,1)S(1)}, u32[]{:S(2)}) copy-start(bf16[32,96,256]{2,1,0:T(8,128)(2,1)S(1)} %get-tuple-element.87) | copy-start | bytes 4718596
  112.6 37.3 %collective-permute-start.2 = (bf16[32,96,256]{2,1,0:T(8,128)(2,1)S(1)}, bf16[32,96,256]{2,1,0:T(8,128)(2,1)S(1)}, u32[]{:S(2)}, u32[]{:S(2)}) collective-permute-start(bf16[32,96,256]{2,1,0:T(8,128)(2,1)S(1)} %get-tuple-element.87), channel_id=1, source_target_pairs={{0,1},{1,0},{2,3},{3,2},{4,5},{5,4},{6,7},{7,6},{8,9},{9,8},{10,11... | collective-permute-start | bytes 4718600 | tf_op jit(solution)/shard_map/ppermute | solution.py:140
  114.1 3.5 copy-start.32
  117.0 2.3 copy-start.15
  117.0 2.2 copy-start.26
  117.0 71.2 %collective-permute-start.3 = (bf16[32,96,256]{2,1,0:T(8,128)(2,1)S(1)}, bf16[32,96,256]{2,1,0:T(8,128)(2,1)S(1)}, u32[]{:S(2)}, u32[]{:S(2)}) collective-permute-start(bf16[32,96,256]{2,1,0:T(8,128)(2,1)S(1)} %get-tuple-element.90), channel_id=1, source_target_pairs={{0,1},{1,0},{2,3},{3,2},{4,5},{5,4},{6,7},{7,6},{8,9},{9,8},{10,11... | collective-permute-start | bytes 4718600 | tf_op jit(solution)/shard_map/ppermute | solution.py:140
  119.2 30.7 %copy-start.24 = (bf16[512,1024]{1,0:T(8,128)(2,1)}, bf16[512,1024]{1,0:T(8,128)(2,1)S(1)}, u32[]{:S(2)}) copy-start(bf16[512,1024]{1,0:T(8,128)(2,1)S(1)} %convert_element_type.217) | copy-start | bytes 3145732
  119.3 6.5 %copy-start.22 = (bf16[1024,512]{1,0:T(8,128)(2,1)}, bf16[1024,512]{1,0:T(8,128)(2,1)S(1)}, u32[]{:S(2)}) copy-start(bf16[1024,512]{1,0:T(8,128)(2,1)S(1)} %convert_element_type.219) | copy-start | bytes 3145732
  149.9 7.9 %copy-start.20 = (bf16[32,96,256]{2,1,0:T(8,128)(2,1)}, bf16[32,96,256]{2,1,0:T(8,128)(2,1)S(1)}, u32[]{:S(2)}) copy-start(bf16[32,96,256]{2,1,0:T(8,128)(2,1)S(1)} %collective-permute-done.2) | copy-start | bytes 4718596
  208.0 6.6 %copy-start = (bf16[32,96,1024]{2,1,0:T(8,128)(2,1)S(1)}, bf16[32,96,1024]{2,1,0:T(8,128)(2,1)}, u32[]{:S(2)}) copy-start(bf16[32,96,1024]{2,1,0:T(8,128)(2,1)} %add_convert_fusion) | copy-start | bytes 18874372
  212.9 31.3 %collective-permute-start.4 = (bf16[32,96,256]{2,1,0:T(8,128)(2,1)S(1)}, bf16[32,96,256]{2,1,0:T(8,128)(2,1)S(1)}, u32[]{:S(2)}, u32[]{:S(2)}) collective-permute-start(bf16[32,96,256]{2,1,0:T(8,128)(2,1)S(1)} %convolution_convert_fusion.3), channel_id=1, source_target_pairs={{0,1},{1,0},{2,3},{3,2},{4,5},{5,4},{6,7},{7,6},{8,9},{9,8},{10,11... | collective-permute-start | bytes 4718600 | tf_op jit(solution)/shard_map/ppermute | solution.py:140
  214.4 3.7 slice-start
  214.7 3.5 slice-start.1
  216.5 2.0 copy-start.16
  218.5 2.8 copy-start.21
  221.3 23.0 %copy-start.25 = (bf16[512,1024]{1,0:T(8,128)(2,1)S(1)}, bf16[512,1024]{1,0:T(8,128)(2,1)}, u32[]{:S(2)}) copy-start(bf16[512,1024]{1,0:T(8,128)(2,1)} %copy-done.24) | copy-start | bytes 3145732
  221.3 23.0 %copy-start.27 = (f32[32,96,256]{2,1,0:T(8,128)S(1)}, f32[32,96,256]{2,1,0:T(8,128)}, u32[]{:S(2)}) copy-start(f32[32,96,256]{2,1,0:T(8,128)} %get-tuple-element.91) | copy-start | bytes 9437188
  223.1 25.6 %copy-start.17 = (f32[512,1024]{1,0:T(8,128)}, f32[512,1024]{1,0:T(8,128)S(1)}, u32[]{:S(2)}) copy-start(f32[512,1024]{1,0:T(8,128)S(1)} %fusion.96) | copy-start | bytes 6291460
  248.7 8.0 %copy-start.19 = (bf16[32,96,256]{2,1,0:T(8,128)(2,1)S(1)}, bf16[32,96,256]{2,1,0:T(8,128)(2,1)}, u32[]{:S(2)}) copy-start(bf16[32,96,256]{2,1,0:T(8,128)(2,1)} %copy-done.18) | copy-start | bytes 4718596
  255.9 30.7 %collective-permute-start.5 = (bf16[32,96,256]{2,1,0:T(8,128)(2,1)}, bf16[32,96,256]{2,1,0:T(8,128)(2,1)}, u32[]{:S(2)}, u32[]{:S(2)}) collective-permute-start(bf16[32,96,256]{2,1,0:T(8,128)(2,1)} %get-tuple-element.93), channel_id=1, source_target_pairs={{0,1},{1,0},{2,3},{3,2},{4,5},{5,4},{6,7},{7,6},{8,9},{9,8},{10,11... | collective-permute-start | bytes 4718600 | tf_op jit(solution)/shard_map/ppermute | solution.py:140
  269.6 167.9 %reduce-scatter.3.cloned.1.call-start = ((), (), s32[]{:S(2)}) async-start(), calls=%async_computation.2 | async-start | bytes 7798784 | tf_op jit(solution)/shard_map/reduce_scatter | solution.py:328
  269.7 5.2 %copy-start.4 = (bf16[32,96,4,64]{1,3,2,0:T(8,128)(2,1)S(1)}, bf16[32,96,4,64]{1,3,2,0:T(8,128)(2,1)}, u32[]{:S(2)}) copy-start(bf16[32,96,4,64]{1,3,2,0:T(8,128)(2,1)} %copy-done.3) | copy-start | bytes 4718596
  289.8 3.9 copy-start.55
  293.7 3.9 copy-start.1
  302.8 1.9 copy-start.9
  306.0 3.1 copy-start.5
  330.2 5.6 %copy-start.35 = (f32[16,64,128]{2,1,0:T(8,128)S(1)}, f32[16,64,128]{2,1,0:T(8,128)}, u32[]{:S(2)}) copy-start(f32[16,64,128]{2,1,0:T(8,128)} %reshape_reshape.16) | copy-start | bytes 1572868
  342.2 12.9 %copy-start.34 = (bf16[512,256]{1,0:T(8,128)(2,1)S(1)}, bf16[512,256]{1,0:T(8,128)(2,1)}, u32[]{:S(2)}) copy-start(bf16[512,256]{1,0:T(8,128)(2,1)} %convert_element_type.192) | copy-start | bytes 786436
  347.9 34.6 %collective-permute-start.6 = (bf16[32,96,256]{2,1,0:T(8,128)(2,1)}, bf16[32,96,256]{2,1,0:T(8,128)(2,1)}, u32[]{:S(2)}, u32[]{:S(2)}) collective-permute-start(bf16[32,96,256]{2,1,0:T(8,128)(2,1)} %convolution_convert_fusion.4), channel_id=1, source_target_pairs={{0,1},{1,0},{2,3},{3,2},{4,5},{5,4},{6,7},{7,6},{8,9},{9,8},{10,11... | collective-permute-start | bytes 4718600 | tf_op jit(solution)/shard_map/ppermute | solution.py:140
  355.0 27.8 %copy-start.31 = (f32[32,96,256]{2,1,0:T(8,128)S(1)}, f32[32,96,256]{2,1,0:T(8,128)}, u32[]{:S(2)}) copy-start(f32[32,96,256]{2,1,0:T(8,128)} %get-tuple-element.88) | copy-start | bytes 9437188
  357.0 25.8 %copy-start.12 = (f32[32,96,256]{2,1,0:T(8,128)S(1)}, f32[32,96,256]{2,1,0:T(8,128)}, u32[]{:S(2)}) copy-start(f32[32,96,256]{2,1,0:T(8,128)} %copy-done.11) | copy-start | bytes 9437188
  382.5 29.1 %collective-permute-start.7 = (bf16[32,96,256]{2,1,0:T(8,128)(2,1)}, bf16[32,96,256]{2,1,0:T(8,128)(2,1)}, u32[]{:S(2)}, u32[]{:S(2)}) collective-permute-start(bf16[32,96,256]{2,1,0:T(8,128)(2,1)} %convolution_convert_fusion.1), channel_id=1, source_target_pairs={{0,1},{1,0},{2,3},{3,2},{4,5},{5,4},{6,7},{7,6},{8,9},{9,8},{10,11... | collective-permute-start | bytes 4718600 | tf_op jit(solution)/shard_map/ppermute | solution.py:140
  382.8 5.9 %copy-start.38 = (bf16[32,96,96]{2,1,0:T(8,128)(2,1)S(1)}, bf16[32,96,96]{2,1,0:T(8,128)(2,1)}, u32[]{:S(2)}) copy-start(bf16[32,96,96]{2,1,0:T(8,128)(2,1)} %copy-done.37) | copy-start | bytes 1769476
  382.8 5.9 %copy-start.45 = (f32[32,96]{1,0:T(8,128)S(1)}, f32[32,96]{1,0:T(8,128)}, u32[]{:S(2)}) copy-start(f32[32,96]{1,0:T(8,128)} %copy-done.44) | copy-start | bytes 36868
  388.7 22.9 %copy-start.10 = (f32[32,96,256]{2,1,0:T(8,128)S(1)}, f32[32,96,256]{2,1,0:T(8,128)}, u32[]{:S(2)}) copy-start(f32[32,96,256]{2,1,0:T(8,128)} %fusion.154) | copy-start | bytes 9437188
  411.6 29.2 %copy-start.41 = (f32[4,192,128]{2,1,0:T(8,128)S(1)}, f32[4,192,128]{2,1,0:T(8,128)}, u32[]{:S(2)}) copy-start(f32[4,192,128]{2,1,0:T(8,128)} %param.41) | copy-start | bytes 1179652
  416.5 26.6 %copy-start.43 = (f32[256,32]{0,1:T(8,128)S(1)}, f32[256,32]{0,1:T(8,128)}, u32[]{:S(2)}) copy-start(f32[256,32]{0,1:T(8,128)} %copy.110) | copy-start | bytes 98308
  416.5 26.6 %copy-start.46 = (f32[256,32]{0,1:T(8,128)S(1)}, f32[256,32]{0,1:T(8,128)}, u32[]{:S(2)}) copy-start(f32[256,32]{0,1:T(8,128)} %param.43) | copy-start | bytes 98308
  416.5 26.6 %copy-start.47 = (f32[256,32]{0,1:T(8,128)S(1)}, f32[256,32]{0,1:T(8,128)}, u32[]{:S(2)}) copy-start(f32[256,32]{0,1:T(8,128)} %param.42) | copy-start | bytes 98308
  (4 other events, 5.4 us)
Sparse Core Ops, SparseCore 0:
  269.7 73.0 reduce-scatter.4
  346.8 90.6 reduce-scatter.2

commit v3 on v2

--- a/solution.py
+++ b/solution.py
@@ -336,8 +336,24 @@
             offset += rows
         return parts
 
+    def summed_over_dp(grads_axes):
+        laid = [lead(grad, axis_number) for grad, axis_number in grads_axes]
+        joined = jnp.concatenate([flat for flat, _ in laid], axis=1)
+        rows = joined.shape[1]
+        arrived = lax.all_to_all(
+            joined.astype(jnp.bfloat16).reshape(-1, lanes), "dp", 0, 0, tiled=True
+        )
+        reduced = jnp.sum(arrived.astype(jnp.float32).reshape(dp_count, rows, lanes), axis=0)
+        parts = []
+        offset = 0
+        for flat, owned_shape in laid:
+            size = flat.shape[1]
+            parts.append(reduced[offset : offset + size].reshape(owned_shape))
+            offset += size
+        return parts
+
     inner_part, outer_part_t = reduced_over_dp([(inner_grad, 0), (outer_grad_t, 0)])
-    mixer_part, output_part_t, query_part = reduced_over_dp(
+    mixer_part, output_part_t, query_part = summed_over_dp(
         [(mixer_full, 1), (output_grad_t, 0), (query_grad, 0)]
     )
     output_part = jnp.transpose(output_part_t)

time: 455 us -> 442 us (0.971)
  waiting for transfers between devices: 160 us -> 137 us
  starting transfers between devices: 10 us -> 17.2 us
  local copies, waits for them, and re-layouts: 46.5 us -> 39.4 us
  matrix products: 140 us -> 147 us
    reduce_scatter x2 -> x1, waiting for transfers between devices: 21.1 us -> 0.01 us  [reduced_over_dp(): lax.psum_scatter(joined.reshape(-1, lanes), 'dp', scatter_dimension=0, ti...]
    dot_general x35, matrix products: 123 us -> 130 us  [product(): return jnp.einsum(form, left, right, preferred_element_type=jnp.float32)]
    concatenate x2 -> x1, other arithmetic: 9.7 us -> 4.64 us  [reduced_over_dp(): joined = jnp.concatenate([flat for flat, _ in laid], axis=1)]
    all_to_all x0 -> x1, starting transfers between devices: none -> 4.96 us  [summed_over_dp(): lax.all_to_all(joined.astype(jnp.bfloat16).reshape(-1, lanes), 'dp', 0, 0...]
    unnamed x118 -> x116, local copies, waits for them, and re-layouts: 9.92 us -> 8.41 us
  transfers between devices with their start and end apart: 10 -> 10, of which waited for: 8 -> 7; matrix products, arithmetic and copies ran while one was open for 41% -> 43% of each run, Pallas kernels for 0% -> 0%
where the time goes in v3:
time: 442 us; the launch traced here: 437 us
  matrix products  147 us (33%)
  waiting for transfers between devices  137 us (31%)
  other arithmetic  81.9 us (19%)
  local copies, waits for them, and re-layouts  39.4 us (9%)
  starting transfers between devices  17.2 us (4%)
  between operations  15 us (3%)
    ppermute x8, waiting for transfers between devices, swap(): return lax.ppermute(values, 'head', pairs)  137 us
    dot_general x35, matrix products, product(): return jnp.einsum(form, left, right, preferred_element_type=jnp.float32)  130 us
    convert_element_type x1, other arithmetic, chunk_pass(): hidden = activated.astype(jnp.bfloat16)  30.5 us
    ppermute x8, starting transfers between devices, swap(): return lax.ppermute(values, 'head', pairs)  12.2 us
    dot_general x2, matrix products, trend_local(): jnp.einsum('wts,wsd->wtd', tiled, parts, preferred_element_type=jnp.float32)  9.66 us
  transfers between devices with their start and end apart: 10, of which 7 were waited for; matrix products, arithmetic and copies ran while one was open for 43% of the time, Pallas kernels for 0%

profile of v3, /device:TPU:0, one launch (start us, length us, event | category | flops | bytes accessed | tf_op | source)
XLA Modules:
  0.0 437.4 jit_solution(11842214498548884625)
XLA Ops:
  7.2 3.3 convert_element_type.200
  10.6 3.0 collective-permute-start
  14.3 3.2 convert_element_type.198
  17.6 2.1 fusion.160
  19.7 4.0 slice_negate_fusion
  23.7 24.6 %collective-permute-done = bf16[32,96,256]{2,1,0:T(8,128)(2,1)} collective-permute-done((bf16[32,96,256]{2,1,0:T(8,128)(2,1)}, bf16[32,96,256]{2,1,0:T(8,128)(2,1)}, u32[]{:S(2)}, u32[]{:S(2)}) %collective-permute-start) | collective-permute-done | bytes 1572896 | tf_op jit(solution)/shard_map/ppermute | solution.py:140
  48.3 3.2 fusion.91
  51.4 4.0 copy.64
  55.4 3.9 fusion.72
  59.4 2.2 fusion.69
  63.5 3.1 fusion.95
  71.3 1.8 collective-permute-start.1
  73.3 7.0 %select_convert_fusion = (bf16[32,96,96]{2,1,0:T(8,128)(2,1)}, bf16[32,96,96]{2,1,0:T(8,128)(2,1)}) fusion(bf16[96,96]{1,0:T(8,128)(2,1)S(1)} %copy-done.48, bf16[96,96]{1,0:T(8,128)(2,1)S(1)} %copy-done.49, bf16[96,96]{1,0:T(8,128)(2,1)S(1)} %copy-done.50, bf16[96,96]{1,0:T(8,128)(2,1)S(1)} %copy-done.51, bf16[96,96]{1,0:T(8,128)(2,1)S(1)} %copy-done.52, ...), kind=kLoop, calls=%fused_computation.132 | loop fusion | flops 2949120 | bytes 1302528 | tf_op jit(solution)/shard_map/convert_element_type | solution.py:66
  80.3 2.5 multiply_convert_fusion.2
  82.7 24.2 %collective-permute-done.1 = bf16[32,96,256]{2,1,0:T(8,128)(2,1)S(1)} collective-permute-done((bf16[32,96,256]{2,1,0:T(8,128)(2,1)S(1)}, bf16[32,96,256]{2,1,0:T(8,128)(2,1)S(1)}, u32[]{:S(2)}, u32[]{:S(2)}) %collective-permute-start.1) | collective-permute-done | bytes 1572896 | tf_op jit(solution)/shard_map/ppermute | solution.py:140
  107.0 2.3 fusion.248
  109.3 6.3 %fusion.112 = (bf16[32,96,256]{2,1,0:T(8,128)(2,1)S(1)}, f32[32,96,256]{2,1,0:T(8,128)}) fusion(f32[32,96,256]{2,1,0:T(8,128)S(1)} %get-tuple-element.86, f32[32,96]{1,0:T(8,128)S(1)} %get-tuple-element.78, bf16[32,96,256]{2,1,0:T(8,128)(2,1)S(1)} %get-tuple-element.62, bf16[32,96,256]{2,1,0:T(8,128)(2,1)} %get-tuple-element.63, ...), kind=kOutput, calls=%fused_computation.147 | convolution fusion | flops 474808320 | bytes 13185024 | tf_op jit(solution)/shard_map/wts,wsd->wtd/dot_general | solution.py:81
  117.1 3.9 fusion.253
  123.3 6.4 %fusion.122 = f32[32,96,1024]{2,1,0:T(8,128)} fusion(bf16[32,96,256]{2,1,0:T(8,128)(2,1)S(1)} %get-tuple-element.90, bf16[1024,512]{1,0:T(8,128)(2,1)S(1)} %convert_element_type.226, s32[]{:T(128)S(6)} %select_n.186), kind=kOutput, calls=%fused_computation.157 | convolution fusion | flops 1610612736 | bytes 14680068 | tf_op jit(solution)/shard_map/wtd,fd->wtf/dot_general | solution.py:44
  129.8 2.4 pad_maximum_fusion.2
  132.2 1.8 fusion.131
  134.0 18.9 %collective-permute-done.2 = bf16[32,96,256]{2,1,0:T(8,128)(2,1)S(1)} collective-permute-done((bf16[32,96,256]{2,1,0:T(8,128)(2,1)S(1)}, bf16[32,96,256]{2,1,0:T(8,128)(2,1)S(1)}, u32[]{:S(2)}, u32[]{:S(2)}) %collective-permute-start.2) | collective-permute-done | bytes 1572896 | tf_op jit(solution)/shard_map/ppermute | solution.py:140
  152.9 7.9 %convert_reduce_fusion.1 = (u32[96,1024]{1,0:T(8,128)S(1)}, u32[96,1024]{1,0:T(8,128)S(1)}, f32[32,96,1024]{2,1,0:T(8,128)}) fusion(f32[32,96,1024]{2,1,0:T(8,128)S(1)} %fusion.131, bf16[32,96,256]{2,1,0:T(8,128)(2,1)S(1)} %collective-permute-done.2, bf16[512,1024]{1,0:T(8,128)(2,1)S(1)} %convert_element_type.224, s32[]{:T(128)S(6)} %select_n.188), kind=kOutput, calls=%fused_computation.6 | convolution fusion | flops 1648164864 | bytes 28049412 | tf_op jit(solution)/shard_map/wtd,de->wte/dot_general | solution.py:44
  160.8 30.5 %multiply_convert_fusion = (bf16[32,96,1024]{2,1,0:T(8,128)(2,1)}, f32[32,96,1024]{2,1,0:T(8,128)}) fusion(f32[32,96,1024]{2,1,0:T(8,128)} %get-tuple-element.89, u32[96,1024]{1,0:T(8,128)S(1)} %get-tuple-element.22, u32[96,1024]{1,0:T(8,128)S(1)} %get-tuple-element.21), kind=kLoop, calls=%fused_computation.8 | loop fusion | flops 213909504 | bytes 32243712 | tf_op jit(solution)/shard_map/convert_element_type | solution.py:222
  192.5 18.2 %add_convert_fusion = bf16[32,96,1024]{2,1,0:T(8,128)(2,1)} fusion(f32[32,96,1024]{2,1,0:T(8,128)} %get-tuple-element.45, f32[32,96,1024]{2,1,0:T(8,128)} %fusion.122, f32[32,96,1024]{2,1,0:T(8,128)} %get-tuple-element.89, bf16[32,96,256]{2,1,0:T(8,128)(2,1)} %copy-done.13, bf16[1024,512]{1,0:T(8,128)(2,1)} %copy-done.17, s32[]{:T(128)S(6)} %select_n.188), kind=kOutput, calls=%fused_computation.7 | convolution fusion | flops 1657798656 | bytes 46137348 | tf_op jit(solution)/shard_map/wtd,fd->wtf/dot_general | solution.py:44
  210.7 6.1 %convolution_convert_fusion.3 = bf16[32,96,256]{2,1,0:T(8,128)(2,1)} fusion(bf16[32,96,1024]{2,1,0:T(8,128)(2,1)} %add_convert_fusion, bf16[512,1024]{1,0:T(8,128)(2,1)} %copy-done.19, s32[]{:T(128)S(6)} %select_n.193), kind=kOutput, calls=%fused_computation.116 | convolution fusion | flops 1611399168 | bytes 8388612 | tf_op jit(solution)/shard_map/wte,ed->wtd/dot_general | solution.py:44
  219.8 2.8 fusion.101
  222.6 2.8 fusion.100
  225.4 2.7 reshape_reshape.21
  230.1 6.2 %fusion.99 = f32[512,1024]{1,0:T(8,128)} fusion(f32[512,1024]{1,0:T(8,128)} %broadcast.229.clone, s32[]{:T(128)S(6)} %select_n.186, bf16[32,96,256]{2,1,0:T(8,128)(2,1)S(1)} %copy-done.12, bf16[32,96,1024]{2,1,0:T(8,128)(2,1)} %get-tuple-element.44), kind=kOutput, calls=%fused_computation.140 | convolution fusion | flops 1610612736 | bytes 8912900 | tf_op jit(solution)/shard_map/wtd,wtf->df/dot_general | solution.py:44
  236.2 12.2 %collective-permute-done.4 = bf16[32,96,256]{2,1,0:T(8,128)(2,1)} collective-permute-done((bf16[32,96,256]{2,1,0:T(8,128)(2,1)}, bf16[32,96,256]{2,1,0:T(8,128)(2,1)}, u32[]{:S(2)}, u32[]{:S(2)}) %collective-permute-start.4) | collective-permute-done | bytes 1572896 | tf_op jit(solution)/shard_map/ppermute | solution.py:140
  248.4 3.8 multiply_convert_fusion.1
  252.3 3.8 fusion.254
  256.9 2.8 fusion.98
  259.7 2.7 reshape_reshape.22
  262.4 4.6 %pad_maximum_fusion = f32[16,512,128]{2,1,0:T(8,128)} fusion(f32[16,256,128]{2,1,0:T(8,128)} %reshape_reshape.22, f32[16,256,128]{2,1,0:T(8,128)} %reshape_reshape.21), kind=kLoop, calls=%fused_computation.49 | loop fusion | flops 1048576 | bytes 8388608 | tf_op jit(solution)/shard_map/concatenate | solution.py:327
  267.8 3.5 fusion.114
  271.3 2.0 fusion.151
  273.4 13.4 %collective-permute-done.5 = bf16[32,96,256]{2,1,0:T(8,128)(2,1)} collective-permute-done((bf16[32,96,256]{2,1,0:T(8,128)(2,1)}, bf16[32,96,256]{2,1,0:T(8,128)(2,1)}, u32[]{:S(2)}, u32[]{:S(2)}) %collective-permute-start.5) | collective-permute-done | bytes 1572896 | tf_op jit(solution)/shard_map/ppermute | solution.py:140
  286.8 3.2 add_convert_fusion.3
  290.0 4.2 copy.75
  294.2 3.9 bitcast_negate_fusion
  298.2 2.2 fusion.78
  300.4 2.9 maximum_bitcast_fusion
  306.7 1.9 copy.86
  309.1 2.9 fusion.113
  313.1 7.9 %fusion.92 = bf16[32,4,48,128]{3,0,2,1:T(8,128)(2,1)} fusion(bf16[32,4,48,128]{3,2,0,1:T(8,128)(2,1)} %get-tuple-element.67, bf16[4,48,64,64]{3,2,1,0:T(8,128)(2,1)} %get-tuple-element.65, bf16[4,48,64,64]{3,2,1,0:T(8,128)(2,1)} %get-tuple-element.64, bf16[4,48,64,128]{3,2,1,0:T(8,128)(2,1)S(1)} %bitcast.243), kind=kOutput, calls=%fused_computation.135 | convolution fusion | flops 220987392 | bytes 9437184 | tf_op jit(solution)/shard_map/whmo,hmio->whmi/dot_general | solution.py:44
  320.9 2.6 fusion.249
  326.9 2.0 convolution_bitcast_fusion.4
  329.0 2.0 convolution_bitcast_fusion.5
  331.3 3.4 pad_maximum_fusion.1
  334.8 5.0 %all-to-all-start = ((bf16[16,896,128]{2,1,0:T(8,128)(2,1)}), bf16[16,896,128]{2,1,0:T(8,128)(2,1)}, u32[]{:S(2)}, u32[]{:S(2)}) async-start(bf16[16,896,128]{2,1,0:T(8,128)(2,1)} %pad_maximum_fusion.1), calls=%async_computation | async-start | bytes 7340032 | tf_op jit(solution)/shard_map/all_to_all | solution.py:343
  339.8 5.8 %convolution_convert_fusion.4 = bf16[32,96,256]{2,1,0:T(8,128)(2,1)} fusion(bf16[32,96,1024]{2,1,0:T(8,128)(2,1)} %get-tuple-element.44, bf16[1024,512]{1,0:T(8,128)(2,1)S(1)} %copy-done.18, s32[]{:T(128)S(6)} %select_n.193), kind=kOutput, calls=%fused_computation.117 | convolution fusion | flops 1611399168 | bytes 8388612 | tf_op jit(solution)/shard_map/wte,ed->wtd/dot_general | solution.py:44
  347.0 2.0 constant_dynamic-slice_fusion
  353.6 2.0 convolution_convert_fusion.1
  355.6 2.5 fusion.158
  358.1 24.4 %collective-permute-done.6 = bf16[32,96,256]{2,1,0:T(8,128)(2,1)} collective-permute-done((bf16[32,96,256]{2,1,0:T(8,128)(2,1)}, bf16[32,96,256]{2,1,0:T(8,128)(2,1)}, u32[]{:S(2)}, u32[]{:S(2)}) %collective-permute-start.6) | collective-permute-done | bytes 1572896 | tf_op jit(solution)/shard_map/ppermute | solution.py:140
  384.0 5.8 %fusion.247 = (bf16[32,96,256]{2,1,0:T(8,128)(2,1)S(1)}, bf16[32,96,256]{2,1,0:T(8,128)(2,1)S(1)}, bf16[32,96,256]{2,1,0:T(8,128)(2,1)S(1)}, f32[32,96,256]{2,1,0:T(8,128)S(1)}) fusion(bf16[32,96,256]{2,1,0:T(8,128)(2,1)} %collective-permute-done.6, bf16[32,96,1024]{2,1,0:T(8,128)(2,1)} %get-tuple-element.44, bf16[1024,512]{1,0:T(8,128)(2,1)S(1)} %copy-done.18, ...), kind=kOutput, calls=%fused_computation.305 | convolution fusion | flops 1620049920 | bytes 22560772 | tf_op jit(solution)/shard_map/wte,ed->wtd/dot_general | solution.py:44
  389.9 3.4 multiply_subtract_fusion
  395.9 1.8 multiply_add_fusion.3
  399.5 19.1 %collective-permute-done.7 = bf16[32,96,256]{2,1,0:T(8,128)(2,1)} collective-permute-done((bf16[32,96,256]{2,1,0:T(8,128)(2,1)}, bf16[32,96,256]{2,1,0:T(8,128)(2,1)}, u32[]{:S(2)}, u32[]{:S(2)}) %collective-permute-start.7) | collective-permute-done | bytes 1572896 | tf_op jit(solution)/shard_map/ppermute | solution.py:140
  418.6 4.8 %add_add_fusion = f32[32,96,256]{2,1,0:T(8,128)} fusion(f32[32,96,256]{2,1,0:T(8,128)} %get-tuple-element.94, f32[32,96,256]{2,1,0:T(8,128)S(1)} %copy-done.6, bf16[32,96,256]{2,1,0:T(8,128)(2,1)} %collective-permute-done.7), kind=kLoop, calls=%fused_computation.59 | loop fusion | flops 2359296 | bytes 11010048 | tf_op jit(solution)/shard_map/add | solution.py:282
  423.4 2.7 convert_reduce_fusion.2
  427.6 2.1 multiply_add_fusion
  (167 shorter events, 41.6 us)
Async XLA Ops:
  7.2 6.4 %copy-start.36 = (f32[512,256]{1,0:T(8,128)S(1)}, f32[512,256]{1,0:T(8,128)}, u32[]{:S(2)}) copy-start(f32[512,256]{1,0:T(8,128)} %param.33) | copy-start | bytes 1572868
  7.2 386.1 %reduce-scatter.2.cloned.1.call-start = ((), (), s32[]{:S(2)}) async-start(), calls=%async_computation.2 | async-start | bytes 4456448 | tf_op jit(solution)/shard_map/reduce_scatter | solution.py:328
  10.6 37.7 %collective-permute-start = (bf16[32,96,256]{2,1,0:T(8,128)(2,1)}, bf16[32,96,256]{2,1,0:T(8,128)(2,1)}, u32[]{:S(2)}, u32[]{:S(2)}) collective-permute-start(bf16[32,96,256]{2,1,0:T(8,128)(2,1)} %convert_element_type.200), channel_id=1, source_target_pairs={{0,1},{1,0},{2,3},{3,2},{4,5},{5,4},{6,7},{7,6},{8,9},{9,8},{10,11... | collective-permute-start | bytes 4718600 | tf_op jit(solution)/shard_map/ppermute | solution.py:140
  14.3 3.3 copy-start.32
  14.3 3.3 copy-start.39
  19.7 28.6 %copy-start.29 = (bf16[512,256]{1,0:T(8,128)(2,1)S(1)}, bf16[512,256]{1,0:T(8,128)(2,1)}, u32[]{:S(2)}) copy-start(bf16[512,256]{1,0:T(8,128)(2,1)} %convert_element_type.199) | copy-start | bytes 786436
  55.4 4.0 copy-start.2
  59.4 3.1 copy-start.26
  70.2 3.0 copy-start.47
  70.2 3.0 copy-start.48
  70.2 3.0 copy-start.49
  70.2 3.0 copy-start.50
  70.2 3.0 copy-start.51
  70.3 3.0 copy-start.52
  70.5 36.5 %copy-start.3 = (bf16[32,96,4,64]{1,3,2,0:T(8,128)(2,1)}, bf16[32,96,4,64]{1,3,2,0:T(8,128)(2,1)S(1)}, u32[]{:S(2)}) copy-start(bf16[32,96,4,64]{1,3,2,0:T(8,128)(2,1)S(1)} %copy.70) | copy-start | bytes 4718596
  70.5 9.8 %copy-start.24 = (f32[32,96,256]{2,1,0:T(8,128)S(1)}, f32[32,96,256]{2,1,0:T(8,128)}, u32[]{:S(2)}) copy-start(f32[32,96,256]{2,1,0:T(8,128)} %param.30) | copy-start | bytes 9437188
  71.3 35.6 %collective-permute-start.1 = (bf16[32,96,256]{2,1,0:T(8,128)(2,1)S(1)}, bf16[32,96,256]{2,1,0:T(8,128)(2,1)S(1)}, u32[]{:S(2)}, u32[]{:S(2)}) collective-permute-start(bf16[32,96,256]{2,1,0:T(8,128)(2,1)S(1)} %convolution_convert_fusion.5), channel_id=1, source_target_pairs={{0,1},{1,0},{2,3},{3,2},{4,5},{5,4},{6,7},{7,6},{8,9},{9,8},{10,11... | collective-permute-start | bytes 4718600 | tf_op jit(solution)/shard_map/ppermute | solution.py:140
  73.2 9.5 %copy-start.41 = (f32[32,96]{1,0:T(8,128)}, f32[32,96]{1,0:T(8,128)S(1)}, u32[]{:S(2)}) copy-start(f32[32,96]{1,0:T(8,128)S(1)} %get-tuple-element.38) | copy-start | bytes 36868
  80.3 26.7 %copy-start.5 = (f32[32,96,256]{2,1,0:T(8,128)S(1)}, f32[32,96,256]{2,1,0:T(8,128)}, u32[]{:S(2)}) copy-start(f32[32,96,256]{2,1,0:T(8,128)} %param.29) | copy-start | bytes 9437188
  109.3 6.3 %copy-start.7 = (f32[32,96,256]{2,1,0:T(8,128)}, f32[32,96,256]{2,1,0:T(8,128)S(1)}, u32[]{:S(2)}) copy-start(f32[32,96,256]{2,1,0:T(8,128)S(1)} %get-tuple-element.86) | copy-start | bytes 9437188
  109.3 7.7 %copy-start.31 = (bf16[32,96,256]{2,1,0:T(8,128)(2,1)S(1)}, bf16[32,96,256]{2,1,0:T(8,128)(2,1)}, u32[]{:S(2)}) copy-start(bf16[32,96,256]{2,1,0:T(8,128)(2,1)} %get-tuple-element.56) | copy-start | bytes 4718596
  109.3 7.7 %copy-start.33 = (bf16[32,96,96]{2,1,0:T(8,128)(2,1)S(1)}, bf16[32,96,96]{2,1,0:T(8,128)(2,1)}, u32[]{:S(2)}) copy-start(bf16[32,96,96]{2,1,0:T(8,128)(2,1)} %get-tuple-element.76) | copy-start | bytes 1769476
  115.6 16.6 %copy-start.9 = (bf16[32,96,256]{2,1,0:T(8,128)(2,1)}, bf16[32,96,256]{2,1,0:T(8,128)(2,1)S(1)}, u32[]{:S(2)}) copy-start(bf16[32,96,256]{2,1,0:T(8,128)(2,1)S(1)} %get-tuple-element.87) | copy-start | bytes 4718596
  115.6 37.3 %collective-permute-start.2 = (bf16[32,96,256]{2,1,0:T(8,128)(2,1)S(1)}, bf16[32,96,256]{2,1,0:T(8,128)(2,1)S(1)}, u32[]{:S(2)}, u32[]{:S(2)}) collective-permute-start(bf16[32,96,256]{2,1,0:T(8,128)(2,1)S(1)} %get-tuple-element.87), channel_id=1, source_target_pairs={{0,1},{1,0},{2,3},{3,2},{4,5},{5,4},{6,7},{7,6},{8,9},{9,8},{10,11... | collective-permute-start | bytes 4718600 | tf_op jit(solution)/shard_map/ppermute | solution.py:140
  117.1 4.5 %copy-start.28 = (f32[512,1024]{1,0:T(8,128)S(1)}, f32[512,1024]{1,0:T(8,128)}, u32[]{:S(2)}) copy-start(f32[512,1024]{1,0:T(8,128)} %param.36) | copy-start | bytes 6291460
  121.0 2.3 copy-start.11
  121.0 2.2 copy-start.21
  121.0 70.3 %collective-permute-start.3 = (bf16[32,96,256]{2,1,0:T(8,128)(2,1)S(1)}, bf16[32,96,256]{2,1,0:T(8,128)(2,1)S(1)}, u32[]{:S(2)}, u32[]{:S(2)}) collective-permute-start(bf16[32,96,256]{2,1,0:T(8,128)(2,1)S(1)} %get-tuple-element.90), channel_id=1, source_target_pairs={{0,1},{1,0},{2,3},{3,2},{4,5},{5,4},{6,7},{7,6},{8,9},{9,8},{10,11... | collective-permute-start | bytes 4718600 | tf_op jit(solution)/shard_map/ppermute | solution.py:140
  123.1 29.7 %copy-start.19 = (bf16[512,1024]{1,0:T(8,128)(2,1)}, bf16[512,1024]{1,0:T(8,128)(2,1)S(1)}, u32[]{:S(2)}) copy-start(bf16[512,1024]{1,0:T(8,128)(2,1)S(1)} %convert_element_type.224) | copy-start | bytes 3145732
  123.3 6.5 %copy-start.17 = (bf16[1024,512]{1,0:T(8,128)(2,1)}, bf16[1024,512]{1,0:T(8,128)(2,1)S(1)}, u32[]{:S(2)}) copy-start(bf16[1024,512]{1,0:T(8,128)(2,1)S(1)} %convert_element_type.226) | copy-start | bytes 3145732
  152.9 7.9 %copy-start.15 = (bf16[32,96,256]{2,1,0:T(8,128)(2,1)}, bf16[32,96,256]{2,1,0:T(8,128)(2,1)S(1)}, u32[]{:S(2)}) copy-start(bf16[32,96,256]{2,1,0:T(8,128)(2,1)S(1)} %collective-permute-done.2) | copy-start | bytes 4718596
  210.7 9.1 %copy-start = (bf16[32,96,1024]{2,1,0:T(8,128)(2,1)S(1)}, bf16[32,96,1024]{2,1,0:T(8,128)(2,1)}, u32[]{:S(2)}) copy-start(bf16[32,96,1024]{2,1,0:T(8,128)(2,1)} %add_convert_fusion) | copy-start | bytes 18874372
  216.8 3.0 copy-start.10
  216.8 31.6 %collective-permute-start.4 = (bf16[32,96,256]{2,1,0:T(8,128)(2,1)}, bf16[32,96,256]{2,1,0:T(8,128)(2,1)}, u32[]{:S(2)}, u32[]{:S(2)}) collective-permute-start(bf16[32,96,256]{2,1,0:T(8,128)(2,1)} %convolution_convert_fusion.3), channel_id=1, source_target_pairs={{0,1},{1,0},{2,3},{3,2},{4,5},{5,4},{6,7},{7,6},{8,9},{9,8},{10,11... | collective-permute-start | bytes 4718600 | tf_op jit(solution)/shard_map/ppermute | solution.py:140
  219.8 2.8 copy-start.16
  228.2 20.2 %slice-start.2 = ((s8[6291456]{0:T(1024)(128)(4,1)}), s8[4194304]{0:T(1024)(128)(4,1)S(1)}, s32[]{:S(2)}) async-start(s8[6291456]{0:T(1024)(128)(4,1)} %bitcast.239), calls=%async_computation.5 | async-start | bytes 8388608
  230.0 18.3 %slice-start.3 = ((s8[6291456]{0:T(1024)(128)(4,1)}), s8[2097152]{0:T(1024)(128)(4,1)S(1)}, s32[]{:S(2)}) async-start(s8[6291456]{0:T(1024)(128)(4,1)} %bitcast.239), calls=%async_computation.6 | async-start | bytes 4194304
  230.0 18.3 %copy-start.20 = (bf16[512,1024]{1,0:T(8,128)(2,1)S(1)}, bf16[512,1024]{1,0:T(8,128)(2,1)}, u32[]{:S(2)}) copy-start(bf16[512,1024]{1,0:T(8,128)(2,1)} %copy-done.19) | copy-start | bytes 3145732
  230.0 18.4 %copy-start.22 = (f32[32,96,256]{2,1,0:T(8,128)S(1)}, f32[32,96,256]{2,1,0:T(8,128)}, u32[]{:S(2)}) copy-start(f32[32,96,256]{2,1,0:T(8,128)} %get-tuple-element.91) | copy-start | bytes 9437188
  248.4 3.8 copy-start.35
  248.4 8.5 %slice-start = ((s8[6291456]{0:T(1024)(128)(4,1)}), s8[4194304]{0:T(1024)(128)(4,1)S(1)}, s32[]{:S(2)}) async-start(s8[6291456]{0:T(1024)(128)(4,1)} %bitcast.237), calls=%async_computation.3 | async-start | bytes 8388608
  252.2 4.7 %slice-start.1 = ((s8[6291456]{0:T(1024)(128)(4,1)}), s8[2097152]{0:T(1024)(128)(4,1)S(1)}, s32[]{:S(2)}) async-start(s8[6291456]{0:T(1024)(128)(4,1)} %bitcast.237), calls=%async_computation.4 | async-start | bytes 4194304
  252.3 4.7 %copy-start.14 = (bf16[32,96,256]{2,1,0:T(8,128)(2,1)S(1)}, bf16[32,96,256]{2,1,0:T(8,128)(2,1)}, u32[]{:S(2)}) copy-start(bf16[32,96,256]{2,1,0:T(8,128)(2,1)} %copy-done.13) | copy-start | bytes 4718596
  256.0 30.7 %collective-permute-start.5 = (bf16[32,96,256]{2,1,0:T(8,128)(2,1)}, bf16[32,96,256]{2,1,0:T(8,128)(2,1)}, u32[]{:S(2)}, u32[]{:S(2)}) collective-permute-start(bf16[32,96,256]{2,1,0:T(8,128)(2,1)} %get-tuple-element.93), channel_id=1, source_target_pairs={{0,1},{1,0},{2,3},{3,2},{4,5},{5,4},{6,7},{7,6},{8,9},{9,8},{10,11... | collective-permute-start | bytes 4718600 | tf_op jit(solution)/shard_map/ppermute | solution.py:140
  294.2 3.9 copy-start.1
  303.3 1.9 copy-start.23
  306.7 2.4 copy-start.4
  334.8 5.0 %copy-start.18 = (bf16[1024,512]{1,0:T(8,128)(2,1)S(1)}, bf16[1024,512]{1,0:T(8,128)(2,1)}, u32[]{:S(2)}) copy-start(bf16[1024,512]{1,0:T(8,128)(2,1)} %copy-done.17) | copy-start | bytes 3145732
  334.8 88.7 %all-to-all-start = ((bf16[16,896,128]{2,1,0:T(8,128)(2,1)}), bf16[16,896,128]{2,1,0:T(8,128)(2,1)}, u32[]{:S(2)}, u32[]{:S(2)}) async-start(bf16[16,896,128]{2,1,0:T(8,128)(2,1)} %pad_maximum_fusion.1), calls=%async_computation | async-start | bytes 7340032 | tf_op jit(solution)/shard_map/all_to_all | solution.py:343
  339.7 13.8 %copy-start.30 = (bf16[512,256]{1,0:T(8,128)(2,1)S(1)}, bf16[512,256]{1,0:T(8,128)(2,1)}, u32[]{:S(2)}) copy-start(bf16[512,256]{1,0:T(8,128)(2,1)} %convert_element_type.199) | copy-start | bytes 786436
  345.5 37.0 %collective-permute-start.6 = (bf16[32,96,256]{2,1,0:T(8,128)(2,1)}, bf16[32,96,256]{2,1,0:T(8,128)(2,1)}, u32[]{:S(2)}, u32[]{:S(2)}) collective-permute-start(bf16[32,96,256]{2,1,0:T(8,128)(2,1)} %convolution_convert_fusion.4), channel_id=1, source_target_pairs={{0,1},{1,0},{2,3},{3,2},{4,5},{5,4},{6,7},{7,6},{8,9},{9,8},{10,11... | collective-permute-start | bytes 4718600 | tf_op jit(solution)/shard_map/ppermute | solution.py:140
  353.6 30.5 %copy-start.27 = (f32[32,96,256]{2,1,0:T(8,128)S(1)}, f32[32,96,256]{2,1,0:T(8,128)}, u32[]{:S(2)}) copy-start(f32[32,96,256]{2,1,0:T(8,128)} %get-tuple-element.88) | copy-start | bytes 9437188
  355.6 28.5 %copy-start.8 = (f32[32,96,256]{2,1,0:T(8,128)S(1)}, f32[32,96,256]{2,1,0:T(8,128)}, u32[]{:S(2)}) copy-start(f32[32,96,256]{2,1,0:T(8,128)} %copy-done.7) | copy-start | bytes 9437188
  382.5 36.1 %collective-permute-start.7 = (bf16[32,96,256]{2,1,0:T(8,128)(2,1)}, bf16[32,96,256]{2,1,0:T(8,128)(2,1)}, u32[]{:S(2)}, u32[]{:S(2)}) collective-permute-start(bf16[32,96,256]{2,1,0:T(8,128)(2,1)} %convolution_convert_fusion.1), channel_id=1, source_target_pairs={{0,1},{1,0},{2,3},{3,2},{4,5},{5,4},{6,7},{7,6},{8,9},{9,8},{10,11... | collective-permute-start | bytes 4718600 | tf_op jit(solution)/shard_map/ppermute | solution.py:140
  384.0 5.9 %copy-start.34 = (bf16[32,96,96]{2,1,0:T(8,128)(2,1)S(1)}, bf16[32,96,96]{2,1,0:T(8,128)(2,1)}, u32[]{:S(2)}) copy-start(bf16[32,96,96]{2,1,0:T(8,128)(2,1)} %get-tuple-element.76) | copy-start | bytes 1769476
  384.0 5.9 %copy-start.42 = (f32[32,96]{1,0:T(8,128)S(1)}, f32[32,96]{1,0:T(8,128)}, u32[]{:S(2)}) copy-start(f32[32,96]{1,0:T(8,128)} %copy-done.41) | copy-start | bytes 36868
  389.9 28.7 %copy-start.6 = (f32[32,96,256]{2,1,0:T(8,128)S(1)}, f32[32,96,256]{2,1,0:T(8,128)}, u32[]{:S(2)}) copy-start(f32[32,96,256]{2,1,0:T(8,128)} %fusion.158) | copy-start | bytes 9437188
  423.4 2.8 copy-start.43
  423.4 2.8 copy-start.44
  423.4 4.2 copy-start.37
  423.4 4.2 copy-start.38
  423.4 6.3 %copy-start.40 = (f32[256,32]{0,1:T(8,128)S(1)}, f32[256,32]{0,1:T(8,128)}, u32[]{:S(2)}) copy-start(f32[256,32]{0,1:T(8,128)} %copy.110) | copy-start | bytes 98308
  423.4 6.3 %copy-start.45 = (f32[256,32]{0,1:T(8,128)S(1)}, f32[256,32]{0,1:T(8,128)}, u32[]{:S(2)}) copy-start(f32[256,32]{0,1:T(8,128)} %param.43) | copy-start | bytes 98308
  423.4 6.3 %copy-start.46 = (f32[256,32]{0,1:T(8,128)S(1)}, f32[256,32]{0,1:T(8,128)}, u32[]{:S(2)}) copy-start(f32[256,32]{0,1:T(8,128)} %param.42) | copy-start | bytes 98308
  (3 other events, 4.9 us)
Sparse Core Ops, SparseCore 0:
  267.2 73.0 reduce-scatter.1

commit v4 on v3

--- a/solution.py
+++ b/solution.py
@@ -6,11 +6,11 @@
 from jax import lax
 from jax.sharding import PartitionSpec as P
 
+
 D = 512
 FF = 2048
 
 
-highest = lax.Precision.HIGHEST
 pool_sizes = (7, 12, 14, 24, 48)
 mixer_spread = 0.07
 momentum_decay = 0.9
@@ -127,7 +127,6 @@
     windows, length, local_width = inputs.shape
     head_count, mode_count = modes.shape
     head_size = local_width // head_count
-    hidden_width = inner_weight.shape[1]
     head_parts = lax.axis_size("head")
     me = lax.axis_index("head")
     shifts = list(range(1, head_parts))
@@ -170,12 +169,6 @@
         out = jnp.zeros((total_rows,) + parts[0][1].shape[1:], jnp.float32)
         for block, part in parts:
             out = lax.dynamic_update_slice_in_dim(out, part, block * size, 0)
-        return out
-
-    def placed_cols(parts, size, total_cols):
-        out = jnp.zeros(parts[0][1].shape[:1] + (total_cols,), jnp.float32)
-        for block, part in parts:
-            out = lax.dynamic_update_slice_in_dim(out, part, block * size, 1)
         return out
 
     model_width = local_width * head_parts

time: 442 us -> 442 us (level)
  no operation moved by 1% of the time
where the time goes in v4:
time: 442 us; the launch traced here: 438 us
  matrix products  147 us (33%)
  waiting for transfers between devices  137 us (31%)
  other arithmetic  81.9 us (19%)
  local copies, waits for them, and re-layouts  39.5 us (9%)
  starting transfers between devices  17.2 us (4%)
  between operations  15.1 us (3%)
    ppermute x8, waiting for transfers between devices, swap(): return lax.ppermute(values, 'head', pairs)  137 us
    dot_general x35, matrix products, product(): return jnp.einsum(form, left, right, preferred_element_type=jnp.float32)  130 us
    convert_element_type x1, other arithmetic, chunk_pass(): hidden = activated.astype(jnp.bfloat16)  30.8 us
    ppermute x8, starting transfers between devices, swap(): return lax.ppermute(values, 'head', pairs)  12.2 us
    dot_general x2, matrix products, trend_local(): jnp.einsum('wts,wsd->wtd', tiled, parts, preferred_element_type=jnp.float32)  9.66 us
  transfers between devices with their start and end apart: 10, of which 7 were waited for; matrix products, arithmetic and copies ran while one was open for 43% of the time, Pallas kernels for 0%

profile of v4, /device:TPU:0, one launch (start us, length us, event | category | flops | bytes accessed | tf_op | source)
XLA Modules:
  0.0 437.8 jit_solution(11842214498548884625)
XLA Ops:
  7.2 3.3 convert_element_type.200
  10.6 3.0 collective-permute-start
  14.3 3.2 convert_element_type.198
  17.6 2.1 fusion.160
  19.7 4.0 slice_negate_fusion
  23.7 24.6 %collective-permute-done = bf16[32,96,256]{2,1,0:T(8,128)(2,1)} collective-permute-done((bf16[32,96,256]{2,1,0:T(8,128)(2,1)}, bf16[32,96,256]{2,1,0:T(8,128)(2,1)}, u32[]{:S(2)}, u32[]{:S(2)}) %collective-permute-start) | collective-permute-done | bytes 1572896 | tf_op jit(solution)/shard_map/ppermute | solution.py:139
  48.3 3.1 fusion.91
  51.4 4.3 copy.64
  55.7 3.9 fusion.72
  59.7 2.2 fusion.69
  63.8 3.1 fusion.95
  71.6 1.8 collective-permute-start.1
  73.5 7.0 %select_convert_fusion = (bf16[32,96,96]{2,1,0:T(8,128)(2,1)}, bf16[32,96,96]{2,1,0:T(8,128)(2,1)}) fusion(bf16[96,96]{1,0:T(8,128)(2,1)S(1)} %copy-done.48, bf16[96,96]{1,0:T(8,128)(2,1)S(1)} %copy-done.49, bf16[96,96]{1,0:T(8,128)(2,1)S(1)} %copy-done.50, bf16[96,96]{1,0:T(8,128)(2,1)S(1)} %copy-done.51, bf16[96,96]{1,0:T(8,128)(2,1)S(1)} %copy-done.52, ...), kind=kLoop, calls=%fused_computation.132 | loop fusion | flops 2949120 | bytes 1302528 | tf_op jit(solution)/shard_map/convert_element_type | solution.py:66
  80.6 2.2 multiply_convert_fusion.2
  82.8 24.5 %collective-permute-done.1 = bf16[32,96,256]{2,1,0:T(8,128)(2,1)S(1)} collective-permute-done((bf16[32,96,256]{2,1,0:T(8,128)(2,1)S(1)}, bf16[32,96,256]{2,1,0:T(8,128)(2,1)S(1)}, u32[]{:S(2)}, u32[]{:S(2)}) %collective-permute-start.1) | collective-permute-done | bytes 1572896 | tf_op jit(solution)/shard_map/ppermute | solution.py:139
  107.3 2.3 fusion.248
  109.6 6.3 %fusion.112 = (bf16[32,96,256]{2,1,0:T(8,128)(2,1)S(1)}, f32[32,96,256]{2,1,0:T(8,128)}) fusion(f32[32,96,256]{2,1,0:T(8,128)S(1)} %get-tuple-element.86, f32[32,96]{1,0:T(8,128)S(1)} %get-tuple-element.78, bf16[32,96,256]{2,1,0:T(8,128)(2,1)S(1)} %get-tuple-element.62, bf16[32,96,256]{2,1,0:T(8,128)(2,1)} %get-tuple-element.63, ...), kind=kOutput, calls=%fused_computation.147 | convolution fusion | flops 474808320 | bytes 13185024 | tf_op jit(solution)/shard_map/wts,wsd->wtd/dot_general | solution.py:81
  117.3 3.9 fusion.253
  123.6 6.4 %fusion.122 = f32[32,96,1024]{2,1,0:T(8,128)} fusion(bf16[32,96,256]{2,1,0:T(8,128)(2,1)S(1)} %get-tuple-element.90, bf16[1024,512]{1,0:T(8,128)(2,1)S(1)} %convert_element_type.226, s32[]{:T(128)S(6)} %select_n.186), kind=kOutput, calls=%fused_computation.157 | convolution fusion | flops 1610612736 | bytes 14680068 | tf_op jit(solution)/shard_map/wtd,fd->wtf/dot_general | solution.py:44
  130.0 2.4 pad_maximum_fusion.2
  132.4 1.8 fusion.131
  134.3 18.9 %collective-permute-done.2 = bf16[32,96,256]{2,1,0:T(8,128)(2,1)S(1)} collective-permute-done((bf16[32,96,256]{2,1,0:T(8,128)(2,1)S(1)}, bf16[32,96,256]{2,1,0:T(8,128)(2,1)S(1)}, u32[]{:S(2)}, u32[]{:S(2)}) %collective-permute-start.2) | collective-permute-done | bytes 1572896 | tf_op jit(solution)/shard_map/ppermute | solution.py:139
  153.1 7.9 %convert_reduce_fusion.1 = (u32[96,1024]{1,0:T(8,128)S(1)}, u32[96,1024]{1,0:T(8,128)S(1)}, f32[32,96,1024]{2,1,0:T(8,128)}) fusion(f32[32,96,1024]{2,1,0:T(8,128)S(1)} %fusion.131, bf16[32,96,256]{2,1,0:T(8,128)(2,1)S(1)} %collective-permute-done.2, bf16[512,1024]{1,0:T(8,128)(2,1)S(1)} %convert_element_type.224, s32[]{:T(128)S(6)} %select_n.188), kind=kOutput, calls=%fused_computation.6 | convolution fusion | flops 1648164864 | bytes 28049412 | tf_op jit(solution)/shard_map/wtd,de->wte/dot_general | solution.py:44
  161.1 30.8 %multiply_convert_fusion = (bf16[32,96,1024]{2,1,0:T(8,128)(2,1)}, f32[32,96,1024]{2,1,0:T(8,128)}) fusion(f32[32,96,1024]{2,1,0:T(8,128)} %get-tuple-element.89, u32[96,1024]{1,0:T(8,128)S(1)} %get-tuple-element.22, u32[96,1024]{1,0:T(8,128)S(1)} %get-tuple-element.21), kind=kLoop, calls=%fused_computation.8 | loop fusion | flops 213909504 | bytes 32243712 | tf_op jit(solution)/shard_map/convert_element_type | solution.py:215
  193.0 18.2 %add_convert_fusion = bf16[32,96,1024]{2,1,0:T(8,128)(2,1)} fusion(f32[32,96,1024]{2,1,0:T(8,128)} %get-tuple-element.45, f32[32,96,1024]{2,1,0:T(8,128)} %fusion.122, f32[32,96,1024]{2,1,0:T(8,128)} %get-tuple-element.89, bf16[32,96,256]{2,1,0:T(8,128)(2,1)} %copy-done.13, bf16[1024,512]{1,0:T(8,128)(2,1)} %copy-done.17, s32[]{:T(128)S(6)} %select_n.188), kind=kOutput, calls=%fused_computation.7 | convolution fusion | flops 1657798656 | bytes 46137348 | tf_op jit(solution)/shard_map/wtd,fd->wtf/dot_general | solution.py:44
  211.2 6.1 %convolution_convert_fusion.3 = bf16[32,96,256]{2,1,0:T(8,128)(2,1)} fusion(bf16[32,96,1024]{2,1,0:T(8,128)(2,1)} %add_convert_fusion, bf16[512,1024]{1,0:T(8,128)(2,1)} %copy-done.19, s32[]{:T(128)S(6)} %select_n.193), kind=kOutput, calls=%fused_computation.116 | convolution fusion | flops 1611399168 | bytes 8388612 | tf_op jit(solution)/shard_map/wte,ed->wtd/dot_general | solution.py:44
  220.3 2.8 fusion.101
  223.1 2.8 fusion.100
  225.9 2.7 reshape_reshape.21
  230.6 6.2 %fusion.99 = f32[512,1024]{1,0:T(8,128)} fusion(f32[512,1024]{1,0:T(8,128)} %broadcast.229.clone, s32[]{:T(128)S(6)} %select_n.186, bf16[32,96,256]{2,1,0:T(8,128)(2,1)S(1)} %copy-done.12, bf16[32,96,1024]{2,1,0:T(8,128)(2,1)} %get-tuple-element.44), kind=kOutput, calls=%fused_computation.140 | convolution fusion | flops 1610612736 | bytes 8912900 | tf_op jit(solution)/shard_map/wtd,wtf->df/dot_general | solution.py:44
  236.7 12.2 %collective-permute-done.4 = bf16[32,96,256]{2,1,0:T(8,128)(2,1)} collective-permute-done((bf16[32,96,256]{2,1,0:T(8,128)(2,1)}, bf16[32,96,256]{2,1,0:T(8,128)(2,1)}, u32[]{:S(2)}, u32[]{:S(2)}) %collective-permute-start.4) | collective-permute-done | bytes 1572896 | tf_op jit(solution)/shard_map/ppermute | solution.py:139
  249.0 3.8 multiply_convert_fusion.1
  252.8 3.8 fusion.254
  257.4 2.8 fusion.98
  260.2 2.7 reshape_reshape.22
  262.9 4.6 %pad_maximum_fusion = f32[16,512,128]{2,1,0:T(8,128)} fusion(f32[16,256,128]{2,1,0:T(8,128)} %reshape_reshape.22, f32[16,256,128]{2,1,0:T(8,128)} %reshape_reshape.21), kind=kLoop, calls=%fused_computation.49 | loop fusion | flops 1048576 | bytes 8388608 | tf_op jit(solution)/shard_map/concatenate | solution.py:320
  268.3 3.5 fusion.114
  271.9 2.0 fusion.151
  273.9 13.4 %collective-permute-done.5 = bf16[32,96,256]{2,1,0:T(8,128)(2,1)} collective-permute-done((bf16[32,96,256]{2,1,0:T(8,128)(2,1)}, bf16[32,96,256]{2,1,0:T(8,128)(2,1)}, u32[]{:S(2)}, u32[]{:S(2)}) %collective-permute-start.5) | collective-permute-done | bytes 1572896 | tf_op jit(solution)/shard_map/ppermute | solution.py:139
  287.3 3.2 add_convert_fusion.3
  290.5 4.0 copy.75
  294.5 3.9 bitcast_negate_fusion
  298.5 2.2 fusion.78
  300.6 2.9 maximum_bitcast_fusion
  307.0 1.9 copy.86
  309.4 2.9 fusion.113
  313.4 7.9 %fusion.92 = bf16[32,4,48,128]{3,0,2,1:T(8,128)(2,1)} fusion(bf16[32,4,48,128]{3,2,0,1:T(8,128)(2,1)} %get-tuple-element.67, bf16[4,48,64,64]{3,2,1,0:T(8,128)(2,1)} %get-tuple-element.65, bf16[4,48,64,64]{3,2,1,0:T(8,128)(2,1)} %get-tuple-element.64, bf16[4,48,64,128]{3,2,1,0:T(8,128)(2,1)S(1)} %bitcast.243), kind=kOutput, calls=%fused_computation.135 | convolution fusion | flops 220987392 | bytes 9437184 | tf_op jit(solution)/shard_map/whmo,hmio->whmi/dot_general | solution.py:44
  321.3 2.6 fusion.249
  327.2 2.0 convolution_bitcast_fusion.4
  329.4 2.0 convolution_bitcast_fusion.5
  331.7 3.4 pad_maximum_fusion.1
  335.1 4.9 %all-to-all-start = ((bf16[16,896,128]{2,1,0:T(8,128)(2,1)}), bf16[16,896,128]{2,1,0:T(8,128)(2,1)}, u32[]{:S(2)}, u32[]{:S(2)}) async-start(bf16[16,896,128]{2,1,0:T(8,128)(2,1)} %pad_maximum_fusion.1), calls=%async_computation | async-start | bytes 7340032 | tf_op jit(solution)/shard_map/all_to_all | solution.py:336
  340.1 5.8 %convolution_convert_fusion.4 = bf16[32,96,256]{2,1,0:T(8,128)(2,1)} fusion(bf16[32,96,1024]{2,1,0:T(8,128)(2,1)} %get-tuple-element.44, bf16[1024,512]{1,0:T(8,128)(2,1)S(1)} %copy-done.18, s32[]{:T(128)S(6)} %select_n.193), kind=kOutput, calls=%fused_computation.117 | convolution fusion | flops 1611399168 | bytes 8388612 | tf_op jit(solution)/shard_map/wte,ed->wtd/dot_general | solution.py:44
  347.4 2.0 constant_dynamic-slice_fusion
  353.9 2.0 convolution_convert_fusion.1
  355.9 2.5 fusion.158
  358.4 24.4 %collective-permute-done.6 = bf16[32,96,256]{2,1,0:T(8,128)(2,1)} collective-permute-done((bf16[32,96,256]{2,1,0:T(8,128)(2,1)}, bf16[32,96,256]{2,1,0:T(8,128)(2,1)}, u32[]{:S(2)}, u32[]{:S(2)}) %collective-permute-start.6) | collective-permute-done | bytes 1572896 | tf_op jit(solution)/shard_map/ppermute | solution.py:139
  384.4 5.8 %fusion.247 = (bf16[32,96,256]{2,1,0:T(8,128)(2,1)S(1)}, bf16[32,96,256]{2,1,0:T(8,128)(2,1)S(1)}, bf16[32,96,256]{2,1,0:T(8,128)(2,1)S(1)}, f32[32,96,256]{2,1,0:T(8,128)S(1)}) fusion(bf16[32,96,256]{2,1,0:T(8,128)(2,1)} %collective-permute-done.6, bf16[32,96,1024]{2,1,0:T(8,128)(2,1)} %get-tuple-element.44, bf16[1024,512]{1,0:T(8,128)(2,1)S(1)} %copy-done.18, ...), kind=kOutput, calls=%fused_computation.305 | convolution fusion | flops 1620049920 | bytes 22560772 | tf_op jit(solution)/shard_map/wte,ed->wtd/dot_general | solution.py:44
  390.2 3.4 multiply_subtract_fusion
  396.3 1.8 multiply_add_fusion.3
  399.8 19.1 %collective-permute-done.7 = bf16[32,96,256]{2,1,0:T(8,128)(2,1)} collective-permute-done((bf16[32,96,256]{2,1,0:T(8,128)(2,1)}, bf16[32,96,256]{2,1,0:T(8,128)(2,1)}, u32[]{:S(2)}, u32[]{:S(2)}) %collective-permute-start.7) | collective-permute-done | bytes 1572896 | tf_op jit(solution)/shard_map/ppermute | solution.py:139
  418.9 4.8 %add_add_fusion = f32[32,96,256]{2,1,0:T(8,128)} fusion(f32[32,96,256]{2,1,0:T(8,128)} %get-tuple-element.94, f32[32,96,256]{2,1,0:T(8,128)S(1)} %copy-done.6, bf16[32,96,256]{2,1,0:T(8,128)(2,1)} %collective-permute-done.7), kind=kLoop, calls=%fused_computation.59 | loop fusion | flops 2359296 | bytes 11010048 | tf_op jit(solution)/shard_map/add | solution.py:275
  423.8 2.7 convert_reduce_fusion.2
  427.9 2.1 multiply_add_fusion
  (167 shorter events, 41.7 us)
Async XLA Ops:
  7.2 6.4 %copy-start.36 = (f32[512,256]{1,0:T(8,128)S(1)}, f32[512,256]{1,0:T(8,128)}, u32[]{:S(2)}) copy-start(f32[512,256]{1,0:T(8,128)} %param.33) | copy-start | bytes 1572868
  7.2 386.5 %reduce-scatter.2.cloned.1.call-start = ((), (), s32[]{:S(2)}) async-start(), calls=%async_computation.2 | async-start | bytes 4456448 | tf_op jit(solution)/shard_map/reduce_scatter | solution.py:321
  10.6 37.7 %collective-permute-start = (bf16[32,96,256]{2,1,0:T(8,128)(2,1)}, bf16[32,96,256]{2,1,0:T(8,128)(2,1)}, u32[]{:S(2)}, u32[]{:S(2)}) collective-permute-start(bf16[32,96,256]{2,1,0:T(8,128)(2,1)} %convert_element_type.200), channel_id=1, source_target_pairs={{0,1},{1,0},{2,3},{3,2},{4,5},{5,4},{6,7},{7,6},{8,9},{9,8},{10,11... | collective-permute-start | bytes 4718600 | tf_op jit(solution)/shard_map/ppermute | solution.py:139
  14.3 3.3 copy-start.32
  14.3 3.3 copy-start.39
  19.7 28.6 %copy-start.29 = (bf16[512,256]{1,0:T(8,128)(2,1)S(1)}, bf16[512,256]{1,0:T(8,128)(2,1)}, u32[]{:S(2)}) copy-start(bf16[512,256]{1,0:T(8,128)(2,1)} %convert_element_type.199) | copy-start | bytes 786436
  55.7 4.0 copy-start.2
  59.7 3.1 copy-start.26
  70.5 3.0 copy-start.47
  70.5 3.0 copy-start.48
  70.5 3.0 copy-start.49
  70.5 3.0 copy-start.50
  70.5 3.0 copy-start.51
  70.5 3.0 copy-start.52
  70.8 36.5 %copy-start.3 = (bf16[32,96,4,64]{1,3,2,0:T(8,128)(2,1)}, bf16[32,96,4,64]{1,3,2,0:T(8,128)(2,1)S(1)}, u32[]{:S(2)}) copy-start(bf16[32,96,4,64]{1,3,2,0:T(8,128)(2,1)S(1)} %copy.70) | copy-start | bytes 4718596
  70.8 9.8 %copy-start.24 = (f32[32,96,256]{2,1,0:T(8,128)S(1)}, f32[32,96,256]{2,1,0:T(8,128)}, u32[]{:S(2)}) copy-start(f32[32,96,256]{2,1,0:T(8,128)} %param.30) | copy-start | bytes 9437188
  71.6 35.6 %collective-permute-start.1 = (bf16[32,96,256]{2,1,0:T(8,128)(2,1)S(1)}, bf16[32,96,256]{2,1,0:T(8,128)(2,1)S(1)}, u32[]{:S(2)}, u32[]{:S(2)}) collective-permute-start(bf16[32,96,256]{2,1,0:T(8,128)(2,1)S(1)} %convolution_convert_fusion.5), channel_id=1, source_target_pairs={{0,1},{1,0},{2,3},{3,2},{4,5},{5,4},{6,7},{7,6},{8,9},{9,8},{10,11... | collective-permute-start | bytes 4718600 | tf_op jit(solution)/shard_map/ppermute | solution.py:139
  73.5 9.3 %copy-start.41 = (f32[32,96]{1,0:T(8,128)}, f32[32,96]{1,0:T(8,128)S(1)}, u32[]{:S(2)}) copy-start(f32[32,96]{1,0:T(8,128)S(1)} %get-tuple-element.38) | copy-start | bytes 36868
  80.6 26.7 %copy-start.5 = (f32[32,96,256]{2,1,0:T(8,128)S(1)}, f32[32,96,256]{2,1,0:T(8,128)}, u32[]{:S(2)}) copy-start(f32[32,96,256]{2,1,0:T(8,128)} %param.29) | copy-start | bytes 9437188
  109.6 6.3 %copy-start.7 = (f32[32,96,256]{2,1,0:T(8,128)}, f32[32,96,256]{2,1,0:T(8,128)S(1)}, u32[]{:S(2)}) copy-start(f32[32,96,256]{2,1,0:T(8,128)S(1)} %get-tuple-element.86) | copy-start | bytes 9437188
  109.6 7.7 %copy-start.31 = (bf16[32,96,256]{2,1,0:T(8,128)(2,1)S(1)}, bf16[32,96,256]{2,1,0:T(8,128)(2,1)}, u32[]{:S(2)}) copy-start(bf16[32,96,256]{2,1,0:T(8,128)(2,1)} %get-tuple-element.56) | copy-start | bytes 4718596
  109.6 7.7 %copy-start.33 = (bf16[32,96,96]{2,1,0:T(8,128)(2,1)S(1)}, bf16[32,96,96]{2,1,0:T(8,128)(2,1)}, u32[]{:S(2)}) copy-start(bf16[32,96,96]{2,1,0:T(8,128)(2,1)} %get-tuple-element.76) | copy-start | bytes 1769476
  115.9 16.6 %copy-start.9 = (bf16[32,96,256]{2,1,0:T(8,128)(2,1)}, bf16[32,96,256]{2,1,0:T(8,128)(2,1)S(1)}, u32[]{:S(2)}) copy-start(bf16[32,96,256]{2,1,0:T(8,128)(2,1)S(1)} %get-tuple-element.87) | copy-start | bytes 4718596
  115.9 37.3 %collective-permute-start.2 = (bf16[32,96,256]{2,1,0:T(8,128)(2,1)S(1)}, bf16[32,96,256]{2,1,0:T(8,128)(2,1)S(1)}, u32[]{:S(2)}, u32[]{:S(2)}) collective-permute-start(bf16[32,96,256]{2,1,0:T(8,128)(2,1)S(1)} %get-tuple-element.87), channel_id=1, source_target_pairs={{0,1},{1,0},{2,3},{3,2},{4,5},{5,4},{6,7},{7,6},{8,9},{9,8},{10,11... | collective-permute-start | bytes 4718600 | tf_op jit(solution)/shard_map/ppermute | solution.py:139
  117.3 4.5 %copy-start.28 = (f32[512,1024]{1,0:T(8,128)S(1)}, f32[512,1024]{1,0:T(8,128)}, u32[]{:S(2)}) copy-start(f32[512,1024]{1,0:T(8,128)} %param.36) | copy-start | bytes 6291460
  121.3 2.3 copy-start.11
  121.3 2.2 copy-start.21
  121.3 70.6 %collective-permute-start.3 = (bf16[32,96,256]{2,1,0:T(8,128)(2,1)S(1)}, bf16[32,96,256]{2,1,0:T(8,128)(2,1)S(1)}, u32[]{:S(2)}, u32[]{:S(2)}) collective-permute-start(bf16[32,96,256]{2,1,0:T(8,128)(2,1)S(1)} %get-tuple-element.90), channel_id=1, source_target_pairs={{0,1},{1,0},{2,3},{3,2},{4,5},{5,4},{6,7},{7,6},{8,9},{9,8},{10,11... | collective-permute-start | bytes 4718600 | tf_op jit(solution)/shard_map/ppermute | solution.py:139
  123.4 29.7 %copy-start.19 = (bf16[512,1024]{1,0:T(8,128)(2,1)}, bf16[512,1024]{1,0:T(8,128)(2,1)S(1)}, u32[]{:S(2)}) copy-start(bf16[512,1024]{1,0:T(8,128)(2,1)S(1)} %convert_element_type.224) | copy-start | bytes 3145732
  123.6 6.5 %copy-start.17 = (bf16[1024,512]{1,0:T(8,128)(2,1)}, bf16[1024,512]{1,0:T(8,128)(2,1)S(1)}, u32[]{:S(2)}) copy-start(bf16[1024,512]{1,0:T(8,128)(2,1)S(1)} %convert_element_type.226) | copy-start | bytes 3145732
  153.1 7.9 %copy-start.15 = (bf16[32,96,256]{2,1,0:T(8,128)(2,1)}, bf16[32,96,256]{2,1,0:T(8,128)(2,1)S(1)}, u32[]{:S(2)}) copy-start(bf16[32,96,256]{2,1,0:T(8,128)(2,1)S(1)} %collective-permute-done.2) | copy-start | bytes 4718596
  211.2 9.1 %copy-start = (bf16[32,96,1024]{2,1,0:T(8,128)(2,1)S(1)}, bf16[32,96,1024]{2,1,0:T(8,128)(2,1)}, u32[]{:S(2)}) copy-start(bf16[32,96,1024]{2,1,0:T(8,128)(2,1)} %add_convert_fusion) | copy-start | bytes 18874372
  217.3 3.0 copy-start.10
  217.3 31.6 %collective-permute-start.4 = (bf16[32,96,256]{2,1,0:T(8,128)(2,1)}, bf16[32,96,256]{2,1,0:T(8,128)(2,1)}, u32[]{:S(2)}, u32[]{:S(2)}) collective-permute-start(bf16[32,96,256]{2,1,0:T(8,128)(2,1)} %convolution_convert_fusion.3), channel_id=1, source_target_pairs={{0,1},{1,0},{2,3},{3,2},{4,5},{5,4},{6,7},{7,6},{8,9},{9,8},{10,11... | collective-permute-start | bytes 4718600 | tf_op jit(solution)/shard_map/ppermute | solution.py:139
  220.3 2.8 copy-start.16
  228.7 20.2 %slice-start.2 = ((s8[6291456]{0:T(1024)(128)(4,1)}), s8[4194304]{0:T(1024)(128)(4,1)S(1)}, s32[]{:S(2)}) async-start(s8[6291456]{0:T(1024)(128)(4,1)} %bitcast.239), calls=%async_computation.5 | async-start | bytes 8388608
  230.6 18.3 %slice-start.3 = ((s8[6291456]{0:T(1024)(128)(4,1)}), s8[2097152]{0:T(1024)(128)(4,1)S(1)}, s32[]{:S(2)}) async-start(s8[6291456]{0:T(1024)(128)(4,1)} %bitcast.239), calls=%async_computation.6 | async-start | bytes 4194304
  230.6 18.3 %copy-start.20 = (bf16[512,1024]{1,0:T(8,128)(2,1)S(1)}, bf16[512,1024]{1,0:T(8,128)(2,1)}, u32[]{:S(2)}) copy-start(bf16[512,1024]{1,0:T(8,128)(2,1)} %copy-done.19) | copy-start | bytes 3145732
  230.6 18.4 %copy-start.22 = (f32[32,96,256]{2,1,0:T(8,128)S(1)}, f32[32,96,256]{2,1,0:T(8,128)}, u32[]{:S(2)}) copy-start(f32[32,96,256]{2,1,0:T(8,128)} %get-tuple-element.91) | copy-start | bytes 9437188
  248.9 3.8 copy-start.35
  248.9 8.5 %slice-start = ((s8[6291456]{0:T(1024)(128)(4,1)}), s8[4194304]{0:T(1024)(128)(4,1)S(1)}, s32[]{:S(2)}) async-start(s8[6291456]{0:T(1024)(128)(4,1)} %bitcast.237), calls=%async_computation.3 | async-start | bytes 8388608
  252.8 4.7 %slice-start.1 = ((s8[6291456]{0:T(1024)(128)(4,1)}), s8[2097152]{0:T(1024)(128)(4,1)S(1)}, s32[]{:S(2)}) async-start(s8[6291456]{0:T(1024)(128)(4,1)} %bitcast.237), calls=%async_computation.4 | async-start | bytes 4194304
  252.8 4.7 %copy-start.14 = (bf16[32,96,256]{2,1,0:T(8,128)(2,1)S(1)}, bf16[32,96,256]{2,1,0:T(8,128)(2,1)}, u32[]{:S(2)}) copy-start(bf16[32,96,256]{2,1,0:T(8,128)(2,1)} %copy-done.13) | copy-start | bytes 4718596
  256.5 30.7 %collective-permute-start.5 = (bf16[32,96,256]{2,1,0:T(8,128)(2,1)}, bf16[32,96,256]{2,1,0:T(8,128)(2,1)}, u32[]{:S(2)}, u32[]{:S(2)}) collective-permute-start(bf16[32,96,256]{2,1,0:T(8,128)(2,1)} %get-tuple-element.93), channel_id=1, source_target_pairs={{0,1},{1,0},{2,3},{3,2},{4,5},{5,4},{6,7},{7,6},{8,9},{9,8},{10,11... | collective-permute-start | bytes 4718600 | tf_op jit(solution)/shard_map/ppermute | solution.py:139
  294.5 3.9 copy-start.1
  303.5 1.9 copy-start.23
  307.0 2.4 copy-start.4
  335.1 4.9 %copy-start.18 = (bf16[1024,512]{1,0:T(8,128)(2,1)S(1)}, bf16[1024,512]{1,0:T(8,128)(2,1)}, u32[]{:S(2)}) copy-start(bf16[1024,512]{1,0:T(8,128)(2,1)} %copy-done.17) | copy-start | bytes 3145732
  335.1 88.6 %all-to-all-start = ((bf16[16,896,128]{2,1,0:T(8,128)(2,1)}), bf16[16,896,128]{2,1,0:T(8,128)(2,1)}, u32[]{:S(2)}, u32[]{:S(2)}) async-start(bf16[16,896,128]{2,1,0:T(8,128)(2,1)} %pad_maximum_fusion.1), calls=%async_computation | async-start | bytes 7340032 | tf_op jit(solution)/shard_map/all_to_all | solution.py:336
  340.1 13.8 %copy-start.30 = (bf16[512,256]{1,0:T(8,128)(2,1)S(1)}, bf16[512,256]{1,0:T(8,128)(2,1)}, u32[]{:S(2)}) copy-start(bf16[512,256]{1,0:T(8,128)(2,1)} %convert_element_type.199) | copy-start | bytes 786436
  345.9 37.0 %collective-permute-start.6 = (bf16[32,96,256]{2,1,0:T(8,128)(2,1)}, bf16[32,96,256]{2,1,0:T(8,128)(2,1)}, u32[]{:S(2)}, u32[]{:S(2)}) collective-permute-start(bf16[32,96,256]{2,1,0:T(8,128)(2,1)} %convolution_convert_fusion.4), channel_id=1, source_target_pairs={{0,1},{1,0},{2,3},{3,2},{4,5},{5,4},{6,7},{7,6},{8,9},{9,8},{10,11... | collective-permute-start | bytes 4718600 | tf_op jit(solution)/shard_map/ppermute | solution.py:139
  353.9 30.5 %copy-start.27 = (f32[32,96,256]{2,1,0:T(8,128)S(1)}, f32[32,96,256]{2,1,0:T(8,128)}, u32[]{:S(2)}) copy-start(f32[32,96,256]{2,1,0:T(8,128)} %get-tuple-element.88) | copy-start | bytes 9437188
  355.9 28.5 %copy-start.8 = (f32[32,96,256]{2,1,0:T(8,128)S(1)}, f32[32,96,256]{2,1,0:T(8,128)}, u32[]{:S(2)}) copy-start(f32[32,96,256]{2,1,0:T(8,128)} %copy-done.7) | copy-start | bytes 9437188
  382.8 36.1 %collective-permute-start.7 = (bf16[32,96,256]{2,1,0:T(8,128)(2,1)}, bf16[32,96,256]{2,1,0:T(8,128)(2,1)}, u32[]{:S(2)}, u32[]{:S(2)}) collective-permute-start(bf16[32,96,256]{2,1,0:T(8,128)(2,1)} %convolution_convert_fusion.1), channel_id=1, source_target_pairs={{0,1},{1,0},{2,3},{3,2},{4,5},{5,4},{6,7},{7,6},{8,9},{9,8},{10,11... | collective-permute-start | bytes 4718600 | tf_op jit(solution)/shard_map/ppermute | solution.py:139
  384.4 5.9 %copy-start.34 = (bf16[32,96,96]{2,1,0:T(8,128)(2,1)S(1)}, bf16[32,96,96]{2,1,0:T(8,128)(2,1)}, u32[]{:S(2)}) copy-start(bf16[32,96,96]{2,1,0:T(8,128)(2,1)} %get-tuple-element.76) | copy-start | bytes 1769476
  384.4 5.9 %copy-start.42 = (f32[32,96]{1,0:T(8,128)S(1)}, f32[32,96]{1,0:T(8,128)}, u32[]{:S(2)}) copy-start(f32[32,96]{1,0:T(8,128)} %copy-done.41) | copy-start | bytes 36868
  390.2 28.7 %copy-start.6 = (f32[32,96,256]{2,1,0:T(8,128)S(1)}, f32[32,96,256]{2,1,0:T(8,128)}, u32[]{:S(2)}) copy-start(f32[32,96,256]{2,1,0:T(8,128)} %fusion.158) | copy-start | bytes 9437188
  423.7 2.8 copy-start.43
  423.7 2.8 copy-start.44
  423.7 4.2 copy-start.37
  423.7 4.2 copy-start.38
  423.7 6.3 %copy-start.40 = (f32[256,32]{0,1:T(8,128)S(1)}, f32[256,32]{0,1:T(8,128)}, u32[]{:S(2)}) copy-start(f32[256,32]{0,1:T(8,128)} %copy.110) | copy-start | bytes 98308
  423.7 6.3 %copy-start.45 = (f32[256,32]{0,1:T(8,128)S(1)}, f32[256,32]{0,1:T(8,128)}, u32[]{:S(2)}) copy-start(f32[256,32]{0,1:T(8,128)} %param.43) | copy-start | bytes 98308
  423.7 6.3 %copy-start.46 = (f32[256,32]{0,1:T(8,128)S(1)}, f32[256,32]{0,1:T(8,128)}, u32[]{:S(2)}) copy-start(f32[256,32]{0,1:T(8,128)} %param.42) | copy-start | bytes 98308
  (3 other events, 4.9 us)
Sparse Core Ops, SparseCore 0:
  267.7 73.0 reduce-scatter.1

commit v5 on v4

--- a/solution.py
+++ b/solution.py
@@ -346,9 +346,8 @@
         return parts
 
     inner_part, outer_part_t = reduced_over_dp([(inner_grad, 0), (outer_grad_t, 0)])
-    mixer_part, output_part_t, query_part = summed_over_dp(
-        [(mixer_full, 1), (output_grad_t, 0), (query_grad, 0)]
-    )
+    mixer_part, output_part_t = summed_over_dp([(mixer_full, 1), (output_grad_t, 0)])
+    (query_part,) = summed_over_dp([(query_grad, 0)])
     output_part = jnp.transpose(output_part_t)
     outer_part = jnp.transpose(outer_part_t)
     token_total = windows * length * dp_count

time: 442 us -> 451 us (1.020)
    all_to_all x1 -> x2, starting transfers between devices: 4.91 us -> 9.33 us  [summed_over_dp(): lax.all_to_all(joined.astype(jnp.bfloat16).reshape(-1, lanes), 'dp', 0, 0...]
    unnamed x116 -> x120, local copies, waits for them, and re-layouts: 8.42 us -> 10.1 us
  transfers between devices with their start and end apart: 10 -> 11, of which waited for: 7 -> 8; matrix products, arithmetic and copies ran while one was open for 43% -> 44% of each run, Pallas kernels for 0% -> 0%
where the time goes in v5:
time: 451 us; the launch traced here: 447 us
  matrix products  149 us (33%)
  waiting for transfers between devices  136 us (30%)
  other arithmetic  83.2 us (18%)
  local copies, waits for them, and re-layouts  41.9 us (9%)
  starting transfers between devices  21.6 us (5%)
  between operations  15.1 us (3%)
    ppermute x8, waiting for transfers between devices, swap(): return lax.ppermute(values, 'head', pairs)  134 us
    dot_general x35, matrix products, product(): return jnp.einsum(form, left, right, preferred_element_type=jnp.float32)  132 us
    convert_element_type x1, other arithmetic, chunk_pass(): hidden = activated.astype(jnp.bfloat16)  30.8 us
    ppermute x8, starting transfers between devices, swap(): return lax.ppermute(values, 'head', pairs)  12.2 us
    unnamed x120, local copies, waits for them, and re-layouts  10.1 us
    dot_general x2, matrix products, trend_local(): jnp.einsum('wts,wsd->wtd', tiled, parts, preferred_element_type=jnp.float32)  9.75 us
    all_to_all x2, starting transfers between devices, summed_over_dp(): lax.all_to_all(joined.astype(jnp.bfloat16).reshape(-1, lanes), 'dp', 0, 0...  9.33 us
  transfers between devices with their start and end apart: 11, of which 8 were waited for; matrix products, arithmetic and copies ran while one was open for 44% of the time, Pallas kernels for 0%

profile of v5, /device:TPU:0, one launch (start us, length us, event | category | flops | bytes accessed | tf_op | source)
XLA Modules:
  0.0 446.6 jit_solution(1173025403278755306)
XLA Ops:
  7.2 3.3 convert_element_type.212
  10.6 3.0 collective-permute-start
  14.3 3.2 convert_element_type.210
  17.6 2.1 fusion.160
  19.7 4.0 slice_negate_fusion
  23.7 24.6 %collective-permute-done = bf16[32,96,256]{2,1,0:T(8,128)(2,1)} collective-permute-done((bf16[32,96,256]{2,1,0:T(8,128)(2,1)}, bf16[32,96,256]{2,1,0:T(8,128)(2,1)}, u32[]{:S(2)}, u32[]{:S(2)}) %collective-permute-start) | collective-permute-done | bytes 1572896 | tf_op jit(solution)/shard_map/ppermute | solution.py:139
  48.3 3.1 fusion.91
  51.4 4.3 copy.64
  55.7 3.9 fusion.72
  59.7 2.2 fusion.69
  63.8 3.1 fusion.95
  73.5 7.0 %select_convert_fusion = (bf16[32,96,96]{2,1,0:T(8,128)(2,1)}, bf16[32,96,96]{2,1,0:T(8,128)(2,1)}) fusion(bf16[96,96]{1,0:T(8,128)(2,1)S(1)} %copy-done.50, bf16[96,96]{1,0:T(8,128)(2,1)S(1)} %copy-done.51, bf16[96,96]{1,0:T(8,128)(2,1)S(1)} %copy-done.52, bf16[96,96]{1,0:T(8,128)(2,1)S(1)} %copy-done.53, bf16[96,96]{1,0:T(8,128)(2,1)S(1)} %copy-done.54, ...), kind=kLoop, calls=%fused_computation.132 | loop fusion | flops 2949120 | bytes 1302528 | tf_op jit(solution)/shard_map/convert_element_type | solution.py:66
  80.6 2.2 multiply_convert_fusion.2
  82.8 24.5 %collective-permute-done.1 = bf16[32,96,256]{2,1,0:T(8,128)(2,1)S(1)} collective-permute-done((bf16[32,96,256]{2,1,0:T(8,128)(2,1)S(1)}, bf16[32,96,256]{2,1,0:T(8,128)(2,1)S(1)}, u32[]{:S(2)}, u32[]{:S(2)}) %collective-permute-start.1) | collective-permute-done | bytes 1572896 | tf_op jit(solution)/shard_map/ppermute | solution.py:139
  107.3 2.3 fusion.248
  109.6 6.4 %fusion.112 = (bf16[32,96,256]{2,1,0:T(8,128)(2,1)S(1)}, f32[32,96,256]{2,1,0:T(8,128)}) fusion(f32[32,96,256]{2,1,0:T(8,128)S(1)} %get-tuple-element.84, f32[32,96]{1,0:T(8,128)S(1)} %get-tuple-element.76, bf16[32,96,256]{2,1,0:T(8,128)(2,1)S(1)} %get-tuple-element.62, bf16[32,96,256]{2,1,0:T(8,128)(2,1)} %get-tuple-element.63, ...), kind=kOutput, calls=%fused_computation.147 | convolution fusion | flops 474808320 | bytes 13185024 | tf_op jit(solution)/shard_map/wts,wsd->wtd/dot_general | solution.py:81
  117.4 3.9 fusion.252
  123.7 6.4 %fusion.122 = f32[32,96,1024]{2,1,0:T(8,128)} fusion(bf16[32,96,256]{2,1,0:T(8,128)(2,1)S(1)} %get-tuple-element.88, bf16[1024,512]{1,0:T(8,128)(2,1)S(1)} %convert_element_type.238, s32[]{:T(128)S(6)} %select_n.186), kind=kOutput, calls=%fused_computation.157 | convolution fusion | flops 1610612736 | bytes 14680068 | tf_op jit(solution)/shard_map/wtd,fd->wtf/dot_general | solution.py:44
  130.1 2.4 pad_maximum_fusion.2
  134.4 18.9 %collective-permute-done.2 = bf16[32,96,256]{2,1,0:T(8,128)(2,1)S(1)} collective-permute-done((bf16[32,96,256]{2,1,0:T(8,128)(2,1)S(1)}, bf16[32,96,256]{2,1,0:T(8,128)(2,1)S(1)}, u32[]{:S(2)}, u32[]{:S(2)}) %collective-permute-start.2) | collective-permute-done | bytes 1572896 | tf_op jit(solution)/shard_map/ppermute | solution.py:139
  153.2 7.9 %convert_reduce_fusion.1 = (u32[96,1024]{1,0:T(8,128)S(1)}, u32[96,1024]{1,0:T(8,128)S(1)}, f32[32,96,1024]{2,1,0:T(8,128)}) fusion(f32[32,96,1024]{2,1,0:T(8,128)S(1)} %fusion.131, bf16[32,96,256]{2,1,0:T(8,128)(2,1)S(1)} %collective-permute-done.2, bf16[512,1024]{1,0:T(8,128)(2,1)S(1)} %convert_element_type.236, s32[]{:T(128)S(6)} %select_n.188), kind=kOutput, calls=%fused_computation.6 | convolution fusion | flops 1648164864 | bytes 28049412 | tf_op jit(solution)/shard_map/wtd,de->wte/dot_general | solution.py:44
  161.2 30.8 %multiply_convert_fusion = (bf16[32,96,1024]{2,1,0:T(8,128)(2,1)}, f32[32,96,1024]{2,1,0:T(8,128)}) fusion(f32[32,96,1024]{2,1,0:T(8,128)} %get-tuple-element.87, u32[96,1024]{1,0:T(8,128)S(1)} %get-tuple-element.22, u32[96,1024]{1,0:T(8,128)S(1)} %get-tuple-element.21), kind=kLoop, calls=%fused_computation.8 | loop fusion | flops 213909504 | bytes 32243712 | tf_op jit(solution)/shard_map/convert_element_type | solution.py:215
  193.1 18.2 %add_convert_fusion = bf16[32,96,1024]{2,1,0:T(8,128)(2,1)} fusion(f32[32,96,1024]{2,1,0:T(8,128)} %get-tuple-element.45, f32[32,96,1024]{2,1,0:T(8,128)} %fusion.122, f32[32,96,1024]{2,1,0:T(8,128)} %get-tuple-element.87, bf16[32,96,256]{2,1,0:T(8,128)(2,1)} %copy-done.16, bf16[1024,512]{1,0:T(8,128)(2,1)} %copy-done.20, s32[]{:T(128)S(6)} %select_n.188), kind=kOutput, calls=%fused_computation.7 | convolution fusion | flops 1657798656 | bytes 46137348 | tf_op jit(solution)/shard_map/wtd,fd->wtf/dot_general | solution.py:44
  211.3 6.1 %convolution_convert_fusion.3 = bf16[32,96,256]{2,1,0:T(8,128)(2,1)} fusion(bf16[32,96,1024]{2,1,0:T(8,128)(2,1)} %add_convert_fusion, bf16[512,1024]{1,0:T(8,128)(2,1)} %copy-done.22, s32[]{:T(128)S(6)} %select_n.193), kind=kOutput, calls=%fused_computation.116 | convolution fusion | flops 1611399168 | bytes 8388612 | tf_op jit(solution)/shard_map/wte,ed->wtd/dot_general | solution.py:44
  220.4 2.8 fusion.101
  223.2 2.8 fusion.100
  226.0 2.7 reshape_reshape.17
  230.7 6.2 %fusion.99 = f32[512,1024]{1,0:T(8,128)} fusion(f32[512,1024]{1,0:T(8,128)} %broadcast.229.clone, s32[]{:T(128)S(6)} %select_n.186, bf16[32,96,256]{2,1,0:T(8,128)(2,1)S(1)} %copy-done.14, bf16[32,96,1024]{2,1,0:T(8,128)(2,1)} %get-tuple-element.44), kind=kOutput, calls=%fused_computation.140 | convolution fusion | flops 1610612736 | bytes 8912900 | tf_op jit(solution)/shard_map/wtd,wtf->df/dot_general | solution.py:44
  236.8 12.2 %collective-permute-done.4 = bf16[32,96,256]{2,1,0:T(8,128)(2,1)} collective-permute-done((bf16[32,96,256]{2,1,0:T(8,128)(2,1)}, bf16[32,96,256]{2,1,0:T(8,128)(2,1)}, u32[]{:S(2)}, u32[]{:S(2)}) %collective-permute-start.4) | collective-permute-done | bytes 1572896 | tf_op jit(solution)/shard_map/ppermute | solution.py:139
  249.1 3.8 multiply_convert_fusion.1
  252.9 3.8 fusion.253
  257.5 2.8 fusion.98
  260.3 2.7 reshape_reshape.18
  263.0 4.6 %pad_maximum_fusion = f32[16,512,128]{2,1,0:T(8,128)} fusion(f32[16,256,128]{2,1,0:T(8,128)} %reshape_reshape.18, f32[16,256,128]{2,1,0:T(8,128)} %reshape_reshape.17), kind=kLoop, calls=%fused_computation.49 | loop fusion | flops 1048576 | bytes 8388608 | tf_op jit(solution)/shard_map/concatenate | solution.py:320
  268.4 3.5 fusion.114
  272.0 2.0 fusion.151
  274.0 13.4 %collective-permute-done.5 = bf16[32,96,256]{2,1,0:T(8,128)(2,1)} collective-permute-done((bf16[32,96,256]{2,1,0:T(8,128)(2,1)}, bf16[32,96,256]{2,1,0:T(8,128)(2,1)}, u32[]{:S(2)}, u32[]{:S(2)}) %collective-permute-start.5) | collective-permute-done | bytes 1572896 | tf_op jit(solution)/shard_map/ppermute | solution.py:139
  287.4 3.2 add_convert_fusion.3
  290.6 4.0 copy.75
  294.6 3.9 bitcast_negate_fusion
  298.6 2.2 fusion.78
  300.8 3.4 maximum_bitcast_fusion
  304.2 7.9 %fusion.92 = bf16[32,4,48,128]{3,0,2,1:T(8,128)(2,1)} fusion(bf16[32,4,48,128]{3,2,0,1:T(8,128)(2,1)} %get-tuple-element.67, bf16[4,48,64,64]{3,2,1,0:T(8,128)(2,1)} %get-tuple-element.65, bf16[4,48,64,64]{3,2,1,0:T(8,128)(2,1)} %get-tuple-element.64, bf16[4,48,64,128]{3,2,1,0:T(8,128)(2,1)S(1)} %bitcast.243), kind=kOutput, calls=%fused_computation.135 | convolution fusion | flops 220987392 | bytes 9437184 | tf_op jit(solution)/shard_map/whmo,hmio->whmi/dot_general | solution.py:44
  312.2 2.7 fusion.249
  323.1 2.0 convolution_bitcast_fusion.6
  325.2 1.9 copy.90
  327.2 2.0 convolution_bitcast_fusion.7
  330.3 4.8 %all-to-all-start = ((bf16[16,64,128]{2,1,0:T(8,128)(2,1)}), bf16[16,64,128]{2,1,0:T(8,128)(2,1)S(1)}, u32[]{:S(2)}, u32[]{:S(2)}) async-start(bf16[16,64,128]{2,1,0:T(8,128)(2,1)} %convert_element_type.271), calls=%async_computation | async-start | bytes 524288 | tf_op jit(solution)/shard_map/all_to_all | solution.py:336
  335.1 3.6 fusion.113
  339.7 3.9 pad_maximum_fusion.1
  343.6 1.8 all-to-all-done
  346.2 4.5 %all-to-all-start.1 = ((bf16[16,832,128]{2,1,0:T(8,128)(2,1)}), bf16[16,832,128]{2,1,0:T(8,128)(2,1)}, u32[]{:S(2)}, u32[]{:S(2)}) async-start(bf16[16,832,128]{2,1,0:T(8,128)(2,1)} %pad_maximum_fusion.1), calls=%async_computation.1 | async-start | bytes 6815744 | tf_op jit(solution)/shard_map/all_to_all | solution.py:336
  350.7 5.8 %convolution_convert_fusion.4 = bf16[32,96,256]{2,1,0:T(8,128)(2,1)} fusion(bf16[32,96,1024]{2,1,0:T(8,128)(2,1)} %get-tuple-element.44, bf16[1024,512]{1,0:T(8,128)(2,1)S(1)} %copy-done.21, s32[]{:T(128)S(6)} %select_n.193), kind=kOutput, calls=%fused_computation.117 | convolution fusion | flops 1611399168 | bytes 8388612 | tf_op jit(solution)/shard_map/wte,ed->wtd/dot_general | solution.py:44
  358.0 2.0 constant_dynamic-slice_fusion
  364.5 2.0 convolution_convert_fusion.1
  366.5 2.5 fusion.158
  370.5 22.8 %collective-permute-done.6 = bf16[32,96,256]{2,1,0:T(8,128)(2,1)} collective-permute-done((bf16[32,96,256]{2,1,0:T(8,128)(2,1)}, bf16[32,96,256]{2,1,0:T(8,128)(2,1)}, u32[]{:S(2)}, u32[]{:S(2)}) %collective-permute-start.6) | collective-permute-done | bytes 1572896 | tf_op jit(solution)/shard_map/ppermute | solution.py:139
  394.8 7.4 %fusion.247 = (bf16[32,96,256]{2,1,0:T(8,128)(2,1)S(1)}, bf16[32,96,256]{2,1,0:T(8,128)(2,1)S(1)}, bf16[32,96,256]{2,1,0:T(8,128)(2,1)S(1)}, f32[32,96,256]{2,1,0:T(8,128)S(1)}) fusion(bf16[32,96,256]{2,1,0:T(8,128)(2,1)} %collective-permute-done.6, bf16[32,96,1024]{2,1,0:T(8,128)(2,1)} %get-tuple-element.44, bf16[1024,512]{1,0:T(8,128)(2,1)S(1)} %copy-done.21, ...), kind=kOutput, calls=%fused_computation.306 | convolution fusion | flops 1620049920 | bytes 22560772 | tf_op jit(solution)/shard_map/wte,ed->wtd/dot_general | solution.py:44
  402.3 3.4 multiply_subtract_fusion
  408.3 1.8 multiply_add_fusion.3
  411.9 17.4 %collective-permute-done.7 = bf16[32,96,256]{2,1,0:T(8,128)(2,1)} collective-permute-done((bf16[32,96,256]{2,1,0:T(8,128)(2,1)}, bf16[32,96,256]{2,1,0:T(8,128)(2,1)}, u32[]{:S(2)}, u32[]{:S(2)}) %collective-permute-start.7) | collective-permute-done | bytes 1572896 | tf_op jit(solution)/shard_map/ppermute | solution.py:139
  429.3 4.8 %add_add_fusion = f32[32,96,256]{2,1,0:T(8,128)} fusion(f32[32,96,256]{2,1,0:T(8,128)} %get-tuple-element.92, f32[32,96,256]{2,1,0:T(8,128)S(1)} %copy-done.9, bf16[32,96,256]{2,1,0:T(8,128)(2,1)} %collective-permute-done.7), kind=kLoop, calls=%fused_computation.59 | loop fusion | flops 2359296 | bytes 11010048 | tf_op jit(solution)/shard_map/add | solution.py:275
  434.1 2.5 convert_reduce_fusion.2
  436.7 2.1 multiply_add_fusion
  (174 shorter events, 47.6 us)
Async XLA Ops:
  7.2 6.4 %copy-start.40 = (f32[512,256]{1,0:T(8,128)S(1)}, f32[512,256]{1,0:T(8,128)}, u32[]{:S(2)}) copy-start(f32[512,256]{1,0:T(8,128)} %param.33) | copy-start | bytes 1572868
  7.2 398.5 %reduce-scatter.2.cloned.1.call-start = ((), (), s32[]{:S(2)}) async-start(), calls=%async_computation.3 | async-start | bytes 4456448 | tf_op jit(solution)/shard_map/reduce_scatter | solution.py:321
  10.6 37.7 %collective-permute-start = (bf16[32,96,256]{2,1,0:T(8,128)(2,1)}, bf16[32,96,256]{2,1,0:T(8,128)(2,1)}, u32[]{:S(2)}, u32[]{:S(2)}) collective-permute-start(bf16[32,96,256]{2,1,0:T(8,128)(2,1)} %convert_element_type.212), channel_id=1, source_target_pairs={{0,1},{1,0},{2,3},{3,2},{4,5},{5,4},{6,7},{7,6},{8,9},{9,8},{10,11... | collective-permute-start | bytes 4718600 | tf_op jit(solution)/shard_map/ppermute | solution.py:139
  14.3 3.3 copy-start.36
  14.3 3.3 copy-start.43
  19.7 28.6 %copy-start.31 = (bf16[512,256]{1,0:T(8,128)(2,1)S(1)}, bf16[512,256]{1,0:T(8,128)(2,1)}, u32[]{:S(2)}) copy-start(bf16[512,256]{1,0:T(8,128)(2,1)} %convert_element_type.211) | copy-start | bytes 786436
  55.7 4.0 copy-start.2
  59.7 3.1 copy-start.29
  61.9 1.9 copy-start.28
  70.5 3.0 copy-start.49
  70.5 3.0 copy-start.50
  70.5 3.0 copy-start.51
  70.5 3.0 copy-start.52
  70.5 3.0 copy-start.53
  70.5 3.0 copy-start.54
  70.8 36.5 %copy-start.3 = (bf16[32,96,4,64]{1,3,2,0:T(8,128)(2,1)}, bf16[32,96,4,64]{1,3,2,0:T(8,128)(2,1)S(1)}, u32[]{:S(2)}) copy-start(bf16[32,96,4,64]{1,3,2,0:T(8,128)(2,1)S(1)} %copy.70) | copy-start | bytes 4718596
  70.8 9.8 %copy-start.27 = (f32[32,96,256]{2,1,0:T(8,128)S(1)}, f32[32,96,256]{2,1,0:T(8,128)}, u32[]{:S(2)}) copy-start(f32[32,96,256]{2,1,0:T(8,128)} %param.30) | copy-start | bytes 9437188
  71.6 35.6 %collective-permute-start.1 = (bf16[32,96,256]{2,1,0:T(8,128)(2,1)S(1)}, bf16[32,96,256]{2,1,0:T(8,128)(2,1)S(1)}, u32[]{:S(2)}, u32[]{:S(2)}) collective-permute-start(bf16[32,96,256]{2,1,0:T(8,128)(2,1)S(1)} %convolution_convert_fusion.5), channel_id=1, source_target_pairs={{0,1},{1,0},{2,3},{3,2},{4,5},{5,4},{6,7},{7,6},{8,9},{9,8},{10,11... | collective-permute-start | bytes 4718600 | tf_op jit(solution)/shard_map/ppermute | solution.py:139
  73.5 9.3 %copy-start.45 = (f32[32,96]{1,0:T(8,128)}, f32[32,96]{1,0:T(8,128)S(1)}, u32[]{:S(2)}) copy-start(f32[32,96]{1,0:T(8,128)S(1)} %get-tuple-element.38) | copy-start | bytes 36868
  80.6 26.7 %copy-start.8 = (f32[32,96,256]{2,1,0:T(8,128)S(1)}, f32[32,96,256]{2,1,0:T(8,128)}, u32[]{:S(2)}) copy-start(f32[32,96,256]{2,1,0:T(8,128)} %param.29) | copy-start | bytes 9437188
  109.6 6.4 %copy-start.10 = (f32[32,96,256]{2,1,0:T(8,128)}, f32[32,96,256]{2,1,0:T(8,128)S(1)}, u32[]{:S(2)}) copy-start(f32[32,96,256]{2,1,0:T(8,128)S(1)} %get-tuple-element.84) | copy-start | bytes 9437188
  109.6 7.8 %copy-start.33 = (bf16[32,96,256]{2,1,0:T(8,128)(2,1)S(1)}, bf16[32,96,256]{2,1,0:T(8,128)(2,1)}, u32[]{:S(2)}) copy-start(bf16[32,96,256]{2,1,0:T(8,128)(2,1)} %get-tuple-element.56) | copy-start | bytes 4718596
  109.6 7.8 %copy-start.37 = (bf16[32,96,96]{2,1,0:T(8,128)(2,1)S(1)}, bf16[32,96,96]{2,1,0:T(8,128)(2,1)}, u32[]{:S(2)}) copy-start(bf16[32,96,96]{2,1,0:T(8,128)(2,1)} %get-tuple-element.74) | copy-start | bytes 1769476
  116.0 16.6 %copy-start.11 = (bf16[32,96,256]{2,1,0:T(8,128)(2,1)}, bf16[32,96,256]{2,1,0:T(8,128)(2,1)S(1)}, u32[]{:S(2)}) copy-start(bf16[32,96,256]{2,1,0:T(8,128)(2,1)S(1)} %get-tuple-element.85) | copy-start | bytes 4718596
  116.0 37.3 %collective-permute-start.2 = (bf16[32,96,256]{2,1,0:T(8,128)(2,1)S(1)}, bf16[32,96,256]{2,1,0:T(8,128)(2,1)S(1)}, u32[]{:S(2)}, u32[]{:S(2)}) collective-permute-start(bf16[32,96,256]{2,1,0:T(8,128)(2,1)S(1)} %get-tuple-element.85), channel_id=1, source_target_pairs={{0,1},{1,0},{2,3},{3,2},{4,5},{5,4},{6,7},{7,6},{8,9},{9,8},{10,11... | collective-permute-start | bytes 4718600 | tf_op jit(solution)/shard_map/ppermute | solution.py:139
  117.4 4.5 %copy-start.30 = (f32[512,1024]{1,0:T(8,128)S(1)}, f32[512,1024]{1,0:T(8,128)}, u32[]{:S(2)}) copy-start(f32[512,1024]{1,0:T(8,128)} %param.36) | copy-start | bytes 6291460
  121.4 2.3 copy-start.13
  121.4 2.2 copy-start.24
  121.4 70.6 %collective-permute-start.3 = (bf16[32,96,256]{2,1,0:T(8,128)(2,1)S(1)}, bf16[32,96,256]{2,1,0:T(8,128)(2,1)S(1)}, u32[]{:S(2)}, u32[]{:S(2)}) collective-permute-start(bf16[32,96,256]{2,1,0:T(8,128)(2,1)S(1)} %get-tuple-element.88), channel_id=1, source_target_pairs={{0,1},{1,0},{2,3},{3,2},{4,5},{5,4},{6,7},{7,6},{8,9},{9,8},{10,11... | collective-permute-start | bytes 4718600 | tf_op jit(solution)/shard_map/ppermute | solution.py:139
  123.5 29.7 %copy-start.22 = (bf16[512,1024]{1,0:T(8,128)(2,1)}, bf16[512,1024]{1,0:T(8,128)(2,1)S(1)}, u32[]{:S(2)}) copy-start(bf16[512,1024]{1,0:T(8,128)(2,1)S(1)} %convert_element_type.236) | copy-start | bytes 3145732
  123.7 6.5 %copy-start.20 = (bf16[1024,512]{1,0:T(8,128)(2,1)}, bf16[1024,512]{1,0:T(8,128)(2,1)S(1)}, u32[]{:S(2)}) copy-start(bf16[1024,512]{1,0:T(8,128)(2,1)S(1)} %convert_element_type.238) | copy-start | bytes 3145732
  153.2 7.9 %copy-start.18 = (bf16[32,96,256]{2,1,0:T(8,128)(2,1)}, bf16[32,96,256]{2,1,0:T(8,128)(2,1)S(1)}, u32[]{:S(2)}) copy-start(bf16[32,96,256]{2,1,0:T(8,128)(2,1)S(1)} %collective-permute-done.2) | copy-start | bytes 4718596
  211.3 9.1 %copy-start = (bf16[32,96,1024]{2,1,0:T(8,128)(2,1)S(1)}, bf16[32,96,1024]{2,1,0:T(8,128)(2,1)}, u32[]{:S(2)}) copy-start(bf16[32,96,1024]{2,1,0:T(8,128)(2,1)} %add_convert_fusion) | copy-start | bytes 18874372
  217.4 3.0 copy-start.12
  217.4 31.6 %collective-permute-start.4 = (bf16[32,96,256]{2,1,0:T(8,128)(2,1)}, bf16[32,96,256]{2,1,0:T(8,128)(2,1)}, u32[]{:S(2)}, u32[]{:S(2)}) collective-permute-start(bf16[32,96,256]{2,1,0:T(8,128)(2,1)} %convolution_convert_fusion.3), channel_id=1, source_target_pairs={{0,1},{1,0},{2,3},{3,2},{4,5},{5,4},{6,7},{7,6},{8,9},{9,8},{10,11... | collective-permute-start | bytes 4718600 | tf_op jit(solution)/shard_map/ppermute | solution.py:139
  220.4 2.8 copy-start.19
  228.8 20.2 %slice-start.2 = ((s8[6291456]{0:T(1024)(128)(4,1)}), s8[4194304]{0:T(1024)(128)(4,1)S(1)}, s32[]{:S(2)}) async-start(s8[6291456]{0:T(1024)(128)(4,1)} %bitcast.239), calls=%async_computation.6 | async-start | bytes 8388608
  230.7 18.4 %slice-start.3 = ((s8[6291456]{0:T(1024)(128)(4,1)}), s8[2097152]{0:T(1024)(128)(4,1)S(1)}, s32[]{:S(2)}) async-start(s8[6291456]{0:T(1024)(128)(4,1)} %bitcast.239), calls=%async_computation.7 | async-start | bytes 4194304
  230.7 18.4 %copy-start.23 = (bf16[512,1024]{1,0:T(8,128)(2,1)S(1)}, bf16[512,1024]{1,0:T(8,128)(2,1)}, u32[]{:S(2)}) copy-start(bf16[512,1024]{1,0:T(8,128)(2,1)} %copy-done.22) | copy-start | bytes 3145732
  230.7 18.4 %copy-start.25 = (f32[32,96,256]{2,1,0:T(8,128)S(1)}, f32[32,96,256]{2,1,0:T(8,128)}, u32[]{:S(2)}) copy-start(f32[32,96,256]{2,1,0:T(8,128)} %get-tuple-element.89) | copy-start | bytes 9437188
  249.0 3.8 copy-start.39
  249.0 8.5 %slice-start = ((s8[6291456]{0:T(1024)(128)(4,1)}), s8[4194304]{0:T(1024)(128)(4,1)S(1)}, s32[]{:S(2)}) async-start(s8[6291456]{0:T(1024)(128)(4,1)} %bitcast.237), calls=%async_computation.4 | async-start | bytes 8388608
  252.9 4.7 %slice-start.1 = ((s8[6291456]{0:T(1024)(128)(4,1)}), s8[2097152]{0:T(1024)(128)(4,1)S(1)}, s32[]{:S(2)}) async-start(s8[6291456]{0:T(1024)(128)(4,1)} %bitcast.237), calls=%async_computation.5 | async-start | bytes 4194304
  252.9 4.7 %copy-start.17 = (bf16[32,96,256]{2,1,0:T(8,128)(2,1)S(1)}, bf16[32,96,256]{2,1,0:T(8,128)(2,1)}, u32[]{:S(2)}) copy-start(bf16[32,96,256]{2,1,0:T(8,128)(2,1)} %copy-done.16) | copy-start | bytes 4718596
  256.6 30.7 %collective-permute-start.5 = (bf16[32,96,256]{2,1,0:T(8,128)(2,1)}, bf16[32,96,256]{2,1,0:T(8,128)(2,1)}, u32[]{:S(2)}, u32[]{:S(2)}) collective-permute-start(bf16[32,96,256]{2,1,0:T(8,128)(2,1)} %get-tuple-element.91), channel_id=1, source_target_pairs={{0,1},{1,0},{2,3},{3,2},{4,5},{5,4},{6,7},{7,6},{8,9},{9,8},{10,11... | collective-permute-start | bytes 4718600 | tf_op jit(solution)/shard_map/ppermute | solution.py:139
  294.6 3.9 copy-start.1
  298.6 5.6 %copy-start.4 = (bf16[4,32,64,48]{2,3,1,0:T(8,128)(2,1)}, bf16[4,32,64,48]{2,3,1,0:T(8,128)(2,1)S(1)}, u32[]{:S(2)}) copy-start(bf16[4,32,64,48]{2,3,1,0:T(8,128)(2,1)S(1)} %get-tuple-element.95) | copy-start | bytes 2359300
  300.8 3.5 copy-start.6
  319.7 1.9 copy-start.26
  330.3 15.2 %all-to-all-start = ((bf16[16,64,128]{2,1,0:T(8,128)(2,1)}), bf16[16,64,128]{2,1,0:T(8,128)(2,1)S(1)}, u32[]{:S(2)}, u32[]{:S(2)}) async-start(bf16[16,64,128]{2,1,0:T(8,128)(2,1)} %convert_element_type.271), calls=%async_computation | async-start | bytes 524288 | tf_op jit(solution)/shard_map/all_to_all | solution.py:336
  343.6 7.1 %copy-start.21 = (bf16[1024,512]{1,0:T(8,128)(2,1)S(1)}, bf16[1024,512]{1,0:T(8,128)(2,1)}, u32[]{:S(2)}) copy-start(bf16[1024,512]{1,0:T(8,128)(2,1)} %copy-done.20) | copy-start | bytes 3145732
  346.2 87.9 %all-to-all-start.1 = ((bf16[16,832,128]{2,1,0:T(8,128)(2,1)}), bf16[16,832,128]{2,1,0:T(8,128)(2,1)}, u32[]{:S(2)}, u32[]{:S(2)}) async-start(bf16[16,832,128]{2,1,0:T(8,128)(2,1)} %pad_maximum_fusion.1), calls=%async_computation.1 | async-start | bytes 6815744 | tf_op jit(solution)/shard_map/all_to_all | solution.py:336
  350.7 13.8 %copy-start.32 = (bf16[512,256]{1,0:T(8,128)(2,1)S(1)}, bf16[512,256]{1,0:T(8,128)(2,1)}, u32[]{:S(2)}) copy-start(bf16[512,256]{1,0:T(8,128)(2,1)} %convert_element_type.211) | copy-start | bytes 786436
  356.5 36.8 %collective-permute-start.6 = (bf16[32,96,256]{2,1,0:T(8,128)(2,1)}, bf16[32,96,256]{2,1,0:T(8,128)(2,1)}, u32[]{:S(2)}, u32[]{:S(2)}) collective-permute-start(bf16[32,96,256]{2,1,0:T(8,128)(2,1)} %convolution_convert_fusion.4), channel_id=1, source_target_pairs={{0,1},{1,0},{2,3},{3,2},{4,5},{5,4},{6,7},{7,6},{8,9},{9,8},{10,11... | collective-permute-start | bytes 4718600 | tf_op jit(solution)/shard_map/ppermute | solution.py:139
  366.5 2.5 copy-start.35
  393.3 36.0 %collective-permute-start.7 = (bf16[32,96,256]{2,1,0:T(8,128)(2,1)}, bf16[32,96,256]{2,1,0:T(8,128)(2,1)}, u32[]{:S(2)}, u32[]{:S(2)}) collective-permute-start(bf16[32,96,256]{2,1,0:T(8,128)(2,1)} %convolution_convert_fusion.1), channel_id=1, source_target_pairs={{0,1},{1,0},{2,3},{3,2},{4,5},{5,4},{6,7},{7,6},{8,9},{9,8},{10,11... | collective-permute-start | bytes 4718600 | tf_op jit(solution)/shard_map/ppermute | solution.py:139
  394.8 7.4 %copy-start.38 = (bf16[32,96,96]{2,1,0:T(8,128)(2,1)S(1)}, bf16[32,96,96]{2,1,0:T(8,128)(2,1)}, u32[]{:S(2)}) copy-start(bf16[32,96,96]{2,1,0:T(8,128)(2,1)} %get-tuple-element.74) | copy-start | bytes 1769476
  394.8 7.4 %copy-start.46 = (f32[32,96]{1,0:T(8,128)S(1)}, f32[32,96]{1,0:T(8,128)}, u32[]{:S(2)}) copy-start(f32[32,96]{1,0:T(8,128)} %copy-done.45) | copy-start | bytes 36868
  402.3 27.0 %copy-start.9 = (f32[32,96,256]{2,1,0:T(8,128)S(1)}, f32[32,96,256]{2,1,0:T(8,128)}, u32[]{:S(2)}) copy-start(f32[32,96,256]{2,1,0:T(8,128)} %fusion.158) | copy-start | bytes 9437188
  434.1 2.6 copy-start.41
  434.1 2.7 copy-start.42
  434.1 4.8 %copy-start.44 = (f32[256,32]{0,1:T(8,128)S(1)}, f32[256,32]{0,1:T(8,128)}, u32[]{:S(2)}) copy-start(f32[256,32]{0,1:T(8,128)} %copy.110) | copy-start | bytes 98308
  434.1 4.8 %copy-start.47 = (f32[256,32]{0,1:T(8,128)S(1)}, f32[256,32]{0,1:T(8,128)}, u32[]{:S(2)}) copy-start(f32[256,32]{0,1:T(8,128)} %param.43) | copy-start | bytes 98308
  434.1 4.8 %copy-start.48 = (f32[256,32]{0,1:T(8,128)S(1)}, f32[256,32]{0,1:T(8,128)}, u32[]{:S(2)}) copy-start(f32[256,32]{0,1:T(8,128)} %param.42) | copy-start | bytes 98308
  (6 other events, 8.8 us)
Sparse Core Ops, SparseCore 0:
  267.8 74.8 reduce-scatter.1

commit v6 on v5

--- a/solution.py
+++ b/solution.py
@@ -183,6 +183,8 @@
     inner_t = jnp.transpose(inner_low)
     query_t = jnp.transpose(query_low)
     block = mixer_block(mixer_weight.astype(jnp.bfloat16), head_size)
+    fwd_pairs = jnp.stack([fwd_cos, fwd_sin], axis=2).reshape(head_count, 2 * mode_count, length)
+    inv_pairs = jnp.stack([inv_cos, inv_sin], axis=3).reshape(head_count, length, 2 * mode_count)
 
     def chunk_pass(inputs, out_grad, first_rows, second_rows):
         windows = inputs.shape[0]
@@ -194,16 +196,11 @@
         grad_feed_recv = {s: swap(grad_feed_mine, s) for s in shifts}
         query = query.astype(jnp.bfloat16)
         query_heads = query.reshape(windows, length, head_count, head_size)
-        spectrum = jnp.concatenate(
-            [
-                product("hmt,wthe->whme", fwd_cos, query_heads),
-                product("hmt,wthe->whme", fwd_sin, query_heads),
-            ],
-            axis=-1,
-        ).astype(jnp.bfloat16)
+        spectrum = product("hkt,wthe->whke", fwd_pairs, query_heads).astype(jnp.bfloat16)
+        spectrum = spectrum.reshape(windows, head_count, mode_count, 2 * head_size)
         mixed = product("whmi,hmio->whmo", spectrum, block).astype(jnp.bfloat16)
-        field = product("htm,whme->wthe", inv_cos, mixed[..., :head_size]) + product(
-            "htm,whme->wthe", inv_sin, mixed[..., head_size:]
+        field = product(
+            "htk,whke->wthe", inv_pairs, mixed.reshape(windows, head_count, 2 * mode_count, head_size)
         )
         field = field.reshape(windows, length, local_width).astype(jnp.bfloat16)
         attended, _ = scattered_product(field, output_low, local_width)
@@ -253,16 +250,13 @@
             )
         grad_field = grad_field.astype(jnp.bfloat16)
         grad_field = grad_field.reshape(windows, length, head_count, head_size)
-        grad_mixed = jnp.concatenate(
-            [
-                product("htm,wthe->whme", inv_cos, grad_field),
-                product("htm,wthe->whme", inv_sin, grad_field),
-            ],
-            axis=-1,
-        ).astype(jnp.bfloat16)
+        grad_mixed = product("htk,wthe->whke", inv_pairs, grad_field).astype(jnp.bfloat16)
+        grad_mixed = grad_mixed.reshape(windows, head_count, mode_count, 2 * head_size)
         grad_spectrum = product("whmo,hmio->whmi", grad_mixed, block).astype(jnp.bfloat16)
-        grad_query = product("hmt,whme->wthe", fwd_cos, grad_spectrum[..., :head_size]) + product(
-            "hmt,whme->wthe", fwd_sin, grad_spectrum[..., head_size:]
+        grad_query = product(
+            "hkt,whke->wthe",
+            fwd_pairs,
+            grad_spectrum.reshape(windows, head_count, 2 * mode_count, head_size),
         )
         grad_query = grad_query.reshape(windows, length, local_width).astype(jnp.bfloat16)
         query_grad = placed_rows(
@@ -315,20 +309,6 @@
         owned_shape = shape[:axis_number] + (shape[axis_number] // dp_count,) + shape[axis_number + 1 :]
         return jnp.moveaxis(grad.reshape(split), axis_number, 0).reshape(dp_count, -1, lanes), owned_shape
 
-    def reduced_over_dp(grads_axes):
-        laid = [lead(grad, axis_number) for grad, axis_number in grads_axes]
-        joined = jnp.concatenate([flat for flat, _ in laid], axis=1)
-        reduced = lax.psum_scatter(
-            joined.reshape(-1, lanes), "dp", scatter_dimension=0, tiled=True
-        )
-        parts = []
-        offset = 0
-        for flat, owned_shape in laid:
-            rows = flat.shape[1]
-            parts.append(reduced[offset : offset + rows].reshape(owned_shape))
-            offset += rows
-        return parts
-
     def summed_over_dp(grads_axes):
         laid = [lead(grad, axis_number) for grad, axis_number in grads_axes]
         joined = jnp.concatenate([flat for flat, _ in laid], axis=1)
@@ -345,7 +325,7 @@
             offset += size
         return parts
 
-    inner_part, outer_part_t = reduced_over_dp([(inner_grad, 0), (outer_grad_t, 0)])
+    inner_part, outer_part_t = summed_over_dp([(inner_grad, 0), (outer_grad_t, 0)])
     mixer_part, output_part_t = summed_over_dp([(mixer_full, 1), (output_grad_t, 0)])
     (query_part,) = summed_over_dp([(query_grad, 0)])
     output_part = jnp.transpose(output_part_t)

time: 451 us -> 506 us (1.12)
  waiting for transfers between devices: 136 us -> 179 us
  local copies, waits for them, and re-layouts: 41.9 us -> 78.4 us
  other arithmetic: 83.2 us -> 68.7 us
  between operations: 15.1 us -> 1.74 us
  starting transfers between devices: 21.6 us -> 34.8 us
  matrix products: 149 us -> 138 us
    ppermute x8, waiting for transfers between devices: 134 us -> 166 us  [swap(): return lax.ppermute(values, 'head', pairs)]
    reshape x2 -> x7, local copies, waits for them, and re-layouts: 0.96 us -> 24.2 us  [the longest x2 8.27 us: chunk_pass(): grad_spectrum.reshape(windows, head_count, 2 * mode_count, head_size)]
    convert_element_type x0 -> x3, local copies, waits for them, and re-layouts: none -> 14.1 us  [the longest x2 10.8 us: chunk_pass(): product('hkt,wthe->whke', fwd_pairs, query_heads).astype(jnp.bfloat16)]
    all_to_all x2 -> x3, starting transfers between devices: 9.33 us -> 22.5 us  [summed_over_dp(): lax.all_to_all(joined.astype(jnp.bfloat16).reshape(-1, lanes), 'dp', 0, 0...]
    dot_general x35 -> x31, matrix products: 132 us -> 120 us  [product(): return jnp.einsum(form, left, right, preferred_element_type=jnp.float32)]
    all_to_all x2 -> x3, waiting for transfers between devices: 1.84 us -> 12.8 us  [summed_over_dp(): lax.all_to_all(joined.astype(jnp.bfloat16).reshape(-1, lanes), 'dp', 0, 0...]
    concatenate x3 -> x0, other arithmetic: 7.91 us -> none  [the longest x1 4.64 us: reduced_over_dp(): joined = jnp.concatenate([flat for flat, _ in laid], axis=1)]
    slice x3 -> x0, local copies, waits for them, and re-layouts: 5.08 us -> none  [the longest x1 2.72 us: chunk_pass(): grad_spectrum[..., head_size:]]
  transfers between devices with their start and end apart: 11 -> 11, of which waited for: 8 -> 8; matrix products, arithmetic and copies ran while one was open for 44% -> 32% of each run, Pallas kernels for 0% -> 0%
where the time goes in v6:
time: 506 us; the launch traced here: 500 us
  waiting for transfers between devices  179 us (35%)
  matrix products  138 us (27%)
  local copies, waits for them, and re-layouts  78.4 us (15%)
  other arithmetic  68.7 us (14%)
  starting transfers between devices  34.8 us (7%)
    ppermute x8, waiting for transfers between devices, swap(): return lax.ppermute(values, 'head', pairs)  166 us
    dot_general x31, matrix products, product(): return jnp.einsum(form, left, right, preferred_element_type=jnp.float32)  120 us
    convert_element_type x1, other arithmetic, chunk_pass(): hidden = activated.astype(jnp.bfloat16)  30.3 us
    all_to_all x3, starting transfers between devices, summed_over_dp(): lax.all_to_all(joined.astype(jnp.bfloat16).reshape(-1, lanes), 'dp', 0, 0...  22.5 us
    all_to_all x3, waiting for transfers between devices, summed_over_dp(): lax.all_to_all(joined.astype(jnp.bfloat16).reshape(-1, lanes), 'dp', 0, 0...  12.8 us
    ppermute x8, starting transfers between devices, swap(): return lax.ppermute(values, 'head', pairs)  12.3 us
    convert_element_type x2, local copies, waits for them, and re-layouts, chunk_pass(): product('hkt,wthe->whke', fwd_pairs, query_heads).astype(jnp.bfloat16)  10.8 us
    dot_general x2, matrix products, trend_back(): jnp.einsum('wts,wtd->wsd', tiled, parts, preferred_element_type=jnp.float32)  10.2 us
  transfers between devices with their start and end apart: 11, of which 8 were waited for; matrix products, arithmetic and copies ran while one was open for 32% of the time, Pallas kernels for 0%

profile of v6, /device:TPU:0, one launch (start us, length us, event | category | flops | bytes accessed | tf_op | source)
XLA Modules:
  0.0 500.3 jit_solution(3864509196030147549)
XLA Ops:
  0.7 3.4 convert_element_type.271
  4.1 3.0 collective-permute-start
  8.4 3.3 convert_element_type.269
  13.4 2.1 fusion.136
  15.5 4.0 slice_negate_fusion
  19.5 22.3 %collective-permute-done = bf16[32,96,256]{2,1,0:T(8,128)(2,1)} collective-permute-done((bf16[32,96,256]{2,1,0:T(8,128)(2,1)}, bf16[32,96,256]{2,1,0:T(8,128)(2,1)}, u32[]{:S(2)}, u32[]{:S(2)}) %collective-permute-start) | collective-permute-done | bytes 1572896 | tf_op jit(solution)/shard_map/ppermute | solution.py:139
  41.8 3.1 fusion.69
  44.9 4.1 copy.128
  49.0 3.6 convert_bitcast_fusion.3
  52.6 4.5 copy.131
  57.0 5.2 %reshape.313 = bf16[32,4,48,128]{3,2,1,0:T(8,128)(2,1)} reshape(bf16[32,4,96,64]{3,2,1,0:T(8,128)(2,1)} %copy.131) | data formatting | bytes 3145728 | tf_op jit(solution)/shard_map/reshape | solution.py:200
  62.3 5.9 %fusion.71 = bf16[32,4,48,128]{3,0,2,1:T(8,128)(2,1)S(1)} fusion(bf16[32,4,48,128]{3,2,1,0:T(8,128)(2,1)} %reshape.313, bf16[4,48,64,64]{3,2,1,0:T(8,128)(2,1)} %get-tuple-element.65, bf16[4,48,64,64]{3,2,1,0:T(8,128)(2,1)} %get-tuple-element.64, bf16[4,48,64,128]{3,2,1,0:T(8,128)(2,1)S(1)} %bitcast.237), kind=kOutput, calls=%fused_computation.120 | convolution fusion | flops 220987392 | bytes 9437184 | tf_op jit(solution)/shard_map/whmi,hmio->whmo/dot_general | solution.py:44
  69.9 3.9 reshape.349
  73.8 2.0 convert_bitcast_fusion.2
  78.9 4.6 select_convert_fusion
  84.3 28.2 %collective-permute-done.1 = bf16[32,96,256]{2,1,0:T(8,128)(2,1)S(1)} collective-permute-done((bf16[32,96,256]{2,1,0:T(8,128)(2,1)S(1)}, bf16[32,96,256]{2,1,0:T(8,128)(2,1)S(1)}, u32[]{:S(2)}, u32[]{:S(2)}) %collective-permute-start.1) | collective-permute-done | bytes 1572896 | tf_op jit(solution)/shard_map/ppermute | solution.py:139
  113.7 3.8 fusion.88
  119.0 3.2 fusion.191
  123.9 6.4 %fusion.98 = f32[32,96,1024]{2,1,0:T(8,128)} fusion(bf16[32,96,256]{2,1,0:T(8,128)(2,1)S(1)} %get-tuple-element.88, bf16[1024,512]{1,0:T(8,128)(2,1)S(1)} %convert_element_type.299, s32[]{:T(128)S(6)} %select_n.208), kind=kOutput, calls=%fused_computation.141 | convolution fusion | flops 1610612736 | bytes 14680068 | tf_op jit(solution)/shard_map/wtd,fd->wtf/dot_general | solution.py:44
  132.2 22.7 %collective-permute-done.2 = bf16[32,96,256]{2,1,0:T(8,128)(2,1)} collective-permute-done((bf16[32,96,256]{2,1,0:T(8,128)(2,1)S(1)}, bf16[32,96,256]{2,1,0:T(8,128)(2,1)}, u32[]{:S(2)}, u32[]{:S(2)}) %collective-permute-start.2) | collective-permute-done | bytes 1572896 | tf_op jit(solution)/shard_map/ppermute | solution.py:139
  154.9 7.3 %convert_reduce_fusion.1 = (u32[96,1024]{1,0:T(8,128)}, u32[96,1024]{1,0:T(8,128)}, f32[32,96,1024]{2,1,0:T(8,128)S(1)}) fusion(f32[32,96,1024]{2,1,0:T(8,128)S(1)} %fusion.107, bf16[32,96,256]{2,1,0:T(8,128)(2,1)} %collective-permute-done.2, bf16[512,1024]{1,0:T(8,128)(2,1)} %copy-done.15, s32[]{:T(128)S(6)} %select_n.210), kind=kOutput, calls=%fused_computation.6 | convolution fusion | flops 1648164864 | bytes 28049412 | tf_op jit(solution)/shard_map/wtd,de->wte/dot_general | solution.py:44
  162.2 30.3 %multiply_convert_fusion = (bf16[32,96,1024]{2,1,0:T(8,128)(2,1)}, f32[32,96,1024]{2,1,0:T(8,128)}) fusion(f32[32,96,1024]{2,1,0:T(8,128)S(1)} %get-tuple-element.87, u32[96,1024]{1,0:T(8,128)} %get-tuple-element.22, u32[96,1024]{1,0:T(8,128)} %get-tuple-element.21), kind=kLoop, calls=%fused_computation.8 | loop fusion | flops 213909504 | bytes 32243712 | tf_op jit(solution)/shard_map/convert_element_type | solution.py:212
  192.5 18.4 %add_convert_fusion = bf16[32,96,1024]{2,1,0:T(8,128)(2,1)} fusion(f32[32,96,1024]{2,1,0:T(8,128)} %get-tuple-element.45, f32[32,96,1024]{2,1,0:T(8,128)} %fusion.98, f32[32,96,1024]{2,1,0:T(8,128)} %copy-done.8, bf16[32,96,256]{2,1,0:T(8,128)(2,1)} %collective-permute-done.3, bf16[1024,512]{1,0:T(8,128)(2,1)} %copy-done.14, s32[]{:T(128)S(6)} %select_n.210), kind=kOutput, calls=%fused_computation.7 | convolution fusion | flops 1657798656 | bytes 46137348 | tf_op jit(solution)/shard_map/wtd,fd->wtf/dot_general | solution.py:44
  211.0 4.8 convolution_convert_fusion.3
  219.2 27.9 %collective-permute-done.4 = bf16[32,96,256]{2,1,0:T(8,128)(2,1)S(1)} collective-permute-done((bf16[32,96,256]{2,1,0:T(8,128)(2,1)S(1)}, bf16[32,96,256]{2,1,0:T(8,128)(2,1)S(1)}, u32[]{:S(2)}, u32[]{:S(2)}) %collective-permute-start.4) | collective-permute-done | bytes 1572896 | tf_op jit(solution)/shard_map/ppermute | solution.py:139
  247.1 4.5 multiply_convert_fusion.1
  251.7 7.0 %fusion.192 = (bf16[32,96,256]{2,1,0:T(8,128)(2,1)S(1)}, f32[32,96,256]{2,1,0:T(8,128)}) fusion(f32[32,96,256]{2,1,0:T(8,128)} %get-tuple-element.90, bf16[32,96,256]{2,1,0:T(8,128)(2,1)} %get-tuple-element.53, bf16[32,96,256]{2,1,0:T(8,128)(2,1)} %get-tuple-element.54, bf16[32,96,256]{2,1,0:T(8,128)(2,1)} %get-tuple-element.52, ...), kind=kOutput, calls=%fused_computation.268 | convolution fusion | flops 474021888 | bytes 13172736 | tf_op jit(solution)/shard_map/wts,wtd->wsd/dot_general | solution.py:89
  261.5 3.6 fusion.76
  265.8 23.3 %collective-permute-done.5 = bf16[32,96,256]{2,1,0:T(8,128)(2,1)S(1)} collective-permute-done((bf16[32,96,256]{2,1,0:T(8,128)(2,1)S(1)}, bf16[32,96,256]{2,1,0:T(8,128)(2,1)S(1)}, u32[]{:S(2)}, u32[]{:S(2)}) %collective-permute-start.5) | collective-permute-done | bytes 1572896 | tf_op jit(solution)/shard_map/ppermute | solution.py:139
  292.0 3.1 copy.142
  295.1 2.0 convert_bitcast_fusion.1
  297.1 3.2 copy.145
  300.4 2.8 reshape.317
  303.2 8.8 %fusion.70 = bf16[32,4,48,128]{3,0,2,1:T(8,128)(2,1)} fusion(bf16[4,48,64,64]{3,2,1,0:T(8,128)(2,1)} %get-tuple-element.65, bf16[4,48,64,64]{3,2,1,0:T(8,128)(2,1)} %get-tuple-element.64, bf16[4,48,64,128]{3,2,1,0:T(8,128)(2,1)} %bitcast.238, bf16[32,4,48,128]{3,2,1,0:T(8,128)(2,1)} %reshape.317), kind=kOutput, calls=%fused_computation.119 | convolution fusion | flops 220987392 | bytes 9437184 | tf_op jit(solution)/shard_map/whmo,hmio->whmi/dot_general | solution.py:44
  312.0 3.2 copy.189
  315.2 5.1 %reshape.350 = bf16[32,4,96,64]{3,2,0,1:T(8,128)(2,1)} reshape(bf16[32,4,48,128]{3,2,0,1:T(8,128)(2,1)} %copy.189) | data formatting | bytes 3145728 | tf_op jit(solution)/shard_map/reshape | solution.py:259
  320.3 3.0 convert_bitcast_fusion
  323.4 2.9 convolution_bitcast_fusion.7
  326.3 2.1 convolution_bitcast_fusion.6
  331.0 4.7 all-to-all-start
  335.7 5.9 %fusion.74 = bf16[512,1024]{1,0:T(8,128)(2,1)} fusion(bf16[512,1024]{1,0:T(8,128)(2,1)} %copy-done.18, s32[]{:T(128)S(6)} %select_n.210, bf16[32,96,256]{2,1,0:T(8,128)(2,1)} %collective-permute-done.3, bf16[32,96,1024]{2,1,0:T(8,128)(2,1)} %get-tuple-element.44), kind=kOutput, calls=%fused_computation.122 | convolution fusion | flops 1610612736 | bytes 8912900 | tf_op jit(solution)/shard_map/wtd,wtf->df/dot_general | solution.py:44
  341.7 2.3 reshape_reshape.23
  344.0 2.3 reshape_reshape.24
  346.3 3.1 pad_maximum_fusion.1
  349.3 6.5 %all-to-all-start.2 = ((bf16[16,512,128]{2,1,0:T(8,128)(2,1)}), bf16[16,512,128]{2,1,0:T(8,128)(2,1)}, u32[]{:S(2)}, u32[]{:S(2)}) async-start(bf16[16,512,128]{2,1,0:T(8,128)(2,1)} %pad_maximum_fusion.1), calls=%async_computation.2 | async-start | bytes 4194304 | tf_op jit(solution)/shard_map/all_to_all | solution.py:316
  355.8 6.4 %copy.156 = bf16[32,4,96,64]{3,0,2,1:T(8,128)(2,1)} copy(bf16[32,4,96,64]{2,3,0,1:T(8,128)(2,1)} %convert_bitcast_fusion.3) | data formatting | bytes 3145728 | tf_op jit(solution)/shard_map/convert_element_type | solution.py:199
  362.9 3.5 fusion.90
  366.5 2.2 copy.146
  368.7 2.6 stack_reshape.3
  371.3 2.5 copy.160
  382.1 2.0 pad_maximum_fusion
  384.1 12.8 %all-to-all-done.2 = bf16[16,512,128]{2,1,0:T(8,128)(2,1)} async-done(((bf16[16,512,128]{2,1,0:T(8,128)(2,1)}), bf16[16,512,128]{2,1,0:T(8,128)(2,1)}, u32[]{:S(2)}, u32[]{:S(2)}) %all-to-all-start.2) | async-done | bytes 2097184 | tf_op jit(solution)/shard_map/all_to_all | solution.py:316
  396.8 11.4 %all-to-all-start.1 = ((bf16[16,832,128]{2,1,0:T(8,128)(2,1)}), bf16[16,832,128]{2,1,0:T(8,128)(2,1)S(1)}, u32[]{:S(2)}, u32[]{:S(2)}) async-start(bf16[16,832,128]{2,1,0:T(8,128)(2,1)} %pad_maximum_fusion), calls=%async_computation.1 | async-start | bytes 6815744 | tf_op jit(solution)/shard_map/all_to_all | solution.py:316
  408.2 2.0 constant_dynamic-slice_fusion
  414.7 5.9 %convolution_convert_fusion.4 = bf16[32,96,256]{2,1,0:T(8,128)(2,1)} fusion(bf16[32,96,1024]{2,1,0:T(8,128)(2,1)} %get-tuple-element.44, bf16[1024,512]{1,0:T(8,128)(2,1)} %copy-done.14, s32[]{:T(128)S(6)} %select_n.215), kind=kOutput, calls=%fused_computation.111 | convolution fusion | flops 1611399168 | bytes 8388612 | tf_op jit(solution)/shard_map/wte,ed->wtd/dot_general | solution.py:44
  422.2 2.5 fusion.134
  424.7 2.0 convolution_convert_fusion.1
  430.2 1.9 convert_reduce_fusion.3
  439.6 18.2 %collective-permute-done.6 = bf16[32,96,256]{2,1,0:T(8,128)(2,1)} collective-permute-done((bf16[32,96,256]{2,1,0:T(8,128)(2,1)}, bf16[32,96,256]{2,1,0:T(8,128)(2,1)}, u32[]{:S(2)}, u32[]{:S(2)}) %collective-permute-start.6) | collective-permute-done | bytes 1572896 | tf_op jit(solution)/shard_map/ppermute | solution.py:139
  459.3 7.6 %fusion.187 = (bf16[32,96,256]{2,1,0:T(8,128)(2,1)S(1)}, bf16[32,96,256]{2,1,0:T(8,128)(2,1)S(1)}, bf16[32,96,256]{2,1,0:T(8,128)(2,1)S(1)}, f32[32,96,256]{2,1,0:T(8,128)S(1)}) fusion(bf16[32,96,256]{2,1,0:T(8,128)(2,1)} %collective-permute-done.6, bf16[32,96,1024]{2,1,0:T(8,128)(2,1)} %get-tuple-element.44, bf16[1024,512]{1,0:T(8,128)(2,1)} %copy-done.14, ...), kind=kOutput, calls=%fused_computation.263 | convolution fusion | flops 1620049920 | bytes 22556676 | tf_op jit(solution)/shard_map/wte,ed->wtd/dot_general | solution.py:44
  467.0 3.4 multiply_subtract_fusion
  470.4 23.6 %collective-permute-done.7 = bf16[32,96,256]{2,1,0:T(8,128)(2,1)S(1)} collective-permute-done((bf16[32,96,256]{2,1,0:T(8,128)(2,1)}, bf16[32,96,256]{2,1,0:T(8,128)(2,1)S(1)}, u32[]{:S(2)}, u32[]{:S(2)}) %collective-permute-start.7) | collective-permute-done | bytes 1572896 | tf_op jit(solution)/shard_map/ppermute | solution.py:139
  494.0 2.6 add_add_fusion
  497.1 2.4 multiply_add_fusion
  (169 shorter events, 55.9 us)
Async XLA Ops:
  0.7 6.4 %copy-start.49 = (s32[4,48]{1,0:T(4,128)S(1)}, s32[4,48]{1,0:T(4,128)}, u32[]{:S(2)}) copy-start(s32[4,48]{1,0:T(4,128)} %param.31) | copy-start | bytes 2308
  0.7 6.9 %copy-start.37 = (f32[512,256]{1,0:T(8,128)S(1)}, f32[512,256]{1,0:T(8,128)}, u32[]{:S(2)}) copy-start(f32[512,256]{1,0:T(8,128)} %param.33) | copy-start | bytes 1572868
  4.1 37.7 %collective-permute-start = (bf16[32,96,256]{2,1,0:T(8,128)(2,1)}, bf16[32,96,256]{2,1,0:T(8,128)(2,1)}, u32[]{:S(2)}, u32[]{:S(2)}) collective-permute-start(bf16[32,96,256]{2,1,0:T(8,128)(2,1)} %convert_element_type.271), channel_id=1, source_target_pairs={{0,1},{1,0},{2,3},{3,2},{4,5},{5,4},{6,7},{7,6},{8,9},{9,8},{10,11... | collective-permute-start | bytes 4718600 | tf_op jit(solution)/shard_map/ppermute | solution.py:139
  8.4 4.9 copy-start.33
  11.7 50.6 %copy-start.1 = (bf16[4,3072,128]{2,1,0:T(8,128)(2,1)}, bf16[4,3072,128]{2,1,0:T(8,128)(2,1)S(1)}, u32[]{:S(2)}) copy-start(bf16[4,3072,128]{2,1,0:T(8,128)(2,1)S(1)} %convert_element_type.269) | copy-start | bytes 9437188
  15.5 26.3 %copy-start.25 = (bf16[512,256]{1,0:T(8,128)(2,1)S(1)}, bf16[512,256]{1,0:T(8,128)(2,1)}, u32[]{:S(2)}) copy-start(bf16[512,256]{1,0:T(8,128)(2,1)} %convert_element_type.270) | copy-start | bytes 786436
  75.8 3.0 copy-start.43
  75.8 3.0 copy-start.44
  75.8 3.0 copy-start.45
  75.8 3.0 copy-start.46
  75.8 3.0 copy-start.47
  75.9 3.0 copy-start.48
  76.1 36.5 %copy-start.4 = (bf16[32,96,4,64]{1,3,2,0:T(8,128)(2,1)}, bf16[32,96,4,64]{1,3,2,0:T(8,128)(2,1)S(1)}, u32[]{:S(2)}) copy-start(bf16[32,96,4,64]{1,3,2,0:T(8,128)(2,1)S(1)} %copy.137) | copy-start | bytes 4718596
  76.1 7.4 %copy-start.22 = (f32[32,96,256]{2,1,0:T(8,128)S(1)}, f32[32,96,256]{2,1,0:T(8,128)}, u32[]{:S(2)}) copy-start(f32[32,96,256]{2,1,0:T(8,128)} %param.30) | copy-start | bytes 9437188
  76.9 35.6 %collective-permute-start.1 = (bf16[32,96,256]{2,1,0:T(8,128)(2,1)S(1)}, bf16[32,96,256]{2,1,0:T(8,128)(2,1)S(1)}, u32[]{:S(2)}, u32[]{:S(2)}) collective-permute-start(bf16[32,96,256]{2,1,0:T(8,128)(2,1)S(1)} %convolution_convert_fusion.5), channel_id=1, source_target_pairs={{0,1},{1,0},{2,3},{3,2},{4,5},{5,4},{6,7},{7,6},{8,9},{9,8},{10,11... | collective-permute-start | bytes 4718600 | tf_op jit(solution)/shard_map/ppermute | solution.py:139
  78.8 5.5 %copy-start.39 = (f32[32,96]{1,0:T(8,128)}, f32[32,96]{1,0:T(8,128)S(1)}, u32[]{:S(2)}) copy-start(f32[32,96]{1,0:T(8,128)S(1)} %get-tuple-element.38) | copy-start | bytes 36868
  83.4 30.2 %copy-start.36 = (bf16[32,96,96]{2,1,0:T(8,128)(2,1)}, bf16[32,96,96]{2,1,0:T(8,128)(2,1)S(1)}, u32[]{:S(2)}) copy-start(bf16[32,96,96]{2,1,0:T(8,128)(2,1)S(1)} %get-tuple-element.71) | copy-start | bytes 1769476
  83.5 35.5 %copy-start.34 = (bf16[32,96,96]{2,1,0:T(8,128)(2,1)}, bf16[32,96,96]{2,1,0:T(8,128)(2,1)S(1)}, u32[]{:S(2)}) copy-start(bf16[32,96,96]{2,1,0:T(8,128)(2,1)S(1)} %get-tuple-element.70) | copy-start | bytes 1769476
  83.5 29.1 %copy-start.7 = (f32[32,96,256]{2,1,0:T(8,128)S(1)}, f32[32,96,256]{2,1,0:T(8,128)}, u32[]{:S(2)}) copy-start(f32[32,96,256]{2,1,0:T(8,128)} %param.29) | copy-start | bytes 9437188
  113.7 3.8 copy-start.10
  117.5 12.8 %copy-start.11 = (bf16[32,96,256]{2,1,0:T(8,128)(2,1)}, bf16[32,96,256]{2,1,0:T(8,128)(2,1)S(1)}, u32[]{:S(2)}) copy-start(bf16[32,96,256]{2,1,0:T(8,128)(2,1)S(1)} %get-tuple-element.85) | copy-start | bytes 4718596
  117.5 37.4 %collective-permute-start.2 = (bf16[32,96,256]{2,1,0:T(8,128)(2,1)S(1)}, bf16[32,96,256]{2,1,0:T(8,128)(2,1)}, u32[]{:S(2)}, u32[]{:S(2)}) collective-permute-start(bf16[32,96,256]{2,1,0:T(8,128)(2,1)S(1)} %get-tuple-element.85), channel_id=1, source_target_pairs={{0,1},{1,0},{2,3},{3,2},{4,5},{5,4},{6,7},{7,6},{8,9},{9,8},{10,11... | collective-permute-start | bytes 4718600 | tf_op jit(solution)/shard_map/ppermute | solution.py:139
  119.0 3.9 copy-start.24
  122.2 1.6 copy-start.19
  122.2 70.3 %collective-permute-start.3 = (bf16[32,96,256]{2,1,0:T(8,128)(2,1)S(1)}, bf16[32,96,256]{2,1,0:T(8,128)(2,1)}, u32[]{:S(2)}, u32[]{:S(2)}) collective-permute-start(bf16[32,96,256]{2,1,0:T(8,128)(2,1)S(1)} %get-tuple-element.88), channel_id=1, source_target_pairs={{0,1},{1,0},{2,3},{3,2},{4,5},{5,4},{6,7},{7,6},{8,9},{9,8},{10,11... | collective-permute-start | bytes 4718600 | tf_op jit(solution)/shard_map/ppermute | solution.py:139
  123.8 6.6 %copy-start.15 = (bf16[512,1024]{1,0:T(8,128)(2,1)}, bf16[512,1024]{1,0:T(8,128)(2,1)S(1)}, u32[]{:S(2)}) copy-start(bf16[512,1024]{1,0:T(8,128)(2,1)S(1)} %convert_element_type.297) | copy-start | bytes 3145732
  123.9 6.4 %copy-start.14 = (bf16[1024,512]{1,0:T(8,128)(2,1)}, bf16[1024,512]{1,0:T(8,128)(2,1)S(1)}, u32[]{:S(2)}) copy-start(bf16[1024,512]{1,0:T(8,128)(2,1)S(1)} %convert_element_type.299) | copy-start | bytes 3145732
  162.2 30.3 %copy-start.8 = (f32[32,96,1024]{2,1,0:T(8,128)}, f32[32,96,1024]{2,1,0:T(8,128)S(1)}, u32[]{:S(2)}) copy-start(f32[32,96,1024]{2,1,0:T(8,128)S(1)} %get-tuple-element.87) | copy-start | bytes 37748740
  192.5 18.4 %copy-start.16 = (bf16[512,1024]{1,0:T(8,128)(2,1)S(1)}, bf16[512,1024]{1,0:T(8,128)(2,1)}, u32[]{:S(2)}) copy-start(bf16[512,1024]{1,0:T(8,128)(2,1)} %copy-done.15) | copy-start | bytes 3145732
  211.0 6.4 %copy-start = (bf16[32,96,1024]{2,1,0:T(8,128)(2,1)S(1)}, bf16[32,96,1024]{2,1,0:T(8,128)(2,1)}, u32[]{:S(2)}) copy-start(bf16[32,96,1024]{2,1,0:T(8,128)(2,1)} %add_convert_fusion) | copy-start | bytes 18874372
  211.0 6.4 %copy-start.12 = (bf16[32,96,256]{2,1,0:T(8,128)(2,1)S(1)}, bf16[32,96,256]{2,1,0:T(8,128)(2,1)}, u32[]{:S(2)}) copy-start(bf16[32,96,256]{2,1,0:T(8,128)(2,1)} %copy-done.11) | copy-start | bytes 4718596
  215.8 31.3 %collective-permute-start.4 = (bf16[32,96,256]{2,1,0:T(8,128)(2,1)S(1)}, bf16[32,96,256]{2,1,0:T(8,128)(2,1)S(1)}, u32[]{:S(2)}, u32[]{:S(2)}) collective-permute-start(bf16[32,96,256]{2,1,0:T(8,128)(2,1)S(1)} %convolution_convert_fusion.3), channel_id=1, source_target_pairs={{0,1},{1,0},{2,3},{3,2},{4,5},{5,4},{6,7},{7,6},{8,9},{9,8},{10,11... | collective-permute-start | bytes 4718600 | tf_op jit(solution)/shard_map/ppermute | solution.py:139
  217.4 29.7 %copy-start.20 = (f32[32,96,256]{2,1,0:T(8,128)S(1)}, f32[32,96,256]{2,1,0:T(8,128)}, u32[]{:S(2)}) copy-start(f32[32,96,256]{2,1,0:T(8,128)} %get-tuple-element.89) | copy-start | bytes 9437188
  247.1 12.5 %slice-start = ((s8[6291456]{0:T(1024)(128)(4,1)}), s8[4194304]{0:T(1024)(128)(4,1)S(1)}, s32[]{:S(2)}) async-start(s8[6291456]{0:T(1024)(128)(4,1)} %bitcast.234), calls=%async_computation.3 | async-start | bytes 8388608
  251.6 8.0 %slice-start.1 = ((s8[6291456]{0:T(1024)(128)(4,1)}), s8[2097152]{0:T(1024)(128)(4,1)S(1)}, s32[]{:S(2)}) async-start(s8[6291456]{0:T(1024)(128)(4,1)} %bitcast.234), calls=%async_computation.4 | async-start | bytes 4194304
  258.7 6.5 %copy-start.27 = (bf16[32,96,256]{2,1,0:T(8,128)(2,1)}, bf16[32,96,256]{2,1,0:T(8,128)(2,1)S(1)}, u32[]{:S(2)}) copy-start(bf16[32,96,256]{2,1,0:T(8,128)(2,1)S(1)} %get-tuple-element.91) | copy-start | bytes 4718596
  258.7 30.4 %collective-permute-start.5 = (bf16[32,96,256]{2,1,0:T(8,128)(2,1)S(1)}, bf16[32,96,256]{2,1,0:T(8,128)(2,1)S(1)}, u32[]{:S(2)}, u32[]{:S(2)}) collective-permute-start(bf16[32,96,256]{2,1,0:T(8,128)(2,1)S(1)} %get-tuple-element.91), channel_id=1, source_target_pairs={{0,1},{1,0},{2,3},{3,2},{4,5},{5,4},{6,7},{7,6},{8,9},{9,8},{10,11... | collective-permute-start | bytes 4718600 | tf_op jit(solution)/shard_map/ppermute | solution.py:139
  261.5 3.6 copy-start.18
  265.2 23.9 %copy-start.17 = (bf16[512,1024]{1,0:T(8,128)(2,1)}, bf16[512,1024]{1,0:T(8,128)(2,1)S(1)}, u32[]{:S(2)}) copy-start(bf16[512,1024]{1,0:T(8,128)(2,1)S(1)} %fusion.76) | copy-start | bytes 3145732
  289.1 1.1 copy-start.28
  292.0 3.1 copy-start.32
  323.4 2.9 copy-start.2
  331.0 18.3 %all-to-all-start = ((bf16[16,64,128]{2,1,0:T(8,128)(2,1)}), bf16[16,64,128]{2,1,0:T(8,128)(2,1)S(1)}, u32[]{:S(2)}, u32[]{:S(2)}) async-start(bf16[16,64,128]{2,1,0:T(8,128)(2,1)} %convert_element_type.334), calls=%async_computation | async-start | bytes 524288 | tf_op jit(solution)/shard_map/all_to_all | solution.py:316
  349.3 12.9 %copy-start.30 = (bf16[16,64,128]{2,1,0:T(8,128)(2,1)}, bf16[16,64,128]{2,1,0:T(8,128)(2,1)S(1)}, u32[]{:S(2)}) copy-start(bf16[16,64,128]{2,1,0:T(8,128)(2,1)S(1)} %all-to-all-done) | copy-start | bytes 786436
  349.3 47.5 %all-to-all-start.2 = ((bf16[16,512,128]{2,1,0:T(8,128)(2,1)}), bf16[16,512,128]{2,1,0:T(8,128)(2,1)}, u32[]{:S(2)}, u32[]{:S(2)}) async-start(bf16[16,512,128]{2,1,0:T(8,128)(2,1)} %pad_maximum_fusion.1), calls=%async_computation.2 | async-start | bytes 4194304 | tf_op jit(solution)/shard_map/all_to_all | solution.py:316
  362.2 4.2 copy-start.13
  371.3 2.5 copy-start.6
  374.5 1.9 copy-start.21
  377.6 1.6 copy-start.5
  377.6 2.0 copy-start.29
  396.8 99.8 %all-to-all-start.1 = ((bf16[16,832,128]{2,1,0:T(8,128)(2,1)}), bf16[16,832,128]{2,1,0:T(8,128)(2,1)S(1)}, u32[]{:S(2)}, u32[]{:S(2)}) async-start(bf16[16,832,128]{2,1,0:T(8,128)(2,1)} %pad_maximum_fusion), calls=%async_computation.1 | async-start | bytes 6815744 | tf_op jit(solution)/shard_map/all_to_all | solution.py:316
  414.7 7.5 %copy-start.3 = (bf16[32,96,4,64]{1,3,2,0:T(8,128)(2,1)S(1)}, bf16[32,96,4,64]{1,3,2,0:T(8,128)(2,1)}, u32[]{:S(2)}) copy-start(bf16[32,96,4,64]{1,3,2,0:T(8,128)(2,1)} %copy-done.2) | copy-start | bytes 4718596
  414.7 7.5 %copy-start.26 = (bf16[512,256]{1,0:T(8,128)(2,1)S(1)}, bf16[512,256]{1,0:T(8,128)(2,1)}, u32[]{:S(2)}) copy-start(bf16[512,256]{1,0:T(8,128)(2,1)} %convert_element_type.270) | copy-start | bytes 786436
  420.7 37.1 %collective-permute-start.6 = (bf16[32,96,256]{2,1,0:T(8,128)(2,1)}, bf16[32,96,256]{2,1,0:T(8,128)(2,1)}, u32[]{:S(2)}, u32[]{:S(2)}) collective-permute-start(bf16[32,96,256]{2,1,0:T(8,128)(2,1)} %convolution_convert_fusion.4), channel_id=1, source_target_pairs={{0,1},{1,0},{2,3},{3,2},{4,5},{5,4},{6,7},{7,6},{8,9},{9,8},{10,11... | collective-permute-start | bytes 4718600 | tf_op jit(solution)/shard_map/ppermute | solution.py:139
  424.7 2.0 copy-start.31
  457.8 36.2 %collective-permute-start.7 = (bf16[32,96,256]{2,1,0:T(8,128)(2,1)}, bf16[32,96,256]{2,1,0:T(8,128)(2,1)S(1)}, u32[]{:S(2)}, u32[]{:S(2)}) collective-permute-start(bf16[32,96,256]{2,1,0:T(8,128)(2,1)} %convolution_convert_fusion.1), channel_id=1, source_target_pairs={{0,1},{1,0},{2,3},{3,2},{4,5},{5,4},{6,7},{7,6},{8,9},{9,8},{10,11... | collective-permute-start | bytes 4718600 | tf_op jit(solution)/shard_map/ppermute | solution.py:139
  459.3 7.6 %copy-start.35 = (bf16[32,96,96]{2,1,0:T(8,128)(2,1)S(1)}, bf16[32,96,96]{2,1,0:T(8,128)(2,1)}, u32[]{:S(2)}) copy-start(bf16[32,96,96]{2,1,0:T(8,128)(2,1)} %copy-done.34) | copy-start | bytes 1769476
  459.3 7.6 %copy-start.40 = (f32[32,96]{1,0:T(8,128)S(1)}, f32[32,96]{1,0:T(8,128)}, u32[]{:S(2)}) copy-start(f32[32,96]{1,0:T(8,128)} %copy-done.39) | copy-start | bytes 36868
  467.0 27.0 %copy-start.9 = (f32[32,96,256]{2,1,0:T(8,128)S(1)}, f32[32,96,256]{2,1,0:T(8,128)}, u32[]{:S(2)}) copy-start(f32[32,96,256]{2,1,0:T(8,128)} %fusion.134) | copy-start | bytes 9437188
  467.0 27.0 %copy-start.23 = (f32[32,96,256]{2,1,0:T(8,128)S(1)}, f32[32,96,256]{2,1,0:T(8,128)}, u32[]{:S(2)}) copy-start(f32[32,96,256]{2,1,0:T(8,128)} %get-tuple-element.92) | copy-start | bytes 9437188
  496.6 2.9 copy-start.38
  496.6 2.9 copy-start.41
  496.6 2.9 copy-start.42

commit v7 on v5

--- a/solution.py
+++ b/solution.py
@@ -315,28 +315,28 @@
         owned_shape = shape[:axis_number] + (shape[axis_number] // dp_count,) + shape[axis_number + 1 :]
         return jnp.moveaxis(grad.reshape(split), axis_number, 0).reshape(dp_count, -1, lanes), owned_shape
 
-    def reduced_over_dp(grads_axes):
-        laid = [lead(grad, axis_number) for grad, axis_number in grads_axes]
-        joined = jnp.concatenate([flat for flat, _ in laid], axis=1)
-        reduced = lax.psum_scatter(
-            joined.reshape(-1, lanes), "dp", scatter_dimension=0, tiled=True
-        )
-        parts = []
-        offset = 0
-        for flat, owned_shape in laid:
-            rows = flat.shape[1]
-            parts.append(reduced[offset : offset + rows].reshape(owned_shape))
-            offset += rows
-        return parts
+    plane = 4 if dp_count % 4 == 0 else 1
+    planes = dp_count // plane
+    near_groups = [[b * plane + i for i in range(plane)] for b in range(planes)]
+    far_groups = [[i + plane * b for b in range(planes)] for i in range(plane)]
+
+    def summed_in_two_stages(joined):
+        rows = joined.shape[1]
+        by_member = jnp.swapaxes(joined.reshape(planes, plane, rows, lanes), 0, 1)
+        first = lax.all_to_all(
+            by_member.astype(jnp.bfloat16).reshape(-1, lanes), "dp", 0, 0,
+            axis_index_groups=near_groups, tiled=True,
+        )
+        partial = jnp.sum(first.astype(jnp.float32).reshape(plane, planes * rows, lanes), axis=0)
+        second = lax.all_to_all(
+            partial.astype(jnp.bfloat16), "dp", 0, 0, axis_index_groups=far_groups, tiled=True
+        )
+        return jnp.sum(second.astype(jnp.float32).reshape(planes, rows, lanes), axis=0)
 
     def summed_over_dp(grads_axes):
         laid = [lead(grad, axis_number) for grad, axis_number in grads_axes]
         joined = jnp.concatenate([flat for flat, _ in laid], axis=1)
-        rows = joined.shape[1]
-        arrived = lax.all_to_all(
-            joined.astype(jnp.bfloat16).reshape(-1, lanes), "dp", 0, 0, tiled=True
-        )
-        reduced = jnp.sum(arrived.astype(jnp.float32).reshape(dp_count, rows, lanes), axis=0)
+        reduced = summed_in_two_stages(joined)
         parts = []
         offset = 0
         for flat, owned_shape in laid:
@@ -345,7 +345,7 @@
             offset += size
         return parts
 
-    inner_part, outer_part_t = reduced_over_dp([(inner_grad, 0), (outer_grad_t, 0)])
+    inner_part, outer_part_t = summed_over_dp([(inner_grad, 0), (outer_grad_t, 0)])
     mixer_part, output_part_t = summed_over_dp([(mixer_full, 1), (output_grad_t, 0)])
     (query_part,) = summed_over_dp([(query_grad, 0)])
     output_part = jnp.transpose(output_part_t)

time: 451 us -> 458 us (1.016)
  starting transfers between devices: 21.6 us -> 35.7 us
  waiting for transfers between devices: 136 us -> 150 us
  between operations: 15.1 us -> 1.93 us
  local copies, waits for them, and re-layouts: 41.9 us -> 32.6 us
    all_to_all x2 -> x6, starting transfers between devices: 9.33 us -> 25.3 us  [the longest x3 12.7 us: summed_in_two_stages(): lax.all_to_all(by_member.astype(jnp.bfloat16).reshape(-1, lanes), 'dp', 0...]
    all_to_all x2 -> x6, waiting for transfers between devices: 1.84 us -> 13.3 us  [the longest x3 7.45 us: summed_in_two_stages(): lax.all_to_all(by_member.astype(jnp.bfloat16).reshape(-1, lanes), 'dp', 0...]
    concatenate x2 -> x0, other arithmetic: 8.55 us -> none  [the longest x1 4.64 us: reduced_over_dp(): joined = jnp.concatenate([flat for flat, _ in laid], axis=1)]
    another operation x7 -> x4, local copies, waits for them, and re-layouts: 10.3 us -> 2.25 us  [the longest x3 6.48 us: lead(): jnp.moveaxis(grad.reshape(split), axis_number, 0)]
    reduce_sum x2 -> x6, other arithmetic: 2.58 us -> 8.55 us  [the longest x3 7.16 us: summed_in_two_stages(): jnp.sum(first.astype(jnp.float32).reshape(plane, planes * rows, lanes), a...]
    unnamed x120, local copies, waits for them, and re-layouts: 10.1 us -> 5.22 us
  transfers between devices with their start and end apart: 11 -> 14, of which waited for: 8 -> 11; matrix products, arithmetic and copies ran while one was open for 44% -> 37% of each run, Pallas kernels for 0% -> 0%
where the time goes in v7:
time: 458 us; the launch traced here: 453 us
  waiting for transfers between devices  150 us (33%)
  matrix products  148 us (32%)
  other arithmetic  85 us (19%)
  starting transfers between devices  35.7 us (8%)
  local copies, waits for them, and re-layouts  32.6 us (7%)
    ppermute x8, waiting for transfers between devices, swap(): return lax.ppermute(values, 'head', pairs)  137 us
    dot_general x35, matrix products, product(): return jnp.einsum(form, left, right, preferred_element_type=jnp.float32)  134 us
    convert_element_type x1, other arithmetic, chunk_pass(): hidden = activated.astype(jnp.bfloat16)  30.3 us
    all_to_all x3, starting transfers between devices, summed_in_two_stages(): lax.all_to_all(by_member.astype(jnp.bfloat16).reshape(-1, lanes), 'dp', 0...  12.7 us
    all_to_all x3, starting transfers between devices, summed_in_two_stages(): lax.all_to_all(partial.astype(jnp.bfloat16), 'dp', 0, 0, axis_index_group...  12.6 us
    ppermute x8, starting transfers between devices, swap(): return lax.ppermute(values, 'head', pairs)  10.3 us
  transfers between devices with their start and end apart: 14, of which 11 were waited for; matrix products, arithmetic and copies ran while one was open for 37% of the time, Pallas kernels for 0%

profile of v7, /device:TPU:0, one launch (start us, length us, event | category | flops | bytes accessed | tf_op | source)
XLA Modules:
  0.0 453.2 jit_solution(8467721834189530297)
XLA Ops:
  0.7 3.3 convert_element_type.243
  4.0 3.0 collective-permute-start
  7.7 3.2 convert_element_type.241
  11.1 3.1 fusion.160
  14.2 4.0 slice_negate_fusion
  18.2 23.5 %collective-permute-done = bf16[32,96,256]{2,1,0:T(8,128)(2,1)} collective-permute-done((bf16[32,96,256]{2,1,0:T(8,128)(2,1)}, bf16[32,96,256]{2,1,0:T(8,128)(2,1)}, u32[]{:S(2)}, u32[]{:S(2)}) %collective-permute-start) | collective-permute-done | bytes 1572896 | tf_op jit(solution)/shard_map/ppermute | solution.py:139
  41.7 3.1 fusion.91
  44.8 4.4 copy.131
  49.2 3.9 fusion.72
  53.2 2.2 fusion.69
  57.9 3.1 fusion.95
  67.6 4.6 %select_convert_fusion = (bf16[32,96,96]{2,1,0:T(8,128)(2,1)S(1)}, bf16[32,96,96]{2,1,0:T(8,128)(2,1)S(1)}) fusion(bf16[96,96]{1,0:T(8,128)(2,1)S(1)} %copy-done.52, bf16[96,96]{1,0:T(8,128)(2,1)S(1)} %copy-done.53, bf16[96,96]{1,0:T(8,128)(2,1)S(1)} %copy-done.54, bf16[96,96]{1,0:T(8,128)(2,1)S(1)} %copy-done.55, bf16[96,96]{1,0:T(8,128)(2,1)S(1)} %copy-done.56, ...), kind=kLoop, calls=%fused_computation.132 | loop fusion | flops 2949120 | bytes 1302528 | tf_op jit(solution)/shard_map/convert_element_type | solution.py:66
  73.1 28.2 %collective-permute-done.1 = bf16[32,96,256]{2,1,0:T(8,128)(2,1)S(1)} collective-permute-done((bf16[32,96,256]{2,1,0:T(8,128)(2,1)S(1)}, bf16[32,96,256]{2,1,0:T(8,128)(2,1)S(1)}, u32[]{:S(2)}, u32[]{:S(2)}) %collective-permute-start.1) | collective-permute-done | bytes 1572896 | tf_op jit(solution)/shard_map/ppermute | solution.py:139
  102.5 3.8 fusion.112
  107.8 2.9 fusion.252
  113.0 6.4 %fusion.122 = f32[32,96,1024]{2,1,0:T(8,128)} fusion(bf16[32,96,256]{2,1,0:T(8,128)(2,1)S(1)} %get-tuple-element.88, bf16[1024,512]{1,0:T(8,128)(2,1)S(1)} %convert_element_type.269, s32[]{:T(128)S(6)} %select_n.186), kind=kOutput, calls=%fused_computation.158 | convolution fusion | flops 1610612736 | bytes 14680068 | tf_op jit(solution)/shard_map/wtd,fd->wtf/dot_general | solution.py:44
  121.2 22.5 %collective-permute-done.2 = bf16[32,96,256]{2,1,0:T(8,128)(2,1)} collective-permute-done((bf16[32,96,256]{2,1,0:T(8,128)(2,1)S(1)}, bf16[32,96,256]{2,1,0:T(8,128)(2,1)}, u32[]{:S(2)}, u32[]{:S(2)}) %collective-permute-start.2) | collective-permute-done | bytes 1572896 | tf_op jit(solution)/shard_map/ppermute | solution.py:139
  143.7 7.3 %convert_reduce_fusion.1 = (u32[96,1024]{1,0:T(8,128)}, u32[96,1024]{1,0:T(8,128)}, f32[32,96,1024]{2,1,0:T(8,128)S(1)}) fusion(f32[32,96,1024]{2,1,0:T(8,128)S(1)} %fusion.131, bf16[32,96,256]{2,1,0:T(8,128)(2,1)} %collective-permute-done.2, bf16[512,1024]{1,0:T(8,128)(2,1)} %copy-done.21, s32[]{:T(128)S(6)} %select_n.188), kind=kOutput, calls=%fused_computation.6 | convolution fusion | flops 1648164864 | bytes 28049412 | tf_op jit(solution)/shard_map/wtd,de->wte/dot_general | solution.py:44
  151.0 30.3 %multiply_convert_fusion = (bf16[32,96,1024]{2,1,0:T(8,128)(2,1)}, f32[32,96,1024]{2,1,0:T(8,128)}) fusion(f32[32,96,1024]{2,1,0:T(8,128)S(1)} %get-tuple-element.87, u32[96,1024]{1,0:T(8,128)} %get-tuple-element.22, u32[96,1024]{1,0:T(8,128)} %get-tuple-element.21), kind=kLoop, calls=%fused_computation.8 | loop fusion | flops 213909504 | bytes 32243712 | tf_op jit(solution)/shard_map/convert_element_type | solution.py:215
  181.3 18.7 %add_convert_fusion = bf16[32,96,1024]{2,1,0:T(8,128)(2,1)} fusion(f32[32,96,1024]{2,1,0:T(8,128)} %get-tuple-element.45, f32[32,96,1024]{2,1,0:T(8,128)} %fusion.122, f32[32,96,1024]{2,1,0:T(8,128)} %copy-done.12, bf16[32,96,256]{2,1,0:T(8,128)(2,1)} %collective-permute-done.3, bf16[1024,512]{1,0:T(8,128)(2,1)} %copy-done.19, s32[]{:T(128)S(6)} %select_n.188), kind=kOutput, calls=%fused_computation.7 | convolution fusion | flops 1657798656 | bytes 46137348 | tf_op jit(solution)/shard_map/wtd,fd->wtf/dot_general | solution.py:44
  200.0 6.0 %convolution_convert_fusion.3 = bf16[32,96,256]{2,1,0:T(8,128)(2,1)} fusion(bf16[32,96,1024]{2,1,0:T(8,128)(2,1)} %add_convert_fusion, bf16[512,1024]{1,0:T(8,128)(2,1)S(1)} %copy-done.22, s32[]{:T(128)S(6)} %select_n.193), kind=kOutput, calls=%fused_computation.116 | convolution fusion | flops 1611399168 | bytes 8388612 | tf_op jit(solution)/shard_map/wte,ed->wtd/dot_general | solution.py:44
  207.1 2.6 fusion.101
  211.2 4.1 fusion.100
  215.2 2.5 concatenate.104
  218.8 6.0 %fusion.99 = bf16[512,1024]{1,0:T(8,128)(2,1)} fusion(bf16[512,1024]{1,0:T(8,128)(2,1)} %broadcast.229.clone, s32[]{:T(128)S(6)} %select_n.186, bf16[32,96,256]{2,1,0:T(8,128)(2,1)} %copy-done.16, bf16[32,96,1024]{2,1,0:T(8,128)(2,1)} %get-tuple-element.44), kind=kOutput, calls=%fused_computation.140 | convolution fusion | flops 1610612736 | bytes 8912900 | tf_op jit(solution)/shard_map/wtd,wtf->df/dot_general | solution.py:44
  224.8 4.0 fusion.98
  233.3 4.5 all-to-all-start.4
  237.7 3.5 collective-permute-done.4
  241.3 6.7 %multiply_convert_fusion.1 = (bf16[32,96,256]{2,1,0:T(8,128)(2,1)S(1)}, bf16[32,96,256]{2,1,0:T(8,128)(2,1)S(1)}, bf16[32,96,256]{2,1,0:T(8,128)(2,1)S(1)}, f32[32,96,256]{2,1,0:T(8,128)S(1)}) fusion(f32[32,96]{1,0:T(8,128)S(1)} %get-tuple-element.76, f32[32,96,256]{2,1,0:T(8,128)} %get-tuple-element.89, bf16[32,96,256]{2,1,0:T(8,128)(2,1)} %collective-permute-done.4, ...), kind=kOutput, calls=%fused_computation.73 | convolution fusion | flops 1619263488 | bytes 19415044 | tf_op jit(solution)/shard_map/wte,ed->wtd/dot_general | solution.py:44
  248.0 3.8 fusion.253
  252.7 4.4 pad_maximum_fusion
  257.0 6.4 %all-to-all-done.4 = bf16[4,2048,128]{2,1,0:T(8,128)(2,1)} async-done(((bf16[4,2048,128]{2,1,0:T(8,128)(2,1)}), bf16[4,2048,128]{2,1,0:T(8,128)(2,1)}, u32[]{:S(2)}, u32[]{:S(2)}) %all-to-all-start.4) | async-done | bytes 2097184 | tf_op jit(solution)/shard_map/all_to_all | solution.py:326
  263.5 2.9 reduce_sum.67
  266.4 2.2 fusion.114
  268.6 2.1 fusion.151
  270.7 14.6 %collective-permute-done.5 = bf16[32,96,256]{2,1,0:T(8,128)(2,1)} collective-permute-done((bf16[32,96,256]{2,1,0:T(8,128)(2,1)}, bf16[32,96,256]{2,1,0:T(8,128)(2,1)}, u32[]{:S(2)}, u32[]{:S(2)}) %collective-permute-start.5) | collective-permute-done | bytes 1572896 | tf_op jit(solution)/shard_map/ppermute | solution.py:139
  285.3 3.2 add_convert_fusion.3
  288.5 3.3 copy.142
  291.8 2.2 bitcast_negate_fusion
  294.0 2.2 fusion.78
  296.2 3.4 maximum_bitcast_fusion.2
  299.6 7.9 %fusion.92 = bf16[32,4,48,128]{3,0,2,1:T(8,128)(2,1)} fusion(bf16[32,4,48,128]{3,2,0,1:T(8,128)(2,1)} %get-tuple-element.67, bf16[4,48,64,64]{3,2,1,0:T(8,128)(2,1)} %get-tuple-element.65, bf16[4,48,64,64]{3,2,1,0:T(8,128)(2,1)} %get-tuple-element.64, bf16[4,48,64,128]{3,2,1,0:T(8,128)(2,1)S(1)} %bitcast.251), kind=kOutput, calls=%fused_computation.135 | convolution fusion | flops 220987392 | bytes 9437184 | tf_op jit(solution)/shard_map/whmo,hmio->whmi/dot_general | solution.py:44
  307.6 2.7 fusion.249
  315.4 2.3 convolution_bitcast_fusion.6
  318.8 3.4 all-to-all-start
  322.2 5.0 %pad_maximum_fusion.1 = bf16[32,4,48,2,128]{4,2,0,1,3:T(8,128)(2,1)} fusion(bf16[32,4,48,1,128]{4,2,0,1,3:T(8,128)(2,1)} %get-tuple-element.66, bf16[32,4,48,1,64]{4,2,0,1,3:T(8,128)(2,1)} %bitcast.271, bf16[32,4,48,1,64]{4,2,0,1,3:T(8,128)(2,1)} %bitcast.269), kind=kLoop, calls=%fused_computation.53 | loop fusion | flops 9437184 | bytes 6291456 | tf_op jit(solution)/shard_map/stack | solution.py:279
  328.2 4.9 %all-to-all-start.5 = ((bf16[4,512,128]{2,1,0:T(8,128)(2,1)}), bf16[4,512,128]{2,1,0:T(8,128)(2,1)S(1)}, u32[]{:S(2)}, u32[]{:S(2)}) async-start(bf16[4,512,128]{2,1,0:T(8,128)(2,1)} %bitcast.78), calls=%async_computation.5 | async-start | bytes 1048576 | tf_op jit(solution)/shard_map/all_to_all | solution.py:331
  333.0 4.4 bitcast_convert_fusion
  340.0 2.2 fusion.113
  343.0 4.2 all-to-all-done.5
  347.2 3.3 all-to-all-start.1
  350.5 2.2 maximum_bitcast_fusion
  356.2 4.9 %all-to-all-start.2 = ((bf16[4,3328,128]{2,1,0:T(8,128)(2,1)}), bf16[4,3328,128]{2,1,0:T(8,128)(2,1)}, u32[]{:S(2)}, u32[]{:S(2)}) async-start(bf16[4,3328,128]{2,1,0:T(8,128)(2,1)} %bitcast.272), calls=%async_computation.2 | async-start | bytes 6815744 | tf_op jit(solution)/shard_map/all_to_all | solution.py:326
  361.1 2.0 constant_dynamic-slice_fusion
  365.5 5.8 %convolution_convert_fusion.4 = bf16[32,96,256]{2,1,0:T(8,128)(2,1)} fusion(bf16[32,96,1024]{2,1,0:T(8,128)(2,1)} %get-tuple-element.44, bf16[1024,512]{1,0:T(8,128)(2,1)S(1)} %copy-done.20, s32[]{:T(128)S(6)} %select_n.193), kind=kOutput, calls=%fused_computation.117 | convolution fusion | flops 1611399168 | bytes 8388612 | tf_op jit(solution)/shard_map/wte,ed->wtd/dot_general | solution.py:44
  377.5 2.5 fusion.158
  381.7 26.8 %collective-permute-done.6 = bf16[32,96,256]{2,1,0:T(8,128)(2,1)} collective-permute-done((bf16[32,96,256]{2,1,0:T(8,128)(2,1)}, bf16[32,96,256]{2,1,0:T(8,128)(2,1)}, u32[]{:S(2)}, u32[]{:S(2)}) %collective-permute-start.6) | collective-permute-done | bytes 1572896 | tf_op jit(solution)/shard_map/ppermute | solution.py:139
  409.0 3.6 reduce_sum.65
  412.6 4.5 all-to-all-start.3
  417.1 6.7 %fusion.247 = (bf16[32,96,256]{2,1,0:T(8,128)(2,1)S(1)}, bf16[32,96,256]{2,1,0:T(8,128)(2,1)S(1)}, bf16[32,96,256]{2,1,0:T(8,128)(2,1)S(1)}, f32[32,96,256]{2,1,0:T(8,128)S(1)}) fusion(bf16[32,96,256]{2,1,0:T(8,128)(2,1)} %collective-permute-done.6, bf16[32,96,1024]{2,1,0:T(8,128)(2,1)} %get-tuple-element.44, bf16[1024,512]{1,0:T(8,128)(2,1)} %copy-done.19, ...), kind=kOutput, calls=%fused_computation.307 | convolution fusion | flops 1620049920 | bytes 22556676 | tf_op jit(solution)/shard_map/wte,ed->wtd/dot_general | solution.py:44
  423.8 3.4 multiply_subtract_fusion
  427.2 17.4 %collective-permute-done.7 = bf16[32,96,256]{2,1,0:T(8,128)(2,1)} collective-permute-done((bf16[32,96,256]{2,1,0:T(8,128)(2,1)}, bf16[32,96,256]{2,1,0:T(8,128)(2,1)}, u32[]{:S(2)}, u32[]{:S(2)}) %collective-permute-start.7) | collective-permute-done | bytes 1572896 | tf_op jit(solution)/shard_map/ppermute | solution.py:139
  444.7 4.1 add_add_fusion
  450.2 2.1 multiply_add_fusion
  (185 shorter events, 53.2 us)
Async XLA Ops:
  0.7 6.4 %copy-start.40 = (f32[512,256]{1,0:T(8,128)S(1)}, f32[512,256]{1,0:T(8,128)}, u32[]{:S(2)}) copy-start(f32[512,256]{1,0:T(8,128)} %param.33) | copy-start | bytes 1572868
  4.0 37.7 %collective-permute-start = (bf16[32,96,256]{2,1,0:T(8,128)(2,1)}, bf16[32,96,256]{2,1,0:T(8,128)(2,1)}, u32[]{:S(2)}, u32[]{:S(2)}) collective-permute-start(bf16[32,96,256]{2,1,0:T(8,128)(2,1)} %convert_element_type.243), channel_id=1, source_target_pairs={{0,1},{1,0},{2,3},{3,2},{4,5},{5,4},{6,7},{7,6},{8,9},{9,8},{10,11... | collective-permute-start | bytes 4718600 | tf_op jit(solution)/shard_map/ppermute | solution.py:139
  7.7 3.3 copy-start.35
  7.7 3.3 copy-start.43
  11.0 45.5 %copy-start.1 = (bf16[4,3072,128]{2,1,0:T(8,128)(2,1)}, bf16[4,3072,128]{2,1,0:T(8,128)(2,1)S(1)}, u32[]{:S(2)}) copy-start(bf16[4,3072,128]{2,1,0:T(8,128)(2,1)S(1)} %convert_element_type.241) | copy-start | bytes 9437188
  14.2 27.5 %copy-start.29 = (bf16[512,256]{1,0:T(8,128)(2,1)S(1)}, bf16[512,256]{1,0:T(8,128)(2,1)}, u32[]{:S(2)}) copy-start(bf16[512,256]{1,0:T(8,128)(2,1)} %convert_element_type.242) | copy-start | bytes 786436
  49.2 4.0 copy-start.3
  53.1 3.1 copy-start.7
  53.2 3.4 copy-start.27
  64.6 3.0 copy-start.52
  64.6 3.0 copy-start.53
  64.6 3.0 copy-start.54
  64.6 3.0 copy-start.55
  64.6 3.0 copy-start.56
  64.9 36.5 %copy-start.4 = (bf16[32,96,4,64]{1,3,2,0:T(8,128)(2,1)}, bf16[32,96,4,64]{1,3,2,0:T(8,128)(2,1)S(1)}, u32[]{:S(2)}) copy-start(bf16[32,96,4,64]{1,3,2,0:T(8,128)(2,1)S(1)} %copy.137) | copy-start | bytes 4718596
  64.9 7.4 %copy-start.24 = (f32[32,96,256]{2,1,0:T(8,128)S(1)}, f32[32,96,256]{2,1,0:T(8,128)}, u32[]{:S(2)}) copy-start(f32[32,96,256]{2,1,0:T(8,128)} %param.30) | copy-start | bytes 9437188
  65.7 35.6 %collective-permute-start.1 = (bf16[32,96,256]{2,1,0:T(8,128)(2,1)S(1)}, bf16[32,96,256]{2,1,0:T(8,128)(2,1)S(1)}, u32[]{:S(2)}, u32[]{:S(2)}) collective-permute-start(bf16[32,96,256]{2,1,0:T(8,128)(2,1)S(1)} %convolution_convert_fusion.5), channel_id=1, source_target_pairs={{0,1},{1,0},{2,3},{3,2},{4,5},{5,4},{6,7},{7,6},{8,9},{9,8},{10,11... | collective-permute-start | bytes 4718600 | tf_op jit(solution)/shard_map/ppermute | solution.py:139
  67.6 5.5 %copy-start.45 = (f32[32,96]{1,0:T(8,128)}, f32[32,96]{1,0:T(8,128)S(1)}, u32[]{:S(2)}) copy-start(f32[32,96]{1,0:T(8,128)S(1)} %get-tuple-element.38) | copy-start | bytes 36868
  72.2 30.2 %copy-start.38 = (bf16[32,96,96]{2,1,0:T(8,128)(2,1)}, bf16[32,96,96]{2,1,0:T(8,128)(2,1)S(1)}, u32[]{:S(2)}) copy-start(bf16[32,96,96]{2,1,0:T(8,128)(2,1)S(1)} %get-tuple-element.75) | copy-start | bytes 1769476
  72.2 35.6 %copy-start.36 = (bf16[32,96,96]{2,1,0:T(8,128)(2,1)}, bf16[32,96,96]{2,1,0:T(8,128)(2,1)S(1)}, u32[]{:S(2)}) copy-start(bf16[32,96,96]{2,1,0:T(8,128)(2,1)S(1)} %get-tuple-element.74) | copy-start | bytes 1769476
  72.3 29.1 %copy-start.11 = (f32[32,96,256]{2,1,0:T(8,128)S(1)}, f32[32,96,256]{2,1,0:T(8,128)}, u32[]{:S(2)}) copy-start(f32[32,96,256]{2,1,0:T(8,128)} %param.29) | copy-start | bytes 9437188
  102.5 3.9 copy-start.14
  106.3 13.1 %copy-start.17 = (bf16[32,96,256]{2,1,0:T(8,128)(2,1)}, bf16[32,96,256]{2,1,0:T(8,128)(2,1)S(1)}, u32[]{:S(2)}) copy-start(bf16[32,96,256]{2,1,0:T(8,128)(2,1)S(1)} %get-tuple-element.85) | copy-start | bytes 4718596
  106.3 37.4 %collective-permute-start.2 = (bf16[32,96,256]{2,1,0:T(8,128)(2,1)S(1)}, bf16[32,96,256]{2,1,0:T(8,128)(2,1)}, u32[]{:S(2)}, u32[]{:S(2)}) collective-permute-start(bf16[32,96,256]{2,1,0:T(8,128)(2,1)S(1)} %get-tuple-element.85), channel_id=1, source_target_pairs={{0,1},{1,0},{2,3},{3,2},{4,5},{5,4},{6,7},{7,6},{8,9},{9,8},{10,11... | collective-permute-start | bytes 4718600 | tf_op jit(solution)/shard_map/ppermute | solution.py:139
  107.8 3.4 copy-start.28
  110.7 70.6 %collective-permute-start.3 = (bf16[32,96,256]{2,1,0:T(8,128)(2,1)S(1)}, bf16[32,96,256]{2,1,0:T(8,128)(2,1)}, u32[]{:S(2)}, u32[]{:S(2)}) collective-permute-start(bf16[32,96,256]{2,1,0:T(8,128)(2,1)S(1)} %get-tuple-element.88), channel_id=1, source_target_pairs={{0,1},{1,0},{2,3},{3,2},{4,5},{5,4},{6,7},{7,6},{8,9},{9,8},{10,11... | collective-permute-start | bytes 4718600 | tf_op jit(solution)/shard_map/ppermute | solution.py:139
  112.8 6.6 %copy-start.21 = (bf16[512,1024]{1,0:T(8,128)(2,1)}, bf16[512,1024]{1,0:T(8,128)(2,1)S(1)}, u32[]{:S(2)}) copy-start(bf16[512,1024]{1,0:T(8,128)(2,1)S(1)} %convert_element_type.267) | copy-start | bytes 3145732
  113.0 6.4 %copy-start.19 = (bf16[1024,512]{1,0:T(8,128)(2,1)}, bf16[1024,512]{1,0:T(8,128)(2,1)S(1)}, u32[]{:S(2)}) copy-start(bf16[1024,512]{1,0:T(8,128)(2,1)S(1)} %convert_element_type.269) | copy-start | bytes 3145732
  151.0 30.3 %copy-start.12 = (f32[32,96,1024]{2,1,0:T(8,128)}, f32[32,96,1024]{2,1,0:T(8,128)S(1)}, u32[]{:S(2)}) copy-start(f32[32,96,1024]{2,1,0:T(8,128)S(1)} %get-tuple-element.87) | copy-start | bytes 37748740
  181.3 18.7 %copy-start.22 = (bf16[512,1024]{1,0:T(8,128)(2,1)S(1)}, bf16[512,1024]{1,0:T(8,128)(2,1)}, u32[]{:S(2)}) copy-start(bf16[512,1024]{1,0:T(8,128)(2,1)} %copy-done.21) | copy-start | bytes 3145732
  200.0 7.1 %copy-start = (bf16[32,96,1024]{2,1,0:T(8,128)(2,1)S(1)}, bf16[32,96,1024]{2,1,0:T(8,128)(2,1)}, u32[]{:S(2)}) copy-start(bf16[32,96,1024]{2,1,0:T(8,128)(2,1)} %add_convert_fusion) | copy-start | bytes 18874372
  200.0 7.1 %copy-start.18 = (bf16[32,96,256]{2,1,0:T(8,128)(2,1)S(1)}, bf16[32,96,256]{2,1,0:T(8,128)(2,1)}, u32[]{:S(2)}) copy-start(bf16[32,96,256]{2,1,0:T(8,128)(2,1)} %copy-done.17) | copy-start | bytes 4718596
  209.7 31.6 %collective-permute-start.4 = (bf16[32,96,256]{2,1,0:T(8,128)(2,1)}, bf16[32,96,256]{2,1,0:T(8,128)(2,1)}, u32[]{:S(2)}, u32[]{:S(2)}) collective-permute-start(bf16[32,96,256]{2,1,0:T(8,128)(2,1)} %convolution_convert_fusion.3), channel_id=1, source_target_pairs={{0,1},{1,0},{2,3},{3,2},{4,5},{5,4},{6,7},{7,6},{8,9},{9,8},{10,11... | collective-permute-start | bytes 4718600 | tf_op jit(solution)/shard_map/ppermute | solution.py:139
  215.2 9.6 %slice-start = ((s8[6291456]{0:T(1024)(128)(4,1)}), s8[2097152]{0:T(1024)(128)(4,1)S(1)}, s32[]{:S(2)}) async-start(s8[6291456]{0:T(1024)(128)(4,1)} %bitcast.247), calls=%async_computation.6 | async-start | bytes 4194304
  218.8 6.0 %slice-start.1 = ((s8[6291456]{0:T(1024)(128)(4,1)}), s8[4194304]{0:T(1024)(128)(4,1)S(1)}, s32[]{:S(2)}) async-start(s8[6291456]{0:T(1024)(128)(4,1)} %bitcast.247), calls=%async_computation.7 | async-start | bytes 8388608
  233.3 30.2 %all-to-all-start.4 = ((bf16[4,2048,128]{2,1,0:T(8,128)(2,1)}), bf16[4,2048,128]{2,1,0:T(8,128)(2,1)}, u32[]{:S(2)}, u32[]{:S(2)}) async-start(bf16[4,2048,128]{2,1,0:T(8,128)(2,1)} %bitcast.77), calls=%async_computation.4 | async-start | bytes 4194304 | tf_op jit(solution)/shard_map/all_to_all | solution.py:326
  241.3 6.7 %copy-start.39 = (bf16[32,96,96]{2,1,0:T(8,128)(2,1)S(1)}, bf16[32,96,96]{2,1,0:T(8,128)(2,1)}, u32[]{:S(2)}) copy-start(bf16[32,96,96]{2,1,0:T(8,128)(2,1)} %copy-done.38) | copy-start | bytes 1769476
  251.8 33.5 %collective-permute-start.5 = (bf16[32,96,256]{2,1,0:T(8,128)(2,1)}, bf16[32,96,256]{2,1,0:T(8,128)(2,1)}, u32[]{:S(2)}, u32[]{:S(2)}) collective-permute-start(bf16[32,96,256]{2,1,0:T(8,128)(2,1)} %get-tuple-element.91), channel_id=1, source_target_pairs={{0,1},{1,0},{2,3},{3,2},{4,5},{5,4},{6,7},{7,6},{8,9},{9,8},{10,11... | collective-permute-start | bytes 4718600 | tf_op jit(solution)/shard_map/ppermute | solution.py:139
  252.7 13.7 %copy-start.5 = (bf16[32,96,4,64]{1,3,2,0:T(8,128)(2,1)S(1)}, bf16[32,96,4,64]{1,3,2,0:T(8,128)(2,1)}, u32[]{:S(2)}) copy-start(bf16[32,96,4,64]{1,3,2,0:T(8,128)(2,1)} %copy-done.4) | copy-start | bytes 4718596
  268.6 19.9 %copy-start.33 = (bf16[512,256]{1,0:T(8,128)(2,1)}, bf16[512,256]{1,0:T(8,128)(2,1)S(1)}, u32[]{:S(2)}) copy-start(bf16[512,256]{1,0:T(8,128)(2,1)S(1)} %fusion.114) | copy-start | bytes 786436
  294.0 5.6 %copy-start.9 = (bf16[4,32,64,48]{2,3,1,0:T(8,128)(2,1)}, bf16[4,32,64,48]{2,3,1,0:T(8,128)(2,1)S(1)}, u32[]{:S(2)}) copy-start(bf16[4,32,64,48]{2,3,1,0:T(8,128)(2,1)S(1)} %get-tuple-element.95) | copy-start | bytes 2359300
  296.2 3.5 copy-start.10
  296.2 3.4 copy-start.2
  318.8 9.4 %all-to-all-start = ((bf16[4,256,128]{2,1,0:T(8,128)(2,1)}), bf16[4,256,128]{2,1,0:T(8,128)(2,1)S(1)}, u32[]{:S(2)}, u32[]{:S(2)}) async-start(bf16[4,256,128]{2,1,0:T(8,128)(2,1)} %bitcast.53), calls=%async_computation | async-start | bytes 524288 | tf_op jit(solution)/shard_map/all_to_all | solution.py:326
  328.2 19.1 %all-to-all-start.5 = ((bf16[4,512,128]{2,1,0:T(8,128)(2,1)}), bf16[4,512,128]{2,1,0:T(8,128)(2,1)S(1)}, u32[]{:S(2)}, u32[]{:S(2)}) async-start(bf16[4,512,128]{2,1,0:T(8,128)(2,1)} %bitcast.78), calls=%async_computation.5 | async-start | bytes 1048576 | tf_op jit(solution)/shard_map/all_to_all | solution.py:331
  347.2 5.5 %copy-start.31 = (bf16[4,512,128]{2,1,0:T(8,128)(2,1)}, bf16[4,512,128]{2,1,0:T(8,128)(2,1)S(1)}, u32[]{:S(2)}) copy-start(bf16[4,512,128]{2,1,0:T(8,128)(2,1)S(1)} %all-to-all-done.5) | copy-start | bytes 1572868
  347.2 9.0 %all-to-all-start.1 = ((bf16[4,64,128]{2,1,0:T(8,128)(2,1)}), bf16[4,64,128]{2,1,0:T(8,128)(2,1)S(1)}, u32[]{:S(2)}, u32[]{:S(2)}) async-start(bf16[4,64,128]{2,1,0:T(8,128)(2,1)} %bitcast.54), calls=%async_computation.1 | async-start | bytes 131072 | tf_op jit(solution)/shard_map/all_to_all | solution.py:331
  356.2 9.2 %copy-start.20 = (bf16[1024,512]{1,0:T(8,128)(2,1)S(1)}, bf16[1024,512]{1,0:T(8,128)(2,1)}, u32[]{:S(2)}) copy-start(bf16[1024,512]{1,0:T(8,128)(2,1)} %copy-done.19) | copy-start | bytes 3145732
  356.2 52.8 %all-to-all-start.2 = ((bf16[4,3328,128]{2,1,0:T(8,128)(2,1)}), bf16[4,3328,128]{2,1,0:T(8,128)(2,1)}, u32[]{:S(2)}, u32[]{:S(2)}) async-start(bf16[4,3328,128]{2,1,0:T(8,128)(2,1)} %bitcast.272), calls=%async_computation.2 | async-start | bytes 6815744 | tf_op jit(solution)/shard_map/all_to_all | solution.py:326
  365.4 5.8 %copy-start.32 = (bf16[4,512,128]{2,1,0:T(8,128)(2,1)S(1)}, bf16[4,512,128]{2,1,0:T(8,128)(2,1)}, u32[]{:S(2)}) copy-start(bf16[4,512,128]{2,1,0:T(8,128)(2,1)} %copy-done.31) | copy-start | bytes 1572868
  365.4 6.6 %copy-start.44 = (f32[32,1024]{1,0:T(8,128)S(1)}, f32[32,1024]{1,0:T(8,128)}, u32[]{:S(2)}) copy-start(f32[32,1024]{1,0:T(8,128)} %param.45) | copy-start | bytes 393220
  371.3 4.3 copy-start.30
  371.3 37.1 %collective-permute-start.6 = (bf16[32,96,256]{2,1,0:T(8,128)(2,1)}, bf16[32,96,256]{2,1,0:T(8,128)(2,1)}, u32[]{:S(2)}, u32[]{:S(2)}) collective-permute-start(bf16[32,96,256]{2,1,0:T(8,128)(2,1)} %convolution_convert_fusion.4), channel_id=1, source_target_pairs={{0,1},{1,0},{2,3},{3,2},{4,5},{5,4},{6,7},{7,6},{8,9},{9,8},{10,11... | collective-permute-start | bytes 4718600 | tf_op jit(solution)/shard_map/ppermute | solution.py:139
  380.1 37.0 %copy-start.15 = (f32[32,96,256]{2,1,0:T(8,128)S(1)}, f32[32,96,256]{2,1,0:T(8,128)}, u32[]{:S(2)}) copy-start(f32[32,96,256]{2,1,0:T(8,128)} %copy-done.14) | copy-start | bytes 9437188
  408.5 36.2 %collective-permute-start.7 = (bf16[32,96,256]{2,1,0:T(8,128)(2,1)}, bf16[32,96,256]{2,1,0:T(8,128)(2,1)}, u32[]{:S(2)}, u32[]{:S(2)}) collective-permute-start(bf16[32,96,256]{2,1,0:T(8,128)(2,1)} %convolution_convert_fusion.1), channel_id=1, source_target_pairs={{0,1},{1,0},{2,3},{3,2},{4,5},{5,4},{6,7},{7,6},{8,9},{9,8},{10,11... | collective-permute-start | bytes 4718600 | tf_op jit(solution)/shard_map/ppermute | solution.py:139
  412.6 36.2 %all-to-all-start.3 = ((bf16[4,832,128]{2,1,0:T(8,128)(2,1)}), bf16[4,832,128]{2,1,0:T(8,128)(2,1)}, u32[]{:S(2)}, u32[]{:S(2)}) async-start(bf16[4,832,128]{2,1,0:T(8,128)(2,1)} %bitcast.274), calls=%async_computation.3 | async-start | bytes 1703936 | tf_op jit(solution)/shard_map/all_to_all | solution.py:331
  417.1 6.7 %copy-start.37 = (bf16[32,96,96]{2,1,0:T(8,128)(2,1)S(1)}, bf16[32,96,96]{2,1,0:T(8,128)(2,1)}, u32[]{:S(2)}) copy-start(bf16[32,96,96]{2,1,0:T(8,128)(2,1)} %copy-done.36) | copy-start | bytes 1769476
  417.1 6.7 %copy-start.46 = (f32[32,96]{1,0:T(8,128)S(1)}, f32[32,96]{1,0:T(8,128)}, u32[]{:S(2)}) copy-start(f32[32,96]{1,0:T(8,128)} %copy-done.45) | copy-start | bytes 36868
  423.8 20.9 %copy-start.13 = (f32[32,96,256]{2,1,0:T(8,128)S(1)}, f32[32,96,256]{2,1,0:T(8,128)}, u32[]{:S(2)}) copy-start(f32[32,96,256]{2,1,0:T(8,128)} %fusion.158) | copy-start | bytes 9437188
  423.8 20.9 %copy-start.25 = (f32[32,96,256]{2,1,0:T(8,128)S(1)}, f32[32,96,256]{2,1,0:T(8,128)}, u32[]{:S(2)}) copy-start(f32[32,96,256]{2,1,0:T(8,128)} %get-tuple-element.92) | copy-start | bytes 9437188
  444.7 5.5 %copy-start.41 = (f32[4,192,128]{2,1,0:T(8,128)S(1)}, f32[4,192,128]{2,1,0:T(8,128)}, u32[]{:S(2)}) copy-start(f32[4,192,128]{2,1,0:T(8,128)} %param.41) | copy-start | bytes 1179652
  444.7 5.5 %copy-start.42 = (f32[4,192,128]{2,1,0:T(8,128)S(1)}, f32[4,192,128]{2,1,0:T(8,128)}, u32[]{:S(2)}) copy-start(f32[4,192,128]{2,1,0:T(8,128)} %param.40) | copy-start | bytes 1179652
  448.8 3.5 copy-start.49
  448.8 3.5 copy-start.50
  (9 other events, 21.2 us)

commit v8 on v5

--- a/solution.py
+++ b/solution.py
@@ -282,7 +282,7 @@
         mixer_full = product("whmci,whmco->hmio", spectrum_parts, paired).reshape(
             head_count, mode_count * head_size, 2 * head_size
         )
-        return output, input_grad, (query_grad, mixer_full, output_grad_t, inner_grad, outer_grad_t)
+        return output, input_grad, (query_grad, mixer_full, output_grad_t, inner_grad, outer_grad_t), (spectrum, grad_mixed)
 
     chunks = 1
     span = windows // chunks
@@ -315,20 +315,6 @@
         owned_shape = shape[:axis_number] + (shape[axis_number] // dp_count,) + shape[axis_number + 1 :]
         return jnp.moveaxis(grad.reshape(split), axis_number, 0).reshape(dp_count, -1, lanes), owned_shape
 
-    def reduced_over_dp(grads_axes):
-        laid = [lead(grad, axis_number) for grad, axis_number in grads_axes]
-        joined = jnp.concatenate([flat for flat, _ in laid], axis=1)
-        reduced = lax.psum_scatter(
-            joined.reshape(-1, lanes), "dp", scatter_dimension=0, tiled=True
-        )
-        parts = []
-        offset = 0
-        for flat, owned_shape in laid:
-            rows = flat.shape[1]
-            parts.append(reduced[offset : offset + rows].reshape(owned_shape))
-            offset += rows
-        return parts
-
     def summed_over_dp(grads_axes):
         laid = [lead(grad, axis_number) for grad, axis_number in grads_axes]
         joined = jnp.concatenate([flat for flat, _ in laid], axis=1)
@@ -345,8 +331,36 @@
             offset += size
         return parts
 
-    inner_part, outer_part_t = reduced_over_dp([(inner_grad, 0), (outer_grad_t, 0)])
-    mixer_part, output_part_t = summed_over_dp([(mixer_full, 1), (output_grad_t, 0)])
+    inner_part, outer_part_t = summed_over_dp([(inner_grad, 0), (outer_grad_t, 0)])
+    if mode_count % dp_count == 0:
+        per = mode_count // dp_count
+        spectra = jnp.concatenate([r[3][0] for r in results], axis=0)
+        mixed_grads = jnp.concatenate([r[3][1] for r in results], axis=0)
+        all_windows = spectra.shape[0]
+
+        def by_owner(values):
+            split = values.reshape(all_windows, head_count, dp_count, per, 2 * head_size)
+            return jnp.moveaxis(split, 2, 0).reshape(dp_count, -1, lanes)
+
+        spectra_in = lax.all_to_all(by_owner(spectra).reshape(-1, lanes), "dp", 0, 0, tiled=True)
+        gm_flat = by_owner(mixed_grads)
+        gm_rows = gm_flat.shape[1]
+        out_flat, out_shape = lead(output_grad_t, 0)
+        joined = jnp.concatenate([gm_flat, out_flat.astype(jnp.bfloat16)], axis=1)
+        arrived = lax.all_to_all(joined.reshape(-1, lanes), "dp", 0, 0, tiled=True)
+        arrived = arrived.reshape(dp_count, -1, lanes)
+        output_part_t = jnp.sum(arrived[:, gm_rows:].astype(jnp.float32), axis=0).reshape(out_shape)
+        owned = (dp_count, all_windows, head_count, per)
+        spectrum_in = spectra_in.reshape(owned + (2, head_size))
+        gm_in = arrived[:, :gm_rows].reshape(owned + (2 * head_size,))
+        gm_pairs = jnp.stack(
+            [gm_in, jnp.concatenate([gm_in[..., head_size:], -gm_in[..., :head_size]], axis=-1)], axis=4
+        )
+        mixer_part = product("swhmci,swhmco->hmio", spectrum_in, gm_pairs).reshape(
+            head_count, per * head_size, 2 * head_size
+        )
+    else:
+        mixer_part, output_part_t = summed_over_dp([(mixer_full, 1), (output_grad_t, 0)])
     (query_part,) = summed_over_dp([(query_grad, 0)])
     output_part = jnp.transpose(output_part_t)
     outer_part = jnp.transpose(outer_part_t)

time: 451 us -> 463 us (1.027)
  starting transfers between devices: 21.6 us -> 40.8 us
  local copies, waits for them, and re-layouts: 41.9 us -> 56.3 us
  between operations: 15.1 us -> 2.01 us
  other arithmetic: 83.2 us -> 74.2 us
  matrix products: 149 us -> 144 us
  waiting for transfers between devices: 136 us -> 141 us
    all_to_all x0 -> x2, starting transfers between devices: none -> 17.6 us  [the longest x1 11.5 us: on_device(): arrived = lax.all_to_all(joined.reshape(-1, lanes), 'dp', 0, 0, tiled=True)]
    reshape x2, local copies, waits for them, and re-layouts: 0.96 us -> 6.48 us  [the longest x1 6.47 us: on_device(): spectrum_in = spectra_in.reshape(owned + (2, head_size))]
    dot_general x35, matrix products: 132 us -> 126 us  [product(): return jnp.einsum(form, left, right, preferred_element_type=jnp.float32)]
    unnamed x120 -> x138, local copies, waits for them, and re-layouts: 10.1 us -> 15.3 us
  transfers between devices with their start and end apart: 11 -> 12, of which waited for: 8 -> 8; matrix products, arithmetic and copies ran while one was open for 44% -> 43% of each run, Pallas kernels for 0% -> 0%
where the time goes in v8:
time: 463 us; the launch traced here: 459 us
  matrix products  144 us (31%)
  waiting for transfers between devices  141 us (30%)
  other arithmetic  74.2 us (16%)
  local copies, waits for them, and re-layouts  56.3 us (12%)
  starting transfers between devices  40.8 us (9%)
    ppermute x8, waiting for transfers between devices, swap(): return lax.ppermute(values, 'head', pairs)  136 us
    dot_general x35, matrix products, product(): return jnp.einsum(form, left, right, preferred_element_type=jnp.float32)  126 us
    convert_element_type x1, other arithmetic, chunk_pass(): hidden = activated.astype(jnp.bfloat16)  30.3 us
    unnamed x138, local copies, waits for them, and re-layouts  15.3 us
    ppermute x8, starting transfers between devices, swap(): return lax.ppermute(values, 'head', pairs)  12.1 us
    all_to_all x1, starting transfers between devices, on_device(): arrived = lax.all_to_all(joined.reshape(-1, lanes), 'dp', 0, 0, tiled=True)  11.5 us
    all_to_all x2, starting transfers between devices, summed_over_dp(): lax.all_to_all(joined.astype(jnp.bfloat16).reshape(-1, lanes), 'dp', 0, 0...  11.1 us
    dot_general x2, matrix products, trend_back(): jnp.einsum('wts,wtd->wsd', tiled, parts, preferred_element_type=jnp.float32)  10.6 us
  transfers between devices with their start and end apart: 12, of which 8 were waited for; matrix products, arithmetic and copies ran while one was open for 43% of the time, Pallas kernels for 0%

profile of v8, /device:TPU:0, one launch (start us, length us, event | category | flops | bytes accessed | tf_op | source)
XLA Modules:
  0.0 459.0 jit_solution(14428106325982207204)
XLA Ops:
  0.7 3.4 convert_element_type.215
  4.0 3.0 collective-permute-start
  7.8 3.2 convert_element_type.213
  11.1 2.1 fusion.172
  13.2 4.0 slice_negate_fusion
  17.2 24.5 %collective-permute-done = bf16[32,96,256]{2,1,0:T(8,128)(2,1)} collective-permute-done((bf16[32,96,256]{2,1,0:T(8,128)(2,1)}, bf16[32,96,256]{2,1,0:T(8,128)(2,1)}, u32[]{:S(2)}, u32[]{:S(2)}) %collective-permute-start) | collective-permute-done | bytes 1572896 | tf_op jit(solution)/shard_map/ppermute | solution.py:139
  41.7 3.2 fusion.89
  44.9 4.1 copy.102
  49.0 3.9 fusion.102
  53.0 2.2 fusion.105
  57.7 3.1 fusion.93
  65.6 1.8 collective-permute-start.1
  67.5 6.7 %select_convert_fusion = (bf16[32,96,96]{2,1,0:T(8,128)(2,1)}, bf16[32,96,96]{2,1,0:T(8,128)(2,1)S(1)}) fusion(bf16[96,96]{1,0:T(8,128)(2,1)S(1)} %copy-done.56, bf16[96,96]{1,0:T(8,128)(2,1)S(1)} %copy-done.57, bf16[96,96]{1,0:T(8,128)(2,1)S(1)} %copy-done.58, bf16[96,96]{1,0:T(8,128)(2,1)S(1)} %copy-done.59, bf16[96,96]{1,0:T(8,128)(2,1)S(1)} %copy-done.60, ...), kind=kLoop, calls=%fused_computation.134 | loop fusion | flops 2949120 | bytes 1302528 | tf_op jit(solution)/shard_map/convert_element_type | solution.py:66
  74.9 26.3 %collective-permute-done.1 = bf16[32,96,256]{2,1,0:T(8,128)(2,1)S(1)} collective-permute-done((bf16[32,96,256]{2,1,0:T(8,128)(2,1)S(1)}, bf16[32,96,256]{2,1,0:T(8,128)(2,1)S(1)}, u32[]{:S(2)}, u32[]{:S(2)}) %collective-permute-start.1) | collective-permute-done | bytes 1572896 | tf_op jit(solution)/shard_map/ppermute | solution.py:139
  102.3 3.8 fusion.122
  107.6 4.9 %fusion.267 = (bf16[32,96,256]{2,1,0:T(8,128)(2,1)S(1)}, f32[32,96,256]{2,1,0:T(8,128)}) fusion(f32[32,96,256]{2,1,0:T(8,128)S(1)} %copy-done.32, bf16[32,96,256]{2,1,0:T(8,128)(2,1)S(1)} %get-tuple-element.56, bf16[32,96,256]{2,1,0:T(8,128)(2,1)S(1)} %get-tuple-element.57, bf16[32,96,256]{2,1,0:T(8,128)(2,1)S(1)} %get-tuple-element.55, ...), kind=kOutput, calls=%fused_computation.321 | convolution fusion | flops 474021888 | bytes 13172736 | tf_op jit(solution)/shard_map/wts,wtd->wsd/dot_general | solution.py:89
  114.8 6.4 %fusion.132 = f32[32,96,1024]{2,1,0:T(8,128)} fusion(bf16[32,96,256]{2,1,0:T(8,128)(2,1)S(1)} %get-tuple-element.88, bf16[1024,512]{1,0:T(8,128)(2,1)S(1)} %convert_element_type.241, s32[]{:T(128)S(6)} %select_n.186), kind=kOutput, calls=%fused_computation.163 | convolution fusion | flops 1610612736 | bytes 14680068 | tf_op jit(solution)/shard_map/wtd,fd->wtf/dot_general | solution.py:44
  121.3 1.8 fusion.141
  123.1 20.3 %collective-permute-done.2 = bf16[32,96,256]{2,1,0:T(8,128)(2,1)S(1)} collective-permute-done((bf16[32,96,256]{2,1,0:T(8,128)(2,1)S(1)}, bf16[32,96,256]{2,1,0:T(8,128)(2,1)S(1)}, u32[]{:S(2)}, u32[]{:S(2)}) %collective-permute-start.2) | collective-permute-done | bytes 1572896 | tf_op jit(solution)/shard_map/ppermute | solution.py:139
  143.4 7.9 %convert_reduce_fusion.1 = (u32[96,1024]{1,0:T(8,128)S(1)}, u32[96,1024]{1,0:T(8,128)S(1)}, f32[32,96,1024]{2,1,0:T(8,128)}) fusion(f32[32,96,1024]{2,1,0:T(8,128)S(1)} %fusion.141, bf16[32,96,256]{2,1,0:T(8,128)(2,1)S(1)} %collective-permute-done.2, bf16[512,1024]{1,0:T(8,128)(2,1)S(1)} %convert_element_type.239, s32[]{:T(128)S(6)} %select_n.188), kind=kOutput, calls=%fused_computation.6 | convolution fusion | flops 1648164864 | bytes 28049412 | tf_op jit(solution)/shard_map/wtd,de->wte/dot_general | solution.py:44
  151.3 30.3 %multiply_convert_fusion = (bf16[32,96,1024]{2,1,0:T(8,128)(2,1)}, f32[32,96,1024]{2,1,0:T(8,128)}) fusion(f32[32,96,1024]{2,1,0:T(8,128)} %get-tuple-element.87, u32[96,1024]{1,0:T(8,128)S(1)} %get-tuple-element.22, u32[96,1024]{1,0:T(8,128)S(1)} %get-tuple-element.21), kind=kLoop, calls=%fused_computation.8 | loop fusion | flops 213909504 | bytes 32243712 | tf_op jit(solution)/shard_map/convert_element_type | solution.py:215
  182.8 18.4 %add_convert_fusion = bf16[32,96,1024]{2,1,0:T(8,128)(2,1)} fusion(f32[32,96,1024]{2,1,0:T(8,128)} %get-tuple-element.45, f32[32,96,1024]{2,1,0:T(8,128)} %fusion.132, f32[32,96,1024]{2,1,0:T(8,128)} %get-tuple-element.87, bf16[32,96,256]{2,1,0:T(8,128)(2,1)} %copy-done.19, bf16[1024,512]{1,0:T(8,128)(2,1)} %copy-done.22, s32[]{:T(128)S(6)} %select_n.188), kind=kOutput, calls=%fused_computation.7 | convolution fusion | flops 1657798656 | bytes 46137348 | tf_op jit(solution)/shard_map/wtd,fd->wtf/dot_general | solution.py:44
  201.2 6.0 %convolution_convert_fusion.3 = bf16[32,96,256]{2,1,0:T(8,128)(2,1)} fusion(bf16[32,96,1024]{2,1,0:T(8,128)(2,1)} %add_convert_fusion, bf16[512,1024]{1,0:T(8,128)(2,1)} %copy-done.24, s32[]{:T(128)S(6)} %select_n.193), kind=kOutput, calls=%fused_computation.115 | convolution fusion | flops 1611399168 | bytes 8388612 | tf_op jit(solution)/shard_map/wte,ed->wtd/dot_general | solution.py:44
  212.5 6.2 %all-to-all-start.1 = ((bf16[16,384,128]{2,1,0:T(8,128)(2,1)}), bf16[16,384,128]{2,1,0:T(8,128)(2,1)}, u32[]{:S(2)}, u32[]{:S(2)}) async-start(bf16[16,384,128]{2,1,0:T(8,128)(2,1)} %copy.129), calls=%async_computation.1 | async-start | bytes 3145728 | tf_op jit(solution)/shard_map/all_to_all | solution.py:345
  218.8 5.2 %fusion.111 = bf16[512,1024]{1,0:T(8,128)(2,1)S(1)} fusion(bf16[512,1024]{1,0:T(8,128)(2,1)S(1)} %broadcast.229.clone.1, s32[]{:T(128)S(6)} %select_n.186, bf16[32,96,256]{2,1,0:T(8,128)(2,1)} %copy-done.18, bf16[32,96,1024]{2,1,0:T(8,128)(2,1)} %add_convert_fusion), kind=kOutput, calls=%fused_computation.150 | convolution fusion | flops 1610612736 | bytes 8912900 | tf_op jit(solution)/shard_map/wtd,wtf->df/dot_general | solution.py:44
  224.0 14.7 %collective-permute-done.4 = bf16[32,96,256]{2,1,0:T(8,128)(2,1)} collective-permute-done((bf16[32,96,256]{2,1,0:T(8,128)(2,1)}, bf16[32,96,256]{2,1,0:T(8,128)(2,1)}, u32[]{:S(2)}, u32[]{:S(2)}) %collective-permute-start.4) | collective-permute-done | bytes 1572896 | tf_op jit(solution)/shard_map/ppermute | solution.py:139
  238.8 5.8 %multiply_convert_fusion.1 = (bf16[32,96,256]{2,1,0:T(8,128)(2,1)}, bf16[32,96,256]{2,1,0:T(8,128)(2,1)}, bf16[32,96,256]{2,1,0:T(8,128)(2,1)}, f32[32,96,256]{2,1,0:T(8,128)}) fusion(f32[32,96]{1,0:T(8,128)S(1)} %get-tuple-element.76, f32[32,96,256]{2,1,0:T(8,128)S(1)} %copy-done.30, bf16[32,96,256]{2,1,0:T(8,128)(2,1)} %collective-permute-done.4, ...), kind=kOutput, calls=%fused_computation.72 | convolution fusion | flops 1619263488 | bytes 19415044 | tf_op jit(solution)/shard_map/wte,ed->wtd/dot_general | solution.py:44
  244.6 5.7 %fusion.268 = (bf16[32,96,256]{2,1,0:T(8,128)(2,1)}, f32[32,96,256]{2,1,0:T(8,128)}) fusion(f32[32,96,256]{2,1,0:T(8,128)} %get-tuple-element.90, bf16[32,96,256]{2,1,0:T(8,128)(2,1)} %get-tuple-element.53, bf16[32,96,256]{2,1,0:T(8,128)(2,1)} %get-tuple-element.54, bf16[32,96,256]{2,1,0:T(8,128)(2,1)} %get-tuple-element.52, ...), kind=kOutput, calls=%fused_computation.322 | convolution fusion | flops 474021888 | bytes 13172736 | tf_op jit(solution)/shard_map/wts,wtd->wsd/dot_general | solution.py:89
  251.3 1.8 fusion.109
  254.2 1.8 fusion.110
  257.0 2.0 fusion.163
  259.0 21.9 %collective-permute-done.5 = bf16[32,96,256]{2,1,0:T(8,128)(2,1)S(1)} collective-permute-done((bf16[32,96,256]{2,1,0:T(8,128)(2,1)}, bf16[32,96,256]{2,1,0:T(8,128)(2,1)S(1)}, u32[]{:S(2)}, u32[]{:S(2)}) %collective-permute-start.5) | collective-permute-done | bytes 1572896 | tf_op jit(solution)/shard_map/ppermute | solution.py:139
  282.0 1.8 add_convert_fusion.3
  283.8 4.2 copy.113
  288.1 3.9 fusion.99
  292.0 2.2 fusion.96
  295.5 2.0 pad_maximum_fusion.3
  297.5 7.9 %fusion.90 = bf16[32,4,48,128]{3,0,2,1:T(8,128)(2,1)} fusion(bf16[32,4,48,128]{3,2,0,1:T(8,128)(2,1)} %pad_maximum_fusion.3, bf16[4,48,64,64]{3,2,1,0:T(8,128)(2,1)} %get-tuple-element.65, bf16[4,48,64,64]{3,2,1,0:T(8,128)(2,1)} %get-tuple-element.64, bf16[4,48,64,128]{3,2,1,0:T(8,128)(2,1)S(1)} %bitcast.252), kind=kOutput, calls=%fused_computation.137 | convolution fusion | flops 220987392 | bytes 9437184 | tf_op jit(solution)/shard_map/whmo,hmio->whmi/dot_general | solution.py:44
  305.3 2.7 fusion.264
  311.1 2.0 convolution_bitcast_fusion.6
  313.3 2.0 convolution_bitcast_fusion.7
  316.3 4.9 %all-to-all-start = ((bf16[16,64,128]{2,1,0:T(8,128)(2,1)}), bf16[16,64,128]{2,1,0:T(8,128)(2,1)S(1)}, u32[]{:S(2)}, u32[]{:S(2)}) async-start(bf16[16,64,128]{2,1,0:T(8,128)(2,1)} %convert_element_type.274), calls=%async_computation | async-start | bytes 524288 | tf_op jit(solution)/shard_map/all_to_all | solution.py:322
  321.2 6.0 %fusion.108 = bf16[512,1024]{1,0:T(8,128)(2,1)} fusion(bf16[512,1024]{1,0:T(8,128)(2,1)} %copy-done.28, s32[]{:T(128)S(6)} %select_n.188, bf16[32,96,256]{2,1,0:T(8,128)(2,1)} %copy-done.19, bf16[32,96,1024]{2,1,0:T(8,128)(2,1)} %get-tuple-element.44), kind=kOutput, calls=%fused_computation.144 | convolution fusion | flops 1610612736 | bytes 8912900 | tf_op jit(solution)/shard_map/wtd,wtf->df/dot_general | solution.py:44
  330.0 2.7 pad_maximum_fusion
  332.7 6.2 %all-to-all-start.3 = ((bf16[16,512,128]{2,1,0:T(8,128)(2,1)}), bf16[16,512,128]{2,1,0:T(8,128)(2,1)}, u32[]{:S(2)}, u32[]{:S(2)}) async-start(bf16[16,512,128]{2,1,0:T(8,128)(2,1)} %pad_maximum_fusion), calls=%async_computation.3 | async-start | bytes 4194304 | tf_op jit(solution)/shard_map/all_to_all | solution.py:322
  338.9 2.0 constant_dynamic-slice_fusion
  345.5 6.5 %reshape.224 = bf16[16,32,4,3,2,64]{5,4,3,2,1,0:T(2,128)(2,1)} reshape(bf16[16,384,128]{2,1,0:T(8,128)(2,1)} %all-to-all-done.1) | data formatting | bytes 3145728 | tf_op jit(solution)/shard_map/reshape | solution.py:354
  352.0 5.9 %convolution_convert_fusion.4 = bf16[32,96,256]{2,1,0:T(8,128)(2,1)} fusion(bf16[32,96,1024]{2,1,0:T(8,128)(2,1)} %get-tuple-element.44, bf16[1024,512]{1,0:T(8,128)(2,1)S(1)} %copy-done.23, s32[]{:T(128)S(6)} %select_n.193), kind=kOutput, calls=%fused_computation.116 | convolution fusion | flops 1611399168 | bytes 8388612 | tf_op jit(solution)/shard_map/wte,ed->wtd/dot_general | solution.py:44
  357.9 2.4 fusion.124
  362.0 1.8 copy.132
  369.6 2.5 fusion.170
  372.1 2.0 convolution_convert_fusion.1
  374.2 5.7 %all-to-all-done.3 = bf16[16,512,128]{2,1,0:T(8,128)(2,1)} async-done(((bf16[16,512,128]{2,1,0:T(8,128)(2,1)}), bf16[16,512,128]{2,1,0:T(8,128)(2,1)}, u32[]{:S(2)}, u32[]{:S(2)}) %all-to-all-start.3) | async-done | bytes 2097184 | tf_op jit(solution)/shard_map/all_to_all | solution.py:322
  379.9 11.5 %all-to-all-start.2 = ((bf16[16,448,128]{2,1,0:T(8,128)(2,1)}), bf16[16,448,128]{2,1,0:T(8,128)(2,1)}, u32[]{:S(2)}, u32[]{:S(2)}) async-start(bf16[16,448,128]{2,1,0:T(8,128)(2,1)} %copy.136), calls=%async_computation.2 | async-start | bytes 3670016 | tf_op jit(solution)/shard_map/all_to_all | solution.py:350
  394.6 1.9 convert_reduce_fusion.2
  398.1 1.8 multiply_add_fusion.2
  399.9 1.7 multiply_add_fusion.1
  401.7 3.4 collective-permute-done.6
  406.6 6.7 %fusion.261 = (bf16[32,96,256]{2,1,0:T(8,128)(2,1)S(1)}, bf16[32,96,256]{2,1,0:T(8,128)(2,1)S(1)}, bf16[32,96,256]{2,1,0:T(8,128)(2,1)S(1)}, f32[32,96,256]{2,1,0:T(8,128)S(1)}) fusion(bf16[32,96,256]{2,1,0:T(8,128)(2,1)} %collective-permute-done.6, bf16[32,96,1024]{2,1,0:T(8,128)(2,1)} %get-tuple-element.44, bf16[1024,512]{1,0:T(8,128)(2,1)} %copy-done.22, ...), kind=kOutput, calls=%fused_computation.315 | convolution fusion | flops 1620049920 | bytes 22556676 | tf_op jit(solution)/shard_map/wte,ed->wtd/dot_general | solution.py:44
  413.3 3.4 multiply_subtract_fusion
  416.7 24.4 %collective-permute-done.7 = bf16[32,96,256]{2,1,0:T(8,128)(2,1)S(1)} collective-permute-done((bf16[32,96,256]{2,1,0:T(8,128)(2,1)}, bf16[32,96,256]{2,1,0:T(8,128)(2,1)S(1)}, u32[]{:S(2)}, u32[]{:S(2)}) %collective-permute-start.7) | collective-permute-done | bytes 1572896 | tf_op jit(solution)/shard_map/ppermute | solution.py:139
  441.1 2.6 add_add_fusion
  449.2 2.2 copy.140
  456.0 2.1 multiply_add_fusion
  (206 shorter events, 61.5 us)
Async XLA Ops:
  0.7 6.4 %copy-start.46 = (f32[512,256]{1,0:T(8,128)S(1)}, f32[512,256]{1,0:T(8,128)}, u32[]{:S(2)}) copy-start(f32[512,256]{1,0:T(8,128)} %param.33) | copy-start | bytes 1572868
  4.0 37.7 %collective-permute-start = (bf16[32,96,256]{2,1,0:T(8,128)(2,1)}, bf16[32,96,256]{2,1,0:T(8,128)(2,1)}, u32[]{:S(2)}, u32[]{:S(2)}) collective-permute-start(bf16[32,96,256]{2,1,0:T(8,128)(2,1)} %convert_element_type.215), channel_id=1, source_target_pairs={{0,1},{1,0},{2,3},{3,2},{4,5},{5,4},{6,7},{7,6},{8,9},{9,8},{10,11... | collective-permute-start | bytes 4718600 | tf_op jit(solution)/shard_map/ppermute | solution.py:139
  7.8 3.3 copy-start.42
  7.8 3.3 copy-start.49
  11.1 51.8 %copy-start.61 = (f32[4,48]{1,0:T(4,128)}, f32[4,48]{1,0:T(4,128)S(1)}, u32[]{:S(2)}) copy-start(f32[4,48]{1,0:T(4,128)S(1)} %get-tuple-element.82) | copy-start | bytes 2308
  13.2 28.6 %copy-start.37 = (bf16[512,256]{1,0:T(8,128)(2,1)S(1)}, bf16[512,256]{1,0:T(8,128)(2,1)}, u32[]{:S(2)}) copy-start(bf16[512,256]{1,0:T(8,128)(2,1)} %convert_element_type.214) | copy-start | bytes 786436
  49.0 4.0 copy-start.1
  53.0 3.1 copy-start.4
  53.0 3.4 copy-start.35
  55.2 2.5 copy-start.34
  64.4 3.0 copy-start.55
  64.4 3.0 copy-start.56
  64.4 3.0 copy-start.57
  64.4 3.0 copy-start.58
  64.5 3.0 copy-start.59
  64.5 3.0 copy-start.60
  64.7 36.5 %copy-start.2 = (bf16[32,96,4,64]{1,3,2,0:T(8,128)(2,1)}, bf16[32,96,4,64]{1,3,2,0:T(8,128)(2,1)S(1)}, u32[]{:S(2)}) copy-start(bf16[32,96,4,64]{1,3,2,0:T(8,128)(2,1)S(1)} %copy.108) | copy-start | bytes 4718596
  64.7 9.5 %copy-start.32 = (f32[32,96,256]{2,1,0:T(8,128)S(1)}, f32[32,96,256]{2,1,0:T(8,128)}, u32[]{:S(2)}) copy-start(f32[32,96,256]{2,1,0:T(8,128)} %param.30) | copy-start | bytes 9437188
  65.6 35.6 %collective-permute-start.1 = (bf16[32,96,256]{2,1,0:T(8,128)(2,1)S(1)}, bf16[32,96,256]{2,1,0:T(8,128)(2,1)S(1)}, u32[]{:S(2)}, u32[]{:S(2)}) collective-permute-start(bf16[32,96,256]{2,1,0:T(8,128)(2,1)S(1)} %convolution_convert_fusion.5), channel_id=1, source_target_pairs={{0,1},{1,0},{2,3},{3,2},{4,5},{5,4},{6,7},{7,6},{8,9},{9,8},{10,11... | collective-permute-start | bytes 4718600 | tf_op jit(solution)/shard_map/ppermute | solution.py:139
  67.4 7.5 %copy-start.51 = (f32[32,96]{1,0:T(8,128)}, f32[32,96]{1,0:T(8,128)S(1)}, u32[]{:S(2)}) copy-start(f32[32,96]{1,0:T(8,128)S(1)} %get-tuple-element.38) | copy-start | bytes 36868
  74.2 28.1 %copy-start.44 = (bf16[32,96,96]{2,1,0:T(8,128)(2,1)}, bf16[32,96,96]{2,1,0:T(8,128)(2,1)S(1)}, u32[]{:S(2)}) copy-start(bf16[32,96,96]{2,1,0:T(8,128)(2,1)S(1)} %get-tuple-element.75) | copy-start | bytes 1769476
  74.2 27.0 %copy-start.12 = (f32[32,96,256]{2,1,0:T(8,128)S(1)}, f32[32,96,256]{2,1,0:T(8,128)}, u32[]{:S(2)}) copy-start(f32[32,96,256]{2,1,0:T(8,128)} %param.29) | copy-start | bytes 9437188
  102.3 3.9 copy-start.14
  106.1 15.1 %copy-start.18 = (bf16[32,96,256]{2,1,0:T(8,128)(2,1)}, bf16[32,96,256]{2,1,0:T(8,128)(2,1)S(1)}, u32[]{:S(2)}) copy-start(bf16[32,96,256]{2,1,0:T(8,128)(2,1)S(1)} %get-tuple-element.85) | copy-start | bytes 4718596
  106.1 37.3 %collective-permute-start.2 = (bf16[32,96,256]{2,1,0:T(8,128)(2,1)S(1)}, bf16[32,96,256]{2,1,0:T(8,128)(2,1)S(1)}, u32[]{:S(2)}, u32[]{:S(2)}) collective-permute-start(bf16[32,96,256]{2,1,0:T(8,128)(2,1)S(1)} %get-tuple-element.85), channel_id=1, source_target_pairs={{0,1},{1,0},{2,3},{3,2},{4,5},{5,4},{6,7},{7,6},{8,9},{9,8},{10,11... | collective-permute-start | bytes 4718600 | tf_op jit(solution)/shard_map/ppermute | solution.py:139
  107.6 5.5 %copy-start.36 = (f32[512,1024]{1,0:T(8,128)S(1)}, f32[512,1024]{1,0:T(8,128)}, u32[]{:S(2)}) copy-start(f32[512,1024]{1,0:T(8,128)} %param.36) | copy-start | bytes 6291460
  112.5 69.1 %collective-permute-start.3 = (bf16[32,96,256]{2,1,0:T(8,128)(2,1)S(1)}, bf16[32,96,256]{2,1,0:T(8,128)(2,1)S(1)}, u32[]{:S(2)}, u32[]{:S(2)}) collective-permute-start(bf16[32,96,256]{2,1,0:T(8,128)(2,1)S(1)} %get-tuple-element.88), channel_id=1, source_target_pairs={{0,1},{1,0},{2,3},{3,2},{4,5},{5,4},{6,7},{7,6},{8,9},{9,8},{10,11... | collective-permute-start | bytes 4718600 | tf_op jit(solution)/shard_map/ppermute | solution.py:139
  114.7 28.7 %copy-start.24 = (bf16[512,1024]{1,0:T(8,128)(2,1)}, bf16[512,1024]{1,0:T(8,128)(2,1)S(1)}, u32[]{:S(2)}) copy-start(bf16[512,1024]{1,0:T(8,128)(2,1)S(1)} %convert_element_type.239) | copy-start | bytes 3145732
  114.8 6.4 %copy-start.22 = (bf16[1024,512]{1,0:T(8,128)(2,1)}, bf16[1024,512]{1,0:T(8,128)(2,1)S(1)}, u32[]{:S(2)}) copy-start(bf16[1024,512]{1,0:T(8,128)(2,1)S(1)} %convert_element_type.241) | copy-start | bytes 3145732
  143.4 7.9 %copy-start.20 = (bf16[32,96,256]{2,1,0:T(8,128)(2,1)}, bf16[32,96,256]{2,1,0:T(8,128)(2,1)S(1)}, u32[]{:S(2)}) copy-start(bf16[32,96,256]{2,1,0:T(8,128)(2,1)S(1)} %collective-permute-done.2) | copy-start | bytes 4718596
  201.2 7.4 %copy-start.7 = (bf16[32,4,48,64]{3,2,0,1:T(8,128)(2,1)S(1)}, bf16[32,4,48,64]{3,2,0,1:T(8,128)(2,1)}, u32[]{:S(2)}) copy-start(bf16[32,4,48,64]{3,2,0,1:T(8,128)(2,1)} %copy-done.6) | copy-start | bytes 2359300
  207.1 31.6 %collective-permute-start.4 = (bf16[32,96,256]{2,1,0:T(8,128)(2,1)}, bf16[32,96,256]{2,1,0:T(8,128)(2,1)}, u32[]{:S(2)}, u32[]{:S(2)}) collective-permute-start(bf16[32,96,256]{2,1,0:T(8,128)(2,1)} %convolution_convert_fusion.3), channel_id=1, source_target_pairs={{0,1},{1,0},{2,3},{3,2},{4,5},{5,4},{6,7},{7,6},{8,9},{9,8},{10,11... | collective-permute-start | bytes 4718600 | tf_op jit(solution)/shard_map/ppermute | solution.py:139
  212.5 103.8 %all-to-all-start.1 = ((bf16[16,384,128]{2,1,0:T(8,128)(2,1)}), bf16[16,384,128]{2,1,0:T(8,128)(2,1)}, u32[]{:S(2)}, u32[]{:S(2)}) async-start(bf16[16,384,128]{2,1,0:T(8,128)(2,1)} %copy.129), calls=%async_computation.1 | async-start | bytes 3145728 | tf_op jit(solution)/shard_map/all_to_all | solution.py:345
  218.6 20.1 %slice-start.2 = ((s8[6291456]{0:T(1024)(128)(4,1)}), s8[4194304]{0:T(1024)(128)(4,1)S(1)}, s32[]{:S(2)}) async-start(s8[6291456]{0:T(1024)(128)(4,1)} %bitcast.248), calls=%async_computation.6 | async-start | bytes 8388608
  218.8 20.0 %slice-start.3 = ((s8[6291456]{0:T(1024)(128)(4,1)}), s8[2097152]{0:T(1024)(128)(4,1)S(1)}, s32[]{:S(2)}) async-start(s8[6291456]{0:T(1024)(128)(4,1)} %bitcast.248), calls=%async_computation.7 | async-start | bytes 4194304
  218.8 20.0 %copy-start.25 = (bf16[512,1024]{1,0:T(8,128)(2,1)S(1)}, bf16[512,1024]{1,0:T(8,128)(2,1)}, u32[]{:S(2)}) copy-start(bf16[512,1024]{1,0:T(8,128)(2,1)} %copy-done.24) | copy-start | bytes 3145732
  218.8 20.0 %copy-start.30 = (f32[32,96,256]{2,1,0:T(8,128)S(1)}, f32[32,96,256]{2,1,0:T(8,128)}, u32[]{:S(2)}) copy-start(f32[32,96,256]{2,1,0:T(8,128)} %get-tuple-element.89) | copy-start | bytes 9437188
  238.8 5.8 %copy-start.45 = (bf16[32,96,96]{2,1,0:T(8,128)(2,1)S(1)}, bf16[32,96,96]{2,1,0:T(8,128)(2,1)}, u32[]{:S(2)}) copy-start(bf16[32,96,96]{2,1,0:T(8,128)(2,1)} %copy-done.44) | copy-start | bytes 1769476
  238.8 12.5 %slice-start = ((s8[6291456]{0:T(1024)(128)(4,1)}), s8[4194304]{0:T(1024)(128)(4,1)S(1)}, s32[]{:S(2)}) async-start(s8[6291456]{0:T(1024)(128)(4,1)} %bitcast.246), calls=%async_computation.4 | async-start | bytes 8388608
  244.6 6.7 %slice-start.1 = ((s8[6291456]{0:T(1024)(128)(4,1)}), s8[2097152]{0:T(1024)(128)(4,1)S(1)}, s32[]{:S(2)}) async-start(s8[6291456]{0:T(1024)(128)(4,1)} %bitcast.246), calls=%async_computation.5 | async-start | bytes 4194304
  244.6 6.7 %copy-start.17 = (bf16[32,96,256]{2,1,0:T(8,128)(2,1)S(1)}, bf16[32,96,256]{2,1,0:T(8,128)(2,1)}, u32[]{:S(2)}) copy-start(bf16[32,96,256]{2,1,0:T(8,128)(2,1)} %copy-done.16) | copy-start | bytes 4718596
  250.3 30.6 %collective-permute-start.5 = (bf16[32,96,256]{2,1,0:T(8,128)(2,1)}, bf16[32,96,256]{2,1,0:T(8,128)(2,1)S(1)}, u32[]{:S(2)}, u32[]{:S(2)}) collective-permute-start(bf16[32,96,256]{2,1,0:T(8,128)(2,1)} %get-tuple-element.91), channel_id=1, source_target_pairs={{0,1},{1,0},{2,3},{3,2},{4,5},{5,4},{6,7},{7,6},{8,9},{9,8},{10,11... | collective-permute-start | bytes 4718600 | tf_op jit(solution)/shard_map/ppermute | solution.py:139
  251.3 2.9 copy-start.21
  283.8 8.2 %copy-start.62 = (f32[4,48]{1,0:T(4,128)S(1)}, f32[4,48]{1,0:T(4,128)}, u32[]{:S(2)}) copy-start(f32[4,48]{1,0:T(4,128)} %copy-done.61) | copy-start | bytes 2308
  288.1 3.9 copy-start
  316.3 16.4 %all-to-all-start = ((bf16[16,64,128]{2,1,0:T(8,128)(2,1)}), bf16[16,64,128]{2,1,0:T(8,128)(2,1)S(1)}, u32[]{:S(2)}, u32[]{:S(2)}) async-start(bf16[16,64,128]{2,1,0:T(8,128)(2,1)} %convert_element_type.274), calls=%async_computation | async-start | bytes 524288 | tf_op jit(solution)/shard_map/all_to_all | solution.py:322
  321.2 6.0 %copy-start.27 = (bf16[512,1024]{1,0:T(8,128)(2,1)S(1)}, bf16[512,1024]{1,0:T(8,128)(2,1)}, u32[]{:S(2)}) copy-start(bf16[512,1024]{1,0:T(8,128)(2,1)} %copy-done.26) | copy-start | bytes 3145732
  332.7 47.2 %all-to-all-start.3 = ((bf16[16,512,128]{2,1,0:T(8,128)(2,1)}), bf16[16,512,128]{2,1,0:T(8,128)(2,1)}, u32[]{:S(2)}, u32[]{:S(2)}) async-start(bf16[16,512,128]{2,1,0:T(8,128)(2,1)} %pad_maximum_fusion), calls=%async_computation.3 | async-start | bytes 4194304 | tf_op jit(solution)/shard_map/all_to_all | solution.py:322
  340.9 11.0 %copy-start.23 = (bf16[1024,512]{1,0:T(8,128)(2,1)S(1)}, bf16[1024,512]{1,0:T(8,128)(2,1)}, u32[]{:S(2)}) copy-start(bf16[1024,512]{1,0:T(8,128)(2,1)} %copy-done.22) | copy-start | bytes 3145732
  352.0 5.9 %copy-start.3 = (bf16[32,96,4,64]{1,3,2,0:T(8,128)(2,1)S(1)}, bf16[32,96,4,64]{1,3,2,0:T(8,128)(2,1)}, u32[]{:S(2)}) copy-start(bf16[32,96,4,64]{1,3,2,0:T(8,128)(2,1)} %copy-done.2) | copy-start | bytes 4718596
  357.9 2.8 copy-start.11
  361.1 2.6 copy-start.41
  364.8 4.8 %copy-start.38 = (bf16[512,256]{1,0:T(8,128)(2,1)S(1)}, bf16[512,256]{1,0:T(8,128)(2,1)}, u32[]{:S(2)}) copy-start(bf16[512,256]{1,0:T(8,128)(2,1)} %convert_element_type.214) | copy-start | bytes 786436
  368.2 37.0 %collective-permute-start.6 = (bf16[32,96,256]{2,1,0:T(8,128)(2,1)}, bf16[32,96,256]{2,1,0:T(8,128)(2,1)}, u32[]{:S(2)}, u32[]{:S(2)}) collective-permute-start(bf16[32,96,256]{2,1,0:T(8,128)(2,1)} %convolution_convert_fusion.4), channel_id=1, source_target_pairs={{0,1},{1,0},{2,3},{3,2},{4,5},{5,4},{6,7},{7,6},{8,9},{9,8},{10,11... | collective-permute-start | bytes 4718600 | tf_op jit(solution)/shard_map/ppermute | solution.py:139
  379.9 63.8 %all-to-all-start.2 = ((bf16[16,448,128]{2,1,0:T(8,128)(2,1)}), bf16[16,448,128]{2,1,0:T(8,128)(2,1)}, u32[]{:S(2)}, u32[]{:S(2)}) async-start(bf16[16,448,128]{2,1,0:T(8,128)(2,1)} %copy.136), calls=%async_computation.2 | async-start | bytes 3670016 | tf_op jit(solution)/shard_map/all_to_all | solution.py:350
  391.4 15.2 %copy-start.15 = (f32[32,96,256]{2,1,0:T(8,128)S(1)}, f32[32,96,256]{2,1,0:T(8,128)}, u32[]{:S(2)}) copy-start(f32[32,96,256]{2,1,0:T(8,128)} %copy-done.14) | copy-start | bytes 9437188
  405.1 36.0 %collective-permute-start.7 = (bf16[32,96,256]{2,1,0:T(8,128)(2,1)}, bf16[32,96,256]{2,1,0:T(8,128)(2,1)S(1)}, u32[]{:S(2)}, u32[]{:S(2)}) collective-permute-start(bf16[32,96,256]{2,1,0:T(8,128)(2,1)} %convolution_convert_fusion.1), channel_id=1, source_target_pairs={{0,1},{1,0},{2,3},{3,2},{4,5},{5,4},{6,7},{7,6},{8,9},{9,8},{10,11... | collective-permute-start | bytes 4718600 | tf_op jit(solution)/shard_map/ppermute | solution.py:139
  406.6 6.7 %copy-start.43 = (bf16[32,96,96]{2,1,0:T(8,128)(2,1)S(1)}, bf16[32,96,96]{2,1,0:T(8,128)(2,1)}, u32[]{:S(2)}) copy-start(bf16[32,96,96]{2,1,0:T(8,128)(2,1)} %get-tuple-element.74) | copy-start | bytes 1769476
  406.6 6.7 %copy-start.52 = (f32[32,96]{1,0:T(8,128)S(1)}, f32[32,96]{1,0:T(8,128)}, u32[]{:S(2)}) copy-start(f32[32,96]{1,0:T(8,128)} %copy-done.51) | copy-start | bytes 36868
  413.3 27.9 %copy-start.13 = (f32[32,96,256]{2,1,0:T(8,128)S(1)}, f32[32,96,256]{2,1,0:T(8,128)}, u32[]{:S(2)}) copy-start(f32[32,96,256]{2,1,0:T(8,128)} %fusion.170) | copy-start | bytes 9437188
  413.3 27.8 %copy-start.33 = (f32[32,96,256]{2,1,0:T(8,128)S(1)}, f32[32,96,256]{2,1,0:T(8,128)}, u32[]{:S(2)}) copy-start(f32[32,96,256]{2,1,0:T(8,128)} %get-tuple-element.92) | copy-start | bytes 9437188
  454.7 3.5 copy-start.50
  454.7 3.5 copy-start.53
  454.7 3.5 copy-start.54
  (15 other events, 24.6 us)

commit v9 on v5

--- a/solution.py
+++ b/solution.py
@@ -315,20 +315,6 @@
         owned_shape = shape[:axis_number] + (shape[axis_number] // dp_count,) + shape[axis_number + 1 :]
         return jnp.moveaxis(grad.reshape(split), axis_number, 0).reshape(dp_count, -1, lanes), owned_shape
 
-    def reduced_over_dp(grads_axes):
-        laid = [lead(grad, axis_number) for grad, axis_number in grads_axes]
-        joined = jnp.concatenate([flat for flat, _ in laid], axis=1)
-        reduced = lax.psum_scatter(
-            joined.reshape(-1, lanes), "dp", scatter_dimension=0, tiled=True
-        )
-        parts = []
-        offset = 0
-        for flat, owned_shape in laid:
-            rows = flat.shape[1]
-            parts.append(reduced[offset : offset + rows].reshape(owned_shape))
-            offset += rows
-        return parts
-
     def summed_over_dp(grads_axes):
         laid = [lead(grad, axis_number) for grad, axis_number in grads_axes]
         joined = jnp.concatenate([flat for flat, _ in laid], axis=1)
@@ -345,7 +331,7 @@
             offset += size
         return parts
 
-    inner_part, outer_part_t = reduced_over_dp([(inner_grad, 0), (outer_grad_t, 0)])
+    inner_part, outer_part_t = summed_over_dp([(inner_grad, 0), (outer_grad_t, 0)])
     mixer_part, output_part_t = summed_over_dp([(mixer_full, 1), (output_grad_t, 0)])
     (query_part,) = summed_over_dp([(query_grad, 0)])
     output_part = jnp.transpose(output_part_t)

time: 451 us -> 487 us (1.080)
  waiting for transfers between devices: 136 us -> 193 us
  between operations: 15.1 us -> 1.86 us
  starting transfers between devices: 21.6 us -> 34.5 us
  matrix products: 149 us -> 139 us
  local copies, waits for them, and re-layouts: 41.9 us -> 35 us
    ppermute x8, waiting for transfers between devices: 134 us -> 166 us  [swap(): return lax.ppermute(values, 'head', pairs)]
    all_to_all x2 -> x3, waiting for transfers between devices: 1.84 us -> 26.5 us  [summed_over_dp(): lax.all_to_all(joined.astype(jnp.bfloat16).reshape(-1, lanes), 'dp', 0, 0...]
    all_to_all x2 -> x3, starting transfers between devices: 9.33 us -> 22.2 us  [summed_over_dp(): lax.all_to_all(joined.astype(jnp.bfloat16).reshape(-1, lanes), 'dp', 0, 0...]
    dot_general x35, matrix products: 132 us -> 121 us  [product(): return jnp.einsum(form, left, right, preferred_element_type=jnp.float32)]
    unnamed x120 -> x130, local copies, waits for them, and re-layouts: 10.1 us -> 10.5 us
  transfers between devices with their start and end apart: 11 -> 11, of which waited for: 8 -> 8; matrix products, arithmetic and copies ran while one was open for 44% -> 30% of each run, Pallas kernels for 0% -> 0%
where the time goes in v9:
time: 487 us; the launch traced here: 483 us
  waiting for transfers between devices  193 us (40%)
  matrix products  139 us (29%)
  other arithmetic  79.4 us (16%)
  local copies, waits for them, and re-layouts  35 us (7%)
  starting transfers between devices  34.5 us (7%)
    ppermute x8, waiting for transfers between devices, swap(): return lax.ppermute(values, 'head', pairs)  166 us
    dot_general x35, matrix products, product(): return jnp.einsum(form, left, right, preferred_element_type=jnp.float32)  121 us
    convert_element_type x1, other arithmetic, chunk_pass(): hidden = activated.astype(jnp.bfloat16)  30.3 us
    all_to_all x3, waiting for transfers between devices, summed_over_dp(): lax.all_to_all(joined.astype(jnp.bfloat16).reshape(-1, lanes), 'dp', 0, 0...  26.5 us
    all_to_all x3, starting transfers between devices, summed_over_dp(): lax.all_to_all(joined.astype(jnp.bfloat16).reshape(-1, lanes), 'dp', 0, 0...  22.2 us
    ppermute x8, starting transfers between devices, swap(): return lax.ppermute(values, 'head', pairs)  12.3 us
    unnamed x130, local copies, waits for them, and re-layouts  10.5 us
    dot_general x2, matrix products, trend_back(): jnp.einsum('wts,wtd->wsd', tiled, parts, preferred_element_type=jnp.float32)  10.4 us
  transfers between devices with their start and end apart: 11, of which 8 were waited for; matrix products, arithmetic and copies ran while one was open for 30% of the time, Pallas kernels for 0%

profile of v9, /device:TPU:0, one launch (start us, length us, event | category | flops | bytes accessed | tf_op | source)
XLA Modules:
  0.0 482.5 jit_solution(5334577660397203128)
XLA Ops:
  0.7 3.4 convert_element_type.219
  4.0 3.0 collective-permute-start
  7.7 3.2 convert_element_type.217
  11.1 2.1 fusion.160
  13.2 4.0 slice_negate_fusion
  17.2 24.5 %collective-permute-done = bf16[32,96,256]{2,1,0:T(8,128)(2,1)} collective-permute-done((bf16[32,96,256]{2,1,0:T(8,128)(2,1)}, bf16[32,96,256]{2,1,0:T(8,128)(2,1)}, u32[]{:S(2)}, u32[]{:S(2)}) %collective-permute-start) | collective-permute-done | bytes 1572896 | tf_op jit(solution)/shard_map/ppermute | solution.py:139
  41.7 3.1 fusion.91
  44.9 4.1 copy.64
  49.0 3.9 fusion.72
  53.0 2.2 fusion.69
  57.7 3.1 fusion.95
  65.5 1.8 collective-permute-start.1
  67.4 6.7 %select_convert_fusion = (bf16[32,96,96]{2,1,0:T(8,128)(2,1)}, bf16[32,96,96]{2,1,0:T(8,128)(2,1)S(1)}) fusion(bf16[96,96]{1,0:T(8,128)(2,1)S(1)} %copy-done.55, bf16[96,96]{1,0:T(8,128)(2,1)S(1)} %copy-done.56, bf16[96,96]{1,0:T(8,128)(2,1)S(1)} %copy-done.57, bf16[96,96]{1,0:T(8,128)(2,1)S(1)} %copy-done.58, bf16[96,96]{1,0:T(8,128)(2,1)S(1)} %copy-done.59, ...), kind=kLoop, calls=%fused_computation.133 | loop fusion | flops 2949120 | bytes 1302528 | tf_op jit(solution)/shard_map/convert_element_type | solution.py:66
  74.8 26.3 %collective-permute-done.1 = bf16[32,96,256]{2,1,0:T(8,128)(2,1)S(1)} collective-permute-done((bf16[32,96,256]{2,1,0:T(8,128)(2,1)S(1)}, bf16[32,96,256]{2,1,0:T(8,128)(2,1)S(1)}, u32[]{:S(2)}, u32[]{:S(2)}) %collective-permute-start.1) | collective-permute-done | bytes 1572896 | tf_op jit(solution)/shard_map/ppermute | solution.py:139
  102.3 3.9 fusion.112
  107.6 4.8 fusion.252
  114.8 6.5 %fusion.122 = f32[32,96,1024]{2,1,0:T(8,128)} fusion(bf16[32,96,256]{2,1,0:T(8,128)(2,1)S(1)} %get-tuple-element.88, bf16[1024,512]{1,0:T(8,128)(2,1)S(1)} %convert_element_type.245, s32[]{:T(128)S(6)} %select_n.186), kind=kOutput, calls=%fused_computation.158 | convolution fusion | flops 1610612736 | bytes 14680068 | tf_op jit(solution)/shard_map/wtd,fd->wtf/dot_general | solution.py:44
  121.2 1.8 fusion.131
  123.0 20.4 %collective-permute-done.2 = bf16[32,96,256]{2,1,0:T(8,128)(2,1)S(1)} collective-permute-done((bf16[32,96,256]{2,1,0:T(8,128)(2,1)S(1)}, bf16[32,96,256]{2,1,0:T(8,128)(2,1)S(1)}, u32[]{:S(2)}, u32[]{:S(2)}) %collective-permute-start.2) | collective-permute-done | bytes 1572896 | tf_op jit(solution)/shard_map/ppermute | solution.py:139
  143.4 7.9 %convert_reduce_fusion.1 = (u32[96,1024]{1,0:T(8,128)S(1)}, u32[96,1024]{1,0:T(8,128)S(1)}, f32[32,96,1024]{2,1,0:T(8,128)}) fusion(f32[32,96,1024]{2,1,0:T(8,128)S(1)} %fusion.131, bf16[32,96,256]{2,1,0:T(8,128)(2,1)S(1)} %collective-permute-done.2, bf16[512,1024]{1,0:T(8,128)(2,1)S(1)} %convert_element_type.243, s32[]{:T(128)S(6)} %select_n.188), kind=kOutput, calls=%fused_computation.6 | convolution fusion | flops 1648164864 | bytes 28049412 | tf_op jit(solution)/shard_map/wtd,de->wte/dot_general | solution.py:44
  151.3 30.3 %multiply_convert_fusion = (bf16[32,96,1024]{2,1,0:T(8,128)(2,1)}, f32[32,96,1024]{2,1,0:T(8,128)}) fusion(f32[32,96,1024]{2,1,0:T(8,128)} %get-tuple-element.87, u32[96,1024]{1,0:T(8,128)S(1)} %get-tuple-element.22, u32[96,1024]{1,0:T(8,128)S(1)} %get-tuple-element.21), kind=kLoop, calls=%fused_computation.8 | loop fusion | flops 213909504 | bytes 32243712 | tf_op jit(solution)/shard_map/convert_element_type | solution.py:215
  182.8 18.3 %add_convert_fusion = bf16[32,96,1024]{2,1,0:T(8,128)(2,1)} fusion(f32[32,96,1024]{2,1,0:T(8,128)} %get-tuple-element.45, f32[32,96,1024]{2,1,0:T(8,128)} %fusion.122, f32[32,96,1024]{2,1,0:T(8,128)} %get-tuple-element.87, bf16[32,96,256]{2,1,0:T(8,128)(2,1)} %copy-done.20, bf16[1024,512]{1,0:T(8,128)(2,1)} %copy-done.23, s32[]{:T(128)S(6)} %select_n.188), kind=kOutput, calls=%fused_computation.7 | convolution fusion | flops 1657798656 | bytes 46137348 | tf_op jit(solution)/shard_map/wtd,fd->wtf/dot_general | solution.py:44
  201.2 4.8 %convolution_convert_fusion.3 = bf16[32,96,256]{2,1,0:T(8,128)(2,1)S(1)} fusion(bf16[32,96,1024]{2,1,0:T(8,128)(2,1)} %add_convert_fusion, bf16[512,1024]{1,0:T(8,128)(2,1)} %copy-done.25, s32[]{:T(128)S(6)} %select_n.193), kind=kOutput, calls=%fused_computation.117 | convolution fusion | flops 1611399168 | bytes 8388612 | tf_op jit(solution)/shard_map/wte,ed->wtd/dot_general | solution.py:44
  207.7 1.8 fusion.101
  209.5 27.9 %collective-permute-done.4 = bf16[32,96,256]{2,1,0:T(8,128)(2,1)S(1)} collective-permute-done((bf16[32,96,256]{2,1,0:T(8,128)(2,1)S(1)}, bf16[32,96,256]{2,1,0:T(8,128)(2,1)S(1)}, u32[]{:S(2)}, u32[]{:S(2)}) %collective-permute-start.4) | collective-permute-done | bytes 1572896 | tf_op jit(solution)/shard_map/ppermute | solution.py:139
  237.4 4.5 multiply_convert_fusion.1
  241.9 5.6 %fusion.253 = (bf16[32,96,256]{2,1,0:T(8,128)(2,1)}, f32[32,96,256]{2,1,0:T(8,128)}) fusion(f32[32,96,256]{2,1,0:T(8,128)} %get-tuple-element.90, bf16[32,96,256]{2,1,0:T(8,128)(2,1)} %get-tuple-element.53, bf16[32,96,256]{2,1,0:T(8,128)(2,1)} %get-tuple-element.54, bf16[32,96,256]{2,1,0:T(8,128)(2,1)} %get-tuple-element.52, ...), kind=kOutput, calls=%fused_computation.313 | convolution fusion | flops 474021888 | bytes 13172736 | tf_op jit(solution)/shard_map/wts,wtd->wsd/dot_general | solution.py:89
  248.5 1.8 fusion.99
  251.3 1.8 fusion.100
  254.2 2.0 fusion.151
  256.2 21.9 %collective-permute-done.5 = bf16[32,96,256]{2,1,0:T(8,128)(2,1)S(1)} collective-permute-done((bf16[32,96,256]{2,1,0:T(8,128)(2,1)}, bf16[32,96,256]{2,1,0:T(8,128)(2,1)S(1)}, u32[]{:S(2)}, u32[]{:S(2)}) %collective-permute-start.5) | collective-permute-done | bytes 1572896 | tf_op jit(solution)/shard_map/ppermute | solution.py:139
  279.3 1.8 add_convert_fusion.3
  281.1 4.0 copy.75
  285.1 3.9 bitcast_negate_fusion
  289.1 2.2 fusion.78
  291.3 3.4 maximum_bitcast_fusion
  294.7 7.9 %fusion.92 = bf16[32,4,48,128]{3,0,2,1:T(8,128)(2,1)} fusion(bf16[32,4,48,128]{3,2,0,1:T(8,128)(2,1)} %get-tuple-element.67, bf16[4,48,64,64]{3,2,1,0:T(8,128)(2,1)} %get-tuple-element.65, bf16[4,48,64,64]{3,2,1,0:T(8,128)(2,1)} %get-tuple-element.64, bf16[4,48,64,128]{3,2,1,0:T(8,128)(2,1)S(1)} %bitcast.240), kind=kOutput, calls=%fused_computation.136 | convolution fusion | flops 220987392 | bytes 9437184 | tf_op jit(solution)/shard_map/whmo,hmio->whmi/dot_general | solution.py:44
  302.5 2.7 fusion.249
  308.3 2.0 convolution_bitcast_fusion.7
  310.4 2.5 convolution_bitcast_fusion.6
  313.9 4.7 all-to-all-start
  318.7 6.0 %fusion.98 = bf16[512,1024]{1,0:T(8,128)(2,1)} fusion(bf16[512,1024]{1,0:T(8,128)(2,1)} %copy-done.29, s32[]{:T(128)S(6)} %select_n.188, bf16[32,96,256]{2,1,0:T(8,128)(2,1)} %copy-done.20, bf16[32,96,1024]{2,1,0:T(8,128)(2,1)} %get-tuple-element.44), kind=kOutput, calls=%fused_computation.139 | convolution fusion | flops 1610612736 | bytes 8912900 | tf_op jit(solution)/shard_map/wtd,wtf->df/dot_general | solution.py:44
  327.4 2.7 pad_maximum_fusion.3
  330.2 6.1 %all-to-all-start.2 = ((bf16[16,512,128]{2,1,0:T(8,128)(2,1)}), bf16[16,512,128]{2,1,0:T(8,128)(2,1)}, u32[]{:S(2)}, u32[]{:S(2)}) async-start(bf16[16,512,128]{2,1,0:T(8,128)(2,1)} %pad_maximum_fusion.3), calls=%async_computation.2 | async-start | bytes 4194304 | tf_op jit(solution)/shard_map/all_to_all | solution.py:322
  336.2 2.7 pad_maximum_fusion.1
  339.0 2.4 fusion.114
  344.0 1.9 copy.90
  346.8 3.9 pad_maximum_fusion
  350.7 26.5 %all-to-all-done.2 = bf16[16,512,128]{2,1,0:T(8,128)(2,1)} async-done(((bf16[16,512,128]{2,1,0:T(8,128)(2,1)}), bf16[16,512,128]{2,1,0:T(8,128)(2,1)}, u32[]{:S(2)}, u32[]{:S(2)}) %all-to-all-start.2) | async-done | bytes 2097184 | tf_op jit(solution)/shard_map/all_to_all | solution.py:322
  377.3 11.4 %all-to-all-start.1 = ((bf16[16,832,128]{2,1,0:T(8,128)(2,1)}), bf16[16,832,128]{2,1,0:T(8,128)(2,1)}, u32[]{:S(2)}, u32[]{:S(2)}) async-start(bf16[16,832,128]{2,1,0:T(8,128)(2,1)} %pad_maximum_fusion), calls=%async_computation.1 | async-start | bytes 6815744 | tf_op jit(solution)/shard_map/all_to_all | solution.py:322
  388.7 2.0 constant_dynamic-slice_fusion
  395.2 5.8 %convolution_convert_fusion.4 = bf16[32,96,256]{2,1,0:T(8,128)(2,1)} fusion(bf16[32,96,1024]{2,1,0:T(8,128)(2,1)} %get-tuple-element.44, bf16[1024,512]{1,0:T(8,128)(2,1)S(1)} %copy-done.24, s32[]{:T(128)S(6)} %select_n.193), kind=kOutput, calls=%fused_computation.118 | convolution fusion | flops 1611399168 | bytes 8388612 | tf_op jit(solution)/shard_map/wte,ed->wtd/dot_general | solution.py:44
  402.5 2.5 fusion.158
  405.0 2.1 convolution_convert_fusion.1
  410.3 1.9 convert_reduce_fusion.3
  413.8 1.8 multiply_add_fusion.3
  415.6 1.7 multiply_add_fusion.2
  417.4 20.7 %collective-permute-done.6 = bf16[32,96,256]{2,1,0:T(8,128)(2,1)} collective-permute-done((bf16[32,96,256]{2,1,0:T(8,128)(2,1)}, bf16[32,96,256]{2,1,0:T(8,128)(2,1)}, u32[]{:S(2)}, u32[]{:S(2)}) %collective-permute-start.6) | collective-permute-done | bytes 1572896 | tf_op jit(solution)/shard_map/ppermute | solution.py:139
  439.6 6.7 %fusion.247 = (bf16[32,96,256]{2,1,0:T(8,128)(2,1)S(1)}, bf16[32,96,256]{2,1,0:T(8,128)(2,1)S(1)}, bf16[32,96,256]{2,1,0:T(8,128)(2,1)S(1)}, f32[32,96,256]{2,1,0:T(8,128)S(1)}) fusion(bf16[32,96,256]{2,1,0:T(8,128)(2,1)} %collective-permute-done.6, bf16[32,96,1024]{2,1,0:T(8,128)(2,1)} %get-tuple-element.44, bf16[1024,512]{1,0:T(8,128)(2,1)} %copy-done.23, ...), kind=kOutput, calls=%fused_computation.307 | convolution fusion | flops 1620049920 | bytes 22556676 | tf_op jit(solution)/shard_map/wte,ed->wtd/dot_general | solution.py:44
  446.3 3.4 multiply_subtract_fusion
  449.8 24.5 %collective-permute-done.7 = bf16[32,96,256]{2,1,0:T(8,128)(2,1)S(1)} collective-permute-done((bf16[32,96,256]{2,1,0:T(8,128)(2,1)}, bf16[32,96,256]{2,1,0:T(8,128)(2,1)S(1)}, u32[]{:S(2)}, u32[]{:S(2)}) %collective-permute-start.7) | collective-permute-done | bytes 1572896 | tf_op jit(solution)/shard_map/ppermute | solution.py:139
  474.3 2.6 add_add_fusion
  476.9 2.5 convert_reduce_fusion.2
  479.6 2.1 multiply_add_fusion
  (183 shorter events, 44.0 us)
Async XLA Ops:
  0.7 6.4 %copy-start.45 = (f32[512,256]{1,0:T(8,128)S(1)}, f32[512,256]{1,0:T(8,128)}, u32[]{:S(2)}) copy-start(f32[512,256]{1,0:T(8,128)} %param.33) | copy-start | bytes 1572868
  4.0 37.7 %collective-permute-start = (bf16[32,96,256]{2,1,0:T(8,128)(2,1)}, bf16[32,96,256]{2,1,0:T(8,128)(2,1)}, u32[]{:S(2)}, u32[]{:S(2)}) collective-permute-start(bf16[32,96,256]{2,1,0:T(8,128)(2,1)} %convert_element_type.219), channel_id=1, source_target_pairs={{0,1},{1,0},{2,3},{3,2},{4,5},{5,4},{6,7},{7,6},{8,9},{9,8},{10,11... | collective-permute-start | bytes 4718600 | tf_op jit(solution)/shard_map/ppermute | solution.py:139
  7.7 3.3 copy-start.41
  7.7 3.3 copy-start.48
  11.1 51.8 %copy-start.60 = (f32[4,48]{1,0:T(4,128)}, f32[4,48]{1,0:T(4,128)S(1)}, u32[]{:S(2)}) copy-start(f32[4,48]{1,0:T(4,128)S(1)} %get-tuple-element.82) | copy-start | bytes 2308
  13.2 28.6 %copy-start.37 = (bf16[512,256]{1,0:T(8,128)(2,1)S(1)}, bf16[512,256]{1,0:T(8,128)(2,1)}, u32[]{:S(2)}) copy-start(bf16[512,256]{1,0:T(8,128)(2,1)} %convert_element_type.218) | copy-start | bytes 786436
  49.0 4.0 copy-start.2
  52.9 3.1 copy-start.5
  53.0 3.4 copy-start.35
  64.4 3.0 copy-start.54
  64.4 3.0 copy-start.55
  64.4 3.0 copy-start.56
  64.4 3.0 copy-start.57
  64.4 3.0 copy-start.58
  64.4 3.0 copy-start.59
  64.7 36.5 %copy-start.3 = (bf16[32,96,4,64]{1,3,2,0:T(8,128)(2,1)}, bf16[32,96,4,64]{1,3,2,0:T(8,128)(2,1)S(1)}, u32[]{:S(2)}) copy-start(bf16[32,96,4,64]{1,3,2,0:T(8,128)(2,1)S(1)} %copy.70) | copy-start | bytes 4718596
  64.7 9.5 %copy-start.32 = (f32[32,96,256]{2,1,0:T(8,128)S(1)}, f32[32,96,256]{2,1,0:T(8,128)}, u32[]{:S(2)}) copy-start(f32[32,96,256]{2,1,0:T(8,128)} %param.30) | copy-start | bytes 9437188
  65.5 35.6 %collective-permute-start.1 = (bf16[32,96,256]{2,1,0:T(8,128)(2,1)S(1)}, bf16[32,96,256]{2,1,0:T(8,128)(2,1)S(1)}, u32[]{:S(2)}, u32[]{:S(2)}) collective-permute-start(bf16[32,96,256]{2,1,0:T(8,128)(2,1)S(1)} %convolution_convert_fusion.5), channel_id=1, source_target_pairs={{0,1},{1,0},{2,3},{3,2},{4,5},{5,4},{6,7},{7,6},{8,9},{9,8},{10,11... | collective-permute-start | bytes 4718600 | tf_op jit(solution)/shard_map/ppermute | solution.py:139
  67.4 7.4 %copy-start.50 = (f32[32,96]{1,0:T(8,128)}, f32[32,96]{1,0:T(8,128)S(1)}, u32[]{:S(2)}) copy-start(f32[32,96]{1,0:T(8,128)S(1)} %get-tuple-element.38) | copy-start | bytes 36868
  74.1 28.1 %copy-start.43 = (bf16[32,96,96]{2,1,0:T(8,128)(2,1)}, bf16[32,96,96]{2,1,0:T(8,128)(2,1)S(1)}, u32[]{:S(2)}) copy-start(bf16[32,96,96]{2,1,0:T(8,128)(2,1)S(1)} %get-tuple-element.75) | copy-start | bytes 1769476
  74.1 27.0 %copy-start.11 = (f32[32,96,256]{2,1,0:T(8,128)S(1)}, f32[32,96,256]{2,1,0:T(8,128)}, u32[]{:S(2)}) copy-start(f32[32,96,256]{2,1,0:T(8,128)} %param.29) | copy-start | bytes 9437188
  102.2 3.9 copy-start.13
  106.1 15.1 %copy-start.17 = (bf16[32,96,256]{2,1,0:T(8,128)(2,1)}, bf16[32,96,256]{2,1,0:T(8,128)(2,1)S(1)}, u32[]{:S(2)}) copy-start(bf16[32,96,256]{2,1,0:T(8,128)(2,1)S(1)} %get-tuple-element.85) | copy-start | bytes 4718596
  106.2 37.3 %collective-permute-start.2 = (bf16[32,96,256]{2,1,0:T(8,128)(2,1)S(1)}, bf16[32,96,256]{2,1,0:T(8,128)(2,1)S(1)}, u32[]{:S(2)}, u32[]{:S(2)}) collective-permute-start(bf16[32,96,256]{2,1,0:T(8,128)(2,1)S(1)} %get-tuple-element.85), channel_id=1, source_target_pairs={{0,1},{1,0},{2,3},{3,2},{4,5},{5,4},{6,7},{7,6},{8,9},{9,8},{10,11... | collective-permute-start | bytes 4718600 | tf_op jit(solution)/shard_map/ppermute | solution.py:139
  107.6 5.4 %copy-start.36 = (f32[512,1024]{1,0:T(8,128)S(1)}, f32[512,1024]{1,0:T(8,128)}, u32[]{:S(2)}) copy-start(f32[512,1024]{1,0:T(8,128)} %param.36) | copy-start | bytes 6291460
  112.4 69.2 %collective-permute-start.3 = (bf16[32,96,256]{2,1,0:T(8,128)(2,1)S(1)}, bf16[32,96,256]{2,1,0:T(8,128)(2,1)S(1)}, u32[]{:S(2)}, u32[]{:S(2)}) collective-permute-start(bf16[32,96,256]{2,1,0:T(8,128)(2,1)S(1)} %get-tuple-element.88), channel_id=1, source_target_pairs={{0,1},{1,0},{2,3},{3,2},{4,5},{5,4},{6,7},{7,6},{8,9},{9,8},{10,11... | collective-permute-start | bytes 4718600 | tf_op jit(solution)/shard_map/ppermute | solution.py:139
  114.6 28.8 %copy-start.25 = (bf16[512,1024]{1,0:T(8,128)(2,1)}, bf16[512,1024]{1,0:T(8,128)(2,1)S(1)}, u32[]{:S(2)}) copy-start(bf16[512,1024]{1,0:T(8,128)(2,1)S(1)} %convert_element_type.243) | copy-start | bytes 3145732
  114.8 6.5 %copy-start.23 = (bf16[1024,512]{1,0:T(8,128)(2,1)}, bf16[1024,512]{1,0:T(8,128)(2,1)S(1)}, u32[]{:S(2)}) copy-start(bf16[1024,512]{1,0:T(8,128)(2,1)S(1)} %convert_element_type.245) | copy-start | bytes 3145732
  143.4 7.9 %copy-start.21 = (bf16[32,96,256]{2,1,0:T(8,128)(2,1)}, bf16[32,96,256]{2,1,0:T(8,128)(2,1)S(1)}, u32[]{:S(2)}) copy-start(bf16[32,96,256]{2,1,0:T(8,128)(2,1)S(1)} %collective-permute-done.2) | copy-start | bytes 4718596
  201.2 6.5 %copy-start = (bf16[32,96,1024]{2,1,0:T(8,128)(2,1)S(1)}, bf16[32,96,1024]{2,1,0:T(8,128)(2,1)}, u32[]{:S(2)}) copy-start(bf16[32,96,1024]{2,1,0:T(8,128)(2,1)} %add_convert_fusion) | copy-start | bytes 18874372
  201.2 6.5 %copy-start.18 = (bf16[32,96,256]{2,1,0:T(8,128)(2,1)S(1)}, bf16[32,96,256]{2,1,0:T(8,128)(2,1)}, u32[]{:S(2)}) copy-start(bf16[32,96,256]{2,1,0:T(8,128)(2,1)} %copy-done.17) | copy-start | bytes 4718596
  206.0 31.4 %collective-permute-start.4 = (bf16[32,96,256]{2,1,0:T(8,128)(2,1)S(1)}, bf16[32,96,256]{2,1,0:T(8,128)(2,1)S(1)}, u32[]{:S(2)}, u32[]{:S(2)}) collective-permute-start(bf16[32,96,256]{2,1,0:T(8,128)(2,1)S(1)} %convolution_convert_fusion.3), channel_id=1, source_target_pairs={{0,1},{1,0},{2,3},{3,2},{4,5},{5,4},{6,7},{7,6},{8,9},{9,8},{10,11... | collective-permute-start | bytes 4718600 | tf_op jit(solution)/shard_map/ppermute | solution.py:139
  207.7 29.7 %copy-start.26 = (bf16[512,1024]{1,0:T(8,128)(2,1)S(1)}, bf16[512,1024]{1,0:T(8,128)(2,1)}, u32[]{:S(2)}) copy-start(bf16[512,1024]{1,0:T(8,128)(2,1)} %copy-done.25) | copy-start | bytes 3145732
  207.7 29.7 %copy-start.31 = (f32[32,96,256]{2,1,0:T(8,128)S(1)}, f32[32,96,256]{2,1,0:T(8,128)}, u32[]{:S(2)}) copy-start(f32[32,96,256]{2,1,0:T(8,128)} %get-tuple-element.89) | copy-start | bytes 9437188
  237.4 4.5 copy-start.44
  237.4 11.1 %slice-start = ((s8[6291456]{0:T(1024)(128)(4,1)}), s8[4194304]{0:T(1024)(128)(4,1)S(1)}, s32[]{:S(2)}) async-start(s8[6291456]{0:T(1024)(128)(4,1)} %bitcast.236), calls=%async_computation.3 | async-start | bytes 8388608
  241.9 6.6 %slice-start.1 = ((s8[6291456]{0:T(1024)(128)(4,1)}), s8[2097152]{0:T(1024)(128)(4,1)S(1)}, s32[]{:S(2)}) async-start(s8[6291456]{0:T(1024)(128)(4,1)} %bitcast.236), calls=%async_computation.4 | async-start | bytes 4194304
  241.9 6.6 %copy-start.16 = (bf16[32,96,256]{2,1,0:T(8,128)(2,1)S(1)}, bf16[32,96,256]{2,1,0:T(8,128)(2,1)}, u32[]{:S(2)}) copy-start(bf16[32,96,256]{2,1,0:T(8,128)(2,1)} %copy-done.15) | copy-start | bytes 4718596
  247.5 30.6 %collective-permute-start.5 = (bf16[32,96,256]{2,1,0:T(8,128)(2,1)}, bf16[32,96,256]{2,1,0:T(8,128)(2,1)S(1)}, u32[]{:S(2)}, u32[]{:S(2)}) collective-permute-start(bf16[32,96,256]{2,1,0:T(8,128)(2,1)} %get-tuple-element.91), channel_id=1, source_target_pairs={{0,1},{1,0},{2,3},{3,2},{4,5},{5,4},{6,7},{7,6},{8,9},{9,8},{10,11... | collective-permute-start | bytes 4718600 | tf_op jit(solution)/shard_map/ppermute | solution.py:139
  248.5 2.8 copy-start.22
  285.1 3.9 copy-start.1
  285.1 3.9 copy-start.61
  289.1 5.6 %copy-start.7 = (bf16[4,32,64,48]{2,3,1,0:T(8,128)(2,1)}, bf16[4,32,64,48]{2,3,1,0:T(8,128)(2,1)S(1)}, u32[]{:S(2)}) copy-start(bf16[4,32,64,48]{2,3,1,0:T(8,128)(2,1)S(1)} %get-tuple-element.95) | copy-start | bytes 2359300
  291.3 3.4 copy-start.9
  313.9 16.2 %all-to-all-start = ((bf16[16,64,128]{2,1,0:T(8,128)(2,1)}), bf16[16,64,128]{2,1,0:T(8,128)(2,1)S(1)}, u32[]{:S(2)}, u32[]{:S(2)}) async-start(bf16[16,64,128]{2,1,0:T(8,128)(2,1)} %convert_element_type.278), calls=%async_computation | async-start | bytes 524288 | tf_op jit(solution)/shard_map/all_to_all | solution.py:322
  318.7 6.0 %copy-start.28 = (bf16[512,1024]{1,0:T(8,128)(2,1)S(1)}, bf16[512,1024]{1,0:T(8,128)(2,1)}, u32[]{:S(2)}) copy-start(bf16[512,1024]{1,0:T(8,128)(2,1)} %copy-done.27) | copy-start | bytes 3145732
  330.2 47.1 %all-to-all-start.2 = ((bf16[16,512,128]{2,1,0:T(8,128)(2,1)}), bf16[16,512,128]{2,1,0:T(8,128)(2,1)}, u32[]{:S(2)}, u32[]{:S(2)}) async-start(bf16[16,512,128]{2,1,0:T(8,128)(2,1)} %pad_maximum_fusion.3), calls=%async_computation.2 | async-start | bytes 4194304 | tf_op jit(solution)/shard_map/all_to_all | solution.py:322
  336.2 2.8 copy-start.4
  336.2 5.2 %copy-start.19 = (bf16[32,4,48,1,128]{4,2,0,1,3:T(8,128)(2,1)S(1)}, bf16[32,4,48,1,128]{4,2,0,1,3:T(8,128)(2,1)}, u32[]{:S(2)}) copy-start(bf16[32,4,48,1,128]{4,2,0,1,3:T(8,128)(2,1)} %get-tuple-element.66) | copy-start | bytes 4718596
  350.7 44.5 %copy-start.24 = (bf16[1024,512]{1,0:T(8,128)(2,1)S(1)}, bf16[1024,512]{1,0:T(8,128)(2,1)}, u32[]{:S(2)}) copy-start(bf16[1024,512]{1,0:T(8,128)(2,1)} %copy-done.23) | copy-start | bytes 3145732
  377.3 99.7 %all-to-all-start.1 = ((bf16[16,832,128]{2,1,0:T(8,128)(2,1)}), bf16[16,832,128]{2,1,0:T(8,128)(2,1)}, u32[]{:S(2)}, u32[]{:S(2)}) async-start(bf16[16,832,128]{2,1,0:T(8,128)(2,1)} %pad_maximum_fusion), calls=%async_computation.1 | async-start | bytes 6815744 | tf_op jit(solution)/shard_map/all_to_all | solution.py:322
  395.2 7.3 %copy-start.38 = (bf16[512,256]{1,0:T(8,128)(2,1)S(1)}, bf16[512,256]{1,0:T(8,128)(2,1)}, u32[]{:S(2)}) copy-start(bf16[512,256]{1,0:T(8,128)(2,1)} %convert_element_type.218) | copy-start | bytes 786436
  401.0 37.1 %collective-permute-start.6 = (bf16[32,96,256]{2,1,0:T(8,128)(2,1)}, bf16[32,96,256]{2,1,0:T(8,128)(2,1)}, u32[]{:S(2)}, u32[]{:S(2)}) collective-permute-start(bf16[32,96,256]{2,1,0:T(8,128)(2,1)} %convolution_convert_fusion.4), channel_id=1, source_target_pairs={{0,1},{1,0},{2,3},{3,2},{4,5},{5,4},{6,7},{7,6},{8,9},{9,8},{10,11... | collective-permute-start | bytes 4718600 | tf_op jit(solution)/shard_map/ppermute | solution.py:139
  407.1 32.5 %copy-start.14 = (f32[32,96,256]{2,1,0:T(8,128)S(1)}, f32[32,96,256]{2,1,0:T(8,128)}, u32[]{:S(2)}) copy-start(f32[32,96,256]{2,1,0:T(8,128)} %copy-done.13) | copy-start | bytes 9437188
  438.1 36.2 %collective-permute-start.7 = (bf16[32,96,256]{2,1,0:T(8,128)(2,1)}, bf16[32,96,256]{2,1,0:T(8,128)(2,1)S(1)}, u32[]{:S(2)}, u32[]{:S(2)}) collective-permute-start(bf16[32,96,256]{2,1,0:T(8,128)(2,1)} %convolution_convert_fusion.1), channel_id=1, source_target_pairs={{0,1},{1,0},{2,3},{3,2},{4,5},{5,4},{6,7},{7,6},{8,9},{9,8},{10,11... | collective-permute-start | bytes 4718600 | tf_op jit(solution)/shard_map/ppermute | solution.py:139
  439.6 6.7 %copy-start.42 = (bf16[32,96,96]{2,1,0:T(8,128)(2,1)S(1)}, bf16[32,96,96]{2,1,0:T(8,128)(2,1)}, u32[]{:S(2)}) copy-start(bf16[32,96,96]{2,1,0:T(8,128)(2,1)} %get-tuple-element.74) | copy-start | bytes 1769476
  439.6 6.7 %copy-start.51 = (f32[32,96]{1,0:T(8,128)S(1)}, f32[32,96]{1,0:T(8,128)}, u32[]{:S(2)}) copy-start(f32[32,96]{1,0:T(8,128)} %copy-done.50) | copy-start | bytes 36868
  446.3 28.0 %copy-start.12 = (f32[32,96,256]{2,1,0:T(8,128)S(1)}, f32[32,96,256]{2,1,0:T(8,128)}, u32[]{:S(2)}) copy-start(f32[32,96,256]{2,1,0:T(8,128)} %fusion.158) | copy-start | bytes 9437188
  446.3 27.9 %copy-start.33 = (f32[32,96,256]{2,1,0:T(8,128)S(1)}, f32[32,96,256]{2,1,0:T(8,128)}, u32[]{:S(2)}) copy-start(f32[32,96,256]{2,1,0:T(8,128)} %get-tuple-element.92) | copy-start | bytes 9437188
  476.9 2.6 copy-start.46
  476.9 2.7 copy-start.47
  476.9 4.8 copy-start.49
  476.9 4.8 copy-start.52
  476.9 4.8 copy-start.53
  (11 other events, 19.3 us)

commit v10 on v8

--- a/solution.py
+++ b/solution.py
@@ -346,10 +346,16 @@
         gm_flat = by_owner(mixed_grads)
         gm_rows = gm_flat.shape[1]
         out_flat, out_shape = lead(output_grad_t, 0)
-        joined = jnp.concatenate([gm_flat, out_flat.astype(jnp.bfloat16)], axis=1)
+        query_flat, query_shape = lead(query_grad, 0)
+        out_rows = out_flat.shape[1]
+        joined = jnp.concatenate(
+            [gm_flat, out_flat.astype(jnp.bfloat16), query_flat.astype(jnp.bfloat16)], axis=1
+        )
         arrived = lax.all_to_all(joined.reshape(-1, lanes), "dp", 0, 0, tiled=True)
         arrived = arrived.reshape(dp_count, -1, lanes)
-        output_part_t = jnp.sum(arrived[:, gm_rows:].astype(jnp.float32), axis=0).reshape(out_shape)
+        summed = jnp.sum(arrived[:, gm_rows:].astype(jnp.float32), axis=0)
+        output_part_t = summed[:out_rows].reshape(out_shape)
+        query_part = summed[out_rows:].reshape(query_shape)
         owned = (dp_count, all_windows, head_count, per)
         spectrum_in = spectra_in.reshape(owned + (2, head_size))
         gm_in = arrived[:, :gm_rows].reshape(owned + (2 * head_size,))
@@ -361,7 +367,7 @@
         )
     else:
         mixer_part, output_part_t = summed_over_dp([(mixer_full, 1), (output_grad_t, 0)])
-    (query_part,) = summed_over_dp([(query_grad, 0)])
+        (query_part,) = summed_over_dp([(query_grad, 0)])
     output_part = jnp.transpose(output_part_t)
     outer_part = jnp.transpose(outer_part_t)
     token_total = windows * length * dp_count

time: 463 us -> 454 us (0.981)
  waiting for transfers between devices: 141 us -> 115 us
  matrix products: 144 us -> 166 us
  starting transfers between devices: 40.8 us -> 30.2 us
  other arithmetic: 74.2 us -> 80.8 us
    ppermute x8, waiting for transfers between devices: 136 us -> 115 us  [swap(): return lax.ppermute(values, 'head', pairs)]
    dot_general x35, matrix products: 126 us -> 139 us  [product(): return jnp.einsum(form, left, right, preferred_element_type=jnp.float32)]
    dot_general x2, matrix products: 10.6 us -> 19.6 us  [trend_back(): jnp.einsum('wts,wtd->wsd', tiled, parts, preferred_element_type=jnp.float32)]
    unnamed x138 -> x118, local copies, waits for them, and re-layouts: 15.3 us -> 8.69 us
    all_to_all x1, starting transfers between devices: 11.5 us -> 5.66 us  [on_device(): arrived = lax.all_to_all(joined.reshape(-1, lanes), 'dp', 0, 0, tiled=True)]
    all_to_all x2 -> x1, waiting for transfers between devices: 5.75 us -> 0.01 us  [summed_over_dp(): lax.all_to_all(joined.astype(jnp.bfloat16).reshape(-1, lanes), 'dp', 0, 0...]
    all_to_all x2 -> x1, starting transfers between devices: 11.1 us -> 5.77 us  [summed_over_dp(): lax.all_to_all(joined.astype(jnp.bfloat16).reshape(-1, lanes), 'dp', 0, 0...]
  transfers between devices with their start and end apart: 12 -> 11, of which waited for: 8 -> 6; matrix products, arithmetic and copies ran while one was open for 43% -> 54% of each run, Pallas kernels for 0% -> 0%
where the time goes in v10:
time: 454 us; the launch traced here: 450 us
  matrix products  166 us (37%)
  waiting for transfers between devices  115 us (25%)
  other arithmetic  80.8 us (18%)
  local copies, waits for them, and re-layouts  55.1 us (12%)
  starting transfers between devices  30.2 us (7%)
    dot_general x35, matrix products, product(): return jnp.einsum(form, left, right, preferred_element_type=jnp.float32)  139 us
    ppermute x8, waiting for transfers between devices, swap(): return lax.ppermute(values, 'head', pairs)  115 us
    convert_element_type x1, other arithmetic, chunk_pass(): hidden = activated.astype(jnp.bfloat16)  30.4 us
    dot_general x2, matrix products, trend_back(): jnp.einsum('wts,wtd->wsd', tiled, parts, preferred_element_type=jnp.float32)  19.6 us
    ppermute x8, starting transfers between devices, swap(): return lax.ppermute(values, 'head', pairs)  12.9 us
  transfers between devices with their start and end apart: 11, of which 6 were waited for; matrix products, arithmetic and copies ran while one was open for 54% of the time, Pallas kernels for 0%

profile of v10, /device:TPU:0, one launch (start us, length us, event | category | flops | bytes accessed | tf_op | source)
XLA Modules:
  0.0 449.6 jit_solution(16572132197334182113)
XLA Ops:
  0.7 3.4 convert_element_type.209
  4.0 3.0 collective-permute-start
  7.8 3.2 convert_element_type.207
  11.1 2.1 fusion.172
  13.2 4.0 slice_negate_fusion
  17.2 24.6 %collective-permute-done = bf16[32,96,256]{2,1,0:T(8,128)(2,1)} collective-permute-done((bf16[32,96,256]{2,1,0:T(8,128)(2,1)}, bf16[32,96,256]{2,1,0:T(8,128)(2,1)}, u32[]{:S(2)}, u32[]{:S(2)}) %collective-permute-start) | collective-permute-done | bytes 1572896 | tf_op jit(solution)/shard_map/ppermute | solution.py:139
  41.7 3.2 fusion.89
  44.9 4.2 copy.142
  49.1 3.9 fusion.102
  53.1 2.2 fusion.105
  57.8 3.1 fusion.93
  67.5 4.6 %select_convert_fusion = (bf16[32,96,96]{2,1,0:T(8,128)(2,1)S(1)}, bf16[32,96,96]{2,1,0:T(8,128)(2,1)S(1)}) fusion(bf16[96,96]{1,0:T(8,128)(2,1)S(1)} %copy-done.48, bf16[96,96]{1,0:T(8,128)(2,1)S(1)} %copy-done.49, bf16[96,96]{1,0:T(8,128)(2,1)S(1)} %copy-done.50, bf16[96,96]{1,0:T(8,128)(2,1)S(1)} %copy-done.51, bf16[96,96]{1,0:T(8,128)(2,1)S(1)} %copy-done.52, ...), kind=kLoop, calls=%fused_computation.134 | loop fusion | flops 2949120 | bytes 1302528 | tf_op jit(solution)/shard_map/convert_element_type | solution.py:66
  73.0 28.2 %collective-permute-done.1 = bf16[32,96,256]{2,1,0:T(8,128)(2,1)S(1)} collective-permute-done((bf16[32,96,256]{2,1,0:T(8,128)(2,1)S(1)}, bf16[32,96,256]{2,1,0:T(8,128)(2,1)S(1)}, u32[]{:S(2)}, u32[]{:S(2)}) %collective-permute-start.1) | collective-permute-done | bytes 1572896 | tf_op jit(solution)/shard_map/ppermute | solution.py:139
  102.4 4.2 fusion.122
  108.0 15.8 %fusion.268 = (bf16[32,96,256]{2,1,0:T(8,128)(2,1)}, f32[32,96,256]{2,1,0:T(8,128)}) fusion(f32[32,96,256]{2,1,0:T(8,128)S(1)} %copy-done.21, bf16[32,96,256]{2,1,0:T(8,128)(2,1)S(1)} %get-tuple-element.56, bf16[32,96,256]{2,1,0:T(8,128)(2,1)S(1)} %get-tuple-element.57, bf16[32,96,256]{2,1,0:T(8,128)(2,1)S(1)} %get-tuple-element.55, ...), kind=kOutput, calls=%fused_computation.321 | convolution fusion | flops 474021888 | bytes 13172736 | tf_op jit(solution)/shard_map/wts,wtd->wsd/dot_general | solution.py:89
  124.4 2.9 convert_element_type.233
  128.5 8.1 %fusion.132 = f32[32,96,1024]{2,1,0:T(8,128)} fusion(bf16[32,96,256]{2,1,0:T(8,128)(2,1)} %get-tuple-element.90, bf16[1024,512]{1,0:T(8,128)(2,1)} %convert_element_type.235, s32[]{:T(128)S(6)} %select_n.186), kind=kOutput, calls=%fused_computation.164 | convolution fusion | flops 1610612736 | bytes 14680068 | tf_op jit(solution)/shard_map/wtd,fd->wtf/dot_general | solution.py:44
  141.5 5.9 %all-to-all-start.1 = ((bf16[16,384,128]{2,1,0:T(8,128)(2,1)}), bf16[16,384,128]{2,1,0:T(8,128)(2,1)}, u32[]{:S(2)}, u32[]{:S(2)}) async-start(bf16[16,384,128]{2,1,0:T(8,128)(2,1)} %copy.177), calls=%async_computation.1 | async-start | bytes 3145728 | tf_op jit(solution)/shard_map/all_to_all | solution.py:345
  147.4 3.4 fusion.141
  150.8 9.3 %convert_reduce_fusion.1 = (u32[96,1024]{1,0:T(8,128)S(1)}, u32[96,1024]{1,0:T(8,128)S(1)}, f32[32,96,1024]{2,1,0:T(8,128)}) fusion(f32[32,96,1024]{2,1,0:T(8,128)S(1)} %fusion.141, bf16[32,96,256]{2,1,0:T(8,128)(2,1)} %collective-permute-done.2, bf16[512,1024]{1,0:T(8,128)(2,1)S(1)} %copy-done.15, s32[]{:T(128)S(6)} %select_n.188), kind=kOutput, calls=%fused_computation.6 | convolution fusion | flops 1648164864 | bytes 28049412 | tf_op jit(solution)/shard_map/wtd,de->wte/dot_general | solution.py:44
  160.1 30.4 %multiply_convert_fusion = (bf16[32,96,1024]{2,1,0:T(8,128)(2,1)}, f32[32,96,1024]{2,1,0:T(8,128)}) fusion(f32[32,96,1024]{2,1,0:T(8,128)} %get-tuple-element.89, u32[96,1024]{1,0:T(8,128)S(1)} %get-tuple-element.22, u32[96,1024]{1,0:T(8,128)S(1)} %get-tuple-element.21), kind=kLoop, calls=%fused_computation.8 | loop fusion | flops 213909504 | bytes 32243712 | tf_op jit(solution)/shard_map/convert_element_type | solution.py:215
  190.5 18.3 %add_convert_fusion = bf16[32,96,1024]{2,1,0:T(8,128)(2,1)} fusion(f32[32,96,1024]{2,1,0:T(8,128)} %get-tuple-element.45, f32[32,96,1024]{2,1,0:T(8,128)} %fusion.132, f32[32,96,1024]{2,1,0:T(8,128)} %get-tuple-element.89, bf16[32,96,256]{2,1,0:T(8,128)(2,1)} %collective-permute-done.3, bf16[1024,512]{1,0:T(8,128)(2,1)} %convert_element_type.235, ...), kind=kOutput, calls=%fused_computation.7 | convolution fusion | flops 1657798656 | bytes 46137348 | tf_op jit(solution)/shard_map/wtd,fd->wtf/dot_general | solution.py:44
  208.8 5.9 %convolution_convert_fusion.3 = bf16[32,96,256]{2,1,0:T(8,128)(2,1)} fusion(bf16[32,96,1024]{2,1,0:T(8,128)(2,1)} %add_convert_fusion, bf16[512,1024]{1,0:T(8,128)(2,1)} %convert_element_type.233, s32[]{:T(128)S(6)} %select_n.193), kind=kOutput, calls=%fused_computation.115 | convolution fusion | flops 1611399168 | bytes 8388612 | tf_op jit(solution)/shard_map/wte,ed->wtd/dot_general | solution.py:44
  216.2 2.0 constant_dynamic-slice_fusion
  222.7 6.9 %reshape.219 = bf16[16,32,4,3,2,64]{5,4,3,2,1,0:T(2,128)(2,1)} reshape(bf16[16,384,128]{2,1,0:T(8,128)(2,1)} %all-to-all-done.1) | data formatting | bytes 3145728 | tf_op jit(solution)/shard_map/reshape | solution.py:360
  230.7 6.4 %fusion.111 = bf16[512,1024]{1,0:T(8,128)(2,1)} fusion(bf16[512,1024]{1,0:T(8,128)(2,1)} %broadcast.229.clone.1, s32[]{:T(128)S(6)} %select_n.186, bf16[32,96,256]{2,1,0:T(8,128)(2,1)} %get-tuple-element.87, bf16[32,96,1024]{2,1,0:T(8,128)(2,1)} %add_convert_fusion), kind=kOutput, calls=%fused_computation.150 | convolution fusion | flops 1610612736 | bytes 8912900 | tf_op jit(solution)/shard_map/wtd,wtf->df/dot_general | solution.py:44
  237.3 3.4 fusion.109
  241.7 10.0 %collective-permute-done.4 = bf16[32,96,256]{2,1,0:T(8,128)(2,1)} collective-permute-done((bf16[32,96,256]{2,1,0:T(8,128)(2,1)}, bf16[32,96,256]{2,1,0:T(8,128)(2,1)}, u32[]{:S(2)}, u32[]{:S(2)}) %collective-permute-start.4) | collective-permute-done | bytes 1572896 | tf_op jit(solution)/shard_map/ppermute | solution.py:139
  251.7 3.7 multiply_convert_fusion.1
  255.4 3.8 fusion.269
  260.7 4.1 fusion.110
  264.7 2.3 reshape_reshape.11
  267.0 5.9 %fusion.108 = bf16[512,1024]{1,0:T(8,128)(2,1)} fusion(bf16[512,1024]{1,0:T(8,128)(2,1)} %copy-done.17, s32[]{:T(128)S(6)} %select_n.188, bf16[32,96,256]{2,1,0:T(8,128)(2,1)} %collective-permute-done.3, bf16[32,96,1024]{2,1,0:T(8,128)(2,1)} %get-tuple-element.44), kind=kOutput, calls=%fused_computation.144 | convolution fusion | flops 1610612736 | bytes 8912900 | tf_op jit(solution)/shard_map/wtd,wtf->df/dot_general | solution.py:44
  272.9 2.3 reshape_reshape.12
  275.2 3.1 pad_maximum_fusion.1
  278.3 5.8 %all-to-all-start.2 = ((bf16[16,512,128]{2,1,0:T(8,128)(2,1)}), bf16[16,512,128]{2,1,0:T(8,128)(2,1)}, u32[]{:S(2)}, u32[]{:S(2)}) async-start(bf16[16,512,128]{2,1,0:T(8,128)(2,1)} %pad_maximum_fusion.1), calls=%async_computation.2 | async-start | bytes 4194304 | tf_op jit(solution)/shard_map/all_to_all | solution.py:322
  284.8 3.5 fusion.124
  288.4 2.0 fusion.163
  290.4 4.9 %collective-permute-done.5 = bf16[32,96,256]{2,1,0:T(8,128)(2,1)} collective-permute-done((bf16[32,96,256]{2,1,0:T(8,128)(2,1)}, bf16[32,96,256]{2,1,0:T(8,128)(2,1)}, u32[]{:S(2)}, u32[]{:S(2)}) %collective-permute-start.5) | collective-permute-done | bytes 1572896 | tf_op jit(solution)/shard_map/ppermute | solution.py:139
  295.3 3.3 add_convert_fusion.3
  298.6 4.0 copy.153
  302.6 3.9 fusion.99
  306.9 2.2 fusion.96
  312.2 2.9 fusion.123
  318.0 3.9 pad_maximum_fusion.3
  321.9 7.9 %fusion.90 = bf16[32,4,48,128]{3,0,2,1:T(8,128)(2,1)} fusion(bf16[32,4,48,128]{3,2,0,1:T(8,128)(2,1)} %pad_maximum_fusion.3, bf16[4,48,64,64]{3,2,1,0:T(8,128)(2,1)} %get-tuple-element.65, bf16[4,48,64,64]{3,2,1,0:T(8,128)(2,1)} %get-tuple-element.64, bf16[4,48,64,128]{3,2,1,0:T(8,128)(2,1)S(1)} %bitcast.252), kind=kOutput, calls=%fused_computation.137 | convolution fusion | flops 220987392 | bytes 9437184 | tf_op jit(solution)/shard_map/whmo,hmio->whmi/dot_general | solution.py:44
  329.8 2.8 fusion.264
  335.8 2.0 convolution_bitcast_fusion.4
  338.0 2.0 convolution_bitcast_fusion.5
  342.2 1.9 copy.173
  344.1 5.7 %all-to-all-start = ((bf16[16,512,128]{2,1,0:T(8,128)(2,1)}), bf16[16,512,128]{2,1,0:T(8,128)(2,1)}, u32[]{:S(2)}, u32[]{:S(2)}) async-start(bf16[16,512,128]{2,1,0:T(8,128)(2,1)} %copy.173), calls=%async_computation | async-start | bytes 4194304 | tf_op jit(solution)/shard_map/all_to_all | solution.py:354
  349.8 5.8 %convolution_convert_fusion.4 = bf16[32,96,256]{2,1,0:T(8,128)(2,1)} fusion(bf16[32,96,1024]{2,1,0:T(8,128)(2,1)} %get-tuple-element.44, bf16[1024,512]{1,0:T(8,128)(2,1)S(1)} %copy-done.14, s32[]{:T(128)S(6)} %select_n.193), kind=kOutput, calls=%fused_computation.116 | convolution fusion | flops 1611399168 | bytes 8388612 | tf_op jit(solution)/shard_map/wte,ed->wtd/dot_general | solution.py:44
  357.1 2.0 convolution_convert_fusion.1
  359.1 2.5 fusion.170
  361.6 2.1 convert_reduce_fusion.2
  368.9 23.6 %collective-permute-done.6 = bf16[32,96,256]{2,1,0:T(8,128)(2,1)} collective-permute-done((bf16[32,96,256]{2,1,0:T(8,128)(2,1)}, bf16[32,96,256]{2,1,0:T(8,128)(2,1)}, u32[]{:S(2)}, u32[]{:S(2)}) %collective-permute-start.6) | collective-permute-done | bytes 1572896 | tf_op jit(solution)/shard_map/ppermute | solution.py:139
  394.0 6.7 %fusion.261 = (bf16[32,96,256]{2,1,0:T(8,128)(2,1)S(1)}, bf16[32,96,256]{2,1,0:T(8,128)(2,1)S(1)}, bf16[32,96,256]{2,1,0:T(8,128)(2,1)S(1)}, f32[32,96,256]{2,1,0:T(8,128)S(1)}) fusion(bf16[32,96,256]{2,1,0:T(8,128)(2,1)} %collective-permute-done.6, bf16[32,96,1024]{2,1,0:T(8,128)(2,1)} %get-tuple-element.44, bf16[1024,512]{1,0:T(8,128)(2,1)} %convert_element_type.235, ...), kind=kOutput, calls=%fused_computation.314 | convolution fusion | flops 1620049920 | bytes 22556676 | tf_op jit(solution)/shard_map/wte,ed->wtd/dot_general | solution.py:44
  400.7 3.6 multiply_subtract_fusion
  404.4 24.1 %collective-permute-done.7 = bf16[32,96,256]{2,1,0:T(8,128)(2,1)S(1)} collective-permute-done((bf16[32,96,256]{2,1,0:T(8,128)(2,1)}, bf16[32,96,256]{2,1,0:T(8,128)(2,1)S(1)}, u32[]{:S(2)}, u32[]{:S(2)}) %collective-permute-start.7) | collective-permute-done | bytes 1572896 | tf_op jit(solution)/shard_map/ppermute | solution.py:139
  428.5 2.6 add_add_fusion
  435.5 2.2 copy_negate_fusion
  437.7 2.3 copy.181
  441.3 2.4 maximum_bitcast_fusion.2
  446.5 2.1 multiply_add_fusion
  (185 shorter events, 59.4 us)
Async XLA Ops:
  0.7 6.4 %copy-start.33 = (f32[512,256]{1,0:T(8,128)S(1)}, f32[512,256]{1,0:T(8,128)}, u32[]{:S(2)}) copy-start(f32[512,256]{1,0:T(8,128)} %param.33) | copy-start | bytes 1572868
  4.0 37.7 %collective-permute-start = (bf16[32,96,256]{2,1,0:T(8,128)(2,1)}, bf16[32,96,256]{2,1,0:T(8,128)(2,1)}, u32[]{:S(2)}, u32[]{:S(2)}) collective-permute-start(bf16[32,96,256]{2,1,0:T(8,128)(2,1)} %convert_element_type.209), channel_id=1, source_target_pairs={{0,1},{1,0},{2,3},{3,2},{4,5},{5,4},{6,7},{7,6},{8,9},{9,8},{10,11... | collective-permute-start | bytes 4718600 | tf_op jit(solution)/shard_map/ppermute | solution.py:139
  7.7 3.3 copy-start.28
  7.7 3.3 copy-start.36
  13.2 28.6 %copy-start.25 = (bf16[512,256]{1,0:T(8,128)(2,1)S(1)}, bf16[512,256]{1,0:T(8,128)(2,1)}, u32[]{:S(2)}) copy-start(bf16[512,256]{1,0:T(8,128)(2,1)} %convert_element_type.208) | copy-start | bytes 786436
  49.1 4.0 copy-start.1
  53.0 3.1 copy-start.4
  53.1 3.4 copy-start.23
  55.3 2.5 copy-start.22
  64.5 3.0 copy-start.47
  64.5 3.0 copy-start.48
  64.5 3.0 copy-start.49
  64.5 3.0 copy-start.50
  64.5 3.0 copy-start.51
  64.5 3.0 copy-start.52
  64.8 36.5 %copy-start.2 = (bf16[32,96,4,64]{1,3,2,0:T(8,128)(2,1)}, bf16[32,96,4,64]{1,3,2,0:T(8,128)(2,1)S(1)}, u32[]{:S(2)}) copy-start(bf16[32,96,4,64]{1,3,2,0:T(8,128)(2,1)S(1)} %copy.148) | copy-start | bytes 4718596
  64.8 7.4 %copy-start.21 = (f32[32,96,256]{2,1,0:T(8,128)S(1)}, f32[32,96,256]{2,1,0:T(8,128)}, u32[]{:S(2)}) copy-start(f32[32,96,256]{2,1,0:T(8,128)} %param.30) | copy-start | bytes 9437188
  65.6 35.6 %collective-permute-start.1 = (bf16[32,96,256]{2,1,0:T(8,128)(2,1)S(1)}, bf16[32,96,256]{2,1,0:T(8,128)(2,1)S(1)}, u32[]{:S(2)}, u32[]{:S(2)}) collective-permute-start(bf16[32,96,256]{2,1,0:T(8,128)(2,1)S(1)} %convolution_convert_fusion.5), channel_id=1, source_target_pairs={{0,1},{1,0},{2,3},{3,2},{4,5},{5,4},{6,7},{7,6},{8,9},{9,8},{10,11... | collective-permute-start | bytes 4718600 | tf_op jit(solution)/shard_map/ppermute | solution.py:139
  67.5 5.6 %copy-start.41 = (f32[32,96]{1,0:T(8,128)}, f32[32,96]{1,0:T(8,128)S(1)}, u32[]{:S(2)}) copy-start(f32[32,96]{1,0:T(8,128)S(1)} %get-tuple-element.38) | copy-start | bytes 36868
  67.5 34.9 %copy-start.37 = (f32[32,96]{1,0:T(8,128)}, f32[32,96]{1,0:T(8,128)S(1)}, u32[]{:S(2)}) copy-start(f32[32,96]{1,0:T(8,128)S(1)} %get-tuple-element.78) | copy-start | bytes 36868
  72.1 30.3 %copy-start.31 = (bf16[32,96,96]{2,1,0:T(8,128)(2,1)}, bf16[32,96,96]{2,1,0:T(8,128)(2,1)S(1)}, u32[]{:S(2)}) copy-start(bf16[32,96,96]{2,1,0:T(8,128)(2,1)S(1)} %get-tuple-element.75) | copy-start | bytes 1769476
  72.1 35.9 %copy-start.29 = (bf16[32,96,96]{2,1,0:T(8,128)(2,1)}, bf16[32,96,96]{2,1,0:T(8,128)(2,1)S(1)}, u32[]{:S(2)}) copy-start(bf16[32,96,96]{2,1,0:T(8,128)(2,1)S(1)} %get-tuple-element.74) | copy-start | bytes 1769476
  72.2 29.1 %copy-start.10 = (f32[32,96,256]{2,1,0:T(8,128)S(1)}, f32[32,96,256]{2,1,0:T(8,128)}, u32[]{:S(2)}) copy-start(f32[32,96,256]{2,1,0:T(8,128)} %param.29) | copy-start | bytes 9437188
  102.4 4.2 copy-start.12
  106.6 44.3 %collective-permute-start.2 = (bf16[32,96,256]{2,1,0:T(8,128)(2,1)}, bf16[32,96,256]{2,1,0:T(8,128)(2,1)}, u32[]{:S(2)}, u32[]{:S(2)}) collective-permute-start(bf16[32,96,256]{2,1,0:T(8,128)(2,1)} %get-tuple-element.87), channel_id=1, source_target_pairs={{0,1},{1,0},{2,3},{3,2},{4,5},{5,4},{6,7},{7,6},{8,9},{9,8},{10,11... | collective-permute-start | bytes 4718600 | tf_op jit(solution)/shard_map/ppermute | solution.py:139
  123.9 66.6 %collective-permute-start.3 = (bf16[32,96,256]{2,1,0:T(8,128)(2,1)}, bf16[32,96,256]{2,1,0:T(8,128)(2,1)}, u32[]{:S(2)}, u32[]{:S(2)}) collective-permute-start(bf16[32,96,256]{2,1,0:T(8,128)(2,1)} %get-tuple-element.90), channel_id=1, source_target_pairs={{0,1},{1,0},{2,3},{3,2},{4,5},{5,4},{6,7},{7,6},{8,9},{9,8},{10,11... | collective-permute-start | bytes 4718600 | tf_op jit(solution)/shard_map/ppermute | solution.py:139
  124.4 2.9 copy-start.18
  128.5 8.1 %copy-start.7 = (bf16[32,4,48,64]{3,2,0,1:T(8,128)(2,1)S(1)}, bf16[32,4,48,64]{3,2,0,1:T(8,128)(2,1)}, u32[]{:S(2)}) copy-start(bf16[32,4,48,64]{3,2,0,1:T(8,128)(2,1)} %copy-done.6) | copy-start | bytes 2359300
  136.6 1.4 copy-start.5
  141.5 81.2 %all-to-all-start.1 = ((bf16[16,384,128]{2,1,0:T(8,128)(2,1)}), bf16[16,384,128]{2,1,0:T(8,128)(2,1)}, u32[]{:S(2)}, u32[]{:S(2)}) async-start(bf16[16,384,128]{2,1,0:T(8,128)(2,1)} %copy.177), calls=%async_computation.1 | async-start | bytes 3145728 | tf_op jit(solution)/shard_map/all_to_all | solution.py:345
  147.4 3.4 copy-start.15
  214.7 37.0 %collective-permute-start.4 = (bf16[32,96,256]{2,1,0:T(8,128)(2,1)}, bf16[32,96,256]{2,1,0:T(8,128)(2,1)}, u32[]{:S(2)}, u32[]{:S(2)}) collective-permute-start(bf16[32,96,256]{2,1,0:T(8,128)(2,1)} %convolution_convert_fusion.3), channel_id=1, source_target_pairs={{0,1},{1,0},{2,3},{3,2},{4,5},{5,4},{6,7},{7,6},{8,9},{9,8},{10,11... | collective-permute-start | bytes 4718600 | tf_op jit(solution)/shard_map/ppermute | solution.py:139
  229.6 7.6 %slice-start = ((s8[6291456]{0:T(1024)(128)(4,1)}), s8[4194304]{0:T(1024)(128)(4,1)S(1)}, s32[]{:S(2)}) async-start(s8[6291456]{0:T(1024)(128)(4,1)} %bitcast.246), calls=%async_computation.3 | async-start | bytes 8388608
  230.7 6.6 %slice-start.1 = ((s8[6291456]{0:T(1024)(128)(4,1)}), s8[2097152]{0:T(1024)(128)(4,1)S(1)}, s32[]{:S(2)}) async-start(s8[6291456]{0:T(1024)(128)(4,1)} %bitcast.246), calls=%async_computation.4 | async-start | bytes 4194304
  237.1 14.6 %slice-start.2 = ((s8[6291456]{0:T(1024)(128)(4,1)}), s8[4194304]{0:T(1024)(128)(4,1)S(1)}, s32[]{:S(2)}) async-start(s8[6291456]{0:T(1024)(128)(4,1)} %bitcast.248), calls=%async_computation.5 | async-start | bytes 8388608
  237.2 14.4 %slice-start.3 = ((s8[6291456]{0:T(1024)(128)(4,1)}), s8[2097152]{0:T(1024)(128)(4,1)S(1)}, s32[]{:S(2)}) async-start(s8[6291456]{0:T(1024)(128)(4,1)} %bitcast.248), calls=%async_computation.6 | async-start | bytes 4194304
  237.3 14.4 %copy-start.16 = (bf16[512,1024]{1,0:T(8,128)(2,1)S(1)}, bf16[512,1024]{1,0:T(8,128)(2,1)}, u32[]{:S(2)}) copy-start(bf16[512,1024]{1,0:T(8,128)(2,1)} %convert_element_type.233) | copy-start | bytes 3145732
  237.3 14.4 %copy-start.19 = (f32[32,96,256]{2,1,0:T(8,128)S(1)}, f32[32,96,256]{2,1,0:T(8,128)}, u32[]{:S(2)}) copy-start(f32[32,96,256]{2,1,0:T(8,128)} %get-tuple-element.91) | copy-start | bytes 9437188
  237.3 14.4 %copy-start.38 = (f32[32,96]{1,0:T(8,128)S(1)}, f32[32,96]{1,0:T(8,128)}, u32[]{:S(2)}) copy-start(f32[32,96]{1,0:T(8,128)} %copy-done.37) | copy-start | bytes 36868
  251.7 3.7 copy-start.32
  259.2 36.1 %collective-permute-start.5 = (bf16[32,96,256]{2,1,0:T(8,128)(2,1)}, bf16[32,96,256]{2,1,0:T(8,128)(2,1)}, u32[]{:S(2)}, u32[]{:S(2)}) collective-permute-start(bf16[32,96,256]{2,1,0:T(8,128)(2,1)} %get-tuple-element.93), channel_id=1, source_target_pairs={{0,1},{1,0},{2,3},{3,2},{4,5},{5,4},{6,7},{7,6},{8,9},{9,8},{10,11... | collective-permute-start | bytes 4718600 | tf_op jit(solution)/shard_map/ppermute | solution.py:139
  278.3 65.7 %all-to-all-start.2 = ((bf16[16,512,128]{2,1,0:T(8,128)(2,1)}), bf16[16,512,128]{2,1,0:T(8,128)(2,1)}, u32[]{:S(2)}, u32[]{:S(2)}) async-start(bf16[16,512,128]{2,1,0:T(8,128)(2,1)} %pad_maximum_fusion.1), calls=%async_computation.2 | async-start | bytes 4194304 | tf_op jit(solution)/shard_map/all_to_all | solution.py:322
  302.5 4.4 copy-start
  306.5 2.6 copy-start.8
  309.5 2.7 copy-start.3
  344.1 5.7 %copy-start.14 = (bf16[1024,512]{1,0:T(8,128)(2,1)S(1)}, bf16[1024,512]{1,0:T(8,128)(2,1)}, u32[]{:S(2)}) copy-start(bf16[1024,512]{1,0:T(8,128)(2,1)} %convert_element_type.235) | copy-start | bytes 3145732
  344.1 87.1 %all-to-all-start = ((bf16[16,512,128]{2,1,0:T(8,128)(2,1)}), bf16[16,512,128]{2,1,0:T(8,128)(2,1)}, u32[]{:S(2)}, u32[]{:S(2)}) async-start(bf16[16,512,128]{2,1,0:T(8,128)(2,1)} %copy.173), calls=%async_computation | async-start | bytes 4194304 | tf_op jit(solution)/shard_map/all_to_all | solution.py:354
  349.7 7.3 %copy-start.26 = (bf16[512,256]{1,0:T(8,128)(2,1)S(1)}, bf16[512,256]{1,0:T(8,128)(2,1)}, u32[]{:S(2)}) copy-start(bf16[512,256]{1,0:T(8,128)(2,1)} %convert_element_type.208) | copy-start | bytes 786436
  355.5 37.0 %collective-permute-start.6 = (bf16[32,96,256]{2,1,0:T(8,128)(2,1)}, bf16[32,96,256]{2,1,0:T(8,128)(2,1)}, u32[]{:S(2)}, u32[]{:S(2)}) collective-permute-start(bf16[32,96,256]{2,1,0:T(8,128)(2,1)} %convolution_convert_fusion.4), channel_id=1, source_target_pairs={{0,1},{1,0},{2,3},{3,2},{4,5},{5,4},{6,7},{7,6},{8,9},{9,8},{10,11... | collective-permute-start | bytes 4718600 | tf_op jit(solution)/shard_map/ppermute | solution.py:139
  361.6 32.4 %copy-start.13 = (f32[32,96,256]{2,1,0:T(8,128)S(1)}, f32[32,96,256]{2,1,0:T(8,128)}, u32[]{:S(2)}) copy-start(f32[32,96,256]{2,1,0:T(8,128)} %copy-done.12) | copy-start | bytes 9437188
  361.6 32.4 %copy-start.39 = (f32[32,96]{1,0:T(8,128)S(1)}, f32[32,96]{1,0:T(8,128)}, u32[]{:S(2)}) copy-start(f32[32,96]{1,0:T(8,128)} %copy-done.37) | copy-start | bytes 36868
  392.5 36.0 %collective-permute-start.7 = (bf16[32,96,256]{2,1,0:T(8,128)(2,1)}, bf16[32,96,256]{2,1,0:T(8,128)(2,1)S(1)}, u32[]{:S(2)}, u32[]{:S(2)}) collective-permute-start(bf16[32,96,256]{2,1,0:T(8,128)(2,1)} %convolution_convert_fusion.1), channel_id=1, source_target_pairs={{0,1},{1,0},{2,3},{3,2},{4,5},{5,4},{6,7},{7,6},{8,9},{9,8},{10,11... | collective-permute-start | bytes 4718600 | tf_op jit(solution)/shard_map/ppermute | solution.py:139
  394.0 6.7 %copy-start.30 = (bf16[32,96,96]{2,1,0:T(8,128)(2,1)S(1)}, bf16[32,96,96]{2,1,0:T(8,128)(2,1)}, u32[]{:S(2)}) copy-start(bf16[32,96,96]{2,1,0:T(8,128)(2,1)} %copy-done.29) | copy-start | bytes 1769476
  394.0 6.7 %copy-start.42 = (f32[32,96]{1,0:T(8,128)S(1)}, f32[32,96]{1,0:T(8,128)}, u32[]{:S(2)}) copy-start(f32[32,96]{1,0:T(8,128)} %copy-done.41) | copy-start | bytes 36868
  400.7 27.8 %copy-start.11 = (f32[32,96,256]{2,1,0:T(8,128)S(1)}, f32[32,96,256]{2,1,0:T(8,128)}, u32[]{:S(2)}) copy-start(f32[32,96,256]{2,1,0:T(8,128)} %fusion.170) | copy-start | bytes 9437188
  400.7 27.8 %copy-start.24 = (f32[32,96,256]{2,1,0:T(8,128)S(1)}, f32[32,96,256]{2,1,0:T(8,128)}, u32[]{:S(2)}) copy-start(f32[32,96,256]{2,1,0:T(8,128)} %get-tuple-element.94) | copy-start | bytes 9437188
  440.0 3.7 copy-start.27
  441.3 2.4 copy-start.20
  443.7 1.4 copy-start.43
  443.8 2.8 copy-start.34
  443.8 2.8 copy-start.35
  443.8 4.9 %copy-start.40 = (f32[256,32]{0,1:T(8,128)S(1)}, f32[256,32]{0,1:T(8,128)}, u32[]{:S(2)}) copy-start(f32[256,32]{0,1:T(8,128)} %copy.203) | copy-start | bytes 98308
  443.8 4.9 %copy-start.45 = (f32[256,32]{0,1:T(8,128)S(1)}, f32[256,32]{0,1:T(8,128)}, u32[]{:S(2)}) copy-start(f32[256,32]{0,1:T(8,128)} %param.43) | copy-start | bytes 98308
  443.8 4.9 %copy-start.46 = (f32[256,32]{0,1:T(8,128)S(1)}, f32[256,32]{0,1:T(8,128)}, u32[]{:S(2)}) copy-start(f32[256,32]{0,1:T(8,128)} %param.42) | copy-start | bytes 98308
  (4 other events, 4.8 us)
